TPU v7x, 256 devices: a whole 4x4x8 slice. The times are simulated.
256 devices in a mesh: group: 32 (over x, z_lo, core), tp: 8 (over y, z_hi).
Axes of the slice: x: 4, y: 4, z: 8 (z_hi: 2, z_lo: 4; z = z_hi * 4 + z_lo), core: 2. Of those that a mesh axis runs over, the one named last changes fastest.
Arguments:
- prefill_x: bfloat16 [16384, 4096], P('group', 'tp'), may hold values from -6 to 6
- decode_x: bfloat16 [128, 4096], P('group', 'tp'), may hold values from -6 to 6
- ln_gain: float32 [4096], replicated, may hold values from 0.1 to 1.9
- ln_bias: float32 [4096], replicated, may hold values from -3 to 3
- qkv_weight: bfloat16 [4096, 3, 2048], P(None, None, 'tp'), may hold values from -0.09375 to 0.09375
- qkv_bias: float32 [3, 2048], P(None, 'tp'), may hold values from -3 to 3
- prior_cache: bfloat16 [32, 2, 512, 2048], P('group', None, None, 'tp'), may hold values from -144 to 144, as said below
- prefill_offset: int32 [32], P('group'), may hold values from 0 to 512, as said below
- home_cache: bfloat16 [128, 2, 256, 2048], P('group', None, None, 'tp'), may hold values from -144 to 144, as said below
- piece_len: int32 [128, 3], P('group'), may hold values from 0 to 1024, as said below
- side_store: bfloat16 [256, 2, 1024, 2048], P('group', None, None, 'tp'), may hold values from -144 to 144, as said below
Outputs:
- prefill_out: bfloat16 [16384, 2048], P('group', 'tp')
- decode_out: bfloat16 [128, 2048], P('group', 'tp')
Inputs may be any that keep to these rules, and one draw needn't show every extreme that they name: `prior_cache`: keys already rotated. `prefill_offset`: the largest value, 512, and 0 occur in every draw. `home_cache`: keys already rotated. `piece_len`: columns 0 and 2 are at most 1024 and reach it in every draw, 0 meaning no piece on that side; column 1 is 1 to 256 and reaches 256 in every draw. `side_store`: keys already rotated.
All inputs are finite; a program needn't handle non-finite values.
Results may differ from a plain program's by a relative error of at most 0.019.
The roundings to bfloat16 on the way count: a program that leaves them out, or rounds other values in their place, can miss the bound.
Values may be sent and summed in bfloat16 or wider, within the bound.
No kernel may reach another device: no remote copies, remote signals or barrier semaphores. Data moves between devices by JAX's collectives and lax.ppermute only.
A program may use at most 128 MiB of HBM per device.

v0:
```python
from functools import reduce
import math

import jax
import jax.numpy as jnp
from jax import lax
from jax.sharding import PartitionSpec as P

HD = 128
ROT = 32


EPS = 1e-05
NEG = -1e30


def with_halo(block, sides, width):
    for axis, dim in sides:
        count = lax.axis_size(axis)
        forward = [(i, i + 1) for i in range(count - 1)]
        forward.append((count - 1, 0))
        backward = [(target, source) for source, target in forward]
        low = lax.ppermute(
            lax.slice_in_dim(block, block.shape[dim] - width, None, axis=dim), axis, forward
        )
        high = lax.ppermute(lax.slice_in_dim(block, 0, width, axis=dim), axis, backward)
        block = jnp.concatenate([low, block, high], axis=dim)
    return block


def layer_norm(rows, gain, shift):
    rows = rows.astype(jnp.float32)
    middle = jnp.mean(rows, axis=-1, keepdims=True)
    centred = rows - middle
    spread = jnp.mean(centred * centred, axis=-1, keepdims=True)
    return (centred * lax.rsqrt(spread + EPS) * gain + shift).astype(jnp.bfloat16)


def rotate(vectors, positions):
    half = ROT // 2
    steps = jnp.arange(half, dtype=jnp.float32) * (2.0 / ROT)
    frequency = jnp.exp(-math.log(10000.0) * steps)
    angle = positions.astype(jnp.float32)[:, None] * frequency[None, :]
    cosine = jnp.cos(angle)[:, None, :]
    sine = jnp.sin(angle)[:, None, :]
    first = vectors[..., :half]
    second = vectors[..., half:ROT]
    return jnp.concatenate(
        [first * cosine - second * sine, second * cosine + first * sine, vectors[..., ROT:]],
        axis=-1,
    )


def project(normed, weight, bias, positions):
    count = normed.shape[0]
    width = weight.shape[2]
    mixed = jnp.dot(
        normed, weight.reshape(weight.shape[0], 3 * width), preferred_element_type=jnp.float32
    )
    mixed = (mixed + bias.reshape(1, 3 * width)).reshape(count, 3, width // HD, HD)
    query = rotate(mixed[:, 0], positions).astype(jnp.bfloat16)
    fresh_key = rotate(mixed[:, 1], positions).astype(jnp.bfloat16)
    fresh_value = mixed[:, 2].astype(jnp.bfloat16)
    return (query, fresh_key, fresh_value)


def attend_rows(query, keys, values, live):
    scores = jnp.einsum("qhd,khd->hqk", query, keys, preferred_element_type=jnp.float32) * (
        1.0 / math.sqrt(HD)
    )
    masked = jnp.where(live[None], scores, NEG)
    highest = jnp.max(masked, axis=2, keepdims=True)
    weights = jnp.where(live[None], jnp.exp(masked - highest), 0.0)
    total = jnp.sum(weights, axis=2)
    mixed = jnp.einsum(
        "hqk,khd->qhd", weights.astype(jnp.bfloat16), values, preferred_element_type=jnp.float32
    )
    return (mixed / jnp.transpose(total)[:, :, None]).astype(jnp.bfloat16)


def prefill_attend(query, fresh_key, fresh_value, prior, offset):
    count, heads = (query.shape[0], query.shape[1])
    capacity = prior.shape[1]
    keys = jnp.concatenate([prior[0].reshape(capacity, heads, HD), fresh_key], axis=0)
    values = jnp.concatenate([prior[1].reshape(capacity, heads, HD), fresh_value], axis=0)
    block = min(count, 512)

    def one_block(start):
        places = start + jnp.arange(block, dtype=jnp.int32)
        live = jnp.concatenate(
            [
                jnp.broadcast_to(jnp.arange(capacity)[None, :] < offset, (block, capacity)),
                jnp.arange(count)[None, :] <= places[:, None],
            ],
            axis=1,
        )
        return attend_rows(query, keys, values, live)

    starts = jnp.arange(count // block, dtype=jnp.int32) * block
    return lax.map(one_block, starts).reshape(count, heads * HD)


def piece_partial(query, keys, values, live):
    scores = jnp.einsum("hd,khd->hk", query, keys, preferred_element_type=jnp.float32) * (
        1.0 / math.sqrt(HD)
    )
    masked = jnp.where(live[None], scores, NEG)
    highest = jnp.max(masked, axis=1)
    weights = jnp.where(live[None], jnp.exp(masked - highest[:, None]), 0.0)
    total = jnp.sum(weights, axis=1)
    summed = jnp.einsum(
        "hk,khd->hd", weights.astype(jnp.bfloat16), values, preferred_element_type=jnp.float32
    )
    return (highest, total, summed)


def piece_batch(query, store, lengths):
    count, capacity = (store.shape[0], store.shape[2])
    heads = query.shape[1]
    keys = store[:, 0].reshape(count, capacity, heads, HD)
    values = store[:, 1].reshape(count, capacity, heads, HD)
    live = jnp.arange(capacity)[None, :] < lengths[:, None]
    return jax.vmap(piece_partial)(query, keys, values, live)


def home_partial(query, fresh_key, fresh_value, cache, lengths):
    count, capacity = (cache.shape[0], cache.shape[2])
    heads = query.shape[1]
    keys = jnp.concatenate(
        [cache[:, 0].reshape(count, capacity, heads, HD), fresh_key[:, None]], axis=1
    )
    values = jnp.concatenate(
        [cache[:, 1].reshape(count, capacity, heads, HD), fresh_value[:, None]], axis=1
    )
    live = jnp.concatenate(
        [jnp.arange(capacity)[None, :] < lengths[:, None], jnp.ones((count, 1), jnp.bool_)], axis=1
    )
    return jax.vmap(piece_partial)(query, keys, values, live)


def combine(parts):
    highest = reduce(jnp.maximum, [part[0] for part in parts])
    factors = [jnp.exp(part[0] - highest) for part in parts]
    upper = reduce(jnp.add, [factor[:, :, None] * part[2] for factor, part in zip(factors, parts)])
    lower = reduce(jnp.add, [factor * part[1] for factor, part in zip(factors, parts)])
    return (upper / lower[:, :, None]).astype(jnp.bfloat16)


def local(
    prefill_x,
    decode_x,
    ln_gain,
    ln_bias,
    qkv_weight,
    qkv_bias,
    prior_cache,
    prefill_offset,
    home_cache,
    piece_len,
    side_store,
):
    whole_prefill, whole_decode = (
        lax.all_gather(prefill_x, "tp", axis=1, tiled=True),
        lax.all_gather(decode_x, "tp", axis=1, tiled=True),
    )
    normed = jnp.concatenate(
        [layer_norm(whole_prefill, ln_gain, ln_bias), layer_norm(whole_decode, ln_gain, ln_bias)],
        axis=0,
    )
    count = prefill_x.shape[0]
    requests = decode_x.shape[0]
    positions = jnp.concatenate(
        [
            prefill_offset[0] + jnp.arange(count, dtype=jnp.int32),
            piece_len[:, 0] + piece_len[:, 1] + piece_len[:, 2],
        ],
        axis=0,
    )
    query, fresh_key, fresh_value = project(normed, qkv_weight, qkv_bias, positions)
    own_query = query[count:]
    home_parts = home_partial(
        own_query, fresh_key[count:], fresh_value[count:], home_cache, piece_len[:, 1]
    )
    extended = with_halo(side_store, (("group", 0),), requests)
    left_parts = piece_batch(own_query, extended[:requests], piece_len[:, 0])
    right_parts = piece_batch(own_query, extended[3 * requests :], piece_len[:, 2])
    prefill_out = prefill_attend(
        query[:count], fresh_key[:count], fresh_value[:count], prior_cache[0], prefill_offset[0]
    )
    decode_out = combine([left_parts, home_parts, right_parts]).reshape(requests, -1)
    return (prefill_out, decode_out)


def solution(mesh):
    return jax.shard_map(
        local,
        mesh=mesh,
        in_specs=(
            P("group", "tp"),
            P("group", "tp"),
            P(),
            P(),
            P(None, None, "tp"),
            P(None, "tp"),
            P("group", None, None, "tp"),
            P("group"),
            P("group", None, None, "tp"),
            P("group", None),
            P("group", None, None, "tp"),
        ),
        out_specs=(P("group", "tp"), P("group", "tp")),
        check_vma=False,
    )
```

profile of v0, /device:TPU:38, one launch (start us, length us, event | category | flops | bytes accessed | tf_op | source)
XLA Modules:
  0.0 269.2 jit_solution(1345875707312525972)
XLA Ops:
  7.2 0.7 all-gather.2.cloned.1.call-update
  7.9 5.9 %fusion.81 = (bf16[4,2,1024,256]{3,2,1,0:T(8,128)(2,1)}, bf16[4,2,1024,256]{3,2,1,0:T(8,128)(2,1)}) fusion(bf16[8,2,1024,256]{3,2,1,0:T(8,128)(2,1)} %param.21), kind=kLoop, calls=%fused_computation.126 | loop fusion | bytes 16777216 | tf_op jit(solution)/shard_map/slice | solution.py:24
  13.8 1.7 collective-permute-start.1
  16.3 0.2 slice_reduce_fusion.1
  16.5 0.2 multiply_cosine_fusion
  16.7 0.1 copy.48
  16.9 0.9 copy.49
  17.8 0.9 copy.44
  18.6 0.1 copy.79
  18.8 0.8 copy.52
  19.7 0.1 reshape_squeeze.30
  19.8 0.1 reshape_squeeze.27
  20.0 8.8 %copy.45 = bf16[4096,3,256]{0,2,1:T(8,128)(2,1)} copy(bf16[4096,3,256]{2,0,1:T(8,128)(2,1)} %param.15) | data formatting | bytes 12582912 | tf_op args[4]
  28.9 177.0 %all_gather.7 = bf16[4,4096]{1,0:T(4,128)(2,1)S(1)} all-gather(bf16[4,512]{1,0:T(4,128)(2,1)S(1)} %copy-done.13), channel_id=1, replica_groups=mesh['group'=32,'tp'=8] {'tp'}, dimensions={1}, use_global_device_ids=true | all-gather | bytes 36864 | tf_op jit(solution)/shard_map/all_gather | solution.py:164
  206.0 0.1 convert_reduce_fusion.1
  206.1 0.2 fusion.47
  206.5 1.0 pad_add_fusion
  207.6 0.1 fusion.50
  207.7 3.8 %fusion.82 = (bf16[4,1,1024,256]{3,2,1,0:T(8,128)(2,1)}, bf16[4,1,1024,256]{3,2,1,0:T(8,128)(2,1)S(1)}) fusion(bf16[4,2,1024,256]{3,2,1,0:T(8,128)(2,1)} %collective-permute-done), kind=kLoop, calls=%fused_computation.127 | loop fusion | bytes 8388608 | tf_op jit(solution)/shard_map/slice | solution.py:121
  211.5 4.0 %reshape_squeeze.29 = bf16[4,1024,2,128]{3,2,1,0:T(2,128)(2,1)} reshape(bf16[4,1,1024,256]{3,2,1,0:T(8,128)(2,1)} %get-tuple-element.38) | data formatting | bytes 4194304 | tf_op jit(solution)/shard_map/reshape;squeeze | solution.py:121
  215.5 2.5 copy.76
  218.0 3.9 %fusion.83 = (bf16[4,1,1024,256]{3,2,1,0:T(8,128)(2,1)}, bf16[4,1,1024,256]{3,2,1,0:T(8,128)(2,1)S(1)}) fusion(bf16[4,2,1024,256]{3,2,1,0:T(8,128)(2,1)} %collective-permute-done.1), kind=kLoop, calls=%fused_computation.128 | loop fusion | bytes 8388608 | tf_op jit(solution)/shard_map/slice | solution.py:121
  221.8 4.0 %reshape_squeeze.31 = bf16[4,1024,2,128]{3,2,1,0:T(2,128)(2,1)} reshape(bf16[4,1,1024,256]{3,2,1,0:T(8,128)(2,1)} %get-tuple-element.40) | data formatting | bytes 4194304 | tf_op jit(solution)/shard_map/reshape;squeeze | solution.py:121
  225.8 2.4 copy.77
  228.3 3.0 %convert_reduce_fusion = f32[512]{0:T(512)S(1)} fusion(bf16[512,4096]{1,0:T(8,128)(2,1)} %all-gather.2.cloned.1.call-done), kind=kLoop, calls=%fused_computation.2 | loop fusion | flops 4193792 | bytes 4196352 | tf_op jit(solution)/shard_map/reduce_sum | solution.py:33
  231.2 0.5 copy-done
  231.7 1.2 fusion.3
  233.0 2.3 fusion.6
  235.3 4.7 %fusion.21 = f32[516,768]{1,0:T(8,128)} fusion(bf16[4096,768]{0,1:T(8,128)(2,1)S(1)} %bitcast.89, bf16[4,4096]{1,0:T(4,128)(2,1)S(1)} %fusion.50, bf16[512,4096]{1,0:T(8,128)(2,1)S(1)} %fusion.6, f32[768]{0:T(1024)S(1)} %add.99), kind=kOutput, calls=%fused_computation.26 | convolution fusion | flops 3255241728 | bytes 12106752 | tf_op jit(solution)/shard_map/dot_general | solution.py:57
  240.0 2.1 reshape.211
  242.1 2.2 copy.46
  244.3 0.4 fusion.84
  244.7 0.8 slice.138
  245.5 1.7 slice_bitcast_fusion
  247.2 0.1 slice.159
  247.4 0.1 slice.160
  247.6 0.5 subtract_convert_fusion.1
  248.1 0.3 pad_maximum_fusion.2
  248.4 0.3 pad_maximum_fusion.3
  248.7 0.1 copy.56
  248.8 0.7 pad_maximum_fusion
  249.5 0.3 fusion.35
  249.8 0.1 fusion.69
  249.9 0.2 fusion.67
  250.0 0.7 fusion.40
  250.8 2.3 fusion.87
  253.1 0.8 fusion.30
  254.0 0.8 copy.59
  254.8 0.4 fusion.73
  255.2 0.1 fusion.63
  255.3 0.2 fusion.60
  255.5 2.1 fusion.70
  257.6 0.1 fusion.64
  257.7 0.2 fusion.59
  257.9 0.1 copy.58
  258.0 0.1 copy.54
  258.1 0.1 copy.55
  258.2 0.1 copy.57
  258.3 0.7 pad_maximum_fusion.1
  259.0 0.2 fusion.33
  259.2 2.0 fusion.14
  261.2 0.4 fusion.12
  261.6 0.1 fusion.75
  261.7 0.6 copy.126
  (61 shorter events, 0.8 us)
Async XLA Ops:
  7.2 221.1 %all-gather.2.cloned.1.call-start = ((), (), s32[]{:S(2)}) async-start(), calls=%async_computation | async-start | bytes 4718592 | tf_op jit(solution)/shard_map/all_gather | solution.py:163
  7.9 8.3 %copy-start.14 = (f32[3,256]{1,0:T(4,128)S(1)}, f32[3,256]{1,0:T(4,128)}, u32[]{:S(2)}) copy-start(f32[3,256]{1,0:T(4,128)} %param.16) | copy-start | bytes 9220
  7.9 8.4 %copy-start.12 = (s32[4,3]{1,0:T(4,128)S(1)}, s32[4,3]{1,0:T(4,128)}, u32[]{:S(2)}) copy-start(s32[4,3]{1,0:T(4,128)} %param.20) | copy-start | bytes 148
  7.9 9.8 %copy-start.7 = (bf16[1,2,512,256]{3,2,1,0:T(8,128)(2,1)S(1)}, bf16[1,2,512,256]{3,2,1,0:T(8,128)(2,1)}, u32[]{:S(2)}) copy-start(bf16[1,2,512,256]{3,2,1,0:T(8,128)(2,1)} %param.17) | copy-start | bytes 1572868
  7.9 11.7 %copy-start.5 = (bf16[4,2,256,256]{3,2,1,0:T(8,128)(2,1)S(1)}, bf16[4,2,256,256]{3,2,1,0:T(8,128)(2,1)}, u32[]{:S(2)}) copy-start(bf16[4,2,256,256]{3,2,1,0:T(8,128)(2,1)} %param.19) | copy-start | bytes 3145732
  13.8 193.8 %collective-permute-start = (bf16[4,2,1024,256]{3,2,1,0:T(8,128)(2,1)}, bf16[4,2,1024,256]{3,2,1,0:T(8,128)(2,1)}, u32[]{:S(2)}, u32[]{:S(2)}) collective-permute-start(bf16[4,2,1024,256]{3,2,1,0:T(8,128)(2,1)} %get-tuple-element.36), channel_id=1, source_target_pairs={{0,8},{8,16},{16,24},{24,32},{32,40},{40,48},{48,56},{56,64},{64,7... | collective-permute-start | bytes 12582920 | tf_op jit(solution)/shard_map/ppermute | solution.py:23
  13.8 204.1 %collective-permute-start.1 = (bf16[4,2,1024,256]{3,2,1,0:T(8,128)(2,1)}, bf16[4,2,1024,256]{3,2,1,0:T(8,128)(2,1)}, u32[]{:S(2)}, u32[]{:S(2)}) collective-permute-start(bf16[4,2,1024,256]{3,2,1,0:T(8,128)(2,1)} %get-tuple-element.37), channel_id=1, source_target_pairs={{8,0},{16,8},{24,16},{32,24},{40,32},{48,40},{56,48},{64,56},{72,6... | collective-permute-start | bytes 12582920 | tf_op jit(solution)/shard_map/ppermute | solution.py:26
  20.0 9.0 %copy-start.13 = (bf16[4,512]{1,0:T(4,128)(2,1)S(1)}, bf16[4,512]{1,0:T(4,128)(2,1)}, u32[]{:S(2)}) copy-start(bf16[4,512]{1,0:T(4,128)(2,1)} %param.12) | copy-start | bytes 12292
  20.0 187.6 %copy-start.10 = (f32[4096]{0:T(1024)S(1)}, f32[4096]{0:T(1024)}, u32[]{:S(2)}) copy-start(f32[4096]{0:T(1024)} %param.14) | copy-start | bytes 49156
  20.0 187.6 %copy-start.11 = (f32[4096]{0:T(1024)S(1)}, f32[4096]{0:T(1024)}, u32[]{:S(2)}) copy-start(f32[4096]{0:T(1024)} %param.13) | copy-start | bytes 49156
  228.3 3.4 %copy-start = (bf16[512,4096]{1,0:T(8,128)(2,1)S(1)}, bf16[512,4096]{1,0:T(8,128)(2,1)}, u32[]{:S(2)}) copy-start(bf16[512,4096]{1,0:T(8,128)(2,1)} %all-gather.2.cloned.1.call-done) | copy-start | bytes 12582916
  231.7 3.5 %slice-start = ((s8[6291456]{0:T(1024)(128)(4,1)}), s8[4194304]{0:T(1024)(128)(4,1)S(1)}, s32[]{:S(2)}) async-start(s8[6291456]{0:T(1024)(128)(4,1)} %bitcast.87), calls=%async_computation.1 | async-start | bytes 8388608
  233.0 2.3 slice-start.1
  242.1 5.5 %copy-start.3 = (f32[516,16]{1,0:T(8,128)S(1)}, f32[516,16]{1,0:T(8,128)}, u32[]{:S(2)}) copy-start(f32[516,16]{1,0:T(8,128)} %copy.49) | copy-start | bytes 99076
  247.5 2.5 copy-start.4
  248.4 2.3 copy-start.6
  250.8 2.4 copy-start.8
  250.8 2.4 copy-start.9
  253.1 1.7 copy-start.1
  255.2 6.0 %copy-start.2 = (bf16[4,1024,2,128]{3,2,1,0:T(2,128)(2,1)S(1)}, bf16[4,1024,2,128]{3,2,1,0:T(2,128)(2,1)}, u32[]{:S(2)}) copy-start(bf16[4,1024,2,128]{3,2,1,0:T(2,128)(2,1)} %reshape_squeeze.31) | copy-start | bytes 6291460
Sparse Core Ops, SparseCore 0:
  10.5 143.3 all-gather.1
where the time goes:
time: 270 us; the launch traced here: 269 us
  blocking collectives  177 us (66%)
  local copies, waits for them, and re-layouts  48.5 us (18%)
  between operations  15.1 us (6%)
  other arithmetic  14.4 us (5%)
  matrix products  11.6 us (4%)
    all_gather x1, blocking collectives, local(): lax.all_gather(decode_x, 'tp', axis=1, tiled=True)  177 us
    unnamed x38, local copies, waits for them, and re-layouts  11 us
    another operation x2, local copies, waits for them, and re-layouts, piece_batch(): values = store[:, 1].reshape(count, capacity, heads, HD)  7.97 us
    slice x2, local copies, waits for them, and re-layouts, piece_batch(): values = store[:, 1].reshape(count, capacity, heads, HD)  7.68 us
    slice x1, local copies, waits for them, and re-layouts, with_halo(): lax.slice_in_dim(block, block.shape[dim] - width, None, axis=dim)  5.89 us
  transfers between devices with their start and end apart: 3, of which 0 were waited for; matrix products, arithmetic and copies ran while one was open for 15% of the time, Pallas kernels for 0%

commit v1 on v0

--- a/solution.py
+++ b/solution.py
@@ -159,16 +159,12 @@
     piece_len,
     side_store,
 ):
-    whole_prefill, whole_decode = (
-        lax.all_gather(prefill_x, "tp", axis=1, tiled=True),
-        lax.all_gather(decode_x, "tp", axis=1, tiled=True),
-    )
-    normed = jnp.concatenate(
-        [layer_norm(whole_prefill, ln_gain, ln_bias), layer_norm(whole_decode, ln_gain, ln_bias)],
-        axis=0,
-    )
     count = prefill_x.shape[0]
     requests = decode_x.shape[0]
+    whole = lax.all_gather(
+        jnp.concatenate([prefill_x, decode_x], axis=0), "tp", axis=1, tiled=True
+    )
+    normed = layer_norm(whole, ln_gain, ln_bias)
     positions = jnp.concatenate(
         [
             prefill_offset[0] + jnp.arange(count, dtype=jnp.int32),
@@ -181,9 +177,29 @@
     home_parts = home_partial(
         own_query, fresh_key[count:], fresh_value[count:], home_cache, piece_len[:, 1]
     )
-    extended = with_halo(side_store, (("group", 0),), requests)
-    left_parts = piece_batch(own_query, extended[:requests], piece_len[:, 0])
-    right_parts = piece_batch(own_query, extended[3 * requests :], piece_len[:, 2])
+    groups = lax.axis_size("group")
+    forward = [(i, (i + 1) % groups) for i in range(groups)]
+    backward = [((i + 1) % groups, i) for i in range(groups)]
+    heads = own_query.shape[1]
+
+    def ask(lengths, pairs):
+        packed = jnp.concatenate(
+            [own_query.astype(jnp.float32).reshape(requests, -1), lengths[:, None].astype(jnp.float32)],
+            axis=1,
+        )
+        got = lax.ppermute(packed, "group", pairs)
+        return got[:, :-1].reshape(own_query.shape).astype(own_query.dtype), got[:, -1].astype(jnp.int32)
+
+    def answer(parts, pairs):
+        highest, total, summed = parts
+        packed = jnp.concatenate([summed, highest[:, :, None], total[:, :, None]], axis=2)
+        got = lax.ppermute(packed, "group", pairs)
+        return (got[:, :, HD], got[:, :, HD + 1], got[:, :, :HD])
+
+    prev_query, prev_len = ask(piece_len[:, 2], forward)
+    next_query, next_len = ask(piece_len[:, 0], backward)
+    right_parts = answer(piece_batch(prev_query, side_store[:requests], prev_len), backward)
+    left_parts = answer(piece_batch(next_query, side_store[requests:], next_len), forward)
     prefill_out = prefill_attend(
         query[:count], fresh_key[:count], fresh_value[:count], prior_cache[0], prefill_offset[0]
     )

time: 270 us -> 184 us (0.68)
  the two profiles are of different devices: /device:TPU:38 before, /device:TPU:8 now
where the time goes in v1:
time: 184 us
  waiting for transfers between devices  85.2 us (46%)
  local copies, waits for them, and re-layouts  45.2 us (25%)
  matrix products  16.4 us (9%)
  other arithmetic  15.1 us (8%)
  between operations  15 us (8%)
  starting transfers between devices  6.67 us (4%)
    all_gather x1, waiting for transfers between devices, local(): lax.all_gather(jnp.concatenate([prefill_x, decode_x], axis=0), 'tp', axis...  78.6 us
    unnamed x25, local copies, waits for them, and re-layouts  10.4 us
    dot_general x1, matrix products, project(): jnp.dot(normed, weight.reshape(weight.shape[0], 3 * width), preferred_ele...  8.01 us
    another operation x2, local copies, waits for them, and re-layouts, piece_batch(): keys = store[:, 0].reshape(count, capacity, heads, HD)  7.92 us
    ppermute x2, waiting for transfers between devices, answer(): got = lax.ppermute(packed, 'group', pairs)  6.63 us
    another operation x2, local copies, waits for them, and re-layouts, piece_batch(): values = store[:, 1].reshape(count, capacity, heads, HD)  6.02 us
    ppermute x2, starting transfers between devices, ask(): got = lax.ppermute(packed, 'group', pairs)  5.98 us
    slice x1, local copies, waits for them, and re-layouts, piece_batch(): values = store[:, 1].reshape(count, capacity, heads, HD)  5.83 us
  transfers between devices with their start and end apart: 5, of which 2 were waited for; matrix products, arithmetic and copies ran while one was open for 28% of the time, Pallas kernels for 0%

profile of v1, /device:TPU:8, one launch (start us, length us, event | category | flops | bytes accessed | tf_op | source)
XLA Modules:
  0.0 183.6 jit_solution(13133716730967612934)
XLA Ops:
  7.2 1.9 %pad_maximum_fusion = bf16[516,512]{1,0:T(8,128)(2,1)} fusion(bf16[4,512]{1,0:T(4,128)(2,1)} %param.12, bf16[512,512]{1,0:T(8,128)(2,1)} %param.11), kind=kLoop, calls=%fused_computation.38 | loop fusion | flops 1056768 | bytes 1056768 | tf_op jit(solution)/shard_map/concatenate | solution.py:165
  9.2 8.9 %copy.85 = bf16[4096,3,256]{0,2,1:T(8,128)(2,1)} copy(bf16[4096,3,256]{2,0,1:T(8,128)(2,1)} %param.15) | data formatting | bytes 12582912 | tf_op args[4]
  18.7 0.2 slice_convert_fusion.7
  18.9 0.2 multiply_cosine_fusion
  19.2 0.1 copy.89
  19.3 0.8 copy.88
  20.2 0.1 copy.118
  20.3 0.8 copy.92
  21.2 0.8 copy.84
  22.0 5.8 %fusion.85 = (bf16[4,1,1024,256]{3,2,1,0:T(8,128)(2,1)S(1)}, bf16[4,1,1024,256]{3,2,1,0:T(8,128)(2,1)}, bf16[4,1,1024,256]{3,2,1,0:T(8,128)(2,1)}, bf16[4,1,1024,256]{3,2,1,0:T(8,128)(2,1)}) fusion(bf16[8,2,1024,256]{3,2,1,0:T(8,128)(2,1)} %param.21), kind=kLoop, calls=%fused_computation.137 | loop fusion | bytes 16777216 | tf_op jit(solution)/shard_map/slice | solution.py:121
  27.8 4.0 %copy.116 = bf16[4,1,1024,256]{2,3,0,1:T(8,128)(2,1)} copy(bf16[4,1,1024,256]{3,2,1,0:T(8,128)(2,1)} %get-tuple-element.41) | data formatting | bytes 4194304 | tf_op jit(solution)/shard_map/reshape;squeeze | solution.py:120
  31.8 4.0 %reshape_squeeze.30 = bf16[4,1024,2,128]{3,2,1,0:T(2,128)(2,1)} reshape(bf16[4,1,1024,256]{3,2,1,0:T(8,128)(2,1)} %get-tuple-element.40) | data formatting | bytes 4194304 | tf_op jit(solution)/shard_map/reshape;squeeze | solution.py:121
  35.8 2.1 %fusion.87 = (bf16[4,1,256,256]{3,2,1,0:T(8,128)(2,1)S(1)}, bf16[4,1,256,256]{3,2,1,0:T(8,128)(2,1)}) fusion(bf16[4,2,256,256]{3,2,1,0:T(8,128)(2,1)} %param.19), kind=kLoop, calls=%fused_computation.139 | loop fusion | bytes 2097152 | tf_op jit(solution)/shard_map/slice | solution.py:130
  37.9 1.2 reshape_squeeze.31
  39.0 0.9 reshape_squeeze.28
  40.0 4.0 %copy.115 = bf16[4,1,1024,256]{2,3,0,1:T(8,128)(2,1)} copy(bf16[4,1,1024,256]{3,2,1,0:T(8,128)(2,1)} %get-tuple-element.39) | data formatting | bytes 4194304 | tf_op jit(solution)/shard_map/reshape;squeeze | solution.py:120
  43.9 2.1 %reshape_squeeze.27 = bf16[4,1024,2,128]{3,2,1,0:T(2,128)(2,1)} reshape(bf16[4,1,1024,256]{3,2,1,0:T(8,128)(2,1)S(1)} %get-tuple-element.38) | data formatting | bytes 4194304 | tf_op jit(solution)/shard_map/reshape;squeeze | solution.py:121
  46.2 1.0 pad_add_fusion
  47.1 78.6 %all-gather.2.cloned.1.call-done = bf16[516,4096]{1,0:T(8,128)(2,1)} async-done(((bf16[516,512]{1,0:T(8,128)(2,1)}), bf16[516,4096]{1,0:T(8,128)(2,1)}) %all-gather.2.cloned.1.call-update) | async-done | bytes 4227088 | tf_op jit(solution)/shard_map/all_gather | solution.py:164
  125.7 3.0 %convert_reduce_fusion = f32[516]{0:T(1024)S(1)} fusion(bf16[516,4096]{1,0:T(8,128)(2,1)} %all-gather.2.cloned.1.call-done), kind=kLoop, calls=%fused_computation.2 | loop fusion | flops 4226556 | bytes 4229136 | tf_op jit(solution)/shard_map/reduce_sum | solution.py:33
  128.7 0.5 copy-done
  129.2 1.3 fusion.3
  130.5 8.0 %fusion.23 = f32[516,768]{1,0:T(8,128)} fusion(bf16[4096,768]{0,1:T(8,128)(2,1)} %bitcast.117, bf16[516,4096]{1,0:T(8,128)(2,1)S(1)} %copy-done, f32[4096]{0:T(1024)S(1)} %copy-done.9, f32[4096]{0:T(1024)S(1)} %copy-done.10, f32[516]{0:T(1024)S(1)} %add_rsqrt_fusion, f32[516]{0:T(1024)S(1)} %broadcast_multiply_fusion, f32[768]{0:T(1024)S(1)} %add.74), kind=kOutput, calls=%fused_computation.27 | convolution fusion | flops 3259468800 | bytes 12143648 | tf_op jit(solution)/shard_map/dot_general | solution.py:57
  138.5 2.1 %reshape.172 = f32[516,3,2,128]{3,2,1,0:T(2,128)S(1)} reshape(f32[516,768]{1,0:T(8,128)} %fusion.23) | data formatting | bytes 3170304 | tf_op jit(solution)/shard_map/reshape | solution.py:60
  140.6 0.4 fusion.86
  141.0 2.2 %copy.86 = bf16[516,3,2,128]{0,3,2,1:T(8,128)(2,1)} copy(f32[516,3,2,128]{3,2,1,0:T(2,128)S(1)} %reshape.172) | data formatting | bytes 2377728 | tf_op jit(solution)/shard_map/reshape | solution.py:60
  143.2 0.1 slice.249
  143.4 0.1 slice.250
  143.5 1.4 subtract_convert_fusion.1
  145.0 0.3 pad_maximum_fusion.3
  145.3 1.0 slice_bitcast_fusion
  146.4 0.8 slice.182
  147.2 0.3 pad_maximum_fusion.4
  147.6 0.3 collective-permute-start.2
  147.9 0.1 copy.94
  147.9 5.7 %collective-permute-start = (f32[4,257]{1,0:T(4,128)S(1)}, f32[4,257]{1,0:T(4,128)S(1)}, u32[]{:S(2)}, u32[]{:S(2)}) collective-permute-start(f32[4,257]{1,0:T(4,128)S(1)} %get-tuple-element.64), channel_id=1, source_target_pairs={{8,0},{16,8},{24,16},{32,24},{40,32},{48,40},{56,48},{64,56},{72,6... | collective-permute-start | bytes 12344 | tf_op jit(solution)/shard_map/ppermute | solution.py:190
  153.7 0.7 fusion.42
  154.4 2.4 %fusion.89 = (f32[2,512]{1,0:T(2,128)S(1)}, bf16[2,512,1024]{2,1,0:T(8,128)(2,1)S(1)}) fusion(f32[2,512,1024]{2,1,0:T(8,128)S(1)} %fusion.42, pred[512,1024]{1,0:T(8,128)(4,1)S(1)} %copy-done.4), kind=kOutput, calls=%fused_computation.141 | output fusion | flops 8389631 | bytes 6819840 | tf_op jit(solution)/shard_map/while/body/eval_jaxpr/sub | solution.py:73
  156.8 0.7 pad_maximum_fusion.2
  157.5 0.7 pad_maximum_fusion.1
  158.2 0.3 fusion.37
  158.4 0.1 fusion.69
  158.5 0.8 fusion.32
  159.4 0.2 fusion.65
  159.5 0.1 fusion.70
  159.7 2.0 %fusion.91 = f32[4,2,1,1024]{3,2,1,0:T(1,128)S(1)} fusion(bf16[4,2,128,1]{2,3,1,0:T(2,128)(2,1)S(1)} %reshape.194, bf16[4,1024,2,128]{1,3,2,0:T(8,128)(2,1)} %bitcast.116), kind=kOutput, calls=%fused_computation.143 | convolution fusion | flops 2097152 | bytes 2131968 | tf_op jit(solution)/shard_map/vmap(hd,khd->hk)/dot_general | solution.py:104
  161.7 0.1 fusion.64
  161.8 0.2 fusion.59
  162.0 2.0 %fusion.14 = f32[4,2,1,128]{3,2,1,0:T(1,128)S(1)} fusion(bf16[4,1024,2,128]{3,2,1,0:T(2,128)(2,1)} %reshape_squeeze.30, bf16[4,2,1024,1]{2,0,1,3:T(4,128)(2,1)S(1)} %get-tuple-element.58), kind=kOutput, calls=%fused_computation.17 | convolution fusion | flops 2097152 | bytes 2117632 | tf_op jit(solution)/shard_map/vmap(hk,khd->hd)/dot_general | solution.py:111
  164.0 0.2 copy.111
  164.3 0.1 collective-permute-start.3
  164.4 0.1 fusion.71
  164.6 0.4 fusion.90
  165.0 0.1 fusion.63
  165.1 0.2 fusion.60
  165.3 2.0 %fusion.16 = f32[4,2,1,128]{3,2,1,0:T(1,128)S(1)} fusion(bf16[4,1024,2,128]{3,2,1,0:T(2,128)(2,1)} %reshape_squeeze.27, bf16[4,2,1024,1]{2,0,1,3:T(4,128)(2,1)S(1)} %get-tuple-element.56), kind=kOutput, calls=%fused_computation.19 | convolution fusion | flops 2097152 | bytes 2117632 | tf_op jit(solution)/shard_map/vmap(hk,khd->hd)/dot_general | solution.py:111
  167.3 0.2 copy.102
  167.5 0.6 collective-permute-start.1
  168.1 0.2 fusion.35
  168.3 0.9 copy.96
  169.1 0.2 copy.114
  169.3 6.6 %collective-permute-done.1 = f32[4,2,130]{0,1,2:T(2,128)S(1)} collective-permute-done((f32[4,2,130]{0,1,2:T(2,128)S(1)}, f32[4,2,130]{0,1,2:T(2,128)S(1)}, u32[]{:S(2)}, u32[]{:S(2)}) %collective-permute-start.1) | collective-permute-done | bytes 4192 | tf_op jit(solution)/shard_map/ppermute | solution.py:196
  175.9 0.1 fusion.50
  176.1 0.7 copy.95
  (54 shorter events, 1.0 us)
Async XLA Ops:
  7.2 118.6 %all-gather.2.cloned.1.call-start = ((), (), s32[]{:S(2)}) async-start(), calls=%async_computation | async-start | bytes 4792320 | tf_op jit(solution)/shard_map/all_gather | solution.py:164
  9.1 8.9 %copy-start.8 = (f32[3,256]{1,0:T(4,128)S(1)}, f32[3,256]{1,0:T(4,128)}, u32[]{:S(2)}) copy-start(f32[3,256]{1,0:T(4,128)} %param.16) | copy-start | bytes 9220
  9.1 9.6 %copy-start.7 = (s32[4,3]{1,0:T(4,128)S(1)}, s32[4,3]{1,0:T(4,128)}, u32[]{:S(2)}) copy-start(s32[4,3]{1,0:T(4,128)} %param.20) | copy-start | bytes 148
  9.2 11.0 %copy-start.5 = (bf16[1,2,512,256]{3,2,1,0:T(8,128)(2,1)S(1)}, bf16[1,2,512,256]{3,2,1,0:T(8,128)(2,1)}, u32[]{:S(2)}) copy-start(bf16[1,2,512,256]{3,2,1,0:T(8,128)(2,1)} %param.17) | copy-start | bytes 1572868
  125.7 3.5 %copy-start = (bf16[516,4096]{1,0:T(8,128)(2,1)S(1)}, bf16[516,4096]{1,0:T(8,128)(2,1)}, u32[]{:S(2)}) copy-start(bf16[516,4096]{1,0:T(8,128)(2,1)} %all-gather.2.cloned.1.call-done) | copy-start | bytes 12681220
  125.7 4.8 %copy-start.9 = (f32[4096]{0:T(1024)S(1)}, f32[4096]{0:T(1024)}, u32[]{:S(2)}) copy-start(f32[4096]{0:T(1024)} %param.14) | copy-start | bytes 49156
  125.7 4.8 %copy-start.10 = (f32[4096]{0:T(1024)S(1)}, f32[4096]{0:T(1024)}, u32[]{:S(2)}) copy-start(f32[4096]{0:T(1024)} %param.13) | copy-start | bytes 49156
  143.5 10.1 %copy-start.3 = (bf16[512,2,128]{2,0,1:T(8,128)(2,1)S(1)}, bf16[512,2,128]{2,0,1:T(8,128)(2,1)}, u32[]{:S(2)}) copy-start(bf16[512,2,128]{2,0,1:T(8,128)(2,1)} %copy.92) | copy-start | bytes 786436
  145.3 9.1 %copy-start.4 = (pred[512,1024]{1,0:T(8,128)(4,1)S(1)}, pred[512,1024]{1,0:T(8,128)(4,1)}, u32[]{:S(2)}) copy-start(pred[512,1024]{1,0:T(8,128)(4,1)} %pad_add_fusion) | copy-start | bytes 1572868
  147.6 11.9 %collective-permute-start.2 = (f32[4,257]{1,0:T(4,128)S(1)}, f32[4,257]{1,0:T(4,128)S(1)}, u32[]{:S(2)}, u32[]{:S(2)}) collective-permute-start(f32[4,257]{1,0:T(4,128)S(1)} %get-tuple-element.65), channel_id=1, source_target_pairs={{0,8},{8,16},{16,24},{24,32},{32,40},{40,48},{48,56},{56,64},{64,7... | collective-permute-start | bytes 12344 | tf_op jit(solution)/shard_map/ppermute | solution.py:190
  147.9 16.4 %collective-permute-start = (f32[4,257]{1,0:T(4,128)S(1)}, f32[4,257]{1,0:T(4,128)S(1)}, u32[]{:S(2)}, u32[]{:S(2)}) collective-permute-start(f32[4,257]{1,0:T(4,128)S(1)} %get-tuple-element.64), channel_id=1, source_target_pairs={{8,0},{16,8},{24,16},{32,24},{40,32},{48,40},{56,48},{64,56},{72,6... | collective-permute-start | bytes 12344 | tf_op jit(solution)/shard_map/ppermute | solution.py:190
  154.4 3.1 %copy-start.2 = (bf16[4,256,2,128]{3,2,1,0:T(2,128)(2,1)S(1)}, bf16[4,256,2,128]{3,2,1,0:T(2,128)(2,1)}, u32[]{:S(2)}) copy-start(bf16[4,256,2,128]{3,2,1,0:T(2,128)(2,1)} %reshape_squeeze.28) | copy-start | bytes 1572868
  154.4 4.1 %copy-start.6 = (bf16[1,1,512,256]{2,3,1,0:T(8,128)(2,1)S(1)}, bf16[1,1,512,256]{2,3,1,0:T(8,128)(2,1)}, u32[]{:S(2)}) copy-start(bf16[1,1,512,256]{2,3,1,0:T(8,128)(2,1)} %copy.84) | copy-start | bytes 786436
  158.5 6.1 %copy-start.1 = (bf16[4,1,1024,256]{2,3,0,1:T(8,128)(2,1)S(1)}, bf16[4,1,1024,256]{2,3,0,1:T(8,128)(2,1)}, u32[]{:S(2)}) copy-start(bf16[4,1,1024,256]{2,3,0,1:T(8,128)(2,1)} %copy.115) | copy-start | bytes 6291460
  164.3 5.0 %collective-permute-start.3 = (f32[4,2,130]{0,1,2:T(2,128)S(1)}, f32[4,2,130]{0,1,2:T(2,128)S(1)}, u32[]{:S(2)}, u32[]{:S(2)}) collective-permute-start(f32[4,2,130]{0,1,2:T(2,128)S(1)} %pad_maximum_fusion.6), channel_id=1, source_target_pairs={{8,0},{16,8},{24,16},{32,24},{40,32},{48,40},{56,48},{64,56},{72,6... | collective-permute-start | bytes 12488 | tf_op jit(solution)/shard_map/ppermute | solution.py:196
  167.5 8.4 %collective-permute-start.1 = (f32[4,2,130]{0,1,2:T(2,128)S(1)}, f32[4,2,130]{0,1,2:T(2,128)S(1)}, u32[]{:S(2)}, u32[]{:S(2)}) collective-permute-start(f32[4,2,130]{0,1,2:T(2,128)S(1)} %pad_maximum_fusion.5), channel_id=1, source_target_pairs={{0,8},{8,16},{16,24},{24,32},{32,40},{40,48},{48,56},{56,64},{64,7... | collective-permute-start | bytes 12488 | tf_op jit(solution)/shard_map/ppermute | solution.py:196
Sparse Core Ops, SparseCore 0:
  10.5 115.1 all-gather.1

commit v2 on v1

--- a/solution.py
+++ b/solution.py
@@ -161,9 +161,8 @@
 ):
     count = prefill_x.shape[0]
     requests = decode_x.shape[0]
-    whole = lax.all_gather(
-        jnp.concatenate([prefill_x, decode_x], axis=0), "tp", axis=1, tiled=True
-    )
+    half = lax.all_gather(jnp.concatenate([prefill_x, decode_x], axis=0), "tz", axis=1, tiled=True)
+    whole = lax.all_gather(half, "ty", axis=1, tiled=True)
     normed = layer_norm(whole, ln_gain, ln_bias)
     positions = jnp.concatenate(
         [
@@ -208,22 +207,26 @@
 
 
 def solution(mesh):
-    return jax.shard_map(
+    devices = mesh.devices.reshape(mesh.devices.shape[0], -1, 2)
+    split = jax.sharding.Mesh(devices, ("group", "ty", "tz"))
+    tp = ("ty", "tz")
+    inner = jax.shard_map(
         local,
-        mesh=mesh,
+        mesh=split,
         in_specs=(
-            P("group", "tp"),
-            P("group", "tp"),
+            P("group", tp),
+            P("group", tp),
             P(),
             P(),
-            P(None, None, "tp"),
-            P(None, "tp"),
-            P("group", None, None, "tp"),
+            P(None, None, tp),
+            P(None, tp),
+            P("group", None, None, tp),
             P("group"),
-            P("group", None, None, "tp"),
+            P("group", None, None, tp),
             P("group", None),
-            P("group", None, None, "tp"),
+            P("group", None, None, tp),
         ),
-        out_specs=(P("group", "tp"), P("group", "tp")),
+        out_specs=(P("group", tp), P("group", tp)),
         check_vma=False,
     )
+    return inner

time: 184 us -> 163 us (0.89)
  waiting for transfers between devices: 85.2 us -> 63.3 us
    all_gather x1 -> x2, waiting for transfers between devices: 78.6 us -> 56.5 us  [the longest x1 45.9 us: local(): lax.all_gather(jnp.concatenate([prefill_x, decode_x], axis=0), 'tz', axis...]
  transfers between devices with their start and end apart: 5 -> 6, of which waited for: 2 -> 3; matrix products, arithmetic and copies ran while one was open for 28% -> 32% of each run, Pallas kernels for 0% -> 0%
where the time goes in v2:
time: 163 us; the launch traced here: 162 us
  waiting for transfers between devices  63.3 us (39%)
  local copies, waits for them, and re-layouts  45.1 us (28%)
  matrix products  16.4 us (10%)
  other arithmetic  15.1 us (9%)
  between operations  15 us (9%)
  starting transfers between devices  6.72 us (4%)
    all_gather x1, waiting for transfers between devices, local(): lax.all_gather(jnp.concatenate([prefill_x, decode_x], axis=0), 'tz', axis...  45.9 us
    all_gather x1, waiting for transfers between devices, local(): whole = lax.all_gather(half, 'ty', axis=1, tiled=True)  10.7 us
    unnamed x25, local copies, waits for them, and re-layouts  10.4 us
    dot_general x1, matrix products, project(): jnp.dot(normed, weight.reshape(weight.shape[0], 3 * width), preferred_ele...  8.01 us
    another operation x2, local copies, waits for them, and re-layouts, piece_batch(): keys = store[:, 0].reshape(count, capacity, heads, HD)  7.95 us
    ppermute x2, waiting for transfers between devices, answer(): got = lax.ppermute(packed, 'group', pairs)  6.74 us
    another operation x2, local copies, waits for them, and re-layouts, piece_batch(): values = store[:, 1].reshape(count, capacity, heads, HD)  6.02 us
    ppermute x2, starting transfers between devices, ask(): got = lax.ppermute(packed, 'group', pairs)  5.98 us
  transfers between devices with their start and end apart: 6, of which 3 were waited for; matrix products, arithmetic and copies ran while one was open for 32% of the time, Pallas kernels for 0%

profile of v2, /device:TPU:8, one launch (start us, length us, event | category | flops | bytes accessed | tf_op | source)
XLA Modules:
  0.0 161.7 jit_solution(3653281103351488766)
XLA Ops:
  7.2 1.9 %pad_maximum_fusion = bf16[516,512]{1,0:T(8,128)(2,1)} fusion(bf16[4,512]{1,0:T(4,128)(2,1)} %param.12, bf16[512,512]{1,0:T(8,128)(2,1)} %param.11), kind=kLoop, calls=%fused_computation.38 | loop fusion | flops 1056768 | bytes 1056768 | tf_op jit(solution)/shard_map/concatenate | solution.py:164
  9.2 45.9 %all-gather.3.cloned.1.call-done = bf16[516,1024]{1,0:T(8,128)(2,1)} async-done(((bf16[516,512]{1,0:T(8,128)(2,1)}), bf16[516,1024]{1,0:T(8,128)(2,1)}) %all-gather.3.cloned.1.call-update) | async-done | bytes 1056784 | tf_op jit(solution)/shard_map/all_gather | solution.py:164
  55.1 8.9 %copy.85 = bf16[4096,3,256]{0,2,1:T(8,128)(2,1)} copy(bf16[4096,3,256]{2,0,1:T(8,128)(2,1)} %param.15) | data formatting | bytes 12582912 | tf_op args[4]
  64.7 0.2 slice_convert_fusion.7
  64.9 0.2 multiply_cosine_fusion
  65.1 0.1 copy.89
  65.3 0.8 copy.88
  66.1 0.1 copy.118
  66.3 0.8 copy.92
  67.1 0.9 copy.84
  68.0 5.8 %fusion.85 = (bf16[4,1,1024,256]{3,2,1,0:T(8,128)(2,1)S(1)}, bf16[4,1,1024,256]{3,2,1,0:T(8,128)(2,1)}, bf16[4,1,1024,256]{3,2,1,0:T(8,128)(2,1)}, bf16[4,1,1024,256]{3,2,1,0:T(8,128)(2,1)}) fusion(bf16[8,2,1024,256]{3,2,1,0:T(8,128)(2,1)} %param.21), kind=kLoop, calls=%fused_computation.137 | loop fusion | bytes 16777216 | tf_op jit(solution)/shard_map/slice | solution.py:121
  73.8 4.0 %copy.116 = bf16[4,1,1024,256]{2,3,0,1:T(8,128)(2,1)} copy(bf16[4,1,1024,256]{3,2,1,0:T(8,128)(2,1)} %get-tuple-element.41) | data formatting | bytes 4194304 | tf_op jit(solution)/shard_map/reshape;squeeze | solution.py:120
  77.7 4.0 %reshape_squeeze.30 = bf16[4,1024,2,128]{3,2,1,0:T(2,128)(2,1)} reshape(bf16[4,1,1024,256]{3,2,1,0:T(8,128)(2,1)} %get-tuple-element.40) | data formatting | bytes 4194304 | tf_op jit(solution)/shard_map/reshape;squeeze | solution.py:121
  81.7 2.1 %fusion.87 = (bf16[4,1,256,256]{3,2,1,0:T(8,128)(2,1)S(1)}, bf16[4,1,256,256]{3,2,1,0:T(8,128)(2,1)}) fusion(bf16[4,2,256,256]{3,2,1,0:T(8,128)(2,1)} %param.19), kind=kLoop, calls=%fused_computation.139 | loop fusion | bytes 2097152 | tf_op jit(solution)/shard_map/slice | solution.py:130
  83.8 1.2 reshape_squeeze.31
  85.0 0.9 reshape_squeeze.28
  85.9 4.0 %copy.115 = bf16[4,1,1024,256]{2,3,0,1:T(8,128)(2,1)} copy(bf16[4,1,1024,256]{3,2,1,0:T(8,128)(2,1)} %get-tuple-element.39) | data formatting | bytes 4194304 | tf_op jit(solution)/shard_map/reshape;squeeze | solution.py:120
  89.8 2.1 %reshape_squeeze.27 = bf16[4,1024,2,128]{3,2,1,0:T(2,128)(2,1)} reshape(bf16[4,1,1024,256]{3,2,1,0:T(8,128)(2,1)S(1)} %get-tuple-element.38) | data formatting | bytes 4194304 | tf_op jit(solution)/shard_map/reshape;squeeze | solution.py:121
  92.1 1.0 pad_add_fusion
  93.1 10.7 %all-gather.5.cloned.1.call-done = bf16[516,4096]{1,0:T(8,128)(2,1)} async-done(((bf16[516,1024]{1,0:T(8,128)(2,1)}), bf16[516,4096]{1,0:T(8,128)(2,1)}) %all-gather.5.cloned.1.call-update) | async-done | bytes 4227088 | tf_op jit(solution)/shard_map/all_gather | solution.py:165
  103.8 3.0 %convert_reduce_fusion = f32[516]{0:T(1024)S(1)} fusion(bf16[516,4096]{1,0:T(8,128)(2,1)} %all-gather.5.cloned.1.call-done), kind=kLoop, calls=%fused_computation.2 | loop fusion | flops 4226556 | bytes 4229136 | tf_op jit(solution)/shard_map/reduce_sum | solution.py:33
  106.8 0.5 copy-done
  107.2 1.3 fusion.3
  108.5 8.0 %fusion.23 = f32[516,768]{1,0:T(8,128)} fusion(bf16[4096,768]{0,1:T(8,128)(2,1)} %bitcast.117, bf16[516,4096]{1,0:T(8,128)(2,1)S(1)} %copy-done, f32[4096]{0:T(1024)S(1)} %copy-done.9, f32[4096]{0:T(1024)S(1)} %copy-done.10, f32[516]{0:T(1024)S(1)} %add_rsqrt_fusion, f32[516]{0:T(1024)S(1)} %broadcast_multiply_fusion, f32[768]{0:T(1024)S(1)} %add.74), kind=kOutput, calls=%fused_computation.27 | convolution fusion | flops 3259468800 | bytes 12143648 | tf_op jit(solution)/shard_map/dot_general | solution.py:57
  116.5 2.1 %reshape.172 = f32[516,3,2,128]{3,2,1,0:T(2,128)S(1)} reshape(f32[516,768]{1,0:T(8,128)} %fusion.23) | data formatting | bytes 3170304 | tf_op jit(solution)/shard_map/reshape | solution.py:60
  118.6 0.4 fusion.86
  119.0 2.2 %copy.86 = bf16[516,3,2,128]{0,3,2,1:T(8,128)(2,1)} copy(f32[516,3,2,128]{3,2,1,0:T(2,128)S(1)} %reshape.172) | data formatting | bytes 2377728 | tf_op jit(solution)/shard_map/reshape | solution.py:60
  121.3 0.1 slice.249
  121.4 0.1 slice.250
  121.6 1.4 subtract_convert_fusion.1
  123.0 0.3 pad_maximum_fusion.3
  123.4 1.0 slice_bitcast_fusion
  124.4 0.8 slice.182
  125.2 0.3 pad_maximum_fusion.4
  125.6 0.3 collective-permute-start.2
  126.0 5.7 %collective-permute-start = (f32[4,257]{1,0:T(4,128)S(1)}, f32[4,257]{1,0:T(4,128)S(1)}, u32[]{:S(2)}, u32[]{:S(2)}) collective-permute-start(f32[4,257]{1,0:T(4,128)S(1)} %get-tuple-element.64), channel_id=1, source_target_pairs={{8,0},{16,8},{24,16},{32,24},{40,32},{48,40},{56,48},{64,56},{72,6... | collective-permute-start | bytes 12344 | tf_op jit(solution)/shard_map/ppermute | solution.py:189
  131.7 0.7 fusion.42
  132.4 2.4 %fusion.89 = (f32[2,512]{1,0:T(2,128)S(1)}, bf16[2,512,1024]{2,1,0:T(8,128)(2,1)S(1)}) fusion(f32[2,512,1024]{2,1,0:T(8,128)S(1)} %fusion.42, pred[512,1024]{1,0:T(8,128)(4,1)S(1)} %copy-done.4), kind=kOutput, calls=%fused_computation.141 | output fusion | flops 8389631 | bytes 6819840 | tf_op jit(solution)/shard_map/while/body/eval_jaxpr/sub | solution.py:73
  134.8 0.7 pad_maximum_fusion.2
  135.5 0.7 pad_maximum_fusion.1
  136.2 0.3 fusion.37
  136.4 0.1 fusion.69
  136.5 0.8 fusion.32
  137.4 0.2 fusion.65
  137.6 0.1 fusion.70
  137.8 2.0 %fusion.91 = f32[4,2,1,1024]{3,2,1,0:T(1,128)S(1)} fusion(bf16[4,2,128,1]{2,3,1,0:T(2,128)(2,1)S(1)} %reshape.194, bf16[4,1024,2,128]{1,3,2,0:T(8,128)(2,1)} %bitcast.116), kind=kOutput, calls=%fused_computation.143 | convolution fusion | flops 2097152 | bytes 2131968 | tf_op jit(solution)/shard_map/vmap(hd,khd->hk)/dot_general | solution.py:104
  139.7 0.1 fusion.64
  139.9 0.2 fusion.59
  140.0 2.0 %fusion.14 = f32[4,2,1,128]{3,2,1,0:T(1,128)S(1)} fusion(bf16[4,1024,2,128]{3,2,1,0:T(2,128)(2,1)} %reshape_squeeze.30, bf16[4,2,1024,1]{2,0,1,3:T(4,128)(2,1)S(1)} %get-tuple-element.58), kind=kOutput, calls=%fused_computation.17 | convolution fusion | flops 2097152 | bytes 2117632 | tf_op jit(solution)/shard_map/vmap(hk,khd->hd)/dot_general | solution.py:111
  142.0 0.2 copy.111
  142.3 0.2 collective-permute-start.3
  142.5 0.1 fusion.71
  142.7 0.4 fusion.90
  143.1 0.1 fusion.63
  143.2 0.2 fusion.60
  143.4 2.0 %fusion.16 = f32[4,2,1,128]{3,2,1,0:T(1,128)S(1)} fusion(bf16[4,1024,2,128]{3,2,1,0:T(2,128)(2,1)} %reshape_squeeze.27, bf16[4,2,1024,1]{2,0,1,3:T(4,128)(2,1)S(1)} %get-tuple-element.56), kind=kOutput, calls=%fused_computation.19 | convolution fusion | flops 2097152 | bytes 2117632 | tf_op jit(solution)/shard_map/vmap(hk,khd->hd)/dot_general | solution.py:111
  145.4 0.2 copy.102
  145.7 0.4 collective-permute-start.1
  146.1 0.2 fusion.35
  146.3 0.9 copy.96
  147.2 0.2 copy.114
  147.3 6.7 %collective-permute-done.1 = f32[4,2,130]{0,1,2:T(2,128)S(1)} collective-permute-done((f32[4,2,130]{0,1,2:T(2,128)S(1)}, f32[4,2,130]{0,1,2:T(2,128)S(1)}, u32[]{:S(2)}, u32[]{:S(2)}) %collective-permute-start.1) | collective-permute-done | bytes 4192 | tf_op jit(solution)/shard_map/ppermute | solution.py:195
  154.1 0.1 fusion.50
  154.2 0.7 copy.95
  (57 shorter events, 1.1 us)
Async XLA Ops:
  7.2 47.9 %all-gather.3.cloned.1.call-start = ((), (), s32[]{:S(2)}) async-start(), calls=%async_computation | async-start | bytes 1597440 | tf_op jit(solution)/shard_map/all_gather | solution.py:164
  9.1 94.6 %all-gather.5.cloned.1.call-start = ((), (), s32[]{:S(2)}) async-start(), calls=%async_computation.1 | async-start | bytes 5324800 | tf_op jit(solution)/shard_map/all_gather | solution.py:165
  55.1 8.9 %copy-start.8 = (f32[3,256]{1,0:T(4,128)S(1)}, f32[3,256]{1,0:T(4,128)}, u32[]{:S(2)}) copy-start(f32[3,256]{1,0:T(4,128)} %param.16) | copy-start | bytes 9220
  55.1 9.6 %copy-start.7 = (s32[4,3]{1,0:T(4,128)S(1)}, s32[4,3]{1,0:T(4,128)}, u32[]{:S(2)}) copy-start(s32[4,3]{1,0:T(4,128)} %param.20) | copy-start | bytes 148
  55.1 11.0 %copy-start.5 = (bf16[1,2,512,256]{3,2,1,0:T(8,128)(2,1)S(1)}, bf16[1,2,512,256]{3,2,1,0:T(8,128)(2,1)}, u32[]{:S(2)}) copy-start(bf16[1,2,512,256]{3,2,1,0:T(8,128)(2,1)} %param.17) | copy-start | bytes 1572868
  103.7 3.5 %copy-start = (bf16[516,4096]{1,0:T(8,128)(2,1)S(1)}, bf16[516,4096]{1,0:T(8,128)(2,1)}, u32[]{:S(2)}) copy-start(bf16[516,4096]{1,0:T(8,128)(2,1)} %all-gather.5.cloned.1.call-done) | copy-start | bytes 12681220
  103.8 4.8 %copy-start.9 = (f32[4096]{0:T(1024)S(1)}, f32[4096]{0:T(1024)}, u32[]{:S(2)}) copy-start(f32[4096]{0:T(1024)} %param.14) | copy-start | bytes 49156
  103.8 4.8 %copy-start.10 = (f32[4096]{0:T(1024)S(1)}, f32[4096]{0:T(1024)}, u32[]{:S(2)}) copy-start(f32[4096]{0:T(1024)} %param.13) | copy-start | bytes 49156
  121.5 10.1 %copy-start.3 = (bf16[512,2,128]{2,0,1:T(8,128)(2,1)S(1)}, bf16[512,2,128]{2,0,1:T(8,128)(2,1)}, u32[]{:S(2)}) copy-start(bf16[512,2,128]{2,0,1:T(8,128)(2,1)} %copy.92) | copy-start | bytes 786436
  123.4 9.1 %copy-start.4 = (pred[512,1024]{1,0:T(8,128)(4,1)S(1)}, pred[512,1024]{1,0:T(8,128)(4,1)}, u32[]{:S(2)}) copy-start(pred[512,1024]{1,0:T(8,128)(4,1)} %pad_add_fusion) | copy-start | bytes 1572868
  125.6 11.9 %collective-permute-start.2 = (f32[4,257]{1,0:T(4,128)S(1)}, f32[4,257]{1,0:T(4,128)S(1)}, u32[]{:S(2)}, u32[]{:S(2)}) collective-permute-start(f32[4,257]{1,0:T(4,128)S(1)} %get-tuple-element.65), channel_id=1, source_target_pairs={{0,8},{8,16},{16,24},{24,32},{32,40},{40,48},{48,56},{56,64},{64,7... | collective-permute-start | bytes 12344 | tf_op jit(solution)/shard_map/ppermute | solution.py:189
  126.0 16.5 %collective-permute-start = (f32[4,257]{1,0:T(4,128)S(1)}, f32[4,257]{1,0:T(4,128)S(1)}, u32[]{:S(2)}, u32[]{:S(2)}) collective-permute-start(f32[4,257]{1,0:T(4,128)S(1)} %get-tuple-element.64), channel_id=1, source_target_pairs={{8,0},{16,8},{24,16},{32,24},{40,32},{48,40},{56,48},{64,56},{72,6... | collective-permute-start | bytes 12344 | tf_op jit(solution)/shard_map/ppermute | solution.py:189
  132.4 3.1 %copy-start.2 = (bf16[4,256,2,128]{3,2,1,0:T(2,128)(2,1)S(1)}, bf16[4,256,2,128]{3,2,1,0:T(2,128)(2,1)}, u32[]{:S(2)}) copy-start(bf16[4,256,2,128]{3,2,1,0:T(2,128)(2,1)} %reshape_squeeze.28) | copy-start | bytes 1572868
  132.4 4.1 %copy-start.6 = (bf16[1,1,512,256]{2,3,1,0:T(8,128)(2,1)S(1)}, bf16[1,1,512,256]{2,3,1,0:T(8,128)(2,1)}, u32[]{:S(2)}) copy-start(bf16[1,1,512,256]{2,3,1,0:T(8,128)(2,1)} %copy.84) | copy-start | bytes 786436
  136.5 6.2 %copy-start.1 = (bf16[4,1,1024,256]{2,3,0,1:T(8,128)(2,1)S(1)}, bf16[4,1,1024,256]{2,3,0,1:T(8,128)(2,1)}, u32[]{:S(2)}) copy-start(bf16[4,1,1024,256]{2,3,0,1:T(8,128)(2,1)} %copy.115) | copy-start | bytes 6291460
  142.3 5.0 %collective-permute-start.3 = (f32[4,2,130]{0,1,2:T(2,128)S(1)}, f32[4,2,130]{0,1,2:T(2,128)S(1)}, u32[]{:S(2)}, u32[]{:S(2)}) collective-permute-start(f32[4,2,130]{0,1,2:T(2,128)S(1)} %pad_maximum_fusion.6), channel_id=1, source_target_pairs={{8,0},{16,8},{24,16},{32,24},{40,32},{48,40},{56,48},{64,56},{72,6... | collective-permute-start | bytes 12488 | tf_op jit(solution)/shard_map/ppermute | solution.py:195
  145.7 8.4 %collective-permute-start.1 = (f32[4,2,130]{0,1,2:T(2,128)S(1)}, f32[4,2,130]{0,1,2:T(2,128)S(1)}, u32[]{:S(2)}, u32[]{:S(2)}) collective-permute-start(f32[4,2,130]{0,1,2:T(2,128)S(1)} %pad_maximum_fusion.5), channel_id=1, source_target_pairs={{0,8},{8,16},{16,24},{24,32},{32,40},{40,48},{48,56},{56,64},{64,7... | collective-permute-start | bytes 12488 | tf_op jit(solution)/shard_map/ppermute | solution.py:195
Sparse Core Ops, SparseCore 0:
  9.8 45.1 all-gather.2
  56.8 46.8 all-gather.4

commit v3 on v2

--- a/solution.py
+++ b/solution.py
@@ -161,8 +161,14 @@
 ):
     count = prefill_x.shape[0]
     requests = decode_x.shape[0]
-    half = lax.all_gather(jnp.concatenate([prefill_x, decode_x], axis=0), "tz", axis=1, tiled=True)
-    whole = lax.all_gather(half, "ty", axis=1, tiled=True)
+    rows = jnp.concatenate([prefill_x, decode_x], axis=0)
+    partner = lax.ppermute(rows, "tz", [(0, 1), (1, 0)])
+    own_y = lax.all_gather(rows, "ty", axis=1, tiled=True)
+    partner_y = lax.all_gather(partner, "ty", axis=1, tiled=True)
+    lower = lax.axis_index("tz") == 0
+    first = jnp.where(lower, own_y, partner_y).reshape(rows.shape[0], -1, 1, rows.shape[1])
+    second = jnp.where(lower, partner_y, own_y).reshape(rows.shape[0], -1, 1, rows.shape[1])
+    whole = jnp.concatenate([first, second], axis=2).reshape(rows.shape[0], -1)
     normed = layer_norm(whole, ln_gain, ln_bias)
     positions = jnp.concatenate(
         [

time: 163 us -> 199 us (1.22)
  local copies, waits for them, and re-layouts: 45.1 us -> 78.1 us
  waiting for transfers between devices: 63.3 us -> 30.4 us
  other arithmetic: 15.1 us -> 42.6 us
  starting transfers between devices: 6.72 us -> 13.8 us
    all_gather x2, waiting for transfers between devices: 56.5 us -> 9.05 us  [the longest x1 9.05 us: local(): partner_y = lax.all_gather(partner, 'ty', axis=1, tiled=True)]
    reshape x0 -> x2, local copies, waits for them, and re-layouts: none -> 17.9 us  [the longest x1 12.5 us: local(): jnp.where(lower, partner_y, own_y)]
    ppermute x0 -> x1, waiting for transfers between devices: none -> 14.6 us  [local(): partner = lax.ppermute(rows, 'tz', [(0, 1), (1, 0)])]
    reduce_sum x1, other arithmetic: 2.99 us -> 14.9 us  [layer_norm(): middle = jnp.mean(rows, axis=-1, keepdims=True)]
    convert_element_type x0 -> x1, local copies, waits for them, and re-layouts: none -> 10.6 us  [layer_norm(): (centred * lax.rsqrt(spread + EPS) * gain + shift).astype(jnp.bfloat16)]
    convert_element_type x0 -> x1, other arithmetic: none -> 8.79 us  [layer_norm(): (centred * lax.rsqrt(spread + EPS) * gain + shift).astype(jnp.bfloat16)]
    ppermute x0 -> x1, starting transfers between devices: none -> 7.28 us  [local(): partner = lax.ppermute(rows, 'tz', [(0, 1), (1, 0)])]
    reduce_sum x1, other arithmetic: 1.27 us -> 6.13 us  [layer_norm(): spread = jnp.mean(centred * centred, axis=-1, keepdims=True)]
  transfers between devices with their start and end apart: 6 -> 7, of which waited for: 3 -> 3; matrix products, arithmetic and copies ran while one was open for 32% -> 27% of each run, Pallas kernels for 0% -> 0%
where the time goes in v3:
time: 199 us; the launch traced here: 197 us
  local copies, waits for them, and re-layouts  78.1 us (39%)
  other arithmetic  42.6 us (21%)
  waiting for transfers between devices  30.4 us (15%)
  matrix products  17.2 us (9%)
  between operations  15 us (8%)
  starting transfers between devices  13.8 us (7%)
    reduce_sum x1, other arithmetic, layer_norm(): middle = jnp.mean(rows, axis=-1, keepdims=True)  14.9 us
    ppermute x1, waiting for transfers between devices, local(): partner = lax.ppermute(rows, 'tz', [(0, 1), (1, 0)])  14.6 us
    unnamed x24, local copies, waits for them, and re-layouts  12.5 us
    reshape x1, local copies, waits for them, and re-layouts, local(): jnp.where(lower, partner_y, own_y)  12.5 us
    convert_element_type x1, local copies, waits for them, and re-layouts, layer_norm(): (centred * lax.rsqrt(spread + EPS) * gain + shift).astype(jnp.bfloat16)  10.6 us
    all_gather x1, waiting for transfers between devices, local(): partner_y = lax.all_gather(partner, 'ty', axis=1, tiled=True)  9.05 us
    convert_element_type x1, other arithmetic, layer_norm(): (centred * lax.rsqrt(spread + EPS) * gain + shift).astype(jnp.bfloat16)  8.79 us
    dot_general x1, matrix products, project(): jnp.dot(normed, weight.reshape(weight.shape[0], 3 * width), preferred_ele...  8.78 us
  transfers between devices with their start and end apart: 7, of which 3 were waited for; matrix products, arithmetic and copies ran while one was open for 27% of the time, Pallas kernels for 0%

profile of v3, /device:TPU:8, one launch (start us, length us, event | category | flops | bytes accessed | tf_op | source)
XLA Modules:
  0.0 197.1 jit_solution(9359004009411949456)
XLA Ops:
  7.2 1.1 constant_dynamic-update-slice_fusion.1
  8.3 0.7 constant_dynamic-update-slice_fusion
  9.0 0.8 copy-done.1
  9.9 7.3 %collective-permute-start = (bf16[516,512]{1,0:T(8,128)(2,1)}, bf16[516,512]{1,0:T(8,128)(2,1)S(1)}, u32[]{:S(2)}, u32[]{:S(2)}) collective-permute-start(bf16[516,512]{1,0:T(8,128)(2,1)} %copy-done.1), channel_id=1, source_target_pairs={{0,1},{1,0},{2,3},{3,2},{4,5},{5,4},{6,7},{7,6},{8,9},{9,8},{10,11... | collective-permute-start | bytes 1585160 | tf_op jit(solution)/shard_map/ppermute | solution.py:165
  17.1 14.6 %collective-permute-done = bf16[516,512]{1,0:T(8,128)(2,1)S(1)} collective-permute-done((bf16[516,512]{1,0:T(8,128)(2,1)}, bf16[516,512]{1,0:T(8,128)(2,1)S(1)}, u32[]{:S(2)}, u32[]{:S(2)}) %collective-permute-start) | collective-permute-done | bytes 528416 | tf_op jit(solution)/shard_map/ppermute | solution.py:165
  31.7 0.8 copy-done.4
  32.5 0.7 add.81
  33.3 0.7 mul.188
  34.0 8.8 %copy.95 = bf16[4096,3,256]{0,2,1:T(8,128)(2,1)} copy(bf16[4096,3,256]{2,0,1:T(8,128)(2,1)} %param.15) | data formatting | bytes 12582912 | tf_op args[4]
  43.6 0.2 slice_convert_fusion.7
  43.8 0.2 multiply_cosine_fusion
  44.0 0.1 copy.99
  44.2 0.8 copy.98
  45.2 0.8 copy.102
  46.0 0.8 copy.92
  46.9 5.7 %fusion.76 = (bf16[4,1,1024,256]{3,2,1,0:T(8,128)(2,1)S(1)}, bf16[4,1,1024,256]{3,2,1,0:T(8,128)(2,1)}, bf16[4,1,1024,256]{3,2,1,0:T(8,128)(2,1)}, bf16[4,1,1024,256]{3,2,1,0:T(8,128)(2,1)}) fusion(bf16[8,2,1024,256]{3,2,1,0:T(8,128)(2,1)} %param.21), kind=kLoop, calls=%fused_computation.136 | loop fusion | bytes 16777216 | tf_op jit(solution)/shard_map/slice | solution.py:121
  52.6 4.0 %copy.126 = bf16[4,1,1024,256]{2,3,0,1:T(8,128)(2,1)} copy(bf16[4,1,1024,256]{3,2,1,0:T(8,128)(2,1)} %get-tuple-element.43) | data formatting | bytes 4194304 | tf_op jit(solution)/shard_map/reshape;squeeze | solution.py:120
  56.6 4.0 %reshape_squeeze.30 = bf16[4,1024,2,128]{3,2,1,0:T(2,128)(2,1)} reshape(bf16[4,1,1024,256]{3,2,1,0:T(8,128)(2,1)} %get-tuple-element.42) | data formatting | bytes 4194304 | tf_op jit(solution)/shard_map/reshape;squeeze | solution.py:121
  60.5 2.1 %fusion.78 = (bf16[4,1,256,256]{3,2,1,0:T(8,128)(2,1)S(1)}, bf16[4,1,256,256]{3,2,1,0:T(8,128)(2,1)}) fusion(bf16[4,2,256,256]{3,2,1,0:T(8,128)(2,1)} %param.19), kind=kLoop, calls=%fused_computation.138 | loop fusion | bytes 2097152 | tf_op jit(solution)/shard_map/slice | solution.py:130
  62.7 1.2 reshape_squeeze.31
  63.8 1.0 reshape_squeeze.28
  64.8 4.0 %copy.125 = bf16[4,1,1024,256]{2,3,0,1:T(8,128)(2,1)} copy(bf16[4,1,1024,256]{3,2,1,0:T(8,128)(2,1)} %get-tuple-element.41) | data formatting | bytes 4194304 | tf_op jit(solution)/shard_map/reshape;squeeze | solution.py:120
  68.8 2.1 %reshape_squeeze.27 = bf16[4,1024,2,128]{3,2,1,0:T(2,128)(2,1)} reshape(bf16[4,1,1024,256]{3,2,1,0:T(8,128)(2,1)S(1)} %get-tuple-element.40) | data formatting | bytes 4194304 | tf_op jit(solution)/shard_map/reshape;squeeze | solution.py:121
  71.1 1.0 pad_add_fusion
  72.1 9.0 %all-gather.5.cloned.1.call-done = bf16[516,2048]{1,0:T(8,128)(2,1)} async-done(((bf16[516,512]{1,0:T(8,128)(2,1)}), bf16[516,2048]{1,0:T(8,128)(2,1)}) %all-gather.5.cloned.1.call-update) | async-done | bytes 2113552 | tf_op jit(solution)/shard_map/all_gather | solution.py:167
  81.1 3.9 %broadcast_select_fusion.1 = (bf16[516,2048]{1,0:T(8,128)(2,1)S(1)}, bf16[516,2048]{1,0:T(8,128)(2,1)}) fusion(bf16[516,2048]{1,0:T(8,128)(2,1)} %all-gather.3.cloned.1.call-done, bf16[516,2048]{1,0:T(8,128)(2,1)} %all-gather.5.cloned.1.call-done, pred[]{:T(512)S(6)} %eq.3), kind=kLoop, calls=%fused_computation.14 | loop fusion | flops 2113536 | bytes 8454145 | tf_op jit(solution)/shard_map/jit(_where)/select_n | solution.py:169
  85.0 12.5 %reshape.299 = bf16[516,4,1,512]{3,2,1,0:T(2,128)(2,1)} reshape(bf16[516,2048]{1,0:T(8,128)(2,1)} %get-tuple-element.45) | data formatting | bytes 4227072 | tf_op jit(solution)/shard_map/reshape | solution.py:170
  97.5 5.4 %reshape.298 = bf16[516,4,1,512]{3,2,1,0:T(2,128)(2,1)} reshape(bf16[516,2048]{1,0:T(8,128)(2,1)S(1)} %get-tuple-element.44) | data formatting | bytes 4227072 | tf_op jit(solution)/shard_map/reshape | solution.py:169
  102.9 14.9 %convert_reduce_fusion = (f32[516]{0:T(1024)S(1)}, bf16[516,4,2,512]{3,2,1,0:T(2,128)(2,1)S(1)}) fusion(bf16[516,4,1,512]{3,2,1,0:T(2,128)(2,1)} %reshape.299, bf16[516,4,1,512]{3,2,1,0:T(2,128)(2,1)} %reshape.298), kind=kLoop, calls=%fused_computation.2 | loop fusion | flops 12680700 | bytes 8456208 | tf_op jit(solution)/shard_map/reduce_sum | solution.py:33
  117.8 6.1 %fusion.3 = f32[516]{0:T(1024)S(1)} fusion(bf16[516,4,2,512]{3,2,1,0:T(2,128)(2,1)S(1)} %get-tuple-element.39, f32[516]{0:T(1024)S(1)} %broadcast_multiply_fusion), kind=kLoop, calls=%fused_computation.5 | loop fusion | flops 8453628 | bytes 4231200 | tf_op jit(solution)/shard_map/reduce_sum | solution.py:35
  123.9 8.8 %fusion.6 = bf16[516,4,2,512]{3,2,1,0:T(2,128)(2,1)} fusion(bf16[516,4,2,512]{3,2,1,0:T(2,128)(2,1)S(1)} %get-tuple-element.39, f32[516]{0:T(1024)S(1)} %add_rsqrt_fusion, f32[516]{0:T(1024)S(1)} %broadcast_multiply_fusion, f32[4,2,512]{2,1,0:T(2,128)S(1)} %add.81, f32[4,2,512]{2,1,0:T(2,128)S(1)} %mul.188), kind=kLoop, calls=%fused_computation.8 | loop fusion | flops 12681216 | bytes 8491040 | tf_op jit(solution)/shard_map/convert_element_type | solution.py:36
  132.7 10.6 %convert_element_type.82 = bf16[516,4096]{1,0:T(8,128)(2,1)} reshape(bf16[516,4,2,512]{3,2,1,0:T(2,128)(2,1)} %fusion.6) | data formatting | bytes 8454144 | tf_op jit(solution)/shard_map/convert_element_type | solution.py:36
  143.3 8.8 %convolution_add_fusion = f32[516,768]{1,0:T(8,128)} fusion(bf16[516,4096]{1,0:T(8,128)(2,1)} %convert_element_type.82, bf16[4096,768]{0,1:T(8,128)(2,1)} %bitcast.118, f32[768]{0:T(1024)S(1)} %add.84), kind=kOutput, calls=%fused_computation.25 | convolution fusion | flops 3246787584 | bytes 12106752 | tf_op jit(solution)/shard_map/dot_general | solution.py:57
  152.1 2.1 %reshape.279 = f32[516,3,2,128]{3,2,1,0:T(2,128)S(1)} reshape(f32[516,768]{1,0:T(8,128)} %convolution_add_fusion) | data formatting | bytes 3170304 | tf_op jit(solution)/shard_map/reshape | solution.py:60
  154.2 0.4 fusion.77
  154.5 2.2 %copy.96 = bf16[516,3,2,128]{0,3,2,1:T(8,128)(2,1)} copy(f32[516,3,2,128]{3,2,1,0:T(2,128)S(1)} %reshape.279) | data formatting | bytes 2377728 | tf_op jit(solution)/shard_map/reshape | solution.py:60
  157.1 1.4 subtract_convert_fusion.1
  158.6 0.3 pad_maximum_fusion.3
  158.9 1.0 slice_bitcast_fusion
  160.0 0.8 slice.182
  160.8 0.3 pad_maximum_fusion.4
  161.4 5.7 %collective-permute-start.1 = (f32[4,257]{1,0:T(4,128)S(1)}, f32[4,257]{1,0:T(4,128)S(1)}, u32[]{:S(2)}, u32[]{:S(2)}) collective-permute-start(f32[4,257]{1,0:T(4,128)S(1)} %get-tuple-element.68), channel_id=1, source_target_pairs={{8,0},{16,8},{24,16},{32,24},{40,32},{48,40},{56,48},{64,56},{72,6... | collective-permute-start | bytes 12344 | tf_op jit(solution)/shard_map/ppermute | solution.py:195
  167.1 0.7 fusion.33
  167.8 2.4 %fusion.80 = (f32[2,512]{1,0:T(2,128)S(1)}, bf16[2,512,1024]{2,1,0:T(8,128)(2,1)S(1)}) fusion(f32[2,512,1024]{2,1,0:T(8,128)S(1)} %fusion.33, pred[512,1024]{1,0:T(8,128)(4,1)S(1)} %copy-done.5), kind=kOutput, calls=%fused_computation.140 | output fusion | flops 8389631 | bytes 6819840 | tf_op jit(solution)/shard_map/while/body/eval_jaxpr/sub | solution.py:73
  170.2 0.7 pad_maximum_fusion.2
  170.9 0.7 pad_maximum_fusion.1
  171.6 0.3 fusion.28
  171.9 0.8 fusion.23
  172.8 0.2 fusion.56
  173.2 2.0 %fusion.82 = f32[4,2,1,1024]{3,2,1,0:T(1,128)S(1)} fusion(bf16[4,2,128,1]{2,3,1,0:T(2,128)(2,1)S(1)} %reshape.303, bf16[4,1024,2,128]{1,3,2,0:T(8,128)(2,1)} %bitcast.117), kind=kOutput, calls=%fused_computation.142 | convolution fusion | flops 2097152 | bytes 2131968 | tf_op jit(solution)/shard_map/vmap(hd,khd->hk)/dot_general | solution.py:104
  175.2 0.2 fusion.50
  175.4 2.0 %fusion.8 = f32[4,2,1,128]{3,2,1,0:T(1,128)S(1)} fusion(bf16[4,1024,2,128]{3,2,1,0:T(2,128)(2,1)} %reshape_squeeze.30, bf16[4,2,1024,1]{2,0,1,3:T(4,128)(2,1)S(1)} %get-tuple-element.62), kind=kOutput, calls=%fused_computation.15 | convolution fusion | flops 2097152 | bytes 2117632 | tf_op jit(solution)/shard_map/vmap(hk,khd->hd)/dot_general | solution.py:111
  177.4 0.2 copy.121
  177.7 0.2 collective-permute-start.4
  178.1 0.4 fusion.81
  178.6 0.2 fusion.51
  178.8 2.0 %fusion.10 = f32[4,2,1,128]{3,2,1,0:T(1,128)S(1)} fusion(bf16[4,1024,2,128]{3,2,1,0:T(2,128)(2,1)} %reshape_squeeze.27, bf16[4,2,1024,1]{2,0,1,3:T(4,128)(2,1)S(1)} %get-tuple-element.60), kind=kOutput, calls=%fused_computation.17 | convolution fusion | flops 2097152 | bytes 2117632 | tf_op jit(solution)/shard_map/vmap(hk,khd->hd)/dot_general | solution.py:111
  180.8 0.2 copy.112
  181.0 0.5 collective-permute-start.2
  181.5 0.2 fusion.26
  181.7 0.9 copy.106
  182.5 0.2 copy.124
  182.7 6.7 %collective-permute-done.2 = f32[4,2,130]{0,1,2:T(2,128)S(1)} collective-permute-done((f32[4,2,130]{0,1,2:T(2,128)S(1)}, f32[4,2,130]{0,1,2:T(2,128)S(1)}, u32[]{:S(2)}, u32[]{:S(2)}) %collective-permute-start.2) | collective-permute-done | bytes 4192 | tf_op jit(solution)/shard_map/ppermute | solution.py:201
  189.6 0.7 copy.105
  (65 shorter events, 2.3 us)
Async XLA Ops:
  7.2 64.9 %all-gather.3.cloned.1.call-start = ((), (), s32[]{:S(2)}) async-start(), calls=%async_computation | async-start | bytes 2662400 | tf_op jit(solution)/shard_map/all_gather | solution.py:166
  9.0 0.8 copy-start.1
  9.8 71.3 %all-gather.5.cloned.1.call-start = ((), (), s32[]{:S(2)}) async-start(), calls=%async_computation.1 | async-start | bytes 2662400 | tf_op jit(solution)/shard_map/all_gather | solution.py:167
  9.9 21.8 %collective-permute-start = (bf16[516,512]{1,0:T(8,128)(2,1)}, bf16[516,512]{1,0:T(8,128)(2,1)S(1)}, u32[]{:S(2)}, u32[]{:S(2)}) collective-permute-start(bf16[516,512]{1,0:T(8,128)(2,1)} %copy-done.1), channel_id=1, source_target_pairs={{0,1},{1,0},{2,3},{3,2},{4,5},{5,4},{6,7},{7,6},{8,9},{9,8},{10,11... | collective-permute-start | bytes 1585160 | tf_op jit(solution)/shard_map/ppermute | solution.py:165
  31.7 0.8 copy-start.4
  34.0 8.9 %copy-start.9 = (f32[3,256]{1,0:T(4,128)S(1)}, f32[3,256]{1,0:T(4,128)}, u32[]{:S(2)}) copy-start(f32[3,256]{1,0:T(4,128)} %param.16) | copy-start | bytes 9220
  34.0 9.5 %copy-start.8 = (s32[4,3]{1,0:T(4,128)S(1)}, s32[4,3]{1,0:T(4,128)}, u32[]{:S(2)}) copy-start(s32[4,3]{1,0:T(4,128)} %param.20) | copy-start | bytes 148
  34.0 11.0 %copy-start.6 = (bf16[1,2,512,256]{3,2,1,0:T(8,128)(2,1)S(1)}, bf16[1,2,512,256]{3,2,1,0:T(8,128)(2,1)}, u32[]{:S(2)}) copy-start(bf16[1,2,512,256]{3,2,1,0:T(8,128)(2,1)} %param.17) | copy-start | bytes 1572868
  157.1 10.0 %copy-start.3 = (bf16[512,2,128]{2,0,1:T(8,128)(2,1)S(1)}, bf16[512,2,128]{2,0,1:T(8,128)(2,1)}, u32[]{:S(2)}) copy-start(bf16[512,2,128]{2,0,1:T(8,128)(2,1)} %copy.102) | copy-start | bytes 786436
  158.9 8.9 %copy-start.5 = (pred[512,1024]{1,0:T(8,128)(4,1)S(1)}, pred[512,1024]{1,0:T(8,128)(4,1)}, u32[]{:S(2)}) copy-start(pred[512,1024]{1,0:T(8,128)(4,1)} %pad_add_fusion) | copy-start | bytes 1572868
  161.2 11.8 %collective-permute-start.3 = (f32[4,257]{1,0:T(4,128)S(1)}, f32[4,257]{1,0:T(4,128)S(1)}, u32[]{:S(2)}, u32[]{:S(2)}) collective-permute-start(f32[4,257]{1,0:T(4,128)S(1)} %get-tuple-element.69), channel_id=1, source_target_pairs={{0,8},{8,16},{16,24},{24,32},{32,40},{40,48},{48,56},{56,64},{64,7... | collective-permute-start | bytes 12344 | tf_op jit(solution)/shard_map/ppermute | solution.py:195
  161.4 16.5 %collective-permute-start.1 = (f32[4,257]{1,0:T(4,128)S(1)}, f32[4,257]{1,0:T(4,128)S(1)}, u32[]{:S(2)}, u32[]{:S(2)}) collective-permute-start(f32[4,257]{1,0:T(4,128)S(1)} %get-tuple-element.68), channel_id=1, source_target_pairs={{8,0},{16,8},{24,16},{32,24},{40,32},{48,40},{56,48},{64,56},{72,6... | collective-permute-start | bytes 12344 | tf_op jit(solution)/shard_map/ppermute | solution.py:195
  167.8 3.1 %copy-start.2 = (bf16[4,256,2,128]{3,2,1,0:T(2,128)(2,1)S(1)}, bf16[4,256,2,128]{3,2,1,0:T(2,128)(2,1)}, u32[]{:S(2)}) copy-start(bf16[4,256,2,128]{3,2,1,0:T(2,128)(2,1)} %reshape_squeeze.28) | copy-start | bytes 1572868
  167.8 4.1 %copy-start.7 = (bf16[1,1,512,256]{2,3,1,0:T(8,128)(2,1)S(1)}, bf16[1,1,512,256]{2,3,1,0:T(8,128)(2,1)}, u32[]{:S(2)}) copy-start(bf16[1,1,512,256]{2,3,1,0:T(8,128)(2,1)} %copy.92) | copy-start | bytes 786436
  171.9 6.2 %copy-start = (bf16[4,1,1024,256]{2,3,0,1:T(8,128)(2,1)S(1)}, bf16[4,1,1024,256]{2,3,0,1:T(8,128)(2,1)}, u32[]{:S(2)}) copy-start(bf16[4,1,1024,256]{2,3,0,1:T(8,128)(2,1)} %copy.125) | copy-start | bytes 6291460
  177.7 5.0 %collective-permute-start.4 = (f32[4,2,130]{0,1,2:T(2,128)S(1)}, f32[4,2,130]{0,1,2:T(2,128)S(1)}, u32[]{:S(2)}, u32[]{:S(2)}) collective-permute-start(f32[4,2,130]{0,1,2:T(2,128)S(1)} %pad_maximum_fusion.6), channel_id=1, source_target_pairs={{8,0},{16,8},{24,16},{32,24},{40,32},{48,40},{56,48},{64,56},{72,6... | collective-permute-start | bytes 12488 | tf_op jit(solution)/shard_map/ppermute | solution.py:201
  181.0 8.4 %collective-permute-start.2 = (f32[4,2,130]{0,1,2:T(2,128)S(1)}, f32[4,2,130]{0,1,2:T(2,128)S(1)}, u32[]{:S(2)}, u32[]{:S(2)}) collective-permute-start(f32[4,2,130]{0,1,2:T(2,128)S(1)} %pad_maximum_fusion.5), channel_id=1, source_target_pairs={{0,8},{8,16},{16,24},{24,32},{32,40},{40,48},{48,56},{56,64},{64,7... | collective-permute-start | bytes 12488 | tf_op jit(solution)/shard_map/ppermute | solution.py:201
Sparse Core Ops, SparseCore 0:
  9.9 35.5 all-gather.2
  47.4 33.7 all-gather.4

commit v4 on v3

--- a/solution.py
+++ b/solution.py
@@ -100,42 +100,39 @@
     return lax.map(one_block, starts).reshape(count, heads * HD)
 
 
-def piece_partial(query, keys, values, live):
-    scores = jnp.einsum("hd,khd->hk", query, keys, preferred_element_type=jnp.float32) * (
+def piece_rows(query, keys, values, live):
+    count, heads = query.shape[0], query.shape[1]
+    own = jnp.arange(heads)[:, None] == jnp.arange(heads)[None, :]
+    spread = jnp.where(own[None, :, None, :], query[:, :, :, None], jnp.zeros((), query.dtype))
+    spread = spread.reshape(count, heads * HD, heads)
+    scores = jnp.einsum("rkf,rfh->rhk", keys, spread, preferred_element_type=jnp.float32) * (
         1.0 / math.sqrt(HD)
     )
-    masked = jnp.where(live[None], scores, NEG)
-    highest = jnp.max(masked, axis=1)
-    weights = jnp.where(live[None], jnp.exp(masked - highest[:, None]), 0.0)
-    total = jnp.sum(weights, axis=1)
-    summed = jnp.einsum(
-        "hk,khd->hd", weights.astype(jnp.bfloat16), values, preferred_element_type=jnp.float32
-    )
+    masked = jnp.where(live[:, None, :], scores, NEG)
+    highest = jnp.max(masked, axis=2)
+    weights = jnp.where(live[:, None, :], jnp.exp(masked - highest[:, :, None]), 0.0)
+    total = jnp.sum(weights, axis=2)
+    mixed = jnp.einsum(
+        "rhk,rkf->rhf", weights.astype(jnp.bfloat16), values, preferred_element_type=jnp.float32
+    ).reshape(count, heads, heads, HD)
+    summed = jnp.sum(jnp.where(own[None, :, :, None], mixed, 0.0), axis=2)
     return (highest, total, summed)
 
 
 def piece_batch(query, store, lengths):
-    count, capacity = (store.shape[0], store.shape[2])
-    heads = query.shape[1]
-    keys = store[:, 0].reshape(count, capacity, heads, HD)
-    values = store[:, 1].reshape(count, capacity, heads, HD)
+    capacity = store.shape[2]
     live = jnp.arange(capacity)[None, :] < lengths[:, None]
-    return jax.vmap(piece_partial)(query, keys, values, live)
+    return piece_rows(query, store[:, 0], store[:, 1], live)
 
 
 def home_partial(query, fresh_key, fresh_value, cache, lengths):
     count, capacity = (cache.shape[0], cache.shape[2])
-    heads = query.shape[1]
-    keys = jnp.concatenate(
-        [cache[:, 0].reshape(count, capacity, heads, HD), fresh_key[:, None]], axis=1
-    )
-    values = jnp.concatenate(
-        [cache[:, 1].reshape(count, capacity, heads, HD), fresh_value[:, None]], axis=1
-    )
+    keys = jnp.concatenate([cache[:, 0], fresh_key.reshape(count, 1, -1)], axis=1)
+    values = jnp.concatenate([cache[:, 1], fresh_value.reshape(count, 1, -1)], axis=1)
     live = jnp.concatenate(
         [jnp.arange(capacity)[None, :] < lengths[:, None], jnp.ones((count, 1), jnp.bool_)], axis=1
     )
-    return jax.vmap(piece_partial)(query, keys, values, live)
+    return piece_rows(query, keys, values, live)
 
 
 def combine(parts):
@@ -165,11 +162,17 @@
     partner = lax.ppermute(rows, "tz", [(0, 1), (1, 0)])
     own_y = lax.all_gather(rows, "ty", axis=1, tiled=True)
     partner_y = lax.all_gather(partner, "ty", axis=1, tiled=True)
-    lower = lax.axis_index("tz") == 0
-    first = jnp.where(lower, own_y, partner_y).reshape(rows.shape[0], -1, 1, rows.shape[1])
-    second = jnp.where(lower, partner_y, own_y).reshape(rows.shape[0], -1, 1, rows.shape[1])
-    whole = jnp.concatenate([first, second], axis=2).reshape(rows.shape[0], -1)
-    normed = layer_norm(whole, ln_gain, ln_bias)
+    whole = jnp.concatenate([own_y, partner_y], axis=1)
+    z = lax.axis_index("tz")
+
+    def feature_order(table):
+        blocks = table.reshape((-1, 2, rows.shape[1]) + table.shape[1:])
+        own = lax.dynamic_index_in_dim(blocks, z, 1, keepdims=False)
+        other = lax.dynamic_index_in_dim(blocks, 1 - z, 1, keepdims=False)
+        return jnp.concatenate([own, other], axis=0).reshape(table.shape)
+
+    normed = layer_norm(whole, feature_order(ln_gain), feature_order(ln_bias))
+    qkv_weight = feature_order(qkv_weight)
     positions = jnp.concatenate(
         [
             prefill_offset[0] + jnp.arange(count, dtype=jnp.int32),

time: 199 us -> 142 us (0.71)
  local copies, waits for them, and re-layouts: 78.1 us -> 40.7 us
  other arithmetic: 42.6 us -> 17 us
  waiting for transfers between devices: 30.4 us -> 35.9 us
    reshape x2 -> x7, local copies, waits for them, and re-layouts: 17.9 us -> 0.18 us  [the longest x1 0.1 us: home_partial(): fresh_value.reshape(count, 1, -1)]
    dynamic_slice x0 -> x4, local copies, waits for them, and re-layouts: none -> 17.3 us  [the longest x3 12.5 us: feature_order(): own = lax.dynamic_index_in_dim(blocks, z, 1, keepdims=False)]
    another operation x6 -> x0, local copies, waits for them, and re-layouts: 16.2 us -> none  [the longest x2 8.01 us: piece_batch(): keys = store[:, 0].reshape(count, capacity, heads, HD)]
    reduce_sum x1, other arithmetic: 14.9 us -> 3.03 us  [layer_norm(): middle = jnp.mean(rows, axis=-1, keepdims=True)]
    convert_element_type x3 -> x0, local copies, waits for them, and re-layouts: 10.6 us -> none  [the longest x1 10.6 us: layer_norm(): (centred * lax.rsqrt(spread + EPS) * gain + shift).astype(jnp.bfloat16)]
    convert_element_type x4 -> x0, other arithmetic: 9.27 us -> none  [the longest x1 8.79 us: layer_norm(): (centred * lax.rsqrt(spread + EPS) * gain + shift).astype(jnp.bfloat16)]
    slice x2 -> x4, local copies, waits for them, and re-layouts: 7.84 us -> 0.17 us  [answer(): return (got[:, :, HD], got[:, :, HD + 1], got[:, :, :HD])]
    all_gather x1, waiting for transfers between devices: 9.05 us -> 14.4 us  [local(): partner_y = lax.all_gather(partner, 'ty', axis=1, tiled=True)]
  transfers between devices with their start and end apart: 7 -> 7, of which waited for: 3 -> 4; matrix products, arithmetic and copies ran while one was open for 27% -> 31% of each run, Pallas kernels for 0% -> 0%
where the time goes in v4:
time: 142 us
  local copies, waits for them, and re-layouts  40.7 us (29%)
  waiting for transfers between devices  35.9 us (25%)
  matrix products  18.9 us (13%)
  other arithmetic  17 us (12%)
  between operations  15.4 us (11%)
  starting transfers between devices  13.7 us (10%)
    ppermute x1, waiting for transfers between devices, local(): partner = lax.ppermute(rows, 'tz', [(0, 1), (1, 0)])  14.6 us
    all_gather x1, waiting for transfers between devices, local(): partner_y = lax.all_gather(partner, 'ty', axis=1, tiled=True)  14.4 us
    dynamic_slice x3, local copies, waits for them, and re-layouts, feature_order(): own = lax.dynamic_index_in_dim(blocks, z, 1, keepdims=False)  12.5 us
    unnamed x46, local copies, waits for them, and re-layouts  11.3 us
    dot_general x1, matrix products, project(): jnp.dot(normed, weight.reshape(weight.shape[0], 3 * width), preferred_ele...  8.04 us
    ppermute x1, starting transfers between devices, local(): partner = lax.ppermute(rows, 'tz', [(0, 1), (1, 0)])  7.28 us
    ppermute x2, waiting for transfers between devices, answer(): got = lax.ppermute(packed, 'group', pairs)  6.96 us
    ppermute x2, starting transfers between devices, ask(): got = lax.ppermute(packed, 'group', pairs)  5.72 us
  transfers between devices with their start and end apart: 7, of which 4 were waited for; matrix products, arithmetic and copies ran while one was open for 31% of the time, Pallas kernels for 0%

profile of v4, /device:TPU:8, one launch (start us, length us, event | category | flops | bytes accessed | tf_op | source)
XLA Modules:
  0.0 141.7 jit_solution(1339242411152558257)
XLA Ops:
  7.2 1.1 constant_dynamic-update-slice_fusion.1
  8.3 0.7 constant_dynamic-update-slice_fusion
  9.0 0.8 copy-done.2
  9.9 7.3 %collective-permute-start = (bf16[516,512]{1,0:T(8,128)(2,1)}, bf16[516,512]{1,0:T(8,128)(2,1)S(1)}, u32[]{:S(2)}, u32[]{:S(2)}) collective-permute-start(bf16[516,512]{1,0:T(8,128)(2,1)} %copy-done.2), channel_id=1, source_target_pairs={{0,1},{1,0},{2,3},{3,2},{4,5},{5,4},{6,7},{7,6},{8,9},{9,8},{10,11... | collective-permute-start | bytes 1585160 | tf_op jit(solution)/shard_map/ppermute | solution.py:162
  17.1 14.6 %collective-permute-done = bf16[516,512]{1,0:T(8,128)(2,1)S(1)} collective-permute-done((bf16[516,512]{1,0:T(8,128)(2,1)}, bf16[516,512]{1,0:T(8,128)(2,1)S(1)}, u32[]{:S(2)}, u32[]{:S(2)}) %collective-permute-start) | collective-permute-done | bytes 528416 | tf_op jit(solution)/shard_map/ppermute | solution.py:162
  31.7 0.8 copy-done.4
  32.5 6.3 %constant_dynamic-slice_fusion.1 = (bf16[4,1,512,3,256]{4,2,1,0,3:T(8,128)(2,1)}, bf16[4,1,512,3,256]{4,2,1,0,3:T(8,128)(2,1)}) fusion(bf16[4,2,512,3,256]{4,2,1,0,3:T(8,128)(2,1)} %bitcast.138, s32[]{:T(128)S(6)} %select_n.64, s32[]{:T(128)S(6)} %select_n.65), kind=kLoop, calls=%fused_computation.135 | loop fusion | bytes 12582920 | tf_op jit(solution)/shard_map/jit(dynamic_index_in_dim)/dynamic_slice | solution.py:170
  38.8 4.8 %copy.162 = bf16[4,1,512,3,256]{2,0,4,3,1:T(4,128)(2,1)S(1)} copy(bf16[4,1,512,3,256]{4,2,1,0,3:T(8,128)(2,1)} %get-tuple-element.42) | data formatting | bytes 6291456 | tf_op jit(solution)/shard_map/jit(dynamic_index_in_dim)/dynamic_slice | solution.py:171
  43.6 6.2 %copy.161 = bf16[4,1,512,3,256]{2,0,4,3,1:T(4,128)(2,1)} copy(bf16[4,1,512,3,256]{4,2,1,0,3:T(8,128)(2,1)} %get-tuple-element.41) | data formatting | bytes 6291456 | tf_op jit(solution)/shard_map/jit(dynamic_index_in_dim)/dynamic_slice | solution.py:170
  49.8 4.5 %pad_maximum_fusion = bf16[8,512,3,256]{1,0,3,2:T(8,128)(2,1)S(1)} fusion(bf16[4,512,3,256]{1,0,3,2:T(4,128)(2,1)S(1)} %bitcast.132, bf16[4,512,3,256]{1,0,3,2:T(4,128)(2,1)} %bitcast.133), kind=kLoop, calls=%fused_computation.9 | loop fusion | flops 12582912 | bytes 12582912 | tf_op jit(solution)/shard_map/concatenate | solution.py:172
  54.4 6.8 %copy.215 = bf16[96,8,8,512]{3,1,2,0:T(8,128)(2,1)} copy(bf16[96,8,8,512]{3,2,1,0:T(8,128)(2,1)S(1)} %bitcast.131) | data formatting | bytes 12582912
  62.3 0.2 slice_convert_fusion.7
  62.6 0.2 multiply_cosine_fusion
  62.8 0.1 copy.166
  62.9 0.1 copy.165
  63.1 0.1 copy.201
  63.3 0.2 copy.169
  63.5 0.8 copy.160
  64.3 0.1 copy.170
  64.7 1.0 pad_add_fusion
  65.7 1.1 slice_bitcast_fusion.1
  66.8 14.4 %all-gather.5.cloned.1.call-done = bf16[516,2048]{1,0:T(8,128)(2,1)} async-done(((bf16[516,512]{1,0:T(8,128)(2,1)}), bf16[516,2048]{1,0:T(8,128)(2,1)}) %all-gather.5.cloned.1.call-update) | async-done | bytes 2113552 | tf_op jit(solution)/shard_map/all_gather | solution.py:164
  81.1 3.0 %convert_reduce_fusion = f32[516]{0:T(1024)S(1)} fusion(bf16[516,2048]{1,0:T(8,128)(2,1)} %all-gather.5.cloned.1.call-done, bf16[516,2048]{1,0:T(8,128)(2,1)} %all-gather.3.cloned.1.call-done), kind=kLoop, calls=%fused_computation.2 | loop fusion | flops 10567164 | bytes 4229136 | tf_op jit(solution)/shard_map/reduce_sum | solution.py:33
  84.2 3.0 %fusion.3 = f32[516]{0:T(1024)S(1)} fusion(f32[516]{0:T(1024)S(1)} %broadcast_multiply_fusion, bf16[516,2048]{1,0:T(8,128)(2,1)S(1)} %copy-done.1, bf16[516,2048]{1,0:T(8,128)(2,1)S(1)} %copy-done), kind=kLoop, calls=%fused_computation.5 | loop fusion | flops 14794236 | bytes 4231200 | tf_op jit(solution)/shard_map/reduce_sum | solution.py:35
  87.3 8.0 %fusion.31 = f32[516,768]{1,0:T(8,128)} fusion(bf16[4096,768]{0,1:T(8,128)(2,1)} %bitcast.139, f32[4096]{0:T(1024)S(1)} %bitcast.148, f32[4096]{0:T(1024)S(1)} %bitcast.149, f32[516]{0:T(1024)S(1)} %add_rsqrt_fusion, f32[516]{0:T(1024)S(1)} %broadcast_multiply_fusion, bf16[516,2048]{1,0:T(8,128)(2,1)S(1)} %copy-done.1, bf16[516,2048]{1,0:T(8,128)(2,1)S(1)} %copy-done, ...), kind=kOutput, calls=%fused_computation.37 | convolution fusion | flops 3265809408 | bytes 12143648 | tf_op jit(solution)/shard_map/dot_general | solution.py:57
  95.3 2.1 %reshape.239 = f32[516,3,2,128]{3,2,1,0:T(2,128)S(1)} reshape(f32[516,768]{1,0:T(8,128)} %fusion.31) | data formatting | bytes 3170304 | tf_op jit(solution)/shard_map/reshape | solution.py:60
  97.4 0.4 fusion.108
  97.8 2.2 %copy.163 = bf16[516,3,2,128]{0,3,2,1:T(8,128)(2,1)} copy(f32[516,3,2,128]{3,2,1,0:T(2,128)S(1)} %reshape.239) | data formatting | bytes 2377728 | tf_op jit(solution)/shard_map/reshape | solution.py:60
  100.0 0.1 slice.261
  100.2 0.1 slice.262
  100.3 0.5 subtract_convert_fusion.1
  100.8 0.3 pad_maximum_fusion.3
  101.1 1.0 slice_bitcast_fusion.2
  102.1 0.8 slice.182
  103.0 0.3 pad_maximum_fusion.4
  103.5 5.6 %collective-permute-start.1 = (f32[4,257]{1,0:T(4,128)S(1)}, f32[4,257]{1,0:T(4,128)S(1)}, u32[]{:S(2)}, u32[]{:S(2)}) collective-permute-start(f32[4,257]{1,0:T(4,128)S(1)} %get-tuple-element.63), channel_id=1, source_target_pairs={{8,0},{16,8},{24,16},{32,24},{40,32},{48,40},{56,48},{64,56},{72,6... | collective-permute-start | bytes 12344 | tf_op jit(solution)/shard_map/ppermute | solution.py:198
  109.1 0.1 copy.187
  109.2 0.7 fusion.66
  110.0 2.4 %fusion.110 = (f32[2,512]{1,0:T(2,128)S(1)}, bf16[2,512,1024]{2,1,0:T(8,128)(2,1)S(1)}) fusion(f32[2,512,1024]{2,1,0:T(8,128)S(1)} %fusion.66, pred[512,1024]{1,0:T(8,128)(4,1)S(1)} %copy-done.5), kind=kOutput, calls=%fused_computation.173 | output fusion | flops 8389631 | bytes 6819840 | tf_op jit(solution)/shard_map/while/body/eval_jaxpr/sub | solution.py:73
  112.3 0.8 fusion.40
  113.2 0.2 copy-done.8
  113.4 0.3 fusion.113
  113.7 0.2 fusion.59
  114.0 0.1 fusion.76
  114.2 2.3 %fusion.111 = (f32[4,2]{1,0:T(4,128)S(1)}, f32[4,2,1024]{2,1,0:T(2,128)S(1)}) fusion(bf16[8,2,1024,256]{3,2,1,0:T(8,128)(2,1)} %param.21, pred[256,2]{0,1:T(4,128)(4,1)S(1)} %bitcast.156, bf16[4,256]{1,0:T(4,128)(2,1)S(1)} %slice.263, pred[4,1024]{1,0:T(4,128)(4,1)S(1)} %iota_compare_fusion.1), kind=kOutput, calls=%fused_computation.174 | convolution fusion | flops 4220920 | bytes 2136608 | tf_op jit(solution)/shard_map/rkf,rfh->rhk/dot_general | solution.py:108
  116.5 2.0 %fusion.14 = f32[4,2,256]{2,1,0:T(2,128)S(1)} fusion(bf16[8,2,1024,256]{3,2,1,0:T(8,128)(2,1)} %param.21, f32[4,2,1024]{2,1,0:T(2,128)S(1)} %get-tuple-element.73, pred[4,1024]{1,0:T(4,128)(4,1)S(1)} %iota_compare_fusion.1, f32[4,2]{1,0:T(4,128)S(1)} %get-tuple-element.72), kind=kOutput, calls=%fused_computation.19 | convolution fusion | flops 4218880 | bytes 2142240 | tf_op jit(solution)/shard_map/rhk,rkf->rhf/dot_general | solution.py:115
  118.5 0.2 fusion.74
  118.8 0.1 fusion.77
  119.0 2.3 %fusion.112 = (f32[4,2]{1,0:T(4,128)S(1)}, f32[4,2,1024]{2,1,0:T(2,128)S(1)}) fusion(bf16[8,2,1024,256]{3,2,1,0:T(8,128)(2,1)} %param.21, pred[256,2]{0,1:T(4,128)(4,1)S(1)} %bitcast.157, bf16[4,256]{1,0:T(4,128)(2,1)S(1)} %slice.264, pred[4,1024]{1,0:T(4,128)(4,1)S(1)} %iota_compare_fusion.2), kind=kOutput, calls=%fused_computation.175 | convolution fusion | flops 4220920 | bytes 2136608 | tf_op jit(solution)/shard_map/rkf,rfh->rhk/dot_general | solution.py:108
  121.4 2.0 %fusion.18 = f32[4,2,256]{2,1,0:T(2,128)S(1)} fusion(bf16[8,2,1024,256]{3,2,1,0:T(8,128)(2,1)} %param.21, f32[4,2,1024]{2,1,0:T(2,128)S(1)} %get-tuple-element.75, pred[4,1024]{1,0:T(4,128)(4,1)S(1)} %iota_compare_fusion.2, f32[4,2]{1,0:T(4,128)S(1)} %get-tuple-element.74), kind=kOutput, calls=%fused_computation.23 | convolution fusion | flops 4218880 | bytes 2142240 | tf_op jit(solution)/shard_map/rhk,rkf->rhf/dot_general | solution.py:115
  123.4 0.2 fusion.73
  123.7 0.1 copy.182
  123.8 0.1 select_reduce_fusion.2
  123.9 0.2 copy.183
  124.1 0.5 collective-permute-start.4
  124.8 0.2 copy.175
  125.0 0.2 collective-permute-start.2
  125.1 0.2 fusion.84
  125.4 0.8 copy.195
  126.3 2.1 %collective-permute-done.4 = f32[4,2,130]{0,1,2:T(2,128)S(1)} collective-permute-done((f32[4,2,130]{0,1,2:T(2,128)S(1)}, f32[4,2,130]{0,1,2:T(2,128)S(1)}, u32[]{:S(2)}, u32[]{:S(2)}) %collective-permute-start.4) | collective-permute-done | bytes 4192 | tf_op jit(solution)/shard_map/ppermute | solution.py:204
  128.5 4.9 %collective-permute-done.2 = f32[4,2,130]{0,1,2:T(2,128)S(1)} collective-permute-done((f32[4,2,130]{0,1,2:T(2,128)S(1)}, f32[4,2,130]{0,1,2:T(2,128)S(1)}, u32[]{:S(2)}, u32[]{:S(2)}) %collective-permute-start.2) | collective-permute-done | bytes 4192 | tf_op jit(solution)/shard_map/ppermute | solution.py:204
  133.5 0.1 copy.212
  134.0 0.1 copy.193
  134.1 0.7 copy.194
  (90 shorter events, 2.4 us)
Async XLA Ops:
  7.2 59.6 %all-gather.3.cloned.1.call-start = ((), (), s32[]{:S(2)}) async-start(), calls=%async_computation | async-start | bytes 2662400 | tf_op jit(solution)/shard_map/all_gather | solution.py:163
  9.0 0.8 copy-start.2
  9.8 71.3 %all-gather.5.cloned.1.call-start = ((), (), s32[]{:S(2)}) async-start(), calls=%async_computation.1 | async-start | bytes 2662400 | tf_op jit(solution)/shard_map/all_gather | solution.py:164
  9.9 21.8 %collective-permute-start = (bf16[516,512]{1,0:T(8,128)(2,1)}, bf16[516,512]{1,0:T(8,128)(2,1)S(1)}, u32[]{:S(2)}, u32[]{:S(2)}) collective-permute-start(bf16[516,512]{1,0:T(8,128)(2,1)} %copy-done.2), channel_id=1, source_target_pairs={{0,1},{1,0},{2,3},{3,2},{4,5},{5,4},{6,7},{7,6},{8,9},{9,8},{10,11... | collective-permute-start | bytes 1585160 | tf_op jit(solution)/shard_map/ppermute | solution.py:162
  31.7 0.8 copy-start.4
  54.3 6.9 %copy-start.11 = (f32[4096]{0:T(1024)S(1)}, f32[4096]{0:T(1024)}, u32[]{:S(2)}) copy-start(f32[4096]{0:T(1024)} %param.14) | copy-start | bytes 49156
  54.3 6.9 %copy-start.12 = (f32[4096]{0:T(1024)S(1)}, f32[4096]{0:T(1024)}, u32[]{:S(2)}) copy-start(f32[4096]{0:T(1024)} %param.13) | copy-start | bytes 49156
  54.3 7.1 %copy-start.13 = (f32[3,256]{1,0:T(4,128)S(1)}, f32[3,256]{1,0:T(4,128)}, u32[]{:S(2)}) copy-start(f32[3,256]{1,0:T(4,128)} %param.16) | copy-start | bytes 9220
  54.4 8.0 %copy-start.10 = (s32[4,3]{1,0:T(4,128)S(1)}, s32[4,3]{1,0:T(4,128)}, u32[]{:S(2)}) copy-start(s32[4,3]{1,0:T(4,128)} %param.20) | copy-start | bytes 148
  54.4 8.7 %copy-start.6 = (bf16[1,2,512,256]{3,2,1,0:T(8,128)(2,1)S(1)}, bf16[1,2,512,256]{3,2,1,0:T(8,128)(2,1)}, u32[]{:S(2)}) copy-start(bf16[1,2,512,256]{3,2,1,0:T(8,128)(2,1)} %param.17) | copy-start | bytes 1572868
  61.2 4.4 %copy-start.3 = (bf16[4,2,256,256]{3,2,1,0:T(8,128)(2,1)S(1)}, bf16[4,2,256,256]{3,2,1,0:T(8,128)(2,1)}, u32[]{:S(2)}) copy-start(bf16[4,2,256,256]{3,2,1,0:T(8,128)(2,1)} %param.19) | copy-start | bytes 3145732
  66.8 17.4 %copy-start = (bf16[516,2048]{1,0:T(8,128)(2,1)S(1)}, bf16[516,2048]{1,0:T(8,128)(2,1)}, u32[]{:S(2)}) copy-start(bf16[516,2048]{1,0:T(8,128)(2,1)} %all-gather.3.cloned.1.call-done) | copy-start | bytes 6340612
  81.1 3.1 %copy-start.1 = (bf16[516,2048]{1,0:T(8,128)(2,1)S(1)}, bf16[516,2048]{1,0:T(8,128)(2,1)}, u32[]{:S(2)}) copy-start(bf16[516,2048]{1,0:T(8,128)(2,1)} %all-gather.5.cloned.1.call-done) | copy-start | bytes 6340612
  101.1 8.8 %copy-start.5 = (pred[512,1024]{1,0:T(8,128)(4,1)S(1)}, pred[512,1024]{1,0:T(8,128)(4,1)}, u32[]{:S(2)}) copy-start(pred[512,1024]{1,0:T(8,128)(4,1)} %pad_add_fusion) | copy-start | bytes 1572868
  103.4 10.6 %collective-permute-start.3 = (f32[4,257]{1,0:T(4,128)S(1)}, f32[4,257]{1,0:T(4,128)S(1)}, u32[]{:S(2)}, u32[]{:S(2)}) collective-permute-start(f32[4,257]{1,0:T(4,128)S(1)} %get-tuple-element.64), channel_id=1, source_target_pairs={{0,8},{8,16},{16,24},{24,32},{32,40},{40,48},{48,56},{56,64},{64,7... | collective-permute-start | bytes 12344 | tf_op jit(solution)/shard_map/ppermute | solution.py:198
  103.5 15.4 %collective-permute-start.1 = (f32[4,257]{1,0:T(4,128)S(1)}, f32[4,257]{1,0:T(4,128)S(1)}, u32[]{:S(2)}, u32[]{:S(2)}) collective-permute-start(f32[4,257]{1,0:T(4,128)S(1)} %get-tuple-element.63), channel_id=1, source_target_pairs={{8,0},{16,8},{24,16},{32,24},{40,32},{48,40},{56,48},{64,56},{72,6... | collective-permute-start | bytes 12344 | tf_op jit(solution)/shard_map/ppermute | solution.py:198
  109.9 2.4 %copy-start.9 = (bf16[1,1,512,256]{2,3,1,0:T(8,128)(2,1)S(1)}, bf16[1,1,512,256]{2,3,1,0:T(8,128)(2,1)}, u32[]{:S(2)}) copy-start(bf16[1,1,512,256]{2,3,1,0:T(8,128)(2,1)} %copy.160) | copy-start | bytes 786436
  112.3 1.0 copy-start.8
  112.3 1.4 copy-start.7
  124.1 4.2 %collective-permute-start.4 = (f32[4,2,130]{0,1,2:T(2,128)S(1)}, f32[4,2,130]{0,1,2:T(2,128)S(1)}, u32[]{:S(2)}, u32[]{:S(2)}) collective-permute-start(f32[4,2,130]{0,1,2:T(2,128)S(1)} %pad_maximum_fusion.6), channel_id=1, source_target_pairs={{8,0},{16,8},{24,16},{32,24},{40,32},{48,40},{56,48},{64,56},{72,6... | collective-permute-start | bytes 12488 | tf_op jit(solution)/shard_map/ppermute | solution.py:204
  125.0 8.4 %collective-permute-start.2 = (f32[4,2,130]{0,1,2:T(2,128)S(1)}, f32[4,2,130]{0,1,2:T(2,128)S(1)}, u32[]{:S(2)}, u32[]{:S(2)}) collective-permute-start(f32[4,2,130]{0,1,2:T(2,128)S(1)} %pad_maximum_fusion.5), channel_id=1, source_target_pairs={{0,8},{8,16},{16,24},{24,32},{32,40},{40,48},{48,56},{56,64},{64,7... | collective-permute-start | bytes 12488 | tf_op jit(solution)/shard_map/ppermute | solution.py:204
Sparse Core Ops, SparseCore 0:
  9.9 35.5 all-gather.2
  47.4 33.7 all-gather.4

commit v5 on v4

--- a/solution.py
+++ b/solution.py
@@ -4,6 +4,8 @@
 import jax
 import jax.numpy as jnp
 from jax import lax
+from jax.experimental import pallas as pl
+from jax.experimental.pallas import tpu as pltpu
 from jax.sharding import PartitionSpec as P
 
 HD = 128
@@ -51,12 +53,44 @@
     )
 
 
-def project(normed, weight, bias, positions):
+def qkv_kernel(order_ref, x_ref, w_ref, o_ref):
+    @pl.when(pl.program_id(0) == 0)
+    def _():
+        o_ref[...] = jnp.zeros_like(o_ref)
+
+    o_ref[...] += jnp.dot(x_ref[...], w_ref[...], preferred_element_type=jnp.float32)
+
+
+def qkv_matmul(normed, weight, order):
+    rows, depth = normed.shape
+    width = weight.shape[1]
+    blocks = order.shape[0]
+    size = depth // blocks
+    return pl.pallas_call(
+        qkv_kernel,
+        out_shape=jax.ShapeDtypeStruct((rows, width), jnp.float32),
+        grid_spec=pltpu.PrefetchScalarGridSpec(
+            num_scalar_prefetch=1,
+            grid=(blocks,),
+            in_specs=[
+                pl.BlockSpec((rows, size), lambda j, order: (0, j)),
+                pl.BlockSpec((size, width), lambda j, order: (order[j], 0)),
+            ],
+            out_specs=pl.BlockSpec((rows, width), lambda j, order: (0, 0)),
+        ),
+        compiler_params=pltpu.CompilerParams(dimension_semantics=("arbitrary",)),
+        cost_estimate=pl.CostEstimate(
+            flops=2 * rows * depth * width,
+            bytes_accessed=2 * rows * depth + 2 * depth * width + 4 * rows * width,
+            transcendentals=0,
+        ),
+    )(order, normed, weight)
+
+
+def project(normed, weight, bias, positions, order):
     count = normed.shape[0]
     width = weight.shape[2]
-    mixed = jnp.dot(
-        normed, weight.reshape(weight.shape[0], 3 * width), preferred_element_type=jnp.float32
-    )
+    mixed = qkv_matmul(normed, weight.reshape(weight.shape[0], 3 * width), order)
     mixed = (mixed + bias.reshape(1, 3 * width)).reshape(count, 3, width // HD, HD)
     query = rotate(mixed[:, 0], positions).astype(jnp.bfloat16)
     fresh_key = rotate(mixed[:, 1], positions).astype(jnp.bfloat16)
@@ -159,20 +193,31 @@
     count = prefill_x.shape[0]
     requests = decode_x.shape[0]
     rows = jnp.concatenate([prefill_x, decode_x], axis=0)
+    ring = lax.axis_size("ty")
+    y = lax.axis_index("ty")
+    z = lax.axis_index("tz")
+    up = [(i, (i + 1) % ring) for i in range(ring)]
+    down = [(i, (i - 1) % ring) for i in range(ring)]
+    half = rows.shape[0] // 2
+
+    def around(block):
+        below = lax.ppermute(block, "ty", up)
+        above = lax.ppermute(block, "ty", down)
+        across = jnp.concatenate(
+            [lax.ppermute(below[:half], "ty", up), lax.ppermute(above[half:], "ty", down)], axis=0
+        )
+        return [block, below, above, across]
+
     partner = lax.ppermute(rows, "tz", [(0, 1), (1, 0)])
-    own_y = lax.all_gather(rows, "ty", axis=1, tiled=True)
-    partner_y = lax.all_gather(partner, "ty", axis=1, tiled=True)
-    whole = jnp.concatenate([own_y, partner_y], axis=1)
-    z = lax.axis_index("tz")
+    pieces = around(rows) + around(partner)
+    whole = jnp.concatenate(pieces, axis=1)
+    spots = jnp.stack([y, (y + ring - 1) % ring, (y + 1) % ring, (y + 2) % ring])
+    order = jnp.concatenate([spots * 2 + z, spots * 2 + (1 - z)]).astype(jnp.int32)
 
     def feature_order(table):
-        blocks = table.reshape((-1, 2, rows.shape[1]) + table.shape[1:])
-        own = lax.dynamic_index_in_dim(blocks, z, 1, keepdims=False)
-        other = lax.dynamic_index_in_dim(blocks, 1 - z, 1, keepdims=False)
-        return jnp.concatenate([own, other], axis=0).reshape(table.shape)
+        return table.reshape(order.shape[0], -1)[order].reshape(table.shape)
 
     normed = layer_norm(whole, feature_order(ln_gain), feature_order(ln_bias))
-    qkv_weight = feature_order(qkv_weight)
     positions = jnp.concatenate(
         [
             prefill_offset[0] + jnp.arange(count, dtype=jnp.int32),
@@ -180,7 +225,7 @@
         ],
         axis=0,
     )
-    query, fresh_key, fresh_value = project(normed, qkv_weight, qkv_bias, positions)
+    query, fresh_key, fresh_value = project(normed, qkv_weight, qkv_bias, positions, order)
     own_query = query[count:]
     home_parts = home_partial(
         own_query, fresh_key[count:], fresh_value[count:], home_cache, piece_len[:, 1]

time: 142 us -> 140 us (0.986)
  the two profiles are of different devices: /device:TPU:8 before, /device:TPU:255 now
where the time goes in v5:
time: 140 us; the launch traced here: 139 us
  local copies, waits for them, and re-layouts  44.9 us (32%)
  other arithmetic  26.7 us (19%)
  waiting for transfers between devices  24.9 us (18%)
  starting transfers between devices  19.4 us (14%)
  matrix products  10.8 us (8%)
  Pallas kernels  10.4 us (7%)
  between operations  1.74 us (1%)
    unnamed x45, local copies, waits for them, and re-layouts  18.5 us
    ppermute x1, waiting for transfers between devices, local(): partner = lax.ppermute(rows, 'tz', [(0, 1), (1, 0)])  14.9 us
    pallas_call x1, Pallas kernels, qkv_matmul(): pl.pallas_call(qkv_kernel, out_shape=jax.ShapeDtypeStruct((rows, width),...  10.4 us
    ppermute x2, starting transfers between devices, ask(): got = lax.ppermute(packed, 'group', pairs)  9.18 us
    reshape x1, local copies, waits for them, and re-layouts, project(): weight.reshape(weight.shape[0], 3 * width)  8.7 us
    ppermute x2, waiting for transfers between devices, answer(): got = lax.ppermute(packed, 'group', pairs)  7.11 us
    convert_element_type x1, other arithmetic, layer_norm(): (centred * lax.rsqrt(spread + EPS) * gain + shift).astype(jnp.bfloat16)  6.53 us
    ppermute x2, starting transfers between devices, around(): lax.ppermute(below[:half], 'ty', up)  5.24 us
  transfers between devices with their start and end apart: 13, of which 4 were waited for; matrix products, arithmetic and copies ran while one was open for 36% of the time, Pallas kernels for 0%

profile of v5, /device:TPU:255, one launch (start us, length us, event | category | flops | bytes accessed | tf_op | source)
XLA Modules:
  0.0 139.0 jit_solution(11362643489050446486)
XLA Ops:
  0.6 2.1 %constant_dynamic-update-slice_fusion.1 = (bf16[516,512]{1,0:T(8,128)(2,1)S(1)}, bf16[516,4096]{1,0:T(8,128)(2,1)}) fusion(bf16[512,512]{1,0:T(8,128)(2,1)} %param.11), kind=kLoop, calls=%fused_computation.80 | loop fusion | bytes 1572864
  2.7 1.3 constant_dynamic-update-slice_fusion
  4.0 1.5 %collective-permute-start.1 = (bf16[516,512]{1,0:T(8,128)(2,1)S(1)}, bf16[516,512]{1,0:T(8,128)(2,1)S(1)}, u32[]{:S(2)}, u32[]{:S(2)}) collective-permute-start(bf16[516,512]{1,0:T(8,128)(2,1)S(1)} %get-tuple-element.63), channel_id=1, source_target_pairs={{0,6},{2,0},{4,2},{6,4},{1,7},{3,1},{5,3},{7,5},{8,14},{10,8},{12,... | collective-permute-start | bytes 1585160 | tf_op jit(solution)/shard_map/ppermute | solution.py:205
  5.5 1.2 collective-permute-start.4
  6.7 1.6 %slice_convert_fusion.7 = (f32[4,1]{1,0:T(4,128)S(1)}, f32[4,1]{1,0:T(4,128)}, s32[4]{0:T(128)S(1)}, s32[4]{0:T(128)S(1)}) fusion(s32[4,3]{1,0:T(4,128)} %param.20), kind=kLoop, calls=%fused_computation.132 | loop fusion | flops 16 | bytes 112 | tf_op jit(solution)/shard_map/convert_element_type | solution.py:240
  9.0 0.6 iota_compare_fusion.3
  9.7 0.6 broadcast_bitcast_fusion
  10.3 1.1 fusion.100
  11.4 0.5 iota_compare_fusion.4
  12.2 0.6 pad.25.clone
  12.8 1.0 pad_add_fusion
  13.9 1.0 slice_bitcast_fusion.1
  14.9 14.9 %collective-permute-done.4 = bf16[516,512]{1,0:T(8,128)(2,1)} collective-permute-done((bf16[516,512]{1,0:T(8,128)(2,1)S(1)}, bf16[516,512]{1,0:T(8,128)(2,1)}, u32[]{:S(2)}, u32[]{:S(2)}) %collective-permute-start.4) | collective-permute-done | bytes 528416 | tf_op jit(solution)/shard_map/ppermute | solution.py:211
  29.9 1.3 collective-permute-start.5
  31.4 0.7 slice.184
  32.1 2.5 %collective-permute-start.2 = (bf16[258,512]{1,0:T(8,128)(2,1)}, bf16[258,512]{1,0:T(8,128)(2,1)}, u32[]{:S(2)}, u32[]{:S(2)}) collective-permute-start(bf16[258,512]{1,0:T(8,128)(2,1)} %slice.184), channel_id=1, source_target_pairs={{0,2},{2,4},{4,6},{6,0},{1,3},{3,5},{5,7},{7,1},{8,10},{10,12},{12... | collective-permute-start | bytes 792584 | tf_op jit(solution)/shard_map/ppermute | solution.py:207
  34.6 0.8 slice.185
  35.4 0.6 pad_add_fusion.1.order_ref
  35.9 0.6 gather_fusion
  36.5 0.7 reshape.476
  37.2 0.6 gather_fusion.1
  37.8 8.7 %copy.162 = bf16[4096,3,256]{0,2,1:T(8,128)(2,1)} copy(bf16[4096,3,256]{2,0,1:T(8,128)(2,1)} %param.15) | data formatting | bytes 12582912 | tf_op args[4]
  46.6 8.7 %copy.163.w_ref = bf16[4096,768]{1,0:T(8,128)(2,1)} copy(bf16[4096,768]{0,1:T(8,128)(2,1)} %bitcast.116) | data formatting | bytes 12582912 | tf_op jit(solution)/shard_map/reshape | solution.py:93
  55.4 0.8 copy.167
  56.4 0.8 copy.170
  57.2 0.8 copy.161
  58.1 0.9 constant_dynamic-update-slice_fusion.6
  59.0 0.9 constant_dynamic-update-slice_fusion.5
  59.9 1.9 %maximum_dynamic-update-slice_fusion.1 = bf16[516,4096]{1,0:T(8,128)(2,1)} fusion(bf16[516,4096]{1,0:T(8,128)(2,1)} %constant_dynamic-update-slice_fusion.5, bf16[258,512]{1,0:T(8,128)(2,1)} %collective-permute-done.3, bf16[258,512]{1,0:T(8,128)(2,1)} %collective-permute-done.2), kind=kLoop, calls=%fused_computation.53 | loop fusion | flops 1056768 | bytes 1073152
  61.8 2.8 %collective-permute-start.7 = (bf16[258,512]{1,0:T(8,128)(2,1)S(1)}, bf16[258,512]{1,0:T(8,128)(2,1)S(1)}, u32[]{:S(2)}, u32[]{:S(2)}) collective-permute-start(bf16[258,512]{1,0:T(8,128)(2,1)S(1)} %slice.186), channel_id=1, source_target_pairs={{0,2},{2,4},{4,6},{6,0},{1,3},{3,5},{5,7},{7,1},{8,10},{10,12},{12... | collective-permute-start | bytes 792584 | tf_op jit(solution)/shard_map/ppermute | solution.py:207
  64.6 0.3 collective-permute-start.8
  64.9 1.9 %constant_dynamic-update-slice_fusion.4 = bf16[516,4096]{1,0:T(8,128)(2,1)} fusion(bf16[516,4096]{1,0:T(8,128)(2,1)} %maximum_dynamic-update-slice_fusion.1, bf16[516,512]{1,0:T(8,128)(2,1)} %collective-permute-done.4), kind=kLoop, calls=%fused_computation.83 | loop fusion | bytes 1064960
  66.8 0.8 constant_dynamic-update-slice_fusion.3
  67.7 0.9 constant_dynamic-update-slice_fusion.2
  68.6 2.8 %collective-permute-done.8 = bf16[258,512]{1,0:T(8,128)(2,1)S(1)} collective-permute-done((bf16[258,512]{1,0:T(8,128)(2,1)S(1)}, bf16[258,512]{1,0:T(8,128)(2,1)S(1)}, u32[]{:S(2)}, u32[]{:S(2)}) %collective-permute-start.8) | collective-permute-done | bytes 264224 | tf_op jit(solution)/shard_map/ppermute | solution.py:207
  71.4 0.9 maximum_dynamic-update-slice_fusion
  72.3 2.8 %convert_reduce_fusion = f32[516]{0:T(1024)S(1)} fusion(bf16[516,4096]{1,0:T(8,128)(2,1)} %maximum_dynamic-update-slice_fusion), kind=kLoop, calls=%fused_computation.4 | loop fusion | flops 4226556 | bytes 4229136 | tf_op jit(solution)/shard_map/reduce_sum | solution.py:35
  75.2 3.5 %fusion.3 = f32[516]{0:T(1024)S(1)} fusion(bf16[516,4096]{1,0:T(8,128)(2,1)} %maximum_dynamic-update-slice_fusion, f32[516]{0:T(1024)S(1)} %broadcast_multiply_fusion), kind=kLoop, calls=%fused_computation.7 | loop fusion | flops 8453628 | bytes 4231200 | tf_op jit(solution)/shard_map/reduce_sum | solution.py:37
  78.7 6.5 %fusion.6.x_ref = bf16[516,4096]{1,0:T(8,128)(2,1)} fusion(bf16[516,4096]{1,0:T(8,128)(2,1)} %maximum_dynamic-update-slice_fusion, f32[4096]{0:T(1024)S(1)} %bitcast.122, f32[4096]{0:T(1024)S(1)} %bitcast.121, f32[516]{0:T(1024)S(1)} %add_rsqrt_fusion, f32[516]{0:T(1024)S(1)} %broadcast_multiply_fusion), kind=kLoop, calls=%fused_computation.10 | loop fusion | flops 12681216 | bytes 8491040 | tf_op jit(solution)/shard_map/convert_element_type | solution.py:38
  85.2 10.4 %shard_map.122 = f32[516,768]{1,0:T(8,128)} custom-call(s32[8]{0:T(128)} %pad_add_fusion.1.order_ref, bf16[516,4096]{1,0:T(8,128)(2,1)} %fusion.6.x_ref, bf16[4096,768]{1,0:T(8,128)(2,1)} %copy.163.w_ref), custom_call_target="tpu_custom_call" | custom-call | flops 3246391296 | bytes 12103680 | tf_op jit(solution)/shard_map/pallas_call | solution.py:69
  95.6 1.5 %broadcast_add_fusion = f32[516,768]{1,0:T(8,128)S(1)} fusion(f32[516,768]{1,0:T(8,128)} %shard_map.122, f32[768]{0:T(1024)S(1)} %add.154), kind=kLoop, calls=%fused_computation.42 | loop fusion | flops 396288 | bytes 3173376 | tf_op jit(solution)/shard_map/add | solution.py:94
  97.1 0.8 reshape.478
  98.0 0.4 fusion.99
  98.3 2.2 %copy.164 = bf16[516,3,2,128]{0,3,2,1:T(8,128)(2,1)} copy(f32[516,3,2,128]{3,2,1,0:T(2,128)S(1)} %reshape.478) | data formatting | bytes 2377728 | tf_op jit(solution)/shard_map/reshape | solution.py:94
  100.9 0.4 subtract_convert_fusion.1
  101.4 0.3 pad_maximum_fusion
  101.8 0.3 pad_maximum_fusion.1
  102.1 0.8 slice.206
  102.9 1.0 slice_bitcast_fusion.2
  103.9 3.9 %collective-permute-start.9 = (f32[4,257]{1,0:T(4,128)S(1)}, f32[4,257]{1,0:T(4,128)S(1)}, u32[]{:S(2)}, u32[]{:S(2)}) collective-permute-start(f32[4,257]{1,0:T(4,128)S(1)} %get-tuple-element.61), channel_id=1, source_target_pairs={{8,0},{16,8},{24,16},{32,24},{40,32},{48,40},{56,48},{64,56},{72,6... | collective-permute-start | bytes 12344 | tf_op jit(solution)/shard_map/ppermute | solution.py:243
  107.9 5.3 %collective-permute-start.11 = (f32[4,257]{1,0:T(4,128)S(1)}, f32[4,257]{1,0:T(4,128)S(1)}, u32[]{:S(2)}, u32[]{:S(2)}) collective-permute-start(f32[4,257]{1,0:T(4,128)S(1)} %get-tuple-element.62), channel_id=1, source_target_pairs={{0,8},{8,16},{16,24},{24,32},{32,40},{40,48},{48,56},{56,64},{64,7... | collective-permute-start | bytes 12344 | tf_op jit(solution)/shard_map/ppermute | solution.py:243
  113.2 0.7 fusion.57
  114.0 2.3 %fusion.101 = (f32[2,512]{1,0:T(2,128)S(1)}, bf16[2,512,1024]{2,1,0:T(8,128)(2,1)S(1)}) fusion(f32[2,512,1024]{2,1,0:T(8,128)S(1)} %fusion.57, pred[512,1024]{1,0:T(8,128)(4,1)S(1)} %copy-done.3), kind=kOutput, calls=%fused_computation.171 | output fusion | flops 8389631 | bytes 6819840 | tf_op jit(solution)/shard_map/while/body/eval_jaxpr/sub | solution.py:107
  116.3 0.8 fusion.31
  117.3 0.3 fusion.104
  118.2 2.3 %fusion.103 = (f32[4,2]{1,0:T(4,128)S(1)}, f32[4,2,1024]{2,1,0:T(2,128)S(1)}) fusion(bf16[8,2,1024,256]{3,2,1,0:T(8,128)(2,1)} %param.21, pred[256,2]{0,1:T(4,128)(4,1)S(1)} %bitcast.131, bf16[4,256]{1,0:T(4,128)(2,1)S(1)} %slice.288, pred[4,1024]{1,0:T(4,128)(4,1)S(1)} %iota_compare_fusion.2), kind=kOutput, calls=%fused_computation.173 | convolution fusion | flops 4220920 | bytes 2136608 | tf_op jit(solution)/shard_map/rkf,rfh->rhk/dot_general | solution.py:142
  120.5 2.0 %fusion.12 = f32[4,2,256]{2,1,0:T(2,128)S(1)} fusion(bf16[8,2,1024,256]{3,2,1,0:T(8,128)(2,1)} %param.21, f32[4,2,1024]{2,1,0:T(2,128)S(1)} %get-tuple-element.75, pred[4,1024]{1,0:T(4,128)(4,1)S(1)} %iota_compare_fusion.2, f32[4,2]{1,0:T(4,128)S(1)} %get-tuple-element.74), kind=kOutput, calls=%fused_computation.18 | convolution fusion | flops 4218880 | bytes 2142240 | tf_op jit(solution)/shard_map/rhk,rkf->rhf/dot_general | solution.py:149
  123.0 2.3 %fusion.102 = (f32[4,2]{1,0:T(4,128)S(1)}, f32[4,2,1024]{2,1,0:T(2,128)S(1)}) fusion(bf16[8,2,1024,256]{3,2,1,0:T(8,128)(2,1)} %param.21, pred[256,2]{0,1:T(4,128)(4,1)S(1)} %bitcast.132, bf16[4,256]{1,0:T(4,128)(2,1)S(1)} %slice.287, pred[4,1024]{1,0:T(4,128)(4,1)S(1)} %iota_compare_fusion.1), kind=kOutput, calls=%fused_computation.172 | convolution fusion | flops 4220920 | bytes 2136608 | tf_op jit(solution)/shard_map/rkf,rfh->rhk/dot_general | solution.py:142
  125.3 2.0 %fusion.8 = f32[4,2,256]{2,1,0:T(2,128)S(1)} fusion(bf16[8,2,1024,256]{3,2,1,0:T(8,128)(2,1)} %param.21, f32[4,2,1024]{2,1,0:T(2,128)S(1)} %get-tuple-element.73, pred[4,1024]{1,0:T(4,128)(4,1)S(1)} %iota_compare_fusion.1, f32[4,2]{1,0:T(4,128)S(1)} %get-tuple-element.72), kind=kOutput, calls=%fused_computation.14 | convolution fusion | flops 4218880 | bytes 2142240 | tf_op jit(solution)/shard_map/rhk,rkf->rhf/dot_general | solution.py:149
  128.1 0.6 collective-permute-start.10
  129.5 0.8 copy.196
  130.3 1.2 collective-permute-done.10
  131.5 5.9 %collective-permute-done.12 = f32[4,2,130]{0,1,2:T(2,128)S(1)} collective-permute-done((f32[4,2,130]{0,1,2:T(2,128)S(1)}, f32[4,2,130]{0,1,2:T(2,128)S(1)}, u32[]{:S(2)}, u32[]{:S(2)}) %collective-permute-start.12) | collective-permute-done | bytes 4192 | tf_op jit(solution)/shard_map/ppermute | solution.py:249
  138.3 0.7 copy.195
  (110 shorter events, 5.3 us)
Async XLA Ops:
  0.6 13.3 %copy-start.2 = (bf16[4,2,256,256]{3,2,1,0:T(8,128)(2,1)S(1)}, bf16[4,2,256,256]{3,2,1,0:T(8,128)(2,1)}, u32[]{:S(2)}) copy-start(bf16[4,2,256,256]{3,2,1,0:T(8,128)(2,1)} %param.19) | copy-start | bytes 3145732
  0.6 35.3 %copy-start.7 = (f32[4096]{0:T(1024)S(1)}, f32[4096]{0:T(1024)}, u32[]{:S(2)}) copy-start(f32[4096]{0:T(1024)} %param.13) | copy-start | bytes 49156
  4.0 27.4 %collective-permute-start = (bf16[516,512]{1,0:T(8,128)(2,1)S(1)}, bf16[516,512]{1,0:T(8,128)(2,1)S(1)}, u32[]{:S(2)}, u32[]{:S(2)}) collective-permute-start(bf16[516,512]{1,0:T(8,128)(2,1)S(1)} %get-tuple-element.63), channel_id=1, source_target_pairs={{0,2},{2,4},{4,6},{6,0},{1,3},{3,5},{5,7},{7,1},{8,10},{10,12},{12... | collective-permute-start | bytes 1585160 | tf_op jit(solution)/shard_map/ppermute | solution.py:204
  4.0 30.6 %collective-permute-start.1 = (bf16[516,512]{1,0:T(8,128)(2,1)S(1)}, bf16[516,512]{1,0:T(8,128)(2,1)S(1)}, u32[]{:S(2)}, u32[]{:S(2)}) collective-permute-start(bf16[516,512]{1,0:T(8,128)(2,1)S(1)} %get-tuple-element.63), channel_id=1, source_target_pairs={{0,6},{2,0},{4,2},{6,4},{1,7},{3,1},{5,3},{7,5},{8,14},{10,8},{12,... | collective-permute-start | bytes 1585160 | tf_op jit(solution)/shard_map/ppermute | solution.py:205
  5.5 24.4 %collective-permute-start.4 = (bf16[516,512]{1,0:T(8,128)(2,1)S(1)}, bf16[516,512]{1,0:T(8,128)(2,1)}, u32[]{:S(2)}, u32[]{:S(2)}) collective-permute-start(bf16[516,512]{1,0:T(8,128)(2,1)S(1)} %get-tuple-element.63), channel_id=1, source_target_pairs={{0,1},{1,0},{2,3},{3,2},{4,5},{5,4},{6,7},{7,6},{8,9},{9,8},{10,11... | collective-permute-start | bytes 1585160 | tf_op jit(solution)/shard_map/ppermute | solution.py:211
  6.6 28.7 %copy-start.12 = (pred[2,2]{1,0:T(4,128)(4,1)}, pred[2,2]{1,0:T(4,128)(4,1)S(1)}, u32[]{:S(2)}) copy-start(pred[2,2]{1,0:T(4,128)(4,1)S(1)} %iota_compare_fusion.5) | copy-start | bytes 16
  29.9 31.9 %collective-permute-start.5 = (bf16[516,512]{1,0:T(8,128)(2,1)}, bf16[516,512]{1,0:T(8,128)(2,1)S(1)}, u32[]{:S(2)}, u32[]{:S(2)}) collective-permute-start(bf16[516,512]{1,0:T(8,128)(2,1)} %collective-permute-done.4), channel_id=1, source_target_pairs={{0,2},{2,4},{4,6},{6,0},{1,3},{3,5},{5,7},{7,1},{8,10},{10,12},{12... | collective-permute-start | bytes 1585160 | tf_op jit(solution)/shard_map/ppermute | solution.py:204
  31.2 33.4 %collective-permute-start.6 = (bf16[516,512]{1,0:T(8,128)(2,1)}, bf16[516,512]{1,0:T(8,128)(2,1)S(1)}, u32[]{:S(2)}, u32[]{:S(2)}) collective-permute-start(bf16[516,512]{1,0:T(8,128)(2,1)} %collective-permute-done.4), channel_id=1, source_target_pairs={{0,6},{2,0},{4,2},{6,4},{1,7},{3,1},{5,3},{7,5},{8,14},{10,8},{12,... | collective-permute-start | bytes 1585160 | tf_op jit(solution)/shard_map/ppermute | solution.py:205
  32.1 27.8 %collective-permute-start.2 = (bf16[258,512]{1,0:T(8,128)(2,1)}, bf16[258,512]{1,0:T(8,128)(2,1)}, u32[]{:S(2)}, u32[]{:S(2)}) collective-permute-start(bf16[258,512]{1,0:T(8,128)(2,1)} %slice.184), channel_id=1, source_target_pairs={{0,2},{2,4},{4,6},{6,0},{1,3},{3,5},{5,7},{7,1},{8,10},{10,12},{12... | collective-permute-start | bytes 792584 | tf_op jit(solution)/shard_map/ppermute | solution.py:207
  35.4 24.5 %collective-permute-start.3 = (bf16[258,512]{1,0:T(8,128)(2,1)}, bf16[258,512]{1,0:T(8,128)(2,1)}, u32[]{:S(2)}, u32[]{:S(2)}) collective-permute-start(bf16[258,512]{1,0:T(8,128)(2,1)} %slice.185), channel_id=1, source_target_pairs={{0,6},{2,0},{4,2},{6,4},{1,7},{3,1},{5,3},{7,5},{8,14},{10,8},{12,... | collective-permute-start | bytes 792584 | tf_op jit(solution)/shard_map/ppermute | solution.py:207
  46.6 8.7 %copy-start.9 = (f32[3,256]{1,0:T(4,128)S(1)}, f32[3,256]{1,0:T(4,128)}, u32[]{:S(2)}) copy-start(f32[3,256]{1,0:T(4,128)} %param.16) | copy-start | bytes 9220
  46.6 9.7 %copy-start.11 = (pred[1,2,2,128]{3,2,1,0:T(4,128)(4,1)S(1)}, pred[1,2,2,128]{3,2,1,0:T(4,128)(4,1)}, u32[]{:S(2)}) copy-start(pred[1,2,2,128]{3,2,1,0:T(4,128)(4,1)} %broadcast_bitcast_fusion) | copy-start | bytes 1540
  46.6 11.5 %copy-start.10 = (pred[4,256]{1,0:T(4,128)(4,1)S(1)}, pred[4,256]{1,0:T(4,128)(4,1)}, u32[]{:S(2)}) copy-start(pred[4,256]{1,0:T(4,128)(4,1)} %iota_compare_fusion.3) | copy-start | bytes 3076
  61.8 6.8 %collective-permute-start.7 = (bf16[258,512]{1,0:T(8,128)(2,1)S(1)}, bf16[258,512]{1,0:T(8,128)(2,1)S(1)}, u32[]{:S(2)}, u32[]{:S(2)}) collective-permute-start(bf16[258,512]{1,0:T(8,128)(2,1)S(1)} %slice.186), channel_id=1, source_target_pairs={{0,2},{2,4},{4,6},{6,0},{1,3},{3,5},{5,7},{7,1},{8,10},{10,12},{12... | collective-permute-start | bytes 792584 | tf_op jit(solution)/shard_map/ppermute | solution.py:207
  64.6 6.8 %collective-permute-start.8 = (bf16[258,512]{1,0:T(8,128)(2,1)S(1)}, bf16[258,512]{1,0:T(8,128)(2,1)S(1)}, u32[]{:S(2)}, u32[]{:S(2)}) collective-permute-start(bf16[258,512]{1,0:T(8,128)(2,1)S(1)} %slice.187), channel_id=1, source_target_pairs={{0,6},{2,0},{4,2},{6,4},{1,7},{3,1},{5,3},{7,5},{8,14},{10,8},{12,... | collective-permute-start | bytes 792584 | tf_op jit(solution)/shard_map/ppermute | solution.py:207
  98.0 2.9 %copy-start = (f32[516,16]{1,0:T(8,128)S(1)}, f32[516,16]{1,0:T(8,128)}, u32[]{:S(2)}) copy-start(f32[516,16]{1,0:T(8,128)} %copy.167) | copy-start | bytes 99076
  100.7 3.2 %copy-start.8 = (f32[4,1]{1,0:T(4,128)S(1)}, f32[4,1]{1,0:T(4,128)}, u32[]{:S(2)}) copy-start(f32[4,1]{1,0:T(4,128)} %get-tuple-element.67) | copy-start | bytes 52
  100.9 12.3 %copy-start.1 = (bf16[512,2,128]{2,0,1:T(8,128)(2,1)S(1)}, bf16[512,2,128]{2,0,1:T(8,128)(2,1)}, u32[]{:S(2)}) copy-start(bf16[512,2,128]{2,0,1:T(8,128)(2,1)} %copy.170) | copy-start | bytes 786436
  101.7 12.2 %copy-start.3 = (pred[512,1024]{1,0:T(8,128)(4,1)S(1)}, pred[512,1024]{1,0:T(8,128)(4,1)}, u32[]{:S(2)}) copy-start(pred[512,1024]{1,0:T(8,128)(4,1)} %pad_add_fusion) | copy-start | bytes 1572868
  103.9 14.0 %collective-permute-start.9 = (f32[4,257]{1,0:T(4,128)S(1)}, f32[4,257]{1,0:T(4,128)S(1)}, u32[]{:S(2)}, u32[]{:S(2)}) collective-permute-start(f32[4,257]{1,0:T(4,128)S(1)} %get-tuple-element.61), channel_id=1, source_target_pairs={{8,0},{16,8},{24,16},{32,24},{40,32},{48,40},{56,48},{64,56},{72,6... | collective-permute-start | bytes 12344 | tf_op jit(solution)/shard_map/ppermute | solution.py:243
  107.9 14.9 %collective-permute-start.11 = (f32[4,257]{1,0:T(4,128)S(1)}, f32[4,257]{1,0:T(4,128)S(1)}, u32[]{:S(2)}, u32[]{:S(2)}) collective-permute-start(f32[4,257]{1,0:T(4,128)S(1)} %get-tuple-element.62), channel_id=1, source_target_pairs={{0,8},{8,16},{16,24},{24,32},{32,40},{40,48},{48,56},{56,64},{64,7... | collective-permute-start | bytes 12344 | tf_op jit(solution)/shard_map/ppermute | solution.py:243
  113.9 2.4 %copy-start.6 = (bf16[1,1,512,256]{2,3,1,0:T(8,128)(2,1)S(1)}, bf16[1,1,512,256]{2,3,1,0:T(8,128)(2,1)}, u32[]{:S(2)}) copy-start(bf16[1,1,512,256]{2,3,1,0:T(8,128)(2,1)} %copy.161) | copy-start | bytes 786436
  116.3 1.0 copy-start.5
  116.3 1.4 copy-start.4
  118.1 9.6 %copy-start.13 = (pred[2,2]{1,0:T(4,128)(4,1)S(1)}, pred[2,2]{1,0:T(4,128)(4,1)}, u32[]{:S(2)}) copy-start(pred[2,2]{1,0:T(4,128)(4,1)} %copy-done.12) | copy-start | bytes 16
  128.1 3.4 %collective-permute-start.10 = (f32[4,2,130]{0,1,2:T(2,128)S(1)}, f32[4,2,130]{0,1,2:T(2,128)S(1)}, u32[]{:S(2)}, u32[]{:S(2)}) collective-permute-start(f32[4,2,130]{0,1,2:T(2,128)S(1)} %pad_maximum_fusion.2), channel_id=1, source_target_pairs={{0,8},{8,16},{16,24},{24,32},{32,40},{40,48},{48,56},{56,64},{64,7... | collective-permute-start | bytes 12488 | tf_op jit(solution)/shard_map/ppermute | solution.py:249
  129.0 8.4 %collective-permute-start.12 = (f32[4,2,130]{0,1,2:T(2,128)S(1)}, f32[4,2,130]{0,1,2:T(2,128)S(1)}, u32[]{:S(2)}, u32[]{:S(2)}) collective-permute-start(f32[4,2,130]{0,1,2:T(2,128)S(1)} %pad_maximum_fusion.3), channel_id=1, source_target_pairs={{8,0},{16,8},{24,16},{32,24},{40,32},{48,40},{56,48},{64,56},{72,6... | collective-permute-start | bytes 12488 | tf_op jit(solution)/shard_map/ppermute | solution.py:249

commit v6 on v5

--- a/solution.py
+++ b/solution.py
@@ -58,30 +58,34 @@
     def _():
         o_ref[...] = jnp.zeros_like(o_ref)
 
-    o_ref[...] += jnp.dot(x_ref[...], w_ref[...], preferred_element_type=jnp.float32)
+    width = w_ref.shape[2]
+    for c in range(w_ref.shape[0]):
+        o_ref[:, c * width : (c + 1) * width] += jnp.dot(
+            x_ref[...], w_ref[c], preferred_element_type=jnp.float32
+        )
 
 
 def qkv_matmul(normed, weight, order):
     rows, depth = normed.shape
-    width = weight.shape[1]
+    parts, _, width = weight.shape
     blocks = order.shape[0]
     size = depth // blocks
     return pl.pallas_call(
         qkv_kernel,
-        out_shape=jax.ShapeDtypeStruct((rows, width), jnp.float32),
+        out_shape=jax.ShapeDtypeStruct((rows, parts * width), jnp.float32),
         grid_spec=pltpu.PrefetchScalarGridSpec(
             num_scalar_prefetch=1,
             grid=(blocks,),
             in_specs=[
                 pl.BlockSpec((rows, size), lambda j, order: (0, j)),
-                pl.BlockSpec((size, width), lambda j, order: (order[j], 0)),
+                pl.BlockSpec((parts, size, width), lambda j, order: (0, order[j], 0)),
             ],
-            out_specs=pl.BlockSpec((rows, width), lambda j, order: (0, 0)),
+            out_specs=pl.BlockSpec((rows, parts * width), lambda j, order: (0, 0)),
         ),
         compiler_params=pltpu.CompilerParams(dimension_semantics=("arbitrary",)),
         cost_estimate=pl.CostEstimate(
-            flops=2 * rows * depth * width,
-            bytes_accessed=2 * rows * depth + 2 * depth * width + 4 * rows * width,
+            flops=2 * rows * depth * parts * width,
+            bytes_accessed=2 * rows * depth + 2 * depth * parts * width + 4 * rows * parts * width,
             transcendentals=0,
         ),
     )(order, normed, weight)
@@ -90,7 +94,7 @@
 def project(normed, weight, bias, positions, order):
     count = normed.shape[0]
     width = weight.shape[2]
-    mixed = qkv_matmul(normed, weight.reshape(weight.shape[0], 3 * width), order)
+    mixed = qkv_matmul(normed, weight, order)
     mixed = (mixed + bias.reshape(1, 3 * width)).reshape(count, 3, width // HD, HD)
     query = rotate(mixed[:, 0], positions).astype(jnp.bfloat16)
     fresh_key = rotate(mixed[:, 1], positions).astype(jnp.bfloat16)
@@ -217,19 +221,16 @@
     def feature_order(table):
         return table.reshape(order.shape[0], -1)[order].reshape(table.shape)
 
-    normed = layer_norm(whole, feature_order(ln_gain), feature_order(ln_bias))
-    positions = jnp.concatenate(
-        [
-            prefill_offset[0] + jnp.arange(count, dtype=jnp.int32),
-            piece_len[:, 0] + piece_len[:, 1] + piece_len[:, 2],
-        ],
-        axis=0,
-    )
-    query, fresh_key, fresh_value = project(normed, qkv_weight, qkv_bias, positions, order)
-    own_query = query[count:]
-    home_parts = home_partial(
-        own_query, fresh_key[count:], fresh_value[count:], home_cache, piece_len[:, 1]
-    )
+    gain, shift = feature_order(ln_gain), feature_order(ln_bias)
+    weight = jnp.transpose(qkv_weight, (1, 0, 2))
+    own_query, new_key, new_value = project(
+        layer_norm(whole[count:], gain, shift),
+        weight,
+        qkv_bias,
+        piece_len[:, 0] + piece_len[:, 1] + piece_len[:, 2],
+        order,
+    )
+    home_parts = home_partial(own_query, new_key, new_value, home_cache, piece_len[:, 1])
     groups = lax.axis_size("group")
     forward = [(i, (i + 1) % groups) for i in range(groups)]
     backward = [((i + 1) % groups, i) for i in range(groups)]
@@ -253,9 +254,14 @@
     next_query, next_len = ask(piece_len[:, 0], backward)
     right_parts = answer(piece_batch(prev_query, side_store[:requests], prev_len), backward)
     left_parts = answer(piece_batch(next_query, side_store[requests:], next_len), forward)
-    prefill_out = prefill_attend(
-        query[:count], fresh_key[:count], fresh_value[:count], prior_cache[0], prefill_offset[0]
-    )
+    query, fresh_key, fresh_value = project(
+        layer_norm(whole[:count], gain, shift),
+        weight,
+        qkv_bias,
+        prefill_offset[0] + jnp.arange(count, dtype=jnp.int32),
+        order,
+    )
+    prefill_out = prefill_attend(query, fresh_key, fresh_value, prior_cache[0], prefill_offset[0])
     decode_out = combine([left_parts, home_parts, right_parts]).reshape(requests, -1)
     return (prefill_out, decode_out)
 

time: 140 us -> 134 us (0.957)
  the two profiles are of different devices: /device:TPU:255 before, /device:TPU:1 now
where the time goes in v6:
time: 134 us; the launch traced here: 133 us
  starting transfers between devices  34.8 us (26%)
  other arithmetic  30.7 us (23%)
  local copies, waits for them, and re-layouts  26.3 us (20%)
  Pallas kernels  17.5 us (13%)
  waiting for transfers between devices  10.9 us (8%)
  matrix products  10.9 us (8%)
  between operations  1.72 us (1%)
    pallas_call x2, Pallas kernels, qkv_matmul(): pl.pallas_call(qkv_kernel, out_shape=jax.ShapeDtypeStruct((rows, parts *...  17.5 us
    ppermute x2, starting transfers between devices, ask(): got = lax.ppermute(packed, 'group', pairs)  15.3 us
    unnamed x41, local copies, waits for them, and re-layouts  11.5 us
    ppermute x1, starting transfers between devices, local(): partner = lax.ppermute(rows, 'tz', [(0, 1), (1, 0)])  6.91 us
    convert_element_type x2, other arithmetic, layer_norm(): (centred * lax.rsqrt(spread + EPS) * gain + shift).astype(jnp.bfloat16)  6.58 us
    dot_general x3, matrix products, piece_rows(): jnp.einsum('rkf,rfh->rhk', keys, spread, preferred_element_type=jnp.float32)  4.99 us
    ppermute x2, starting transfers between devices, around(): lax.ppermute(above[half:], 'ty', down)  4.82 us
    ppermute x1, waiting for transfers between devices, local(): partner = lax.ppermute(rows, 'tz', [(0, 1), (1, 0)])  4.6 us
  transfers between devices with their start and end apart: 13, of which 4 were waited for; matrix products, arithmetic and copies ran while one was open for 28% of the time, Pallas kernels for 0%

profile of v6, /device:TPU:1, one launch (start us, length us, event | category | flops | bytes accessed | tf_op | source)
XLA Modules:
  0.0 132.8 jit_solution(30161983410478411)
XLA Ops:
  0.7 2.0 %constant_dynamic-update-slice_fusion.1 = (bf16[516,512]{1,0:T(8,128)(2,1)S(1)}, bf16[516,4096]{1,0:T(8,128)(2,1)}) fusion(bf16[512,512]{1,0:T(8,128)(2,1)} %param.11), kind=kLoop, calls=%fused_computation.94 | loop fusion | bytes 1572864
  2.7 1.3 constant_dynamic-update-slice_fusion
  4.0 2.1 %collective-permute-start = (bf16[516,512]{1,0:T(8,128)(2,1)S(1)}, bf16[516,512]{1,0:T(8,128)(2,1)S(1)}, u32[]{:S(2)}, u32[]{:S(2)}) collective-permute-start(bf16[516,512]{1,0:T(8,128)(2,1)S(1)} %get-tuple-element.65), channel_id=1, source_target_pairs={{0,2},{2,4},{4,6},{6,0},{1,3},{3,5},{5,7},{7,1},{8,10},{10,12},{12... | collective-permute-start | bytes 1585160 | tf_op jit(solution)/shard_map/ppermute | solution.py:208
  6.1 1.4 %collective-permute-start.1 = (bf16[516,512]{1,0:T(8,128)(2,1)S(1)}, bf16[516,512]{1,0:T(8,128)(2,1)S(1)}, u32[]{:S(2)}, u32[]{:S(2)}) collective-permute-start(bf16[516,512]{1,0:T(8,128)(2,1)S(1)} %get-tuple-element.65), channel_id=1, source_target_pairs={{0,6},{2,0},{4,2},{6,4},{1,7},{3,1},{5,3},{7,5},{8,14},{10,8},{12,... | collective-permute-start | bytes 1585160 | tf_op jit(solution)/shard_map/ppermute | solution.py:209
  7.5 6.9 %collective-permute-start.4 = (bf16[516,512]{1,0:T(8,128)(2,1)S(1)}, bf16[516,512]{1,0:T(8,128)(2,1)}, u32[]{:S(2)}, u32[]{:S(2)}) collective-permute-start(bf16[516,512]{1,0:T(8,128)(2,1)S(1)} %get-tuple-element.65), channel_id=1, source_target_pairs={{0,1},{1,0},{2,3},{3,2},{4,5},{5,4},{6,7},{7,6},{8,9},{9,8},{10,11... | collective-permute-start | bytes 1585160 | tf_op jit(solution)/shard_map/ppermute | solution.py:215
  14.5 1.0 convert_reduce_fusion.2
  15.5 1.6 %slice_reduce_fusion = (s32[4]{0:T(128)S(1)}, f32[4,1]{1,0:T(4,128)}, f32[4,1]{1,0:T(4,128)}) fusion(s32[4,3]{1,0:T(4,128)} %param.20), kind=kLoop, calls=%fused_computation.158 | loop fusion | flops 8 | bytes 96 | tf_op jit(solution)/shard_map/slice | solution.py:230
  17.1 0.6 iota_compare_fusion.3
  17.8 0.6 broadcast_bitcast_fusion
  19.4 1.1 fusion.115
  20.6 1.0 pad_add_fusion
  21.7 1.1 slice_bitcast_fusion.1
  22.8 4.6 %collective-permute-done.4 = bf16[516,512]{1,0:T(8,128)(2,1)} collective-permute-done((bf16[516,512]{1,0:T(8,128)(2,1)S(1)}, bf16[516,512]{1,0:T(8,128)(2,1)}, u32[]{:S(2)}, u32[]{:S(2)}) %collective-permute-start.4) | collective-permute-done | bytes 528416 | tf_op jit(solution)/shard_map/ppermute | solution.py:215
  27.4 0.5 collective-permute-start.5
  27.9 2.2 %collective-permute-start.6 = (bf16[516,512]{1,0:T(8,128)(2,1)}, bf16[516,512]{1,0:T(8,128)(2,1)S(1)}, u32[]{:S(2)}, u32[]{:S(2)}) collective-permute-start(bf16[516,512]{1,0:T(8,128)(2,1)} %collective-permute-done.4), channel_id=1, source_target_pairs={{0,6},{2,0},{4,2},{6,4},{1,7},{3,1},{5,3},{7,5},{8,14},{10,8},{12,... | collective-permute-start | bytes 1585160 | tf_op jit(solution)/shard_map/ppermute | solution.py:209
  30.1 0.7 slice.202
  30.8 0.8 slice.203
  31.6 2.7 %collective-permute-start.3 = (bf16[258,512]{1,0:T(8,128)(2,1)}, bf16[258,512]{1,0:T(8,128)(2,1)}, u32[]{:S(2)}, u32[]{:S(2)}) collective-permute-start(bf16[258,512]{1,0:T(8,128)(2,1)} %slice.203), channel_id=1, source_target_pairs={{0,6},{2,0},{4,2},{6,4},{1,7},{3,1},{5,3},{7,5},{8,14},{10,8},{12,... | collective-permute-start | bytes 792584 | tf_op jit(solution)/shard_map/ppermute | solution.py:211
  34.3 0.6 pad_add_fusion.1.order_ref
  34.9 0.6 gather_fusion
  35.5 0.6 gather_fusion.1
  36.1 0.7 add.186
  36.8 0.7 copy.270
  37.6 0.8 copy.211
  38.6 0.8 copy.214
  39.4 0.8 copy.207
  40.3 0.6 concatenate.139
  40.9 0.9 constant_dynamic-update-slice_fusion.6
  41.8 0.9 constant_dynamic-update-slice_fusion.5
  42.7 3.1 %collective-permute-done.2 = bf16[258,512]{1,0:T(8,128)(2,1)} collective-permute-done((bf16[258,512]{1,0:T(8,128)(2,1)}, bf16[258,512]{1,0:T(8,128)(2,1)}, u32[]{:S(2)}, u32[]{:S(2)}) %collective-permute-start.2) | collective-permute-done | bytes 264224 | tf_op jit(solution)/shard_map/ppermute | solution.py:211
  45.8 2.0 %maximum_dynamic-update-slice_fusion.1 = bf16[516,4096]{1,0:T(8,128)(2,1)} fusion(bf16[516,4096]{1,0:T(8,128)(2,1)} %constant_dynamic-update-slice_fusion.5, bf16[258,512]{1,0:T(8,128)(2,1)} %collective-permute-done.3, bf16[258,512]{1,0:T(8,128)(2,1)} %collective-permute-done.2), kind=kLoop, calls=%fused_computation.51 | loop fusion | flops 1056768 | bytes 1073152
  47.8 0.9 collective-permute-start.7
  48.7 2.1 %collective-permute-start.8 = (bf16[258,512]{1,0:T(8,128)(2,1)S(1)}, bf16[258,512]{1,0:T(8,128)(2,1)S(1)}, u32[]{:S(2)}, u32[]{:S(2)}) collective-permute-start(bf16[258,512]{1,0:T(8,128)(2,1)S(1)} %slice.205), channel_id=1, source_target_pairs={{0,6},{2,0},{4,2},{6,4},{1,7},{3,1},{5,3},{7,5},{8,14},{10,8},{12,... | collective-permute-start | bytes 792584 | tf_op jit(solution)/shard_map/ppermute | solution.py:211
  50.9 2.0 %constant_dynamic-update-slice_fusion.4 = bf16[516,4096]{1,0:T(8,128)(2,1)} fusion(bf16[516,4096]{1,0:T(8,128)(2,1)} %maximum_dynamic-update-slice_fusion.1, bf16[516,512]{1,0:T(8,128)(2,1)} %collective-permute-done.4), kind=kLoop, calls=%fused_computation.97 | loop fusion | bytes 1064960
  52.9 0.9 constant_dynamic-update-slice_fusion.3
  53.7 0.9 constant_dynamic-update-slice_fusion.2
  54.6 0.9 maximum_dynamic-update-slice_fusion
  55.5 1.0 convert_reduce_fusion.1
  56.5 1.1 fusion.72
  57.6 1.5 %fusion.75.x_ref = bf16[4,4096]{1,0:T(4,128)(2,1)} fusion(f32[4096]{0:T(1024)S(1)} %bitcast.141, f32[4096]{0:T(1024)S(1)} %bitcast.139, f32[4]{0:T(128)S(1)} %add_rsqrt_fusion.1, f32[4]{0:T(128)S(1)} %broadcast_multiply_fusion.1, bf16[516,4096]{1,0:T(8,128)(2,1)} %maximum_dynamic-update-slice_fusion), kind=kLoop, calls=%fused_computation.88 | loop fusion | flops 98304 | bytes 98336 | tf_op jit(solution)/shard_map/convert_element_type | solution.py:38
  59.1 7.1 %shard_map.123 = f32[4,768]{1,0:T(4,128)} custom-call(s32[8]{0:T(128)} %pad_add_fusion.1.order_ref, bf16[4,4096]{1,0:T(4,128)(2,1)} %fusion.75.x_ref, bf16[3,4096,256]{2,1,0:T(8,128)(2,1)} %bitcast.133), custom_call_target="tpu_custom_call" | custom-call | flops 25165824 | bytes 6336512 | tf_op jit(solution)/shard_map/pallas_call | solution.py:73
  66.2 0.7 broadcast_add_fusion.1
  67.1 2.8 %convert_reduce_fusion = f32[512]{0:T(512)S(1)} fusion(bf16[516,4096]{1,0:T(8,128)(2,1)} %maximum_dynamic-update-slice_fusion), kind=kLoop, calls=%fused_computation.4 | loop fusion | flops 4193792 | bytes 4196352 | tf_op jit(solution)/shard_map/reduce_sum | solution.py:35
  69.9 3.4 %fusion.3 = f32[512]{0:T(512)S(1)} fusion(f32[512]{0:T(512)S(1)} %broadcast_multiply_fusion, bf16[516,4096]{1,0:T(8,128)(2,1)} %maximum_dynamic-update-slice_fusion), kind=kLoop, calls=%fused_computation.7 | loop fusion | flops 8388096 | bytes 4198400 | tf_op jit(solution)/shard_map/reduce_sum | solution.py:37
  73.4 5.0 %fusion.6.x_ref = bf16[512,4096]{1,0:T(8,128)(2,1)} fusion(f32[4096]{0:T(1024)S(1)} %bitcast.142, f32[4096]{0:T(1024)S(1)} %bitcast.140, f32[512]{0:T(512)S(1)} %add_rsqrt_fusion, f32[512]{0:T(512)S(1)} %broadcast_multiply_fusion, bf16[516,4096]{1,0:T(8,128)(2,1)} %maximum_dynamic-update-slice_fusion), kind=kLoop, calls=%fused_computation.10 | loop fusion | flops 12582912 | bytes 8425472 | tf_op jit(solution)/shard_map/convert_element_type | solution.py:38
  78.4 10.4 %shard_map.122 = f32[512,768]{1,0:T(8,128)} custom-call(s32[8]{0:T(128)} %pad_add_fusion.1.order_ref, bf16[512,4096]{1,0:T(8,128)(2,1)} %fusion.6.x_ref, bf16[3,4096,256]{2,1,0:T(8,128)(2,1)} %bitcast.134), custom_call_target="tpu_custom_call" | custom-call | flops 3221225472 | bytes 12058624 | tf_op jit(solution)/shard_map/pallas_call | solution.py:73
  88.8 1.5 %broadcast_add_fusion = f32[512,768]{1,0:T(8,128)S(1)} fusion(f32[512,768]{1,0:T(8,128)} %shard_map.122, f32[768]{0:T(1024)S(1)} %add.186), kind=kLoop, calls=%fused_computation.42 | loop fusion | flops 393216 | bytes 3148800 | tf_op jit(solution)/shard_map/add | solution.py:98
  90.3 0.8 reshape.565
  91.5 0.9 slice.207
  92.7 4.5 %collective-permute-start.9 = (f32[4,257]{1,0:T(4,128)S(1)}, f32[4,257]{1,0:T(4,128)S(1)}, u32[]{:S(2)}, u32[]{:S(2)}) collective-permute-start(f32[4,257]{1,0:T(4,128)S(1)} %get-tuple-element.63), channel_id=1, source_target_pairs={{8,0},{16,8},{24,16},{32,24},{40,32},{48,40},{56,48},{64,56},{72,6... | collective-permute-start | bytes 12344 | tf_op jit(solution)/shard_map/ppermute | solution.py:244
  97.2 10.7 %collective-permute-start.11 = (f32[4,257]{1,0:T(4,128)S(1)}, f32[4,257]{1,0:T(4,128)S(1)}, u32[]{:S(2)}, u32[]{:S(2)}) collective-permute-start(f32[4,257]{1,0:T(4,128)S(1)} %get-tuple-element.64), channel_id=1, source_target_pairs={{0,8},{8,16},{16,24},{24,32},{32,40},{40,48},{48,56},{56,64},{64,7... | collective-permute-start | bytes 12344 | tf_op jit(solution)/shard_map/ppermute | solution.py:244
  108.3 1.1 copy.263
  109.4 1.4 %subtract_convert_fusion.1 = (bf16[512,2,16]{2,0,1:T(8,128)(2,1)S(1)}, bf16[512,2,16]{2,0,1:T(8,128)(2,1)S(1)}, bf16[512,2,16]{2,0,1:T(8,128)(2,1)S(1)}, bf16[512,2,16]{2,0,1:T(8,128)(2,1)S(1)}) fusion(f32[512,2,128]{2,0,1:T(8,128)S(1)} %get-tuple-element.84, f32[512,16]{1,0:T(8,128)} %copy.211, f32[512,16]{1,0:T(8,128)S(1)} %copy.210, ...), kind=kLoop, calls=%fused_computation.72 | loop fusion | flops 262144 | bytes 458752 | tf_op jit(solution)/shard_map/convert.21
  110.9 0.8 fusion.57
  111.8 2.3 %fusion.116 = (f32[2,512]{1,0:T(2,128)S(1)}, bf16[2,512,1024]{2,1,0:T(8,128)(2,1)S(1)}) fusion(f32[2,512,1024]{2,1,0:T(8,128)S(1)} %fusion.57, pred[512,1024]{1,0:T(8,128)(4,1)S(1)} %copy-done.2), kind=kOutput, calls=%fused_computation.200 | output fusion | flops 8389631 | bytes 6819840 | tf_op jit(solution)/shard_map/while/body/eval_jaxpr/sub | solution.py:111
  114.2 0.8 fusion.31
  116.0 2.3 %fusion.118 = (f32[4,2]{1,0:T(4,128)S(1)}, f32[4,2,1024]{2,1,0:T(2,128)S(1)}) fusion(bf16[8,2,1024,256]{3,2,1,0:T(8,128)(2,1)} %param.21, pred[256,2]{0,1:T(4,128)(4,1)S(1)} %bitcast.155, bf16[4,256]{1,0:T(4,128)(2,1)S(1)} %slice.333, pred[4,1024]{1,0:T(4,128)(4,1)S(1)} %iota_compare_fusion.2), kind=kOutput, calls=%fused_computation.202 | convolution fusion | flops 4220920 | bytes 2136608 | tf_op jit(solution)/shard_map/rkf,rfh->rhk/dot_general | solution.py:146
  118.3 2.0 %fusion.12 = f32[4,2,256]{2,1,0:T(2,128)S(1)} fusion(bf16[8,2,1024,256]{3,2,1,0:T(8,128)(2,1)} %param.21, f32[4,2,1024]{2,1,0:T(2,128)S(1)} %get-tuple-element.80, pred[4,1024]{1,0:T(4,128)(4,1)S(1)} %iota_compare_fusion.2, f32[4,2]{1,0:T(4,128)S(1)} %get-tuple-element.79), kind=kOutput, calls=%fused_computation.18 | convolution fusion | flops 4218880 | bytes 2142240 | tf_op jit(solution)/shard_map/rhk,rkf->rhf/dot_general | solution.py:153
  120.8 2.3 %fusion.117 = (f32[4,2]{1,0:T(4,128)S(1)}, f32[4,2,1024]{2,1,0:T(2,128)S(1)}) fusion(bf16[8,2,1024,256]{3,2,1,0:T(8,128)(2,1)} %param.21, pred[256,2]{0,1:T(4,128)(4,1)S(1)} %bitcast.156, bf16[4,256]{1,0:T(4,128)(2,1)S(1)} %slice.331, pred[4,1024]{1,0:T(4,128)(4,1)S(1)} %iota_compare_fusion.1), kind=kOutput, calls=%fused_computation.201 | convolution fusion | flops 4220920 | bytes 2136608 | tf_op jit(solution)/shard_map/rkf,rfh->rhk/dot_general | solution.py:146
  123.1 2.0 %fusion.8 = f32[4,2,256]{2,1,0:T(2,128)S(1)} fusion(bf16[8,2,1024,256]{3,2,1,0:T(8,128)(2,1)} %param.21, f32[4,2,1024]{2,1,0:T(2,128)S(1)} %get-tuple-element.78, pred[4,1024]{1,0:T(4,128)(4,1)S(1)} %iota_compare_fusion.1, f32[4,2]{1,0:T(4,128)S(1)} %get-tuple-element.77), kind=kOutput, calls=%fused_computation.14 | convolution fusion | flops 4218880 | bytes 2142240 | tf_op jit(solution)/shard_map/rhk,rkf->rhf/dot_general | solution.py:153
  127.3 0.8 copy.247
  128.1 0.5 collective-permute-done.10
  128.7 2.6 %collective-permute-done.12 = f32[4,2,130]{0,1,2:T(2,128)S(1)} collective-permute-done((f32[4,2,130]{0,1,2:T(2,128)S(1)}, f32[4,2,130]{0,1,2:T(2,128)S(1)}, u32[]{:S(2)}, u32[]{:S(2)}) %collective-permute-start.12) | collective-permute-done | bytes 4192 | tf_op jit(solution)/shard_map/ppermute | solution.py:250
  132.1 0.7 copy.246
  (115 shorter events, 6.7 us)
Async XLA Ops:
  0.6 21.1 %copy-start.1 = (bf16[4,2,256,256]{3,2,1,0:T(8,128)(2,1)S(1)}, bf16[4,2,256,256]{3,2,1,0:T(8,128)(2,1)}, u32[]{:S(2)}) copy-start(bf16[4,2,256,256]{3,2,1,0:T(8,128)(2,1)} %param.19) | copy-start | bytes 3145732
  0.6 34.2 %copy-start.6 = (f32[4096]{0:T(1024)S(1)}, f32[4096]{0:T(1024)}, u32[]{:S(2)}) copy-start(f32[4096]{0:T(1024)} %param.13) | copy-start | bytes 49156
  0.7 34.8 %copy-start.7 = (f32[4096]{0:T(1024)S(1)}, f32[4096]{0:T(1024)}, u32[]{:S(2)}) copy-start(f32[4096]{0:T(1024)} %param.14) | copy-start | bytes 49156
  4.0 26.1 %collective-permute-start = (bf16[516,512]{1,0:T(8,128)(2,1)S(1)}, bf16[516,512]{1,0:T(8,128)(2,1)S(1)}, u32[]{:S(2)}, u32[]{:S(2)}) collective-permute-start(bf16[516,512]{1,0:T(8,128)(2,1)S(1)} %get-tuple-element.65), channel_id=1, source_target_pairs={{0,2},{2,4},{4,6},{6,0},{1,3},{3,5},{5,7},{7,1},{8,10},{10,12},{12... | collective-permute-start | bytes 1585160 | tf_op jit(solution)/shard_map/ppermute | solution.py:208
  6.1 24.7 %collective-permute-start.1 = (bf16[516,512]{1,0:T(8,128)(2,1)S(1)}, bf16[516,512]{1,0:T(8,128)(2,1)S(1)}, u32[]{:S(2)}, u32[]{:S(2)}) collective-permute-start(bf16[516,512]{1,0:T(8,128)(2,1)S(1)} %get-tuple-element.65), channel_id=1, source_target_pairs={{0,6},{2,0},{4,2},{6,4},{1,7},{3,1},{5,3},{7,5},{8,14},{10,8},{12,... | collective-permute-start | bytes 1585160 | tf_op jit(solution)/shard_map/ppermute | solution.py:209
  7.5 19.9 %collective-permute-start.4 = (bf16[516,512]{1,0:T(8,128)(2,1)S(1)}, bf16[516,512]{1,0:T(8,128)(2,1)}, u32[]{:S(2)}, u32[]{:S(2)}) collective-permute-start(bf16[516,512]{1,0:T(8,128)(2,1)S(1)} %get-tuple-element.65), channel_id=1, source_target_pairs={{0,1},{1,0},{2,3},{3,2},{4,5},{5,4},{6,7},{7,6},{8,9},{9,8},{10,11... | collective-permute-start | bytes 1585160 | tf_op jit(solution)/shard_map/ppermute | solution.py:215
  17.0 17.3 %copy-start.10 = (pred[2,2]{1,0:T(4,128)(4,1)}, pred[2,2]{1,0:T(4,128)(4,1)S(1)}, u32[]{:S(2)}) copy-start(pred[2,2]{1,0:T(4,128)(4,1)S(1)} %iota_compare_fusion.5) | copy-start | bytes 16
  27.4 20.4 %collective-permute-start.5 = (bf16[516,512]{1,0:T(8,128)(2,1)}, bf16[516,512]{1,0:T(8,128)(2,1)S(1)}, u32[]{:S(2)}, u32[]{:S(2)}) collective-permute-start(bf16[516,512]{1,0:T(8,128)(2,1)} %collective-permute-done.4), channel_id=1, source_target_pairs={{0,2},{2,4},{4,6},{6,0},{1,3},{3,5},{5,7},{7,1},{8,10},{10,12},{12... | collective-permute-start | bytes 1585160 | tf_op jit(solution)/shard_map/ppermute | solution.py:208
  27.9 20.8 %collective-permute-start.6 = (bf16[516,512]{1,0:T(8,128)(2,1)}, bf16[516,512]{1,0:T(8,128)(2,1)S(1)}, u32[]{:S(2)}, u32[]{:S(2)}) collective-permute-start(bf16[516,512]{1,0:T(8,128)(2,1)} %collective-permute-done.4), channel_id=1, source_target_pairs={{0,6},{2,0},{4,2},{6,4},{1,7},{3,1},{5,3},{7,5},{8,14},{10,8},{12,... | collective-permute-start | bytes 1585160 | tf_op jit(solution)/shard_map/ppermute | solution.py:209
  30.8 14.9 %collective-permute-start.2 = (bf16[258,512]{1,0:T(8,128)(2,1)}, bf16[258,512]{1,0:T(8,128)(2,1)}, u32[]{:S(2)}, u32[]{:S(2)}) collective-permute-start(bf16[258,512]{1,0:T(8,128)(2,1)} %slice.202), channel_id=1, source_target_pairs={{0,2},{2,4},{4,6},{6,0},{1,3},{3,5},{5,7},{7,1},{8,10},{10,12},{12... | collective-permute-start | bytes 792584 | tf_op jit(solution)/shard_map/ppermute | solution.py:211
  31.6 14.2 %collective-permute-start.3 = (bf16[258,512]{1,0:T(8,128)(2,1)}, bf16[258,512]{1,0:T(8,128)(2,1)}, u32[]{:S(2)}, u32[]{:S(2)}) collective-permute-start(bf16[258,512]{1,0:T(8,128)(2,1)} %slice.203), channel_id=1, source_target_pairs={{0,6},{2,0},{4,2},{6,4},{1,7},{3,1},{5,3},{7,5},{8,14},{10,8},{12,... | collective-permute-start | bytes 792584 | tf_op jit(solution)/shard_map/ppermute | solution.py:211
  47.8 6.8 %collective-permute-start.7 = (bf16[258,512]{1,0:T(8,128)(2,1)S(1)}, bf16[258,512]{1,0:T(8,128)(2,1)S(1)}, u32[]{:S(2)}, u32[]{:S(2)}) collective-permute-start(bf16[258,512]{1,0:T(8,128)(2,1)S(1)} %slice.204), channel_id=1, source_target_pairs={{0,2},{2,4},{4,6},{6,0},{1,3},{3,5},{5,7},{7,1},{8,10},{10,12},{12... | collective-permute-start | bytes 792584 | tf_op jit(solution)/shard_map/ppermute | solution.py:211
  48.7 5.9 %collective-permute-start.8 = (bf16[258,512]{1,0:T(8,128)(2,1)S(1)}, bf16[258,512]{1,0:T(8,128)(2,1)S(1)}, u32[]{:S(2)}, u32[]{:S(2)}) collective-permute-start(bf16[258,512]{1,0:T(8,128)(2,1)S(1)} %slice.205), channel_id=1, source_target_pairs={{0,6},{2,0},{4,2},{6,4},{1,7},{3,1},{5,3},{7,5},{8,14},{10,8},{12,... | collective-permute-start | bytes 792584 | tf_op jit(solution)/shard_map/ppermute | solution.py:211
  88.8 3.9 %copy-start.8 = (f32[4,1]{1,0:T(4,128)S(1)}, f32[4,1]{1,0:T(4,128)}, u32[]{:S(2)}) copy-start(f32[4,1]{1,0:T(4,128)} %get-tuple-element.71) | copy-start | bytes 52
  88.8 3.9 %copy-start.9 = (f32[4,1]{1,0:T(4,128)S(1)}, f32[4,1]{1,0:T(4,128)}, u32[]{:S(2)}) copy-start(f32[4,1]{1,0:T(4,128)} %get-tuple-element.72) | copy-start | bytes 52
  92.4 18.5 %copy-start = (bf16[512,2,128]{2,0,1:T(8,128)(2,1)S(1)}, bf16[512,2,128]{2,0,1:T(8,128)(2,1)}, u32[]{:S(2)}) copy-start(bf16[512,2,128]{2,0,1:T(8,128)(2,1)} %copy.214) | copy-start | bytes 786436
  92.7 23.0 %collective-permute-start.9 = (f32[4,257]{1,0:T(4,128)S(1)}, f32[4,257]{1,0:T(4,128)S(1)}, u32[]{:S(2)}, u32[]{:S(2)}) collective-permute-start(f32[4,257]{1,0:T(4,128)S(1)} %get-tuple-element.63), channel_id=1, source_target_pairs={{8,0},{16,8},{24,16},{32,24},{40,32},{48,40},{56,48},{64,56},{72,6... | collective-permute-start | bytes 12344 | tf_op jit(solution)/shard_map/ppermute | solution.py:244
  97.2 23.4 %collective-permute-start.11 = (f32[4,257]{1,0:T(4,128)S(1)}, f32[4,257]{1,0:T(4,128)S(1)}, u32[]{:S(2)}, u32[]{:S(2)}) collective-permute-start(f32[4,257]{1,0:T(4,128)S(1)} %get-tuple-element.64), channel_id=1, source_target_pairs={{0,8},{8,16},{16,24},{24,32},{32,40},{40,48},{48,56},{56,64},{64,7... | collective-permute-start | bytes 12344 | tf_op jit(solution)/shard_map/ppermute | solution.py:244
  109.4 2.3 %copy-start.2 = (pred[512,1024]{1,0:T(8,128)(4,1)S(1)}, pred[512,1024]{1,0:T(8,128)(4,1)}, u32[]{:S(2)}) copy-start(pred[512,1024]{1,0:T(8,128)(4,1)} %pad_add_fusion) | copy-start | bytes 1572868
  111.7 2.4 %copy-start.5 = (bf16[1,1,512,256]{2,3,1,0:T(8,128)(2,1)S(1)}, bf16[1,1,512,256]{2,3,1,0:T(8,128)(2,1)}, u32[]{:S(2)}) copy-start(bf16[1,1,512,256]{2,3,1,0:T(8,128)(2,1)} %copy.207) | copy-start | bytes 786436
  114.1 1.0 copy-start.4
  114.1 1.4 %copy-start.3 = (bf16[4,256,256]{2,1,0:T(8,128)(2,1)S(1)}, bf16[4,256,256]{2,1,0:T(8,128)(2,1)}, u32[]{:S(2)}) copy-start(bf16[4,256,256]{2,1,0:T(8,128)(2,1)} %get-tuple-element.42) | copy-start | bytes 1572868
  116.0 9.6 %copy-start.11 = (pred[2,2]{1,0:T(4,128)(4,1)S(1)}, pred[2,2]{1,0:T(4,128)(4,1)}, u32[]{:S(2)}) copy-start(pred[2,2]{1,0:T(4,128)(4,1)} %copy-done.10) | copy-start | bytes 16
  125.9 2.7 %collective-permute-start.10 = (f32[4,2,130]{0,1,2:T(2,128)S(1)}, f32[4,2,130]{0,1,2:T(2,128)S(1)}, u32[]{:S(2)}, u32[]{:S(2)}) collective-permute-start(f32[4,2,130]{0,1,2:T(2,128)S(1)} %pad_maximum_fusion), channel_id=1, source_target_pairs={{0,8},{8,16},{16,24},{24,32},{32,40},{40,48},{48,56},{56,64},{64,7... | collective-permute-start | bytes 12488 | tf_op jit(solution)/shard_map/ppermute | solution.py:250
  126.5 4.7 %collective-permute-start.12 = (f32[4,2,130]{0,1,2:T(2,128)S(1)}, f32[4,2,130]{0,1,2:T(2,128)S(1)}, u32[]{:S(2)}, u32[]{:S(2)}) collective-permute-start(f32[4,2,130]{0,1,2:T(2,128)S(1)} %pad_maximum_fusion.1), channel_id=1, source_target_pairs={{8,0},{16,8},{24,16},{32,24},{40,32},{48,40},{56,48},{64,56},{72,6... | collective-permute-start | bytes 12488 | tf_op jit(solution)/shard_map/ppermute | solution.py:250

commit v7 on v6

--- a/solution.py
+++ b/solution.py
@@ -252,10 +252,16 @@
 
     prev_query, prev_len = ask(piece_len[:, 2], forward)
     next_query, next_len = ask(piece_len[:, 0], backward)
-    right_parts = answer(piece_batch(prev_query, side_store[:requests], prev_len), backward)
-    left_parts = answer(piece_batch(next_query, side_store[requests:], next_len), forward)
+    normed = layer_norm(whole[:count], gain, shift)
+    right_for_prev = piece_batch(prev_query, side_store[:requests], prev_len)
+    left_for_next = piece_batch(next_query, side_store[requests:], next_len)
+    right_for_prev, left_for_next, normed = lax.optimization_barrier(
+        (right_for_prev, left_for_next, normed)
+    )
+    right_parts = answer(right_for_prev, backward)
+    left_parts = answer(left_for_next, forward)
     query, fresh_key, fresh_value = project(
-        layer_norm(whole[:count], gain, shift),
+        normed,
         weight,
         qkv_bias,
         prefill_offset[0] + jnp.arange(count, dtype=jnp.int32),

time: 134 us -> 135 us (level)
  the two profiles are of different devices: /device:TPU:1 before, /device:TPU:152 now
where the time goes in v7:
time: 135 us; the launch traced here: 134 us
  other arithmetic  29.7 us (22%)
  local copies, waits for them, and re-layouts  27 us (20%)
  waiting for transfers between devices  26.1 us (19%)
  starting transfers between devices  20.9 us (15%)
  Pallas kernels  17.5 us (13%)
  matrix products  10.9 us (8%)
  between operations  1.77 us (1%)
    ppermute x1, waiting for transfers between devices, local(): partner = lax.ppermute(rows, 'tz', [(0, 1), (1, 0)])  19.8 us
    pallas_call x2, Pallas kernels, qkv_matmul(): pl.pallas_call(qkv_kernel, out_shape=jax.ShapeDtypeStruct((rows, parts *...  17.5 us
    unnamed x47, local copies, waits for them, and re-layouts  12.2 us
    convert_element_type x2, other arithmetic, layer_norm(): (centred * lax.rsqrt(spread + EPS) * gain + shift).astype(jnp.bfloat16)  6.64 us
    ppermute x2, starting transfers between devices, answer(): got = lax.ppermute(packed, 'group', pairs)  6.03 us
    ppermute x2, starting transfers between devices, ask(): got = lax.ppermute(packed, 'group', pairs)  5.72 us
    dot_general x3, matrix products, piece_rows(): jnp.einsum('rkf,rfh->rhk', keys, spread, preferred_element_type=jnp.float32)  4.99 us
    ppermute x2, waiting for transfers between devices, around(): lax.ppermute(above[half:], 'ty', down)  4.53 us
  transfers between devices with their start and end apart: 13, of which 6 were waited for; matrix products, arithmetic and copies ran while one was open for 23% of the time, Pallas kernels for 0%

profile of v7, /device:TPU:152, one launch (start us, length us, event | category | flops | bytes accessed | tf_op | source)
XLA Modules:
  0.0 133.8 jit_solution(12128214766620792648)
XLA Ops:
  0.7 2.3 %constant_dynamic-update-slice_fusion.1 = (bf16[516,512]{1,0:T(8,128)(2,1)}, bf16[516,4096]{1,0:T(8,128)(2,1)}) fusion(bf16[512,512]{1,0:T(8,128)(2,1)} %param.11), kind=kLoop, calls=%fused_computation.94 | loop fusion | bytes 1572864
  2.9 1.3 constant_dynamic-update-slice_fusion
  4.4 1.8 %collective-permute-start.1 = (bf16[516,512]{1,0:T(8,128)(2,1)}, bf16[516,512]{1,0:T(8,128)(2,1)S(1)}, u32[]{:S(2)}, u32[]{:S(2)}) collective-permute-start(bf16[516,512]{1,0:T(8,128)(2,1)} %get-tuple-element.81), channel_id=1, source_target_pairs={{0,6},{2,0},{4,2},{6,4},{1,7},{3,1},{5,3},{7,5},{8,14},{10,8},{12,... | collective-permute-start | bytes 1585160 | tf_op jit(solution)/shard_map/ppermute | solution.py:209
  6.2 1.0 convert_reduce_fusion.2
  7.2 1.6 %slice_convert_fusion.10 = (f32[4,1]{1,0:T(4,128)}, f32[4,1]{1,0:T(4,128)}, s32[4]{0:T(128)S(1)}) fusion(s32[4,3]{1,0:T(4,128)} %param.20), kind=kLoop, calls=%fused_computation.159 | loop fusion | flops 8 | bytes 96 | tf_op jit(solution)/shard_map/convert_element_type | solution.py:241
  8.9 0.6 iota_compare_fusion.3
  9.6 0.6 broadcast_bitcast_fusion
  11.2 1.1 fusion.115
  12.4 1.0 pad_add_fusion
  13.6 1.1 slice_bitcast_fusion.1
  14.7 19.8 %collective-permute-done.4 = bf16[516,512]{1,0:T(8,128)(2,1)} collective-permute-done((bf16[516,512]{1,0:T(8,128)(2,1)}, bf16[516,512]{1,0:T(8,128)(2,1)}, u32[]{:S(2)}, u32[]{:S(2)}) %collective-permute-start.4) | collective-permute-done | bytes 528416 | tf_op jit(solution)/shard_map/ppermute | solution.py:215
  34.5 1.5 %collective-permute-start.5 = (bf16[516,512]{1,0:T(8,128)(2,1)}, bf16[516,512]{1,0:T(8,128)(2,1)S(1)}, u32[]{:S(2)}, u32[]{:S(2)}) collective-permute-start(bf16[516,512]{1,0:T(8,128)(2,1)} %collective-permute-done.4), channel_id=1, source_target_pairs={{0,2},{2,4},{4,6},{6,0},{1,3},{3,5},{5,7},{7,1},{8,10},{10,12},{12... | collective-permute-start | bytes 1585160 | tf_op jit(solution)/shard_map/ppermute | solution.py:208
  36.0 0.5 collective-permute-start.6
  36.6 0.7 slice.202
  37.3 2.7 %collective-permute-start.2 = (bf16[258,512]{1,0:T(8,128)(2,1)}, bf16[258,512]{1,0:T(8,128)(2,1)}, u32[]{:S(2)}, u32[]{:S(2)}) collective-permute-start(bf16[258,512]{1,0:T(8,128)(2,1)} %slice.202), channel_id=1, source_target_pairs={{0,2},{2,4},{4,6},{6,0},{1,3},{3,5},{5,7},{7,1},{8,10},{10,12},{12... | collective-permute-start | bytes 792584 | tf_op jit(solution)/shard_map/ppermute | solution.py:211
  40.0 0.8 slice.203
  40.7 0.6 pad_add_fusion.1.order_ref
  41.3 0.6 gather_fusion
  41.9 0.6 gather_fusion.1
  42.5 0.7 add.185
  43.2 1.2 copy.278
  44.6 0.8 copy.223
  45.6 0.8 copy.226
  46.4 0.8 copy.213
  47.2 0.6 concatenate.140
  47.9 0.9 constant_dynamic-update-slice_fusion.6
  48.7 0.9 constant_dynamic-update-slice_fusion.5
  49.9 1.8 %collective-permute-done.3 = bf16[258,512]{1,0:T(8,128)(2,1)} collective-permute-done((bf16[258,512]{1,0:T(8,128)(2,1)}, bf16[258,512]{1,0:T(8,128)(2,1)}, u32[]{:S(2)}, u32[]{:S(2)}) %collective-permute-start.3) | collective-permute-done | bytes 264224 | tf_op jit(solution)/shard_map/ppermute | solution.py:211
  51.7 2.0 %maximum_dynamic-update-slice_fusion.1 = bf16[516,4096]{1,0:T(8,128)(2,1)} fusion(bf16[516,4096]{1,0:T(8,128)(2,1)} %constant_dynamic-update-slice_fusion.5, bf16[258,512]{1,0:T(8,128)(2,1)} %collective-permute-done.3, bf16[258,512]{1,0:T(8,128)(2,1)} %collective-permute-done.2), kind=kLoop, calls=%fused_computation.51 | loop fusion | flops 1056768 | bytes 1073152
  53.7 1.3 collective-permute-start.7
  55.0 1.1 collective-permute-start.8
  56.1 2.0 %constant_dynamic-update-slice_fusion.4 = bf16[516,4096]{1,0:T(8,128)(2,1)} fusion(bf16[516,4096]{1,0:T(8,128)(2,1)} %maximum_dynamic-update-slice_fusion.1, bf16[516,512]{1,0:T(8,128)(2,1)} %collective-permute-done.4), kind=kLoop, calls=%fused_computation.97 | loop fusion | bytes 1064960
  58.1 0.9 constant_dynamic-update-slice_fusion.3
  59.0 0.9 constant_dynamic-update-slice_fusion.2
  59.9 0.4 collective-permute-done.7
  60.3 2.7 %collective-permute-done.8 = bf16[258,512]{1,0:T(8,128)(2,1)S(1)} collective-permute-done((bf16[258,512]{1,0:T(8,128)(2,1)S(1)}, bf16[258,512]{1,0:T(8,128)(2,1)S(1)}, u32[]{:S(2)}, u32[]{:S(2)}) %collective-permute-start.8) | collective-permute-done | bytes 264224 | tf_op jit(solution)/shard_map/ppermute | solution.py:211
  63.0 0.9 maximum_dynamic-update-slice_fusion
  63.9 1.0 convert_reduce_fusion.1
  64.9 2.8 %convert_reduce_fusion = f32[512]{0:T(512)S(1)} fusion(bf16[516,4096]{1,0:T(8,128)(2,1)} %maximum_dynamic-update-slice_fusion), kind=kLoop, calls=%fused_computation.4 | loop fusion | flops 4193792 | bytes 4196352 | tf_op jit(solution)/shard_map/reduce_sum | solution.py:35
  67.7 1.1 fusion.72
  68.8 1.5 %fusion.75.x_ref = bf16[4,4096]{1,0:T(4,128)(2,1)} fusion(f32[4096]{0:T(1024)S(1)} %bitcast.147, f32[4096]{0:T(1024)S(1)} %bitcast.145, f32[4]{0:T(128)S(1)} %add_rsqrt_fusion.1, f32[4]{0:T(128)S(1)} %broadcast_multiply_fusion.1, bf16[516,4096]{1,0:T(8,128)(2,1)} %maximum_dynamic-update-slice_fusion), kind=kLoop, calls=%fused_computation.88 | loop fusion | flops 98304 | bytes 98336 | tf_op jit(solution)/shard_map/convert_element_type | solution.py:38
  70.4 7.1 %shard_map.122 = f32[4,768]{1,0:T(4,128)} custom-call(s32[8]{0:T(128)} %pad_add_fusion.1.order_ref, bf16[4,4096]{1,0:T(4,128)(2,1)} %fusion.75.x_ref, bf16[3,4096,256]{2,1,0:T(8,128)(2,1)} %bitcast.135), custom_call_target="tpu_custom_call" | custom-call | flops 25165824 | bytes 6336512 | tf_op jit(solution)/shard_map/pallas_call | solution.py:73
  77.5 0.7 broadcast_add_fusion.1
  79.4 3.4 %fusion.3 = f32[512]{0:T(512)S(1)} fusion(f32[512]{0:T(512)S(1)} %broadcast_multiply_fusion, bf16[516,4096]{1,0:T(8,128)(2,1)} %maximum_dynamic-update-slice_fusion), kind=kLoop, calls=%fused_computation.7 | loop fusion | flops 8388096 | bytes 4198400 | tf_op jit(solution)/shard_map/reduce_sum | solution.py:37
  82.9 5.1 %fusion.6.x_ref = bf16[512,4096]{1,0:T(8,128)(2,1)} fusion(f32[4096]{0:T(1024)S(1)} %bitcast.148, f32[4096]{0:T(1024)S(1)} %bitcast.146, f32[512]{0:T(512)S(1)} %add_rsqrt_fusion, f32[512]{0:T(512)S(1)} %broadcast_multiply_fusion, bf16[516,4096]{1,0:T(8,128)(2,1)} %maximum_dynamic-update-slice_fusion), kind=kLoop, calls=%fused_computation.10 | loop fusion | flops 12582912 | bytes 8425472 | tf_op jit(solution)/shard_map/convert_element_type | solution.py:38
  88.2 5.6 %collective-permute-start.10 = (f32[4,257]{1,0:T(4,128)S(1)}, f32[4,257]{1,0:T(4,128)S(1)}, u32[]{:S(2)}, u32[]{:S(2)}) collective-permute-start(f32[4,257]{1,0:T(4,128)S(1)} %get-tuple-element.77), channel_id=1, source_target_pairs={{8,0},{16,8},{24,16},{32,24},{40,32},{48,40},{56,48},{64,56},{72,6... | collective-permute-start | bytes 12344 | tf_op jit(solution)/shard_map/ppermute | solution.py:244
  94.1 1.0 collective-permute-done.9
  95.5 2.3 %fusion.116 = (f32[4,2]{1,0:T(4,128)S(1)}, f32[4,2,1024]{2,1,0:T(2,128)S(1)}) fusion(bf16[8,2,1024,256]{3,2,1,0:T(8,128)(2,1)} %param.21, pred[256,2]{0,1:T(4,128)(4,1)S(1)} %bitcast.161, bf16[4,256]{1,0:T(4,128)(2,1)S(1)} %slice.333, pred[4,1024]{1,0:T(4,128)(4,1)S(1)} %iota_compare_fusion.2), kind=kOutput, calls=%fused_computation.200 | convolution fusion | flops 4220920 | bytes 2136608 | tf_op jit(solution)/shard_map/rkf,rfh->rhk/dot_general | solution.py:146
  97.9 2.0 %fusion.12 = f32[4,2,256]{2,1,0:T(2,128)S(1)} fusion(bf16[8,2,1024,256]{3,2,1,0:T(8,128)(2,1)} %param.21, f32[4,2,1024]{2,1,0:T(2,128)S(1)} %get-tuple-element.92, pred[4,1024]{1,0:T(4,128)(4,1)S(1)} %iota_compare_fusion.2, f32[4,2]{1,0:T(4,128)S(1)} %get-tuple-element.32), kind=kOutput, calls=%fused_computation.18 | convolution fusion | flops 4218880 | bytes 2142240 | tf_op jit(solution)/shard_map/rhk,rkf->rhf/dot_general | solution.py:153
  99.9 2.3 %fusion.118 = (f32[4,2]{1,0:T(4,128)S(1)}, f32[4,2,1024]{2,1,0:T(2,128)S(1)}) fusion(bf16[8,2,1024,256]{3,2,1,0:T(8,128)(2,1)} %param.21, pred[256,2]{0,1:T(4,128)(4,1)S(1)} %bitcast.162, bf16[4,256]{1,0:T(4,128)(2,1)S(1)} %slice.332, pred[4,1024]{1,0:T(4,128)(4,1)S(1)} %iota_compare_fusion.1), kind=kOutput, calls=%fused_computation.202 | convolution fusion | flops 4220920 | bytes 2136608 | tf_op jit(solution)/shard_map/rkf,rfh->rhk/dot_general | solution.py:146
  102.2 2.0 %fusion.8 = f32[4,2,256]{2,1,0:T(2,128)S(1)} fusion(bf16[8,2,1024,256]{3,2,1,0:T(8,128)(2,1)} %param.21, f32[4,2,1024]{2,1,0:T(2,128)S(1)} %get-tuple-element.96, pred[4,1024]{1,0:T(4,128)(4,1)S(1)} %iota_compare_fusion.1, f32[4,2]{1,0:T(4,128)S(1)} %get-tuple-element.29), kind=kOutput, calls=%fused_computation.14 | convolution fusion | flops 4218880 | bytes 2142240 | tf_op jit(solution)/shard_map/rhk,rkf->rhf/dot_general | solution.py:153
  104.6 10.4 %shard_map.123 = f32[512,768]{1,0:T(8,128)} custom-call(s32[8]{0:T(128)} %pad_add_fusion.1.order_ref, bf16[512,4096]{1,0:T(8,128)(2,1)} %fusion.6.x_ref, bf16[3,4096,256]{2,1,0:T(8,128)(2,1)} %bitcast.136), custom_call_target="tpu_custom_call" | custom-call | flops 3221225472 | bytes 12058624 | tf_op jit(solution)/shard_map/pallas_call | solution.py:73
  115.0 1.5 %broadcast_add_fusion = f32[512,768]{1,0:T(8,128)S(1)} fusion(f32[512,768]{1,0:T(8,128)} %shard_map.123, f32[768]{0:T(1024)S(1)} %add.185), kind=kLoop, calls=%fused_computation.42 | loop fusion | flops 393216 | bytes 3148800 | tf_op jit(solution)/shard_map/add | solution.py:98
  116.5 0.8 reshape.568
  117.7 0.9 slice.216
  119.0 0.7 collective-permute-start.11
  120.1 5.4 %collective-permute-start.12 = (f32[4,2,130]{0,1,2:T(2,128)S(1)}, f32[4,2,130]{0,1,2:T(2,128)S(1)}, u32[]{:S(2)}, u32[]{:S(2)}) collective-permute-start(f32[4,2,130]{0,1,2:T(2,128)S(1)} %pad_maximum_fusion.1), channel_id=1, source_target_pairs={{8,0},{16,8},{24,16},{32,24},{40,32},{48,40},{56,48},{64,56},{72,6... | collective-permute-start | bytes 12488 | tf_op jit(solution)/shard_map/ppermute | solution.py:250
  125.8 1.1 copy.269
  127.0 0.4 subtract_convert_fusion.1
  127.4 0.8 fusion.57
  128.3 2.3 %fusion.119 = (f32[2,512]{1,0:T(2,128)S(1)}, bf16[2,512,1024]{2,1,0:T(8,128)(2,1)S(1)}) fusion(f32[2,512,1024]{2,1,0:T(8,128)S(1)} %fusion.57, pred[512,1024]{1,0:T(8,128)(4,1)S(1)} %copy-done.3), kind=kOutput, calls=%fused_computation.203 | output fusion | flops 8389631 | bytes 6819840 | tf_op jit(solution)/shard_map/while/body/eval_jaxpr/sub | solution.py:111
  130.6 0.8 fusion.31
  131.4 0.8 copy.253
  133.1 0.7 copy.252
  (119 shorter events, 6.3 us)
Async XLA Ops:
  0.6 12.9 %copy-start.2 = (bf16[4,2,256,256]{3,2,1,0:T(8,128)(2,1)S(1)}, bf16[4,2,256,256]{3,2,1,0:T(8,128)(2,1)}, u32[]{:S(2)}) copy-start(bf16[4,2,256,256]{3,2,1,0:T(8,128)(2,1)} %param.19) | copy-start | bytes 3145732
  0.6 40.7 %copy-start.7 = (f32[4096]{0:T(1024)S(1)}, f32[4096]{0:T(1024)}, u32[]{:S(2)}) copy-start(f32[4096]{0:T(1024)} %param.13) | copy-start | bytes 49156
  0.7 41.3 %copy-start.8 = (f32[4096]{0:T(1024)S(1)}, f32[4096]{0:T(1024)}, u32[]{:S(2)}) copy-start(f32[4096]{0:T(1024)} %param.14) | copy-start | bytes 49156
  4.2 32.3 %collective-permute-start = (bf16[516,512]{1,0:T(8,128)(2,1)}, bf16[516,512]{1,0:T(8,128)(2,1)S(1)}, u32[]{:S(2)}, u32[]{:S(2)}) collective-permute-start(bf16[516,512]{1,0:T(8,128)(2,1)} %get-tuple-element.81), channel_id=1, source_target_pairs={{0,2},{2,4},{4,6},{6,0},{1,3},{3,5},{5,7},{7,1},{8,10},{10,12},{12... | collective-permute-start | bytes 1585160 | tf_op jit(solution)/shard_map/ppermute | solution.py:208
  4.4 35.5 %collective-permute-start.1 = (bf16[516,512]{1,0:T(8,128)(2,1)}, bf16[516,512]{1,0:T(8,128)(2,1)S(1)}, u32[]{:S(2)}, u32[]{:S(2)}) collective-permute-start(bf16[516,512]{1,0:T(8,128)(2,1)} %get-tuple-element.81), channel_id=1, source_target_pairs={{0,6},{2,0},{4,2},{6,4},{1,7},{3,1},{5,3},{7,5},{8,14},{10,8},{12,... | collective-permute-start | bytes 1585160 | tf_op jit(solution)/shard_map/ppermute | solution.py:209
  6.2 28.3 %collective-permute-start.4 = (bf16[516,512]{1,0:T(8,128)(2,1)}, bf16[516,512]{1,0:T(8,128)(2,1)}, u32[]{:S(2)}, u32[]{:S(2)}) collective-permute-start(bf16[516,512]{1,0:T(8,128)(2,1)} %get-tuple-element.81), channel_id=1, source_target_pairs={{0,1},{1,0},{2,3},{3,2},{4,5},{5,4},{6,7},{7,6},{8,9},{9,8},{10,11... | collective-permute-start | bytes 1585160 | tf_op jit(solution)/shard_map/ppermute | solution.py:215
  8.8 2.1 %copy-start.12 = (pred[2,2]{1,0:T(4,128)(4,1)}, pred[2,2]{1,0:T(4,128)(4,1)S(1)}, u32[]{:S(2)}) copy-start(pred[2,2]{1,0:T(4,128)(4,1)S(1)} %iota_compare_fusion.5) | copy-start | bytes 16
  34.5 19.2 %collective-permute-start.5 = (bf16[516,512]{1,0:T(8,128)(2,1)}, bf16[516,512]{1,0:T(8,128)(2,1)S(1)}, u32[]{:S(2)}, u32[]{:S(2)}) collective-permute-start(bf16[516,512]{1,0:T(8,128)(2,1)} %collective-permute-done.4), channel_id=1, source_target_pairs={{0,2},{2,4},{4,6},{6,0},{1,3},{3,5},{5,7},{7,1},{8,10},{10,12},{12... | collective-permute-start | bytes 1585160 | tf_op jit(solution)/shard_map/ppermute | solution.py:208
  36.0 19.0 %collective-permute-start.6 = (bf16[516,512]{1,0:T(8,128)(2,1)}, bf16[516,512]{1,0:T(8,128)(2,1)S(1)}, u32[]{:S(2)}, u32[]{:S(2)}) collective-permute-start(bf16[516,512]{1,0:T(8,128)(2,1)} %collective-permute-done.4), channel_id=1, source_target_pairs={{0,6},{2,0},{4,2},{6,4},{1,7},{3,1},{5,3},{7,5},{8,14},{10,8},{12,... | collective-permute-start | bytes 1585160 | tf_op jit(solution)/shard_map/ppermute | solution.py:209
  37.3 12.6 %collective-permute-start.2 = (bf16[258,512]{1,0:T(8,128)(2,1)}, bf16[258,512]{1,0:T(8,128)(2,1)}, u32[]{:S(2)}, u32[]{:S(2)}) collective-permute-start(bf16[258,512]{1,0:T(8,128)(2,1)} %slice.202), channel_id=1, source_target_pairs={{0,2},{2,4},{4,6},{6,0},{1,3},{3,5},{5,7},{7,1},{8,10},{10,12},{12... | collective-permute-start | bytes 792584 | tf_op jit(solution)/shard_map/ppermute | solution.py:211
  40.7 11.0 %collective-permute-start.3 = (bf16[258,512]{1,0:T(8,128)(2,1)}, bf16[258,512]{1,0:T(8,128)(2,1)}, u32[]{:S(2)}, u32[]{:S(2)}) collective-permute-start(bf16[258,512]{1,0:T(8,128)(2,1)} %slice.203), channel_id=1, source_target_pairs={{0,6},{2,0},{4,2},{6,4},{1,7},{3,1},{5,3},{7,5},{8,14},{10,8},{12,... | collective-permute-start | bytes 792584 | tf_op jit(solution)/shard_map/ppermute | solution.py:211
  53.7 6.5 %collective-permute-start.7 = (bf16[258,512]{1,0:T(8,128)(2,1)S(1)}, bf16[258,512]{1,0:T(8,128)(2,1)S(1)}, u32[]{:S(2)}, u32[]{:S(2)}) collective-permute-start(bf16[258,512]{1,0:T(8,128)(2,1)S(1)} %slice.204), channel_id=1, source_target_pairs={{0,2},{2,4},{4,6},{6,0},{1,3},{3,5},{5,7},{7,1},{8,10},{10,12},{12... | collective-permute-start | bytes 792584 | tf_op jit(solution)/shard_map/ppermute | solution.py:211
  55.0 7.9 %collective-permute-start.8 = (bf16[258,512]{1,0:T(8,128)(2,1)S(1)}, bf16[258,512]{1,0:T(8,128)(2,1)S(1)}, u32[]{:S(2)}, u32[]{:S(2)}) collective-permute-start(bf16[258,512]{1,0:T(8,128)(2,1)S(1)} %slice.205), channel_id=1, source_target_pairs={{0,6},{2,0},{4,2},{6,4},{1,7},{3,1},{5,3},{7,5},{8,14},{10,8},{12,... | collective-permute-start | bytes 792584 | tf_op jit(solution)/shard_map/ppermute | solution.py:211
  67.7 11.0 %copy-start.5 = (bf16[4,256,256]{2,1,0:T(8,128)(2,1)S(1)}, bf16[4,256,256]{2,1,0:T(8,128)(2,1)}, u32[]{:S(2)}) copy-start(bf16[4,256,256]{2,1,0:T(8,128)(2,1)} %get-tuple-element.61) | copy-start | bytes 1572868
  67.7 11.0 %copy-start.11 = (pred[1,2,2,128]{3,1,2,0:T(4,128)(4,1)S(1)}, pred[1,2,2,128]{3,1,2,0:T(4,128)(4,1)}, u32[]{:S(2)}) copy-start(pred[1,2,2,128]{3,1,2,0:T(4,128)(4,1)} %copy.278) | copy-start | bytes 1540
  82.8 5.2 %copy-start.9 = (f32[4,1]{1,0:T(4,128)S(1)}, f32[4,1]{1,0:T(4,128)}, u32[]{:S(2)}) copy-start(f32[4,1]{1,0:T(4,128)} %get-tuple-element.86) | copy-start | bytes 52
  82.8 5.2 %copy-start.10 = (f32[4,1]{1,0:T(4,128)S(1)}, f32[4,1]{1,0:T(4,128)}, u32[]{:S(2)}) copy-start(f32[4,1]{1,0:T(4,128)} %get-tuple-element.87) | copy-start | bytes 52
  82.9 11.0 %copy-start.4 = (bf16[4,256,256]{2,1,0:T(8,128)(2,1)S(1)}, bf16[4,256,256]{2,1,0:T(8,128)(2,1)}, u32[]{:S(2)}) copy-start(bf16[4,256,256]{2,1,0:T(8,128)(2,1)} %get-tuple-element.62) | copy-start | bytes 1572868
  88.1 7.0 %collective-permute-start.9 = (f32[4,257]{1,0:T(4,128)S(1)}, f32[4,257]{1,0:T(4,128)S(1)}, u32[]{:S(2)}, u32[]{:S(2)}) collective-permute-start(f32[4,257]{1,0:T(4,128)S(1)} %get-tuple-element.78), channel_id=1, source_target_pairs={{0,8},{8,16},{16,24},{24,32},{32,40},{40,48},{48,56},{56,64},{64,7... | collective-permute-start | bytes 12344 | tf_op jit(solution)/shard_map/ppermute | solution.py:244
  88.2 7.1 %collective-permute-start.10 = (f32[4,257]{1,0:T(4,128)S(1)}, f32[4,257]{1,0:T(4,128)S(1)}, u32[]{:S(2)}, u32[]{:S(2)}) collective-permute-start(f32[4,257]{1,0:T(4,128)S(1)} %get-tuple-element.77), channel_id=1, source_target_pairs={{8,0},{16,8},{24,16},{32,24},{40,32},{48,40},{56,48},{64,56},{72,6... | collective-permute-start | bytes 12344 | tf_op jit(solution)/shard_map/ppermute | solution.py:244
  95.5 9.0 %copy-start.13 = (pred[2,2]{1,0:T(4,128)(4,1)S(1)}, pred[2,2]{1,0:T(4,128)(4,1)}, u32[]{:S(2)}) copy-start(pred[2,2]{1,0:T(4,128)(4,1)} %copy-done.12) | copy-start | bytes 16
  118.6 8.4 %copy-start = (f32[512,16]{1,0:T(8,128)S(1)}, f32[512,16]{1,0:T(8,128)}, u32[]{:S(2)}) copy-start(f32[512,16]{1,0:T(8,128)} %copy.223) | copy-start | bytes 98308
  118.6 8.8 %copy-start.1 = (bf16[512,2,128]{2,0,1:T(8,128)(2,1)S(1)}, bf16[512,2,128]{2,0,1:T(8,128)(2,1)}, u32[]{:S(2)}) copy-start(bf16[512,2,128]{2,0,1:T(8,128)(2,1)} %copy.226) | copy-start | bytes 786436
  119.0 13.3 %collective-permute-start.11 = (f32[4,2,130]{0,1,2:T(2,128)S(1)}, f32[4,2,130]{0,1,2:T(2,128)S(1)}, u32[]{:S(2)}, u32[]{:S(2)}) collective-permute-start(f32[4,2,130]{0,1,2:T(2,128)S(1)} %pad_maximum_fusion), channel_id=1, source_target_pairs={{0,8},{8,16},{16,24},{24,32},{32,40},{40,48},{48,56},{56,64},{64,7... | collective-permute-start | bytes 12488 | tf_op jit(solution)/shard_map/ppermute | solution.py:250
  120.1 12.2 %collective-permute-start.12 = (f32[4,2,130]{0,1,2:T(2,128)S(1)}, f32[4,2,130]{0,1,2:T(2,128)S(1)}, u32[]{:S(2)}, u32[]{:S(2)}) collective-permute-start(f32[4,2,130]{0,1,2:T(2,128)S(1)} %pad_maximum_fusion.1), channel_id=1, source_target_pairs={{8,0},{16,8},{24,16},{32,24},{40,32},{48,40},{56,48},{64,56},{72,6... | collective-permute-start | bytes 12488 | tf_op jit(solution)/shard_map/ppermute | solution.py:250
  127.0 1.3 copy-start.3
  128.2 2.3 %copy-start.6 = (bf16[1,1,512,256]{2,3,1,0:T(8,128)(2,1)S(1)}, bf16[1,1,512,256]{2,3,1,0:T(8,128)(2,1)}, u32[]{:S(2)}) copy-start(bf16[1,1,512,256]{2,3,1,0:T(8,128)(2,1)} %copy.213) | copy-start | bytes 786436

commit v8 on v6

--- a/solution.py
+++ b/solution.py
@@ -196,7 +196,19 @@
 ):
     count = prefill_x.shape[0]
     requests = decode_x.shape[0]
-    rows = jnp.concatenate([prefill_x, decode_x], axis=0)
+    groups = lax.axis_size("group")
+    forward = [(i, (i + 1) % groups) for i in range(groups)]
+    backward = [((i + 1) % groups, i) for i in range(groups)]
+    mine = jnp.concatenate([decode_x.astype(jnp.float32), piece_len.astype(jnp.float32)], axis=1)
+    width = decode_x.shape[1]
+
+    def neighbour(pairs):
+        got = lax.ppermute(mine, "group", pairs)
+        return got[:, :width].astype(decode_x.dtype), got[:, width:].astype(jnp.int32)
+
+    prev_x, prev_len = neighbour(forward)
+    next_x, next_len = neighbour(backward)
+    rows = jnp.concatenate([prefill_x, decode_x, prev_x, next_x], axis=0)
     ring = lax.axis_size("ty")
     y = lax.axis_index("ty")
     z = lax.axis_index("tz")
@@ -223,26 +235,20 @@
 
     gain, shift = feature_order(ln_gain), feature_order(ln_bias)
     weight = jnp.transpose(qkv_weight, (1, 0, 2))
-    own_query, new_key, new_value = project(
+    lengths = jnp.concatenate([piece_len, prev_len, next_len], axis=0)
+    all_query, all_key, all_value = project(
         layer_norm(whole[count:], gain, shift),
         weight,
         qkv_bias,
-        piece_len[:, 0] + piece_len[:, 1] + piece_len[:, 2],
+        lengths[:, 0] + lengths[:, 1] + lengths[:, 2],
         order,
     )
-    home_parts = home_partial(own_query, new_key, new_value, home_cache, piece_len[:, 1])
-    groups = lax.axis_size("group")
-    forward = [(i, (i + 1) % groups) for i in range(groups)]
-    backward = [((i + 1) % groups, i) for i in range(groups)]
-    heads = own_query.shape[1]
-
-    def ask(lengths, pairs):
-        packed = jnp.concatenate(
-            [own_query.astype(jnp.float32).reshape(requests, -1), lengths[:, None].astype(jnp.float32)],
-            axis=1,
-        )
-        got = lax.ppermute(packed, "group", pairs)
-        return got[:, :-1].reshape(own_query.shape).astype(own_query.dtype), got[:, -1].astype(jnp.int32)
+    own_query = all_query[:requests]
+    prev_query = all_query[requests : 2 * requests]
+    next_query = all_query[2 * requests :]
+    home_parts = home_partial(
+        own_query, all_key[:requests], all_value[:requests], home_cache, piece_len[:, 1]
+    )
 
     def answer(parts, pairs):
         highest, total, summed = parts
@@ -250,12 +256,17 @@
         got = lax.ppermute(packed, "group", pairs)
         return (got[:, :, HD], got[:, :, HD + 1], got[:, :, :HD])
 
-    prev_query, prev_len = ask(piece_len[:, 2], forward)
-    next_query, next_len = ask(piece_len[:, 0], backward)
-    right_parts = answer(piece_batch(prev_query, side_store[:requests], prev_len), backward)
-    left_parts = answer(piece_batch(next_query, side_store[requests:], next_len), forward)
+    right_for_prev = piece_batch(prev_query, side_store[:requests], prev_len[:, 2])
+    left_for_next = piece_batch(next_query, side_store[requests:], next_len[:, 0])
+    right_parts, left_parts, normed = lax.optimization_barrier(
+        (
+            answer(right_for_prev, backward),
+            answer(left_for_next, forward),
+            layer_norm(whole[:count], gain, shift),
+        )
+    )
     query, fresh_key, fresh_value = project(
-        layer_norm(whole[:count], gain, shift),
+        normed,
         weight,
         qkv_bias,
         prefill_offset[0] + jnp.arange(count, dtype=jnp.int32),

time: 134 us -> 141 us (1.052)
  waiting for transfers between devices: 10.9 us -> 20.4 us
  local copies, waits for them, and re-layouts: 26.3 us -> 20 us
  starting transfers between devices: 34.8 us -> 40.1 us
    ppermute x2, starting transfers between devices: 0.66 us -> 19.6 us  [answer(): got = lax.ppermute(packed, 'group', pairs)]
    ppermute x2, starting transfers between devices: 15.3 us -> 3.24 us  [neighbour(): got = lax.ppermute(mine, 'group', pairs)]
    ppermute x2, waiting for transfers between devices: 0.01 us -> 7.89 us  [around(): above = lax.ppermute(block, 'ty', down)]
    unnamed x41 -> x42, local copies, waits for them, and re-layouts: 11.5 us -> 7.47 us
    slice x1 -> x0, other arithmetic: 1.56 us -> none  [local(): piece_len[:, 1]]
    ppermute x2, starting transfers between devices: 2.58 us -> 1.17 us  [around(): below = lax.ppermute(block, 'ty', up)]
  transfers between devices with their start and end apart: 13 -> 13, of which waited for: 4 -> 7; matrix products, arithmetic and copies ran while one was open for 28% -> 12% of each run, Pallas kernels for 0% -> 0%
where the time goes in v8:
time: 141 us; the launch traced here: 140 us
  starting transfers between devices  40.1 us (28%)
  other arithmetic  29.3 us (21%)
  waiting for transfers between devices  20.4 us (14%)
  local copies, waits for them, and re-layouts  20 us (14%)
  Pallas kernels  17.6 us (12%)
  matrix products  10.9 us (8%)
  between operations  1.82 us (1%)
    ppermute x2, starting transfers between devices, answer(): got = lax.ppermute(packed, 'group', pairs)  19.6 us
    pallas_call x2, Pallas kernels, qkv_matmul(): pl.pallas_call(qkv_kernel, out_shape=jax.ShapeDtypeStruct((rows, parts *...  17.6 us
    ppermute x2, waiting for transfers between devices, around(): above = lax.ppermute(block, 'ty', down)  7.89 us
    unnamed x42, local copies, waits for them, and re-layouts  7.47 us
    convert_element_type x2, other arithmetic, layer_norm(): (centred * lax.rsqrt(spread + EPS) * gain + shift).astype(jnp.bfloat16)  6.79 us
    ppermute x1, starting transfers between devices, local(): partner = lax.ppermute(rows, 'tz', [(0, 1), (1, 0)])  6.3 us
    ppermute x1, waiting for transfers between devices, local(): partner = lax.ppermute(rows, 'tz', [(0, 1), (1, 0)])  5.23 us
    ppermute x2, starting transfers between devices, around(): lax.ppermute(above[half:], 'ty', down)  5.2 us
  transfers between devices with their start and end apart: 13, of which 7 were waited for; matrix products, arithmetic and copies ran while one was open for 12% of the time, Pallas kernels for 0%

profile of v8, /device:TPU:1, one launch (start us, length us, event | category | flops | bytes accessed | tf_op | source)
XLA Modules:
  0.0 140.2 jit_solution(968822822398700958)
XLA Ops:
  0.7 0.8 convert_element_type.69
  1.4 0.7 convert_element_type.70
  2.1 3.2 %collective-permute-start.1 = (f32[4,515]{1,0:T(4,128)S(1)}, f32[4,515]{1,0:T(4,128)S(1)}, u32[]{:S(2)}, u32[]{:S(2)}) collective-permute-start(f32[4,515]{1,0:T(4,128)S(1)} %pad_maximum_fusion.1), channel_id=1, source_target_pairs={{8,0},{16,8},{24,16},{32,24},{40,32},{48,40},{56,48},{64,56},{72,6... | collective-permute-start | bytes 24728 | tf_op jit(solution)/shard_map/ppermute | solution.py:206
  5.5 0.9 slice_reduce_fusion
  6.8 2.1 %slice_bitcast_fusion.1 = (bf16[4,256,256]{2,1,0:T(8,128)(2,1)}, bf16[4,256,256]{2,1,0:T(8,128)(2,1)S(1)}) fusion(bf16[4,2,256,256]{3,2,1,0:T(8,128)(2,1)} %param.19), kind=kLoop, calls=%fused_computation.69 | loop fusion | bytes 2097152 | tf_op jit(solution)/shard_map/squeeze | solution.py:168
  9.5 1.1 fusion.104
  10.6 0.2 multiply_cosine_fusion
  10.8 1.0 pad_add_fusion
  11.9 0.6 pad_add_fusion.2.order_ref
  12.6 0.6 gather_fusion
  13.2 0.6 gather_fusion.1
  13.9 0.8 copy.162
  14.9 0.8 copy.165
  15.7 0.8 copy.137
  16.6 0.9 pad_maximum_fusion
  17.6 1.2 collective-permute-start.2
  18.7 1.5 %collective-permute-start.3 = (bf16[524,512]{1,0:T(8,128)(2,1)S(1)}, bf16[524,512]{1,0:T(8,128)(2,1)S(1)}, u32[]{:S(2)}, u32[]{:S(2)}) collective-permute-start(bf16[524,512]{1,0:T(8,128)(2,1)S(1)} %get-tuple-element.61), channel_id=1, source_target_pairs={{0,6},{2,0},{4,2},{6,4},{1,7},{3,1},{5,3},{7,5},{8,14},{10,8},{12,... | collective-permute-start | bytes 1609736 | tf_op jit(solution)/shard_map/ppermute | solution.py:221
  20.2 6.3 %collective-permute-start.6 = (bf16[524,512]{1,0:T(8,128)(2,1)S(1)}, bf16[524,512]{1,0:T(8,128)(2,1)S(1)}, u32[]{:S(2)}, u32[]{:S(2)}) collective-permute-start(bf16[524,512]{1,0:T(8,128)(2,1)S(1)} %get-tuple-element.61), channel_id=1, source_target_pairs={{0,1},{1,0},{2,3},{3,2},{4,5},{5,4},{6,7},{7,6},{8,9},{9,8},{10,11... | collective-permute-start | bytes 1609736 | tf_op jit(solution)/shard_map/ppermute | solution.py:227
  27.3 0.7 collective-permute-done.2
  28.2 2.7 %collective-permute-start.5 = (bf16[262,512]{1,0:T(8,128)(2,1)S(1)}, bf16[262,512]{1,0:T(8,128)(2,1)S(1)}, u32[]{:S(2)}, u32[]{:S(2)}) collective-permute-start(bf16[262,512]{1,0:T(8,128)(2,1)S(1)} %slice.235), channel_id=1, source_target_pairs={{0,6},{2,0},{4,2},{6,4},{1,7},{3,1},{5,3},{7,5},{8,14},{10,8},{12,... | collective-permute-start | bytes 804872 | tf_op jit(solution)/shard_map/ppermute | solution.py:223
  30.9 5.2 %collective-permute-done.6 = bf16[524,512]{1,0:T(8,128)(2,1)S(1)} collective-permute-done((bf16[524,512]{1,0:T(8,128)(2,1)S(1)}, bf16[524,512]{1,0:T(8,128)(2,1)S(1)}, u32[]{:S(2)}, u32[]{:S(2)}) %collective-permute-start.6) | collective-permute-done | bytes 536608 | tf_op jit(solution)/shard_map/ppermute | solution.py:227
  36.2 2.7 %collective-permute-start.8 = (bf16[524,512]{1,0:T(8,128)(2,1)S(1)}, bf16[524,512]{1,0:T(8,128)(2,1)S(1)}, u32[]{:S(2)}, u32[]{:S(2)}) collective-permute-start(bf16[524,512]{1,0:T(8,128)(2,1)S(1)} %collective-permute-done.6), channel_id=1, source_target_pairs={{0,6},{2,0},{4,2},{6,4},{1,7},{3,1},{5,3},{7,5},{8,14},{10,8},{12,... | collective-permute-start | bytes 1609736 | tf_op jit(solution)/shard_map/ppermute | solution.py:221
  38.9 0.9 constant_dynamic-update-slice_fusion.4
  39.8 0.9 constant_dynamic-update-slice_fusion.3
  40.7 1.0 maximum_dynamic-update-slice_fusion.1
  41.7 7.9 %collective-permute-done.8 = bf16[524,512]{1,0:T(8,128)(2,1)S(1)} collective-permute-done((bf16[524,512]{1,0:T(8,128)(2,1)S(1)}, bf16[524,512]{1,0:T(8,128)(2,1)S(1)}, u32[]{:S(2)}, u32[]{:S(2)}) %collective-permute-start.8) | collective-permute-done | bytes 536608 | tf_op jit(solution)/shard_map/ppermute | solution.py:221
  49.7 2.5 %collective-permute-start.10 = (bf16[262,512]{1,0:T(8,128)(2,1)S(1)}, bf16[262,512]{1,0:T(8,128)(2,1)S(1)}, u32[]{:S(2)}, u32[]{:S(2)}) collective-permute-start(bf16[262,512]{1,0:T(8,128)(2,1)S(1)} %slice.237), channel_id=1, source_target_pairs={{0,6},{2,0},{4,2},{6,4},{1,7},{3,1},{5,3},{7,5},{8,14},{10,8},{12,... | collective-permute-start | bytes 804872 | tf_op jit(solution)/shard_map/ppermute | solution.py:223
  52.2 0.3 collective-permute-start.9
  52.4 0.9 constant_dynamic-update-slice_fusion.2
  53.4 0.9 constant_dynamic-update-slice_fusion.1
  54.2 0.9 constant_dynamic-update-slice_fusion
  55.1 0.9 collective-permute-done.10
  56.0 3.0 %collective-permute-done.9 = bf16[262,512]{1,0:T(8,128)(2,1)S(1)} collective-permute-done((bf16[262,512]{1,0:T(8,128)(2,1)S(1)}, bf16[262,512]{1,0:T(8,128)(2,1)S(1)}, u32[]{:S(2)}, u32[]{:S(2)}) %collective-permute-start.9) | collective-permute-done | bytes 268320 | tf_op jit(solution)/shard_map/ppermute | solution.py:223
  58.9 0.9 maximum_dynamic-update-slice_fusion
  59.9 1.0 convert_reduce_fusion.1
  60.9 2.8 %convert_reduce_fusion = f32[512]{0:T(512)S(1)} fusion(bf16[524,4096]{1,0:T(8,128)(2,1)} %maximum_dynamic-update-slice_fusion), kind=kLoop, calls=%fused_computation.4 | loop fusion | flops 4193792 | bytes 4196352 | tf_op jit(solution)/shard_map/reduce_sum | solution.py:35
  63.7 1.1 fusion.67
  64.9 1.7 %fusion.70.x_ref = bf16[12,4096]{1,0:T(8,128)(2,1)} fusion(f32[4096]{0:T(1024)S(1)} %bitcast.130, f32[4096]{0:T(1024)S(1)} %bitcast.128, f32[12]{0:T(128)S(1)} %add_rsqrt_fusion.1, f32[12]{0:T(128)S(1)} %broadcast_multiply_fusion.1, bf16[524,4096]{1,0:T(8,128)(2,1)} %maximum_dynamic-update-slice_fusion), kind=kLoop, calls=%fused_computation.81 | loop fusion | flops 294912 | bytes 229472 | tf_op jit(solution)/shard_map/convert_element_type | solution.py:38
  66.5 7.2 %shard_map.122 = f32[12,768]{1,0:T(8,128)} custom-call(s32[8]{0:T(128)} %pad_add_fusion.2.order_ref, bf16[12,4096]{1,0:T(8,128)(2,1)} %fusion.70.x_ref, bf16[3,4096,256]{2,1,0:T(8,128)(2,1)} %bitcast.118), custom_call_target="tpu_custom_call" | custom-call | flops 75497472 | bytes 6426624 | tf_op jit(solution)/shard_map/pallas_call | solution.py:73
  73.7 0.8 broadcast_add_fusion.1
  75.0 2.3 %fusion.109 = (f32[4,2]{1,0:T(4,128)S(1)}, f32[4,2,1024]{2,1,0:T(2,128)S(1)}) fusion(bf16[8,2,1024,256]{3,2,1,0:T(8,128)(2,1)} %param.21, pred[256,2]{0,1:T(4,128)(4,1)S(1)} %bitcast.144, bf16[4,256]{1,0:T(4,128)(2,1)S(1)} %get-tuple-element.95, pred[4,1024]{1,0:T(4,128)(4,1)S(1)} %iota_compare_fusion.1), kind=kOutput, calls=%fused_computation.197 | convolution fusion | flops 4220920 | bytes 2136608 | tf_op jit(solution)/shard_map/rkf,rfh->rhk/dot_general | solution.py:146
  77.5 2.0 %fusion.8 = f32[4,2,256]{2,1,0:T(2,128)S(1)} fusion(bf16[8,2,1024,256]{3,2,1,0:T(8,128)(2,1)} %param.21, f32[4,2,1024]{2,1,0:T(2,128)S(1)} %get-tuple-element.91, pred[4,1024]{1,0:T(4,128)(4,1)S(1)} %iota_compare_fusion.1, f32[4,2]{1,0:T(4,128)S(1)} %get-tuple-element.90), kind=kOutput, calls=%fused_computation.14 | convolution fusion | flops 4218880 | bytes 2142240 | tf_op jit(solution)/shard_map/rhk,rkf->rhf/dot_general | solution.py:153
  79.5 2.3 %fusion.107 = (f32[4,2]{1,0:T(4,128)S(1)}, f32[4,2,1024]{2,1,0:T(2,128)S(1)}) fusion(bf16[8,2,1024,256]{3,2,1,0:T(8,128)(2,1)} %param.21, pred[256,2]{0,1:T(4,128)(4,1)S(1)} %bitcast.145, bf16[4,256]{1,0:T(4,128)(2,1)S(1)} %bitcast.143, pred[4,1024]{1,0:T(4,128)(4,1)S(1)} %iota_compare_fusion.2), kind=kOutput, calls=%fused_computation.195 | convolution fusion | flops 4220920 | bytes 2136608 | tf_op jit(solution)/shard_map/rkf,rfh->rhk/dot_general | solution.py:146
  81.8 2.0 %fusion.12 = f32[4,2,256]{2,1,0:T(2,128)S(1)} fusion(bf16[8,2,1024,256]{3,2,1,0:T(8,128)(2,1)} %param.21, f32[4,2,1024]{2,1,0:T(2,128)S(1)} %get-tuple-element.87, pred[4,1024]{1,0:T(4,128)(4,1)S(1)} %iota_compare_fusion.2, f32[4,2]{1,0:T(4,128)S(1)} %get-tuple-element.86), kind=kOutput, calls=%fused_computation.18 | convolution fusion | flops 4218880 | bytes 2142240 | tf_op jit(solution)/shard_map/rhk,rkf->rhf/dot_general | solution.py:153
  84.2 3.4 %fusion.3 = f32[512]{0:T(512)S(1)} fusion(f32[512]{0:T(512)S(1)} %broadcast_multiply_fusion, bf16[524,4096]{1,0:T(8,128)(2,1)} %maximum_dynamic-update-slice_fusion), kind=kLoop, calls=%fused_computation.7 | loop fusion | flops 8388096 | bytes 4198400 | tf_op jit(solution)/shard_map/reduce_sum | solution.py:37
  87.6 5.1 %fusion.6.x_ref = bf16[512,4096]{1,0:T(8,128)(2,1)} fusion(f32[4096]{0:T(1024)S(1)} %bitcast.131, f32[4096]{0:T(1024)S(1)} %bitcast.129, f32[512]{0:T(512)S(1)} %add_rsqrt_fusion, f32[512]{0:T(512)S(1)} %broadcast_multiply_fusion, bf16[524,4096]{1,0:T(8,128)(2,1)} %maximum_dynamic-update-slice_fusion), kind=kLoop, calls=%fused_computation.10 | loop fusion | flops 12582912 | bytes 8425472 | tf_op jit(solution)/shard_map/convert_element_type | solution.py:38
  92.9 0.3 fusion.108
  93.4 0.2 fusion.50
  94.0 19.4 %collective-permute-start.12 = (f32[4,2,130]{2,1,0:T(2,128)S(1)}, f32[4,2,130]{2,1,0:T(2,128)S(1)}, u32[]{:S(2)}, u32[]{:S(2)}) collective-permute-start(f32[4,2,130]{2,1,0:T(2,128)S(1)} %pad_maximum_fusion.3), channel_id=1, source_target_pairs={{0,8},{8,16},{16,24},{24,32},{32,40},{40,48},{48,56},{56,64},{64,7... | collective-permute-start | bytes 12488 | tf_op jit(solution)/shard_map/ppermute | solution.py:256
  113.7 0.2 collective-permute-start.11
  113.9 0.2 collective-permute-done.12
  114.4 2.5 %collective-permute-done.11 = f32[4,2,130]{2,1,0:T(2,128)S(1)} collective-permute-done((f32[4,2,130]{2,1,0:T(2,128)S(1)}, f32[4,2,130]{2,1,0:T(2,128)S(1)}, u32[]{:S(2)}, u32[]{:S(2)}) %collective-permute-start.11) | collective-permute-done | bytes 4192 | tf_op jit(solution)/shard_map/ppermute | solution.py:256
  117.3 10.4 %shard_map.123 = f32[512,768]{1,0:T(8,128)} custom-call(s32[8]{0:T(128)} %pad_add_fusion.2.order_ref, bf16[512,4096]{1,0:T(8,128)(2,1)} %fusion.6.x_ref, bf16[3,4096,256]{2,1,0:T(8,128)(2,1)} %bitcast.119), custom_call_target="tpu_custom_call" | custom-call | flops 3221225472 | bytes 12058624 | tf_op jit(solution)/shard_map/pallas_call | solution.py:73
  127.6 1.5 %broadcast_add_fusion = f32[512,768]{1,0:T(8,128)S(1)} fusion(f32[512,768]{1,0:T(8,128)} %shard_map.123, f32[768]{0:T(1024)S(1)} %add.183), kind=kLoop, calls=%fused_computation.42 | loop fusion | flops 393216 | bytes 3148800 | tf_op jit(solution)/shard_map/add | solution.py:98
  129.2 0.8 reshape.518
  130.0 0.4 fusion.103
  130.4 0.9 slice.253
  131.8 0.6 copy.213
  132.7 1.1 copy.195
  133.8 1.4 %subtract_convert_fusion.1 = (bf16[512,2,16]{2,0,1:T(8,128)(2,1)S(1)}, bf16[512,2,16]{2,0,1:T(8,128)(2,1)S(1)}, bf16[512,2,16]{2,0,1:T(8,128)(2,1)S(1)}, bf16[512,2,16]{2,0,1:T(8,128)(2,1)S(1)}) fusion(f32[512,2,128]{2,0,1:T(8,128)S(1)} %bitcast.123, f32[512,16]{1,0:T(8,128)} %copy.162, f32[512,16]{1,0:T(8,128)S(1)} %copy.161, f32[512,2,128]{2,0,1:T(8,128)S(1)} %bitcast.121), kind=kLoop, calls=%fused_computation.73 | loop fusion | flops 262144 | bytes 458752 | tf_op jit(solution)/shard_map/convert.9
  135.3 0.8 fusion.57
  136.1 2.3 %fusion.110 = (f32[2,512]{1,0:T(2,128)S(1)}, bf16[2,512,1024]{2,1,0:T(8,128)(2,1)S(1)}) fusion(f32[2,512,1024]{2,1,0:T(8,128)S(1)} %fusion.57, pred[512,1024]{1,0:T(8,128)(4,1)S(1)} %copy-done.2), kind=kOutput, calls=%fused_computation.198 | output fusion | flops 8389631 | bytes 6819840 | tf_op jit(solution)/shard_map/while/body/eval_jaxpr/sub | solution.py:111
  138.5 0.8 fusion.31
  139.3 0.8 copy.176
  (125 shorter events, 5.3 us)
Async XLA Ops:
  0.6 16.0 %copy-start.8 = (bf16[4,512]{1,0:T(4,128)(2,1)S(1)}, bf16[4,512]{1,0:T(4,128)(2,1)}, u32[]{:S(2)}) copy-start(bf16[4,512]{1,0:T(4,128)(2,1)} %param.12) | copy-start | bytes 12292
  0.6 11.8 %copy-start.5 = (s32[4,3]{1,0:T(4,128)S(1)}, s32[4,3]{1,0:T(4,128)}, u32[]{:S(2)}) copy-start(s32[4,3]{1,0:T(4,128)} %param.20) | copy-start | bytes 148
  0.7 11.9 %copy-start.9 = (f32[4096]{0:T(1024)S(1)}, f32[4096]{0:T(1024)}, u32[]{:S(2)}) copy-start(f32[4096]{0:T(1024)} %param.13) | copy-start | bytes 49156
  0.7 12.5 %copy-start.10 = (f32[4096]{0:T(1024)S(1)}, f32[4096]{0:T(1024)}, u32[]{:S(2)}) copy-start(f32[4096]{0:T(1024)} %param.14) | copy-start | bytes 49156
  0.7 13.1 %copy-start.11 = (f32[3,256]{1,0:T(4,128)S(1)}, f32[3,256]{1,0:T(4,128)}, u32[]{:S(2)}) copy-start(f32[3,256]{1,0:T(4,128)} %param.16) | copy-start | bytes 9220
  0.7 15.9 %copy-start.1 = (bf16[512,512]{1,0:T(8,128)(2,1)S(1)}, bf16[512,512]{1,0:T(8,128)(2,1)}, u32[]{:S(2)}) copy-start(bf16[512,512]{1,0:T(8,128)(2,1)} %param.11) | copy-start | bytes 1572868
  2.1 14.4 %collective-permute-start.1 = (f32[4,515]{1,0:T(4,128)S(1)}, f32[4,515]{1,0:T(4,128)S(1)}, u32[]{:S(2)}, u32[]{:S(2)}) collective-permute-start(f32[4,515]{1,0:T(4,128)S(1)} %pad_maximum_fusion.1), channel_id=1, source_target_pairs={{8,0},{16,8},{24,16},{32,24},{40,32},{48,40},{56,48},{64,56},{72,6... | collective-permute-start | bytes 24728 | tf_op jit(solution)/shard_map/ppermute | solution.py:206
  5.4 11.2 %collective-permute-start = (f32[4,515]{1,0:T(4,128)S(1)}, f32[4,515]{1,0:T(4,128)S(1)}, u32[]{:S(2)}, u32[]{:S(2)}) collective-permute-start(f32[4,515]{1,0:T(4,128)S(1)} %pad_maximum_fusion.1), channel_id=1, source_target_pairs={{0,8},{8,16},{16,24},{24,32},{32,40},{40,48},{48,56},{56,64},{64,7... | collective-permute-start | bytes 24728 | tf_op jit(solution)/shard_map/ppermute | solution.py:206
  17.6 10.5 %collective-permute-start.2 = (bf16[524,512]{1,0:T(8,128)(2,1)S(1)}, bf16[524,512]{1,0:T(8,128)(2,1)S(1)}, u32[]{:S(2)}, u32[]{:S(2)}) collective-permute-start(bf16[524,512]{1,0:T(8,128)(2,1)S(1)} %get-tuple-element.61), channel_id=1, source_target_pairs={{0,2},{2,4},{4,6},{6,0},{1,3},{3,5},{5,7},{7,1},{8,10},{10,12},{12... | collective-permute-start | bytes 1609736 | tf_op jit(solution)/shard_map/ppermute | solution.py:220
  18.7 9.4 %collective-permute-start.3 = (bf16[524,512]{1,0:T(8,128)(2,1)S(1)}, bf16[524,512]{1,0:T(8,128)(2,1)S(1)}, u32[]{:S(2)}, u32[]{:S(2)}) collective-permute-start(bf16[524,512]{1,0:T(8,128)(2,1)S(1)} %get-tuple-element.61), channel_id=1, source_target_pairs={{0,6},{2,0},{4,2},{6,4},{1,7},{3,1},{5,3},{7,5},{8,14},{10,8},{12,... | collective-permute-start | bytes 1609736 | tf_op jit(solution)/shard_map/ppermute | solution.py:221
  20.2 15.9 %collective-permute-start.6 = (bf16[524,512]{1,0:T(8,128)(2,1)S(1)}, bf16[524,512]{1,0:T(8,128)(2,1)S(1)}, u32[]{:S(2)}, u32[]{:S(2)}) collective-permute-start(bf16[524,512]{1,0:T(8,128)(2,1)S(1)} %get-tuple-element.61), channel_id=1, source_target_pairs={{0,1},{1,0},{2,3},{3,2},{4,5},{5,4},{6,7},{7,6},{8,9},{9,8},{10,11... | collective-permute-start | bytes 1609736 | tf_op jit(solution)/shard_map/ppermute | solution.py:227
  28.0 12.7 %collective-permute-start.4 = (bf16[262,512]{1,0:T(8,128)(2,1)S(1)}, bf16[262,512]{1,0:T(8,128)(2,1)S(1)}, u32[]{:S(2)}, u32[]{:S(2)}) collective-permute-start(bf16[262,512]{1,0:T(8,128)(2,1)S(1)} %slice.234), channel_id=1, source_target_pairs={{0,2},{2,4},{4,6},{6,0},{1,3},{3,5},{5,7},{7,1},{8,10},{10,12},{12... | collective-permute-start | bytes 804872 | tf_op jit(solution)/shard_map/ppermute | solution.py:223
  28.2 12.5 %collective-permute-start.5 = (bf16[262,512]{1,0:T(8,128)(2,1)S(1)}, bf16[262,512]{1,0:T(8,128)(2,1)S(1)}, u32[]{:S(2)}, u32[]{:S(2)}) collective-permute-start(bf16[262,512]{1,0:T(8,128)(2,1)S(1)} %slice.235), channel_id=1, source_target_pairs={{0,6},{2,0},{4,2},{6,4},{1,7},{3,1},{5,3},{7,5},{8,14},{10,8},{12,... | collective-permute-start | bytes 804872 | tf_op jit(solution)/shard_map/ppermute | solution.py:223
  36.2 16.0 %collective-permute-start.7 = (bf16[524,512]{1,0:T(8,128)(2,1)S(1)}, bf16[524,512]{1,0:T(8,128)(2,1)S(1)}, u32[]{:S(2)}, u32[]{:S(2)}) collective-permute-start(bf16[524,512]{1,0:T(8,128)(2,1)S(1)} %collective-permute-done.6), channel_id=1, source_target_pairs={{0,2},{2,4},{4,6},{6,0},{1,3},{3,5},{5,7},{7,1},{8,10},{10,12},{12... | collective-permute-start | bytes 1609736 | tf_op jit(solution)/shard_map/ppermute | solution.py:220
  36.2 13.4 %collective-permute-start.8 = (bf16[524,512]{1,0:T(8,128)(2,1)S(1)}, bf16[524,512]{1,0:T(8,128)(2,1)S(1)}, u32[]{:S(2)}, u32[]{:S(2)}) collective-permute-start(bf16[524,512]{1,0:T(8,128)(2,1)S(1)} %collective-permute-done.6), channel_id=1, source_target_pairs={{0,6},{2,0},{4,2},{6,4},{1,7},{3,1},{5,3},{7,5},{8,14},{10,8},{12,... | collective-permute-start | bytes 1609736 | tf_op jit(solution)/shard_map/ppermute | solution.py:221
  49.7 6.3 %collective-permute-start.10 = (bf16[262,512]{1,0:T(8,128)(2,1)S(1)}, bf16[262,512]{1,0:T(8,128)(2,1)S(1)}, u32[]{:S(2)}, u32[]{:S(2)}) collective-permute-start(bf16[262,512]{1,0:T(8,128)(2,1)S(1)} %slice.237), channel_id=1, source_target_pairs={{0,6},{2,0},{4,2},{6,4},{1,7},{3,1},{5,3},{7,5},{8,14},{10,8},{12,... | collective-permute-start | bytes 804872 | tf_op jit(solution)/shard_map/ppermute | solution.py:223
  52.2 6.8 %collective-permute-start.9 = (bf16[262,512]{1,0:T(8,128)(2,1)S(1)}, bf16[262,512]{1,0:T(8,128)(2,1)S(1)}, u32[]{:S(2)}, u32[]{:S(2)}) collective-permute-start(bf16[262,512]{1,0:T(8,128)(2,1)S(1)} %slice.236), channel_id=1, source_target_pairs={{0,2},{2,4},{4,6},{6,0},{1,3},{3,5},{5,7},{7,1},{8,10},{10,12},{12... | collective-permute-start | bytes 804872 | tf_op jit(solution)/shard_map/ppermute | solution.py:223
  87.6 5.3 %copy-start.3 = (bf16[4,256,256]{2,1,0:T(8,128)(2,1)S(1)}, bf16[4,256,256]{2,1,0:T(8,128)(2,1)}, u32[]{:S(2)}) copy-start(bf16[4,256,256]{2,1,0:T(8,128)(2,1)} %get-tuple-element.59) | copy-start | bytes 1572868
  94.0 20.2 %collective-permute-start.12 = (f32[4,2,130]{2,1,0:T(2,128)S(1)}, f32[4,2,130]{2,1,0:T(2,128)S(1)}, u32[]{:S(2)}, u32[]{:S(2)}) collective-permute-start(f32[4,2,130]{2,1,0:T(2,128)S(1)} %pad_maximum_fusion.3), channel_id=1, source_target_pairs={{0,8},{8,16},{16,24},{24,32},{32,40},{40,48},{48,56},{56,64},{64,7... | collective-permute-start | bytes 12488 | tf_op jit(solution)/shard_map/ppermute | solution.py:256
  113.7 3.3 %collective-permute-start.11 = (f32[4,2,130]{2,1,0:T(2,128)S(1)}, f32[4,2,130]{2,1,0:T(2,128)S(1)}, u32[]{:S(2)}, u32[]{:S(2)}) collective-permute-start(f32[4,2,130]{2,1,0:T(2,128)S(1)} %pad_maximum_fusion.2), channel_id=1, source_target_pairs={{8,0},{16,8},{24,16},{32,24},{40,32},{48,40},{56,48},{64,56},{72,6... | collective-permute-start | bytes 12488 | tf_op jit(solution)/shard_map/ppermute | solution.py:256
  114.2 13.5 %copy-start.6 = (f32[4,2,130]{2,1,0:T(2,128)}, f32[4,2,130]{2,1,0:T(2,128)S(1)}, u32[]{:S(2)}) copy-start(f32[4,2,130]{2,1,0:T(2,128)S(1)} %collective-permute-done.12) | copy-start | bytes 12484
  117.0 10.6 %copy-start.7 = (f32[4,2,130]{2,1,0:T(2,128)}, f32[4,2,130]{2,1,0:T(2,128)S(1)}, u32[]{:S(2)}) copy-start(f32[4,2,130]{2,1,0:T(2,128)S(1)} %collective-permute-done.11) | copy-start | bytes 12484
  129.1 2.5 %slice-start = ((f32[4,2,130]{2,1,0:T(2,128)}), f32[4,2,128]{2,1,0:T(2,128)S(1)}, s32[]{:S(2)}) async-start(f32[4,2,130]{2,1,0:T(2,128)} %copy-done.6), calls=%async_computation | async-start | bytes 8192 | tf_op jit(solution)/shard_map/slice | solution.py:257
  129.2 2.5 %slice-start.1 = ((f32[4,2,130]{2,1,0:T(2,128)}), f32[4,2,128]{2,1,0:T(2,128)S(1)}, s32[]{:S(2)}) async-start(f32[4,2,130]{2,1,0:T(2,128)} %copy-done.7), calls=%async_computation.1 | async-start | bytes 8192 | tf_op jit(solution)/shard_map/slice | solution.py:257
  131.3 4.0 %copy-start = (bf16[512,2,128]{2,0,1:T(8,128)(2,1)S(1)}, bf16[512,2,128]{2,0,1:T(8,128)(2,1)}, u32[]{:S(2)}) copy-start(bf16[512,2,128]{2,0,1:T(8,128)(2,1)} %copy.165) | copy-start | bytes 786436
  133.8 2.3 %copy-start.2 = (pred[512,1024]{1,0:T(8,128)(4,1)S(1)}, pred[512,1024]{1,0:T(8,128)(4,1)}, u32[]{:S(2)}) copy-start(pred[512,1024]{1,0:T(8,128)(4,1)} %pad_add_fusion) | copy-start | bytes 1572868
  136.1 2.4 %copy-start.4 = (bf16[1,1,512,256]{2,3,1,0:T(8,128)(2,1)S(1)}, bf16[1,1,512,256]{2,3,1,0:T(8,128)(2,1)}, u32[]{:S(2)}) copy-start(bf16[1,1,512,256]{2,3,1,0:T(8,128)(2,1)} %copy.137) | copy-start | bytes 786436

commit v9 on v6

--- a/solution.py
+++ b/solution.py
@@ -53,48 +53,62 @@
     )
 
 
-def qkv_kernel(order_ref, x_ref, w_ref, o_ref):
-    @pl.when(pl.program_id(0) == 0)
-    def _():
-        o_ref[...] = jnp.zeros_like(o_ref)
-
-    width = w_ref.shape[2]
-    for c in range(w_ref.shape[0]):
-        o_ref[:, c * width : (c + 1) * width] += jnp.dot(
-            x_ref[...], w_ref[c], preferred_element_type=jnp.float32
-        )
-
-
-def qkv_matmul(normed, weight, order):
-    rows, depth = normed.shape
+def qkv_kernel(order_ref, x_ref, gain_ref, shift_ref, w_ref, o_ref):
+    rows = x_ref[...].astype(jnp.float32)
+    middle = jnp.mean(rows, axis=-1, keepdims=True)
+    centred = rows - middle
+    spread = jnp.mean(centred * centred, axis=-1, keepdims=True)
+    normed = (centred * lax.rsqrt(spread + EPS) * gain_ref[...] + shift_ref[...]).astype(
+        jnp.bfloat16
+    )
+    parts, depth, width = w_ref.shape
+    blocks = order_ref.shape[0]
+    size = depth // blocks
+    for c in range(parts):
+        total = jnp.zeros((rows.shape[0], width), jnp.float32)
+        for j in range(blocks):
+            start = pl.multiple_of(order_ref[j] * size, size)
+            total += jnp.dot(
+                normed[:, j * size : (j + 1) * size],
+                w_ref[c, pl.ds(start, size), :],
+                preferred_element_type=jnp.float32,
+            )
+        o_ref[:, c * width : (c + 1) * width] = total
+
+
+def qkv_matmul(whole, gain, shift, weight, order):
+    rows, depth = whole.shape
     parts, _, width = weight.shape
-    blocks = order.shape[0]
-    size = depth // blocks
+    chunk = 128 if rows % 128 == 0 else rows
     return pl.pallas_call(
         qkv_kernel,
         out_shape=jax.ShapeDtypeStruct((rows, parts * width), jnp.float32),
         grid_spec=pltpu.PrefetchScalarGridSpec(
             num_scalar_prefetch=1,
-            grid=(blocks,),
+            grid=(rows // chunk,),
             in_specs=[
-                pl.BlockSpec((rows, size), lambda j, order: (0, j)),
-                pl.BlockSpec((parts, size, width), lambda j, order: (0, order[j], 0)),
+                pl.BlockSpec((chunk, depth), lambda i, order: (i, 0)),
+                pl.BlockSpec((1, depth), lambda i, order: (0, 0)),
+                pl.BlockSpec((1, depth), lambda i, order: (0, 0)),
+                pl.BlockSpec((parts, depth, width), lambda i, order: (0, 0, 0)),
             ],
-            out_specs=pl.BlockSpec((rows, parts * width), lambda j, order: (0, 0)),
+            out_specs=pl.BlockSpec((chunk, parts * width), lambda i, order: (i, 0)),
         ),
-        compiler_params=pltpu.CompilerParams(dimension_semantics=("arbitrary",)),
+        compiler_params=pltpu.CompilerParams(
+            dimension_semantics=("arbitrary",), vmem_limit_bytes=48 * 1024 * 1024
+        ),
         cost_estimate=pl.CostEstimate(
             flops=2 * rows * depth * parts * width,
             bytes_accessed=2 * rows * depth + 2 * depth * parts * width + 4 * rows * parts * width,
-            transcendentals=0,
+            transcendentals=rows,
         ),
-    )(order, normed, weight)
-
-
-def project(normed, weight, bias, positions, order):
-    count = normed.shape[0]
+    )(order, whole, gain.reshape(1, depth), shift.reshape(1, depth), weight)
+
+
+def project(whole, gain, shift, weight, bias, positions, order):
+    count = whole.shape[0]
     width = weight.shape[2]
-    mixed = qkv_matmul(normed, weight, order)
+    mixed = qkv_matmul(whole, gain, shift, weight, order)
     mixed = (mixed + bias.reshape(1, 3 * width)).reshape(count, 3, width // HD, HD)
     query = rotate(mixed[:, 0], positions).astype(jnp.bfloat16)
     fresh_key = rotate(mixed[:, 1], positions).astype(jnp.bfloat16)
@@ -224,7 +238,9 @@
     gain, shift = feature_order(ln_gain), feature_order(ln_bias)
     weight = jnp.transpose(qkv_weight, (1, 0, 2))
     own_query, new_key, new_value = project(
-        layer_norm(whole[count:], gain, shift),
+        whole[count:],
+        gain,
+        shift,
         weight,
         qkv_bias,
         piece_len[:, 0] + piece_len[:, 1] + piece_len[:, 2],
@@ -255,7 +271,9 @@
     right_parts = answer(piece_batch(prev_query, side_store[:requests], prev_len), backward)
     left_parts = answer(piece_batch(next_query, side_store[requests:], next_len), forward)
     query, fresh_key, fresh_value = project(
-        layer_norm(whole[:count], gain, shift),
+        whole[:count],
+        gain,
+        shift,
         weight,
         qkv_bias,
         prefill_offset[0] + jnp.arange(count, dtype=jnp.int32),

time: 134 us -> 116 us (0.87)
  other arithmetic: 30.7 us -> 13.8 us
  local copies, waits for them, and re-layouts: 26.3 us -> 29.9 us
  Pallas kernels: 17.5 us -> 14 us
    reduce_sum x4 -> x0, other arithmetic: 8.27 us -> none  [the longest x2 4.47 us: layer_norm(): spread = jnp.mean(centred * centred, axis=-1, keepdims=True)]
    convert_element_type x2 -> x0, other arithmetic: 6.58 us -> none  [layer_norm(): (centred * lax.rsqrt(spread + EPS) * gain + shift).astype(jnp.bfloat16)]
    slice x0 -> x2, local copies, waits for them, and re-layouts: none -> 3.53 us  [the longest x1 2.68 us: local(): whole[:count]]
    pallas_call x2, Pallas kernels: 17.5 us -> 14 us  [qkv_matmul(): pl.pallas_call(qkv_kernel, out_shape=jax.ShapeDtypeStruct((rows, parts *...]
    add x2, other arithmetic: 2.24 us -> 0.11 us  [project(): mixed + bias.reshape(1, 3 * width)]
    unnamed x41 -> x43, local copies, waits for them, and re-layouts: 11.5 us -> 11.6 us
  transfers between devices with their start and end apart: 13 -> 13, of which waited for: 4 -> 4; matrix products, arithmetic and copies ran while one was open for 28% -> 32% of each run, Pallas kernels for 0% -> 0%
where the time goes in v9:
time: 116 us
  starting transfers between devices  34.6 us (30%)
  local copies, waits for them, and re-layouts  29.9 us (26%)
  Pallas kernels  14 us (12%)
  other arithmetic  13.8 us (12%)
  matrix products  10.9 us (9%)
  waiting for transfers between devices  10.8 us (9%)
  between operations  1.77 us (2%)
    ppermute x2, starting transfers between devices, ask(): got = lax.ppermute(packed, 'group', pairs)  15.1 us
    pallas_call x2, Pallas kernels, qkv_matmul(): pl.pallas_call(qkv_kernel, out_shape=jax.ShapeDtypeStruct((rows, parts *...  14 us
    unnamed x43, local copies, waits for them, and re-layouts  11.6 us
    ppermute x1, starting transfers between devices, local(): partner = lax.ppermute(rows, 'tz', [(0, 1), (1, 0)])  6.91 us
    dot_general x3, matrix products, piece_rows(): jnp.einsum('rkf,rfh->rhk', keys, spread, preferred_element_type=jnp.float32)  4.99 us
    ppermute x2, starting transfers between devices, around(): lax.ppermute(above[half:], 'ty', down)  4.82 us
    dot_general x3, matrix products, piece_rows(): jnp.einsum('rhk,rkf->rhf', weights.astype(jnp.bfloat16), values, preferre...  4.3 us
    ppermute x1, waiting for transfers between devices, local(): partner = lax.ppermute(rows, 'tz', [(0, 1), (1, 0)])  4 us
  transfers between devices with their start and end apart: 13, of which 4 were waited for; matrix products, arithmetic and copies ran while one was open for 32% of the time, Pallas kernels for 0%

profile of v9, /device:TPU:1, one launch (start us, length us, event | category | flops | bytes accessed | tf_op | source)
XLA Modules:
  0.0 115.8 jit_solution(6792170263429835710)
XLA Ops:
  0.7 2.0 %constant_dynamic-update-slice_fusion.1 = (bf16[516,512]{1,0:T(8,128)(2,1)S(1)}, bf16[516,4096]{1,0:T(8,128)(2,1)}) fusion(bf16[512,512]{1,0:T(8,128)(2,1)} %param.11), kind=kLoop, calls=%fused_computation.78 | loop fusion | bytes 1572864
  2.7 1.3 %constant_dynamic-update-slice_fusion = (bf16[516,512]{1,0:T(8,128)(2,1)S(1)}, bf16[516,4096]{1,0:T(8,128)(2,1)}) fusion(bf16[516,512]{1,0:T(8,128)(2,1)S(1)} %get-tuple-element.51, bf16[4,512]{1,0:T(4,128)(2,1)} %param.12, bf16[516,4096]{1,0:T(8,128)(2,1)} %get-tuple-element.52), kind=kLoop, calls=%fused_computation.77 | loop fusion | bytes 12288 | tf_op jit(solution)/shard_map/concatenate | solution.py:213
  4.0 2.1 %collective-permute-start = (bf16[516,512]{1,0:T(8,128)(2,1)S(1)}, bf16[516,512]{1,0:T(8,128)(2,1)S(1)}, u32[]{:S(2)}, u32[]{:S(2)}) collective-permute-start(bf16[516,512]{1,0:T(8,128)(2,1)S(1)} %get-tuple-element.65), channel_id=1, source_target_pairs={{0,2},{2,4},{4,6},{6,0},{1,3},{3,5},{5,7},{7,1},{8,10},{10,12},{12... | collective-permute-start | bytes 1585160 | tf_op jit(solution)/shard_map/ppermute | solution.py:222
  6.1 1.4 %collective-permute-start.1 = (bf16[516,512]{1,0:T(8,128)(2,1)S(1)}, bf16[516,512]{1,0:T(8,128)(2,1)S(1)}, u32[]{:S(2)}, u32[]{:S(2)}) collective-permute-start(bf16[516,512]{1,0:T(8,128)(2,1)S(1)} %get-tuple-element.65), channel_id=1, source_target_pairs={{0,6},{2,0},{4,2},{6,4},{1,7},{3,1},{5,3},{7,5},{8,14},{10,8},{12,... | collective-permute-start | bytes 1585160 | tf_op jit(solution)/shard_map/ppermute | solution.py:223
  7.5 6.9 %collective-permute-start.4 = (bf16[516,512]{1,0:T(8,128)(2,1)S(1)}, bf16[516,512]{1,0:T(8,128)(2,1)}, u32[]{:S(2)}, u32[]{:S(2)}) collective-permute-start(bf16[516,512]{1,0:T(8,128)(2,1)S(1)} %get-tuple-element.65), channel_id=1, source_target_pairs={{0,1},{1,0},{2,3},{3,2},{4,5},{5,4},{6,7},{7,6},{8,9},{9,8},{10,11... | collective-permute-start | bytes 1585160 | tf_op jit(solution)/shard_map/ppermute | solution.py:229
  14.5 1.0 convert_reduce_fusion
  15.4 1.6 %slice_reduce_fusion = (s32[4]{0:T(128)S(1)}, f32[4,1]{1,0:T(4,128)}, f32[4,1]{1,0:T(4,128)}) fusion(s32[4,3]{1,0:T(4,128)} %param.20), kind=kLoop, calls=%fused_computation.141 | loop fusion | flops 8 | bytes 96 | tf_op jit(solution)/shard_map/slice | solution.py:246
  17.1 0.6 iota_compare_fusion.3
  17.8 0.6 broadcast_bitcast_fusion
  19.2 0.7 multiply_cosine_fusion.1
  19.8 0.2 multiply_cosine_fusion
  20.0 1.1 fusion.103
  21.2 1.0 pad_add_fusion
  22.3 1.1 slice_bitcast_fusion.1
  23.4 4.0 %collective-permute-done.4 = bf16[516,512]{1,0:T(8,128)(2,1)} collective-permute-done((bf16[516,512]{1,0:T(8,128)(2,1)S(1)}, bf16[516,512]{1,0:T(8,128)(2,1)}, u32[]{:S(2)}, u32[]{:S(2)}) %collective-permute-start.4) | collective-permute-done | bytes 528416 | tf_op jit(solution)/shard_map/ppermute | solution.py:229
  27.4 0.5 collective-permute-start.5
  27.9 2.2 %collective-permute-start.6 = (bf16[516,512]{1,0:T(8,128)(2,1)}, bf16[516,512]{1,0:T(8,128)(2,1)S(1)}, u32[]{:S(2)}, u32[]{:S(2)}) collective-permute-start(bf16[516,512]{1,0:T(8,128)(2,1)} %collective-permute-done.4), channel_id=1, source_target_pairs={{0,6},{2,0},{4,2},{6,4},{1,7},{3,1},{5,3},{7,5},{8,14},{10,8},{12,... | collective-permute-start | bytes 1585160 | tf_op jit(solution)/shard_map/ppermute | solution.py:223
  30.1 0.7 slice.202
  30.8 0.8 slice.203
  31.6 2.7 %collective-permute-start.3 = (bf16[258,512]{1,0:T(8,128)(2,1)}, bf16[258,512]{1,0:T(8,128)(2,1)}, u32[]{:S(2)}, u32[]{:S(2)}) collective-permute-start(bf16[258,512]{1,0:T(8,128)(2,1)} %slice.203), channel_id=1, source_target_pairs={{0,6},{2,0},{4,2},{6,4},{1,7},{3,1},{5,3},{7,5},{8,14},{10,8},{12,... | collective-permute-start | bytes 792584 | tf_op jit(solution)/shard_map/ppermute | solution.py:225
  34.4 0.6 gather_fusion
  35.0 0.6 gather_fusion.1
  35.6 0.7 add.144
  36.3 0.7 copy.270
  37.1 0.8 copy.211
  38.1 0.8 copy.214
  38.9 0.8 copy.207
  39.7 0.6 concatenate.139
  40.4 0.9 constant_dynamic-update-slice_fusion.6
  41.3 0.9 constant_dynamic-update-slice_fusion.5
  42.1 3.6 %collective-permute-done.2 = bf16[258,512]{1,0:T(8,128)(2,1)} collective-permute-done((bf16[258,512]{1,0:T(8,128)(2,1)}, bf16[258,512]{1,0:T(8,128)(2,1)}, u32[]{:S(2)}, u32[]{:S(2)}) %collective-permute-start.2) | collective-permute-done | bytes 264224 | tf_op jit(solution)/shard_map/ppermute | solution.py:225
  45.8 2.0 %maximum_dynamic-update-slice_fusion.1 = bf16[516,4096]{1,0:T(8,128)(2,1)} fusion(bf16[516,4096]{1,0:T(8,128)(2,1)} %constant_dynamic-update-slice_fusion.5, bf16[258,512]{1,0:T(8,128)(2,1)} %collective-permute-done.3, bf16[258,512]{1,0:T(8,128)(2,1)} %collective-permute-done.2), kind=kLoop, calls=%fused_computation.43 | loop fusion | flops 1056768 | bytes 1073152
  47.7 0.9 collective-permute-start.7
  48.7 2.1 %collective-permute-start.8 = (bf16[258,512]{1,0:T(8,128)(2,1)S(1)}, bf16[258,512]{1,0:T(8,128)(2,1)S(1)}, u32[]{:S(2)}, u32[]{:S(2)}) collective-permute-start(bf16[258,512]{1,0:T(8,128)(2,1)S(1)} %slice.205), channel_id=1, source_target_pairs={{0,6},{2,0},{4,2},{6,4},{1,7},{3,1},{5,3},{7,5},{8,14},{10,8},{12,... | collective-permute-start | bytes 792584 | tf_op jit(solution)/shard_map/ppermute | solution.py:225
  50.8 1.9 %constant_dynamic-update-slice_fusion.4 = bf16[516,4096]{1,0:T(8,128)(2,1)} fusion(bf16[516,4096]{1,0:T(8,128)(2,1)} %maximum_dynamic-update-slice_fusion.1, bf16[516,512]{1,0:T(8,128)(2,1)} %collective-permute-done.4), kind=kLoop, calls=%fused_computation.81 | loop fusion | bytes 1064960
  52.8 0.9 constant_dynamic-update-slice_fusion.3
  53.7 0.9 constant_dynamic-update-slice_fusion.2
  54.7 0.9 maximum_dynamic-update-slice_fusion
  55.6 0.8 slice.216.x_ref
  56.4 4.4 %shard_map.123 = f32[4,768]{1,0:T(4,128)S(1)} custom-call(s32[8]{0:T(128)S(1)} %pad_add_fusion.1.order_ref, bf16[4,4096]{1,0:T(4,128)(2,1)S(1)} %slice.216.x_ref, f32[1,4096]{1,0:T(1,128)S(1)} %bitcast.135, f32[1,4096]{1,0:T(1,128)S(1)} %bitcast.137, bf16[3,4096,256]{2,1,0:T(8,128)(2,1)} %bitcast.139), custom_call_target="tpu_custom_call" | custom-call | flops 25165824 | bytes 6336512 | tf_op jit(solution)/shard_map/pallas_call | solution.py:83
  61.0 2.7 %slice.206.x_ref = bf16[512,4096]{1,0:T(8,128)(2,1)S(1)} slice(bf16[516,4096]{1,0:T(8,128)(2,1)} %maximum_dynamic-update-slice_fusion), slice={[0:512], [0:4096]} | slice | bytes 8388608 | tf_op jit(solution)/shard_map/slice | solution.py:274
  63.7 9.5 %shard_map.122 = f32[512,768]{1,0:T(8,128)S(1)} custom-call(s32[8]{0:T(128)S(1)} %pad_add_fusion.1.order_ref, bf16[512,4096]{1,0:T(8,128)(2,1)S(1)} %slice.206.x_ref, f32[1,4096]{1,0:T(1,128)S(1)} %bitcast.136, f32[1,4096]{1,0:T(1,128)S(1)} %bitcast.138, bf16[3,4096,256]{2,1,0:T(8,128)(2,1)} %bitcast.140), custom_call_target="tpu_custom_call" | custom-call | flops 3221225472 | bytes 12058624 | tf_op jit(solution)/shard_map/pallas_call | solution.py:83
  73.4 0.8 reshape.539
  74.2 0.4 fusion.102
  74.6 0.9 slice.207
  75.8 4.4 %collective-permute-start.9 = (f32[4,257]{1,0:T(4,128)S(1)}, f32[4,257]{1,0:T(4,128)S(1)}, u32[]{:S(2)}, u32[]{:S(2)}) collective-permute-start(f32[4,257]{1,0:T(4,128)S(1)} %get-tuple-element.63), channel_id=1, source_target_pairs={{8,0},{16,8},{24,16},{32,24},{40,32},{48,40},{56,48},{64,56},{72,6... | collective-permute-start | bytes 12344 | tf_op jit(solution)/shard_map/ppermute | solution.py:260
  80.2 10.7 %collective-permute-start.11 = (f32[4,257]{1,0:T(4,128)S(1)}, f32[4,257]{1,0:T(4,128)S(1)}, u32[]{:S(2)}, u32[]{:S(2)}) collective-permute-start(f32[4,257]{1,0:T(4,128)S(1)} %get-tuple-element.64), channel_id=1, source_target_pairs={{0,8},{8,16},{16,24},{24,32},{32,40},{40,48},{48,56},{56,64},{64,7... | collective-permute-start | bytes 12344 | tf_op jit(solution)/shard_map/ppermute | solution.py:260
  91.3 1.1 copy.263
  92.4 1.4 %subtract_convert_fusion.1 = (bf16[512,2,16]{2,0,1:T(8,128)(2,1)S(1)}, bf16[512,2,16]{2,0,1:T(8,128)(2,1)S(1)}, bf16[512,2,16]{2,0,1:T(8,128)(2,1)S(1)}, bf16[512,2,16]{2,0,1:T(8,128)(2,1)S(1)}) fusion(f32[512,2,128]{2,0,1:T(8,128)S(1)} %get-tuple-element.84, f32[512,16]{1,0:T(8,128)} %copy.211, f32[512,16]{1,0:T(8,128)S(1)} %copy.210, ...), kind=kLoop, calls=%fused_computation.64 | loop fusion | flops 262144 | bytes 458752 | tf_op jit(solution)/shard_map/convert.21
  93.9 0.8 fusion.51
  94.7 2.3 %fusion.104 = (f32[2,512]{1,0:T(2,128)S(1)}, bf16[2,512,1024]{2,1,0:T(8,128)(2,1)S(1)}) fusion(f32[2,512,1024]{2,1,0:T(8,128)S(1)} %fusion.51, pred[512,1024]{1,0:T(8,128)(4,1)S(1)} %copy-done.2), kind=kOutput, calls=%fused_computation.180 | output fusion | flops 8389631 | bytes 6819840 | tf_op jit(solution)/shard_map/while/body/eval_jaxpr/sub | solution.py:125
  97.2 0.8 fusion.25
  98.1 0.3 fusion.107
  98.5 0.2 fusion.44
  99.0 2.3 %fusion.106 = (f32[4,2]{1,0:T(4,128)S(1)}, f32[4,2,1024]{2,1,0:T(2,128)S(1)}) fusion(bf16[8,2,1024,256]{3,2,1,0:T(8,128)(2,1)} %param.21, pred[256,2]{0,1:T(4,128)(4,1)S(1)} %bitcast.157, bf16[4,256]{1,0:T(4,128)(2,1)S(1)} %slice.327, pred[4,1024]{1,0:T(4,128)(4,1)S(1)} %iota_compare_fusion.2), kind=kOutput, calls=%fused_computation.182 | convolution fusion | flops 4220920 | bytes 2136608 | tf_op jit(solution)/shard_map/rkf,rfh->rhk/dot_general | solution.py:160
  101.3 2.0 %fusion.6 = f32[4,2,256]{2,1,0:T(2,128)S(1)} fusion(bf16[8,2,1024,256]{3,2,1,0:T(8,128)(2,1)} %param.21, f32[4,2,1024]{2,1,0:T(2,128)S(1)} %get-tuple-element.80, pred[4,1024]{1,0:T(4,128)(4,1)S(1)} %iota_compare_fusion.2, f32[4,2]{1,0:T(4,128)S(1)} %get-tuple-element.79), kind=kOutput, calls=%fused_computation.10 | convolution fusion | flops 4218880 | bytes 2142240 | tf_op jit(solution)/shard_map/rhk,rkf->rhf/dot_general | solution.py:167
  103.8 2.3 %fusion.105 = (f32[4,2]{1,0:T(4,128)S(1)}, f32[4,2,1024]{2,1,0:T(2,128)S(1)}) fusion(bf16[8,2,1024,256]{3,2,1,0:T(8,128)(2,1)} %param.21, pred[256,2]{0,1:T(4,128)(4,1)S(1)} %bitcast.158, bf16[4,256]{1,0:T(4,128)(2,1)S(1)} %slice.325, pred[4,1024]{1,0:T(4,128)(4,1)S(1)} %iota_compare_fusion.1), kind=kOutput, calls=%fused_computation.181 | convolution fusion | flops 4220920 | bytes 2136608 | tf_op jit(solution)/shard_map/rkf,rfh->rhk/dot_general | solution.py:160
  106.1 2.0 %fusion.2 = f32[4,2,256]{2,1,0:T(2,128)S(1)} fusion(bf16[8,2,1024,256]{3,2,1,0:T(8,128)(2,1)} %param.21, f32[4,2,1024]{2,1,0:T(2,128)S(1)} %get-tuple-element.78, pred[4,1024]{1,0:T(4,128)(4,1)S(1)} %iota_compare_fusion.1, f32[4,2]{1,0:T(4,128)S(1)} %get-tuple-element.77), kind=kOutput, calls=%fused_computation.6 | convolution fusion | flops 4218880 | bytes 2142240 | tf_op jit(solution)/shard_map/rhk,rkf->rhf/dot_general | solution.py:167
  108.9 0.3 collective-permute-start.10
  109.5 0.4 collective-permute-start.12
  110.3 0.8 copy.247
  111.1 0.5 collective-permute-done.10
  111.7 2.6 %collective-permute-done.12 = f32[4,2,130]{0,1,2:T(2,128)S(1)} collective-permute-done((f32[4,2,130]{0,1,2:T(2,128)S(1)}, f32[4,2,130]{0,1,2:T(2,128)S(1)}, u32[]{:S(2)}, u32[]{:S(2)}) %collective-permute-start.12) | collective-permute-done | bytes 4192 | tf_op jit(solution)/shard_map/ppermute | solution.py:266
  115.1 0.7 copy.246
  (109 shorter events, 5.0 us)
Async XLA Ops:
  0.6 21.7 %copy-start.1 = (bf16[4,2,256,256]{3,2,1,0:T(8,128)(2,1)S(1)}, bf16[4,2,256,256]{3,2,1,0:T(8,128)(2,1)}, u32[]{:S(2)}) copy-start(bf16[4,2,256,256]{3,2,1,0:T(8,128)(2,1)} %param.19) | copy-start | bytes 3145732
  0.6 33.7 %copy-start.6 = (f32[4096]{0:T(1024)S(1)}, f32[4096]{0:T(1024)}, u32[]{:S(2)}) copy-start(f32[4096]{0:T(1024)} %param.13) | copy-start | bytes 49156
  0.7 34.3 %copy-start.7 = (f32[4096]{0:T(1024)S(1)}, f32[4096]{0:T(1024)}, u32[]{:S(2)}) copy-start(f32[4096]{0:T(1024)} %param.14) | copy-start | bytes 49156
  4.0 26.1 %collective-permute-start = (bf16[516,512]{1,0:T(8,128)(2,1)S(1)}, bf16[516,512]{1,0:T(8,128)(2,1)S(1)}, u32[]{:S(2)}, u32[]{:S(2)}) collective-permute-start(bf16[516,512]{1,0:T(8,128)(2,1)S(1)} %get-tuple-element.65), channel_id=1, source_target_pairs={{0,2},{2,4},{4,6},{6,0},{1,3},{3,5},{5,7},{7,1},{8,10},{10,12},{12... | collective-permute-start | bytes 1585160 | tf_op jit(solution)/shard_map/ppermute | solution.py:222
  6.1 24.7 %collective-permute-start.1 = (bf16[516,512]{1,0:T(8,128)(2,1)S(1)}, bf16[516,512]{1,0:T(8,128)(2,1)S(1)}, u32[]{:S(2)}, u32[]{:S(2)}) collective-permute-start(bf16[516,512]{1,0:T(8,128)(2,1)S(1)} %get-tuple-element.65), channel_id=1, source_target_pairs={{0,6},{2,0},{4,2},{6,4},{1,7},{3,1},{5,3},{7,5},{8,14},{10,8},{12,... | collective-permute-start | bytes 1585160 | tf_op jit(solution)/shard_map/ppermute | solution.py:223
  7.5 19.9 %collective-permute-start.4 = (bf16[516,512]{1,0:T(8,128)(2,1)S(1)}, bf16[516,512]{1,0:T(8,128)(2,1)}, u32[]{:S(2)}, u32[]{:S(2)}) collective-permute-start(bf16[516,512]{1,0:T(8,128)(2,1)S(1)} %get-tuple-element.65), channel_id=1, source_target_pairs={{0,1},{1,0},{2,3},{3,2},{4,5},{5,4},{6,7},{7,6},{8,9},{9,8},{10,11... | collective-permute-start | bytes 1585160 | tf_op jit(solution)/shard_map/ppermute | solution.py:229
  17.0 2.1 %copy-start.11 = (pred[2,2]{1,0:T(4,128)(4,1)}, pred[2,2]{1,0:T(4,128)(4,1)S(1)}, u32[]{:S(2)}) copy-start(pred[2,2]{1,0:T(4,128)(4,1)S(1)} %iota_compare_fusion.5) | copy-start | bytes 16
  27.4 20.3 %collective-permute-start.5 = (bf16[516,512]{1,0:T(8,128)(2,1)}, bf16[516,512]{1,0:T(8,128)(2,1)S(1)}, u32[]{:S(2)}, u32[]{:S(2)}) collective-permute-start(bf16[516,512]{1,0:T(8,128)(2,1)} %collective-permute-done.4), channel_id=1, source_target_pairs={{0,2},{2,4},{4,6},{6,0},{1,3},{3,5},{5,7},{7,1},{8,10},{10,12},{12... | collective-permute-start | bytes 1585160 | tf_op jit(solution)/shard_map/ppermute | solution.py:222
  27.9 20.8 %collective-permute-start.6 = (bf16[516,512]{1,0:T(8,128)(2,1)}, bf16[516,512]{1,0:T(8,128)(2,1)S(1)}, u32[]{:S(2)}, u32[]{:S(2)}) collective-permute-start(bf16[516,512]{1,0:T(8,128)(2,1)} %collective-permute-done.4), channel_id=1, source_target_pairs={{0,6},{2,0},{4,2},{6,4},{1,7},{3,1},{5,3},{7,5},{8,14},{10,8},{12,... | collective-permute-start | bytes 1585160 | tf_op jit(solution)/shard_map/ppermute | solution.py:223
  30.8 14.9 %collective-permute-start.2 = (bf16[258,512]{1,0:T(8,128)(2,1)}, bf16[258,512]{1,0:T(8,128)(2,1)}, u32[]{:S(2)}, u32[]{:S(2)}) collective-permute-start(bf16[258,512]{1,0:T(8,128)(2,1)} %slice.202), channel_id=1, source_target_pairs={{0,2},{2,4},{4,6},{6,0},{1,3},{3,5},{5,7},{7,1},{8,10},{10,12},{12... | collective-permute-start | bytes 792584 | tf_op jit(solution)/shard_map/ppermute | solution.py:225
  31.6 14.2 %collective-permute-start.3 = (bf16[258,512]{1,0:T(8,128)(2,1)}, bf16[258,512]{1,0:T(8,128)(2,1)}, u32[]{:S(2)}, u32[]{:S(2)}) collective-permute-start(bf16[258,512]{1,0:T(8,128)(2,1)} %slice.203), channel_id=1, source_target_pairs={{0,6},{2,0},{4,2},{6,4},{1,7},{3,1},{5,3},{7,5},{8,14},{10,8},{12,... | collective-permute-start | bytes 792584 | tf_op jit(solution)/shard_map/ppermute | solution.py:225
  47.7 6.9 %collective-permute-start.7 = (bf16[258,512]{1,0:T(8,128)(2,1)S(1)}, bf16[258,512]{1,0:T(8,128)(2,1)S(1)}, u32[]{:S(2)}, u32[]{:S(2)}) collective-permute-start(bf16[258,512]{1,0:T(8,128)(2,1)S(1)} %slice.204), channel_id=1, source_target_pairs={{0,2},{2,4},{4,6},{6,0},{1,3},{3,5},{5,7},{7,1},{8,10},{10,12},{12... | collective-permute-start | bytes 792584 | tf_op jit(solution)/shard_map/ppermute | solution.py:225
  48.7 6.0 %collective-permute-start.8 = (bf16[258,512]{1,0:T(8,128)(2,1)S(1)}, bf16[258,512]{1,0:T(8,128)(2,1)S(1)}, u32[]{:S(2)}, u32[]{:S(2)}) collective-permute-start(bf16[258,512]{1,0:T(8,128)(2,1)S(1)} %slice.205), channel_id=1, source_target_pairs={{0,6},{2,0},{4,2},{6,4},{1,7},{3,1},{5,3},{7,5},{8,14},{10,8},{12,... | collective-permute-start | bytes 792584 | tf_op jit(solution)/shard_map/ppermute | solution.py:225
  73.3 2.3 %copy-start.8 = (f32[4,16]{1,0:T(4,128)S(1)}, f32[4,16]{1,0:T(4,128)}, u32[]{:S(2)}) copy-start(f32[4,16]{1,0:T(4,128)} %get-tuple-element.74) | copy-start | bytes 772
  73.3 2.5 %copy-start.9 = (f32[4,1]{1,0:T(4,128)S(1)}, f32[4,1]{1,0:T(4,128)}, u32[]{:S(2)}) copy-start(f32[4,1]{1,0:T(4,128)} %get-tuple-element.71) | copy-start | bytes 52
  73.3 2.5 %copy-start.10 = (f32[4,1]{1,0:T(4,128)S(1)}, f32[4,1]{1,0:T(4,128)}, u32[]{:S(2)}) copy-start(f32[4,1]{1,0:T(4,128)} %get-tuple-element.72) | copy-start | bytes 52
  75.5 18.4 %copy-start = (bf16[512,2,128]{2,0,1:T(8,128)(2,1)S(1)}, bf16[512,2,128]{2,0,1:T(8,128)(2,1)}, u32[]{:S(2)}) copy-start(bf16[512,2,128]{2,0,1:T(8,128)(2,1)} %copy.214) | copy-start | bytes 786436
  75.8 22.9 %collective-permute-start.9 = (f32[4,257]{1,0:T(4,128)S(1)}, f32[4,257]{1,0:T(4,128)S(1)}, u32[]{:S(2)}, u32[]{:S(2)}) collective-permute-start(f32[4,257]{1,0:T(4,128)S(1)} %get-tuple-element.63), channel_id=1, source_target_pairs={{8,0},{16,8},{24,16},{32,24},{40,32},{48,40},{56,48},{64,56},{72,6... | collective-permute-start | bytes 12344 | tf_op jit(solution)/shard_map/ppermute | solution.py:260
  80.2 23.4 %collective-permute-start.11 = (f32[4,257]{1,0:T(4,128)S(1)}, f32[4,257]{1,0:T(4,128)S(1)}, u32[]{:S(2)}, u32[]{:S(2)}) collective-permute-start(f32[4,257]{1,0:T(4,128)S(1)} %get-tuple-element.64), channel_id=1, source_target_pairs={{0,8},{8,16},{16,24},{24,32},{32,40},{40,48},{48,56},{56,64},{64,7... | collective-permute-start | bytes 12344 | tf_op jit(solution)/shard_map/ppermute | solution.py:260
  92.4 2.3 %copy-start.2 = (pred[512,1024]{1,0:T(8,128)(4,1)S(1)}, pred[512,1024]{1,0:T(8,128)(4,1)}, u32[]{:S(2)}) copy-start(pred[512,1024]{1,0:T(8,128)(4,1)} %pad_add_fusion) | copy-start | bytes 1572868
  94.7 2.4 %copy-start.5 = (bf16[1,1,512,256]{2,3,1,0:T(8,128)(2,1)S(1)}, bf16[1,1,512,256]{2,3,1,0:T(8,128)(2,1)}, u32[]{:S(2)}) copy-start(bf16[1,1,512,256]{2,3,1,0:T(8,128)(2,1)} %copy.207) | copy-start | bytes 786436
  97.1 1.0 copy-start.4
  97.1 1.4 %copy-start.3 = (bf16[4,256,256]{2,1,0:T(8,128)(2,1)S(1)}, bf16[4,256,256]{2,1,0:T(8,128)(2,1)}, u32[]{:S(2)}) copy-start(bf16[4,256,256]{2,1,0:T(8,128)(2,1)} %get-tuple-element.42) | copy-start | bytes 1572868
  98.9 9.6 %copy-start.12 = (pred[2,2]{1,0:T(4,128)(4,1)S(1)}, pred[2,2]{1,0:T(4,128)(4,1)}, u32[]{:S(2)}) copy-start(pred[2,2]{1,0:T(4,128)(4,1)} %copy-done.11) | copy-start | bytes 16
  108.9 2.7 %collective-permute-start.10 = (f32[4,2,130]{0,1,2:T(2,128)S(1)}, f32[4,2,130]{0,1,2:T(2,128)S(1)}, u32[]{:S(2)}, u32[]{:S(2)}) collective-permute-start(f32[4,2,130]{0,1,2:T(2,128)S(1)} %pad_maximum_fusion), channel_id=1, source_target_pairs={{0,8},{8,16},{16,24},{24,32},{32,40},{40,48},{48,56},{56,64},{64,7... | collective-permute-start | bytes 12488 | tf_op jit(solution)/shard_map/ppermute | solution.py:266
  109.5 4.7 %collective-permute-start.12 = (f32[4,2,130]{0,1,2:T(2,128)S(1)}, f32[4,2,130]{0,1,2:T(2,128)S(1)}, u32[]{:S(2)}, u32[]{:S(2)}) collective-permute-start(f32[4,2,130]{0,1,2:T(2,128)S(1)} %pad_maximum_fusion.1), channel_id=1, source_target_pairs={{8,0},{16,8},{24,16},{32,24},{40,32},{48,40},{56,48},{64,56},{72,6... | collective-permute-start | bytes 12488 | tf_op jit(solution)/shard_map/ppermute | solution.py:266

commit v10 on v9

--- a/solution.py
+++ b/solution.py
@@ -76,10 +76,11 @@
         o_ref[:, c * width : (c + 1) * width] = total
 
 
-def qkv_matmul(whole, gain, shift, weight, order):
-    rows, depth = whole.shape
+def qkv_matmul(whole, first, rows, gain, shift, weight, order):
+    depth = whole.shape[1]
     parts, _, width = weight.shape
     chunk = 128 if rows % 128 == 0 else rows
+    skip = first // chunk
     return pl.pallas_call(
         qkv_kernel,
         out_shape=jax.ShapeDtypeStruct((rows, parts * width), jnp.float32),
@@ -87,7 +88,7 @@
             num_scalar_prefetch=1,
             grid=(rows // chunk,),
             in_specs=[
-                pl.BlockSpec((chunk, depth), lambda i, order: (i, 0)),
+                pl.BlockSpec((chunk, depth), lambda i, order: (i + skip, 0)),
                 pl.BlockSpec((1, depth), lambda i, order: (0, 0)),
                 pl.BlockSpec((1, depth), lambda i, order: (0, 0)),
                 pl.BlockSpec((parts, depth, width), lambda i, order: (0, 0, 0)),
@@ -105,10 +106,9 @@
     )(order, whole, gain.reshape(1, depth), shift.reshape(1, depth), weight)
 
 
-def project(whole, gain, shift, weight, bias, positions, order):
-    count = whole.shape[0]
+def project(whole, first, count, gain, shift, weight, bias, positions, order):
     width = weight.shape[2]
-    mixed = qkv_matmul(whole, gain, shift, weight, order)
+    mixed = qkv_matmul(whole, first, count, gain, shift, weight, order)
     mixed = (mixed + bias.reshape(1, 3 * width)).reshape(count, 3, width // HD, HD)
     query = rotate(mixed[:, 0], positions).astype(jnp.bfloat16)
     fresh_key = rotate(mixed[:, 1], positions).astype(jnp.bfloat16)
@@ -239,6 +239,8 @@
     weight = jnp.transpose(qkv_weight, (1, 0, 2))
     own_query, new_key, new_value = project(
         whole[count:],
+        0,
+        requests,
         gain,
         shift,
         weight,
@@ -271,7 +273,9 @@
     right_parts = answer(piece_batch(prev_query, side_store[:requests], prev_len), backward)
     left_parts = answer(piece_batch(next_query, side_store[requests:], next_len), forward)
     query, fresh_key, fresh_value = project(
-        whole[:count],
+        whole,
+        0,
+        count,
         gain,
         shift,
         weight,

time: 116 us -> 114 us (0.983)
  local copies, waits for them, and re-layouts: 29.9 us -> 27.3 us
    slice x1 -> x0, local copies, waits for them, and re-layouts: 2.68 us -> none  [local(): whole[:count]]
  transfers between devices with their start and end apart: 13 -> 13, of which waited for: 4 -> 4; matrix products, arithmetic and copies ran while one was open for 32% -> 33% of each run, Pallas kernels for 0% -> 0%
where the time goes in v10:
time: 114 us; the launch traced here: 113 us
  starting transfers between devices  34.6 us (30%)
  local copies, waits for them, and re-layouts  27.3 us (24%)
  Pallas kernels  14.4 us (13%)
  other arithmetic  13.8 us (12%)
  matrix products  10.9 us (10%)
  waiting for transfers between devices  10.8 us (9%)
  between operations  1.76 us (2%)
    ppermute x2, starting transfers between devices, ask(): got = lax.ppermute(packed, 'group', pairs)  15.1 us
    pallas_call x2, Pallas kernels, qkv_matmul(): pl.pallas_call(qkv_kernel, out_shape=jax.ShapeDtypeStruct((rows, parts *...  14.4 us
    unnamed x43, local copies, waits for them, and re-layouts  11.6 us
    ppermute x1, starting transfers between devices, local(): partner = lax.ppermute(rows, 'tz', [(0, 1), (1, 0)])  6.91 us
    dot_general x3, matrix products, piece_rows(): jnp.einsum('rkf,rfh->rhk', keys, spread, preferred_element_type=jnp.float32)  4.99 us
    ppermute x2, starting transfers between devices, around(): lax.ppermute(above[half:], 'ty', down)  4.82 us
    dot_general x3, matrix products, piece_rows(): jnp.einsum('rhk,rkf->rhf', weights.astype(jnp.bfloat16), values, preferre...  4.3 us
    ppermute x1, waiting for transfers between devices, local(): partner = lax.ppermute(rows, 'tz', [(0, 1), (1, 0)])  4 us
  transfers between devices with their start and end apart: 13, of which 4 were waited for; matrix products, arithmetic and copies ran while one was open for 33% of the time, Pallas kernels for 0%

profile of v10, /device:TPU:1, one launch (start us, length us, event | category | flops | bytes accessed | tf_op | source)
XLA Modules:
  0.0 113.5 jit_solution(8289992390554612672)
XLA Ops:
  0.7 2.0 %constant_dynamic-update-slice_fusion.1 = (bf16[516,512]{1,0:T(8,128)(2,1)S(1)}, bf16[516,4096]{1,0:T(8,128)(2,1)}) fusion(bf16[512,512]{1,0:T(8,128)(2,1)} %param.11), kind=kLoop, calls=%fused_computation.78 | loop fusion | bytes 1572864
  2.7 1.3 %constant_dynamic-update-slice_fusion = (bf16[516,512]{1,0:T(8,128)(2,1)S(1)}, bf16[516,4096]{1,0:T(8,128)(2,1)}) fusion(bf16[516,512]{1,0:T(8,128)(2,1)S(1)} %get-tuple-element.51, bf16[4,512]{1,0:T(4,128)(2,1)} %param.12, bf16[516,4096]{1,0:T(8,128)(2,1)} %get-tuple-element.52), kind=kLoop, calls=%fused_computation.77 | loop fusion | bytes 12288 | tf_op jit(solution)/shard_map/concatenate | solution.py:213
  4.0 2.1 %collective-permute-start = (bf16[516,512]{1,0:T(8,128)(2,1)S(1)}, bf16[516,512]{1,0:T(8,128)(2,1)S(1)}, u32[]{:S(2)}, u32[]{:S(2)}) collective-permute-start(bf16[516,512]{1,0:T(8,128)(2,1)S(1)} %get-tuple-element.65), channel_id=1, source_target_pairs={{0,2},{2,4},{4,6},{6,0},{1,3},{3,5},{5,7},{7,1},{8,10},{10,12},{12... | collective-permute-start | bytes 1585160 | tf_op jit(solution)/shard_map/ppermute | solution.py:222
  6.1 1.4 %collective-permute-start.1 = (bf16[516,512]{1,0:T(8,128)(2,1)S(1)}, bf16[516,512]{1,0:T(8,128)(2,1)S(1)}, u32[]{:S(2)}, u32[]{:S(2)}) collective-permute-start(bf16[516,512]{1,0:T(8,128)(2,1)S(1)} %get-tuple-element.65), channel_id=1, source_target_pairs={{0,6},{2,0},{4,2},{6,4},{1,7},{3,1},{5,3},{7,5},{8,14},{10,8},{12,... | collective-permute-start | bytes 1585160 | tf_op jit(solution)/shard_map/ppermute | solution.py:223
  7.5 6.9 %collective-permute-start.4 = (bf16[516,512]{1,0:T(8,128)(2,1)S(1)}, bf16[516,512]{1,0:T(8,128)(2,1)}, u32[]{:S(2)}, u32[]{:S(2)}) collective-permute-start(bf16[516,512]{1,0:T(8,128)(2,1)S(1)} %get-tuple-element.65), channel_id=1, source_target_pairs={{0,1},{1,0},{2,3},{3,2},{4,5},{5,4},{6,7},{7,6},{8,9},{9,8},{10,11... | collective-permute-start | bytes 1585160 | tf_op jit(solution)/shard_map/ppermute | solution.py:229
  14.5 1.0 convert_reduce_fusion
  15.4 1.6 %slice_reduce_fusion = (s32[4]{0:T(128)S(1)}, f32[4,1]{1,0:T(4,128)}, f32[4,1]{1,0:T(4,128)}) fusion(s32[4,3]{1,0:T(4,128)} %param.20), kind=kLoop, calls=%fused_computation.141 | loop fusion | flops 8 | bytes 96 | tf_op jit(solution)/shard_map/slice | solution.py:248
  17.1 0.6 iota_compare_fusion.3
  17.8 0.6 broadcast_bitcast_fusion
  19.2 0.7 multiply_cosine_fusion.1
  19.8 0.2 multiply_cosine_fusion
  20.0 1.1 fusion.103
  21.2 1.0 pad_add_fusion
  22.3 1.1 slice_bitcast_fusion.1
  23.4 4.0 %collective-permute-done.4 = bf16[516,512]{1,0:T(8,128)(2,1)} collective-permute-done((bf16[516,512]{1,0:T(8,128)(2,1)S(1)}, bf16[516,512]{1,0:T(8,128)(2,1)}, u32[]{:S(2)}, u32[]{:S(2)}) %collective-permute-start.4) | collective-permute-done | bytes 528416 | tf_op jit(solution)/shard_map/ppermute | solution.py:229
  27.4 0.5 collective-permute-start.5
  27.9 2.2 %collective-permute-start.6 = (bf16[516,512]{1,0:T(8,128)(2,1)}, bf16[516,512]{1,0:T(8,128)(2,1)S(1)}, u32[]{:S(2)}, u32[]{:S(2)}) collective-permute-start(bf16[516,512]{1,0:T(8,128)(2,1)} %collective-permute-done.4), channel_id=1, source_target_pairs={{0,6},{2,0},{4,2},{6,4},{1,7},{3,1},{5,3},{7,5},{8,14},{10,8},{12,... | collective-permute-start | bytes 1585160 | tf_op jit(solution)/shard_map/ppermute | solution.py:223
  30.1 0.7 slice.198
  30.8 0.8 slice.199
  31.6 2.7 %collective-permute-start.3 = (bf16[258,512]{1,0:T(8,128)(2,1)}, bf16[258,512]{1,0:T(8,128)(2,1)}, u32[]{:S(2)}, u32[]{:S(2)}) collective-permute-start(bf16[258,512]{1,0:T(8,128)(2,1)} %slice.199), channel_id=1, source_target_pairs={{0,6},{2,0},{4,2},{6,4},{1,7},{3,1},{5,3},{7,5},{8,14},{10,8},{12,... | collective-permute-start | bytes 792584 | tf_op jit(solution)/shard_map/ppermute | solution.py:225
  34.4 0.6 gather_fusion
  35.0 0.6 gather_fusion.1
  35.6 0.7 add.144
  36.3 0.7 copy.270
  37.1 0.8 copy.211
  38.1 0.8 copy.214
  38.9 0.8 copy.207
  39.7 0.6 concatenate.139
  40.4 0.9 constant_dynamic-update-slice_fusion.6
  41.3 0.9 constant_dynamic-update-slice_fusion.5
  42.1 3.6 %collective-permute-done.2 = bf16[258,512]{1,0:T(8,128)(2,1)} collective-permute-done((bf16[258,512]{1,0:T(8,128)(2,1)}, bf16[258,512]{1,0:T(8,128)(2,1)}, u32[]{:S(2)}, u32[]{:S(2)}) %collective-permute-start.2) | collective-permute-done | bytes 264224 | tf_op jit(solution)/shard_map/ppermute | solution.py:225
  45.8 2.0 %maximum_dynamic-update-slice_fusion.1 = bf16[516,4096]{1,0:T(8,128)(2,1)} fusion(bf16[516,4096]{1,0:T(8,128)(2,1)} %constant_dynamic-update-slice_fusion.5, bf16[258,512]{1,0:T(8,128)(2,1)} %collective-permute-done.3, bf16[258,512]{1,0:T(8,128)(2,1)} %collective-permute-done.2), kind=kLoop, calls=%fused_computation.43 | loop fusion | flops 1056768 | bytes 1073152
  47.7 0.9 collective-permute-start.7
  48.7 2.1 %collective-permute-start.8 = (bf16[258,512]{1,0:T(8,128)(2,1)S(1)}, bf16[258,512]{1,0:T(8,128)(2,1)S(1)}, u32[]{:S(2)}, u32[]{:S(2)}) collective-permute-start(bf16[258,512]{1,0:T(8,128)(2,1)S(1)} %slice.201), channel_id=1, source_target_pairs={{0,6},{2,0},{4,2},{6,4},{1,7},{3,1},{5,3},{7,5},{8,14},{10,8},{12,... | collective-permute-start | bytes 792584 | tf_op jit(solution)/shard_map/ppermute | solution.py:225
  50.8 1.9 %constant_dynamic-update-slice_fusion.4 = bf16[516,4096]{1,0:T(8,128)(2,1)} fusion(bf16[516,4096]{1,0:T(8,128)(2,1)} %maximum_dynamic-update-slice_fusion.1, bf16[516,512]{1,0:T(8,128)(2,1)} %collective-permute-done.4), kind=kLoop, calls=%fused_computation.81 | loop fusion | bytes 1064960
  52.8 0.9 constant_dynamic-update-slice_fusion.3
  53.7 0.9 constant_dynamic-update-slice_fusion.2
  54.7 0.9 maximum_dynamic-update-slice_fusion.x_ref
  55.6 0.8 slice.211.x_ref
  56.4 4.4 %shard_map.123 = f32[4,768]{1,0:T(4,128)S(1)} custom-call(s32[8]{0:T(128)S(1)} %pad_add_fusion.1.order_ref, bf16[4,4096]{1,0:T(4,128)(2,1)S(1)} %slice.211.x_ref, f32[1,4096]{1,0:T(1,128)S(1)} %bitcast.135, f32[1,4096]{1,0:T(1,128)S(1)} %bitcast.137, bf16[3,4096,256]{2,1,0:T(8,128)(2,1)} %bitcast.139), custom_call_target="tpu_custom_call" | custom-call | flops 25165824 | bytes 6336512 | tf_op jit(solution)/shard_map/pallas_call | solution.py:84
  61.0 9.9 %shard_map.122 = f32[512,768]{1,0:T(8,128)S(1)} custom-call(s32[8]{0:T(128)S(1)} %pad_add_fusion.1.order_ref, bf16[516,4096]{1,0:T(8,128)(2,1)} %maximum_dynamic-update-slice_fusion.x_ref, f32[1,4096]{1,0:T(1,128)S(1)} %bitcast.136, f32[1,4096]{1,0:T(1,128)S(1)} %bitcast.138, bf16[3,4096,256]{2,1,0:T(8,128)(2,1)} %bitcast.140), custom_call_target="tpu_custom_call" | custom-call | flops 3221225472 | bytes 12058624 | tf_op jit(solution)/shard_map/pallas_call | solution.py:84
  71.1 0.8 reshape.539
  71.9 0.4 fusion.102
  72.3 0.9 slice.202
  73.5 4.4 %collective-permute-start.9 = (f32[4,257]{1,0:T(4,128)S(1)}, f32[4,257]{1,0:T(4,128)S(1)}, u32[]{:S(2)}, u32[]{:S(2)}) collective-permute-start(f32[4,257]{1,0:T(4,128)S(1)} %get-tuple-element.63), channel_id=1, source_target_pairs={{8,0},{16,8},{24,16},{32,24},{40,32},{48,40},{56,48},{64,56},{72,6... | collective-permute-start | bytes 12344 | tf_op jit(solution)/shard_map/ppermute | solution.py:262
  77.9 10.7 %collective-permute-start.11 = (f32[4,257]{1,0:T(4,128)S(1)}, f32[4,257]{1,0:T(4,128)S(1)}, u32[]{:S(2)}, u32[]{:S(2)}) collective-permute-start(f32[4,257]{1,0:T(4,128)S(1)} %get-tuple-element.64), channel_id=1, source_target_pairs={{0,8},{8,16},{16,24},{24,32},{32,40},{40,48},{48,56},{56,64},{64,7... | collective-permute-start | bytes 12344 | tf_op jit(solution)/shard_map/ppermute | solution.py:262
  89.0 1.1 copy.263
  90.1 1.4 %subtract_convert_fusion.1 = (bf16[512,2,16]{2,0,1:T(8,128)(2,1)S(1)}, bf16[512,2,16]{2,0,1:T(8,128)(2,1)S(1)}, bf16[512,2,16]{2,0,1:T(8,128)(2,1)S(1)}, bf16[512,2,16]{2,0,1:T(8,128)(2,1)S(1)}) fusion(f32[512,2,128]{2,0,1:T(8,128)S(1)} %get-tuple-element.84, f32[512,16]{1,0:T(8,128)} %copy.211, f32[512,16]{1,0:T(8,128)S(1)} %copy.210, ...), kind=kLoop, calls=%fused_computation.64 | loop fusion | flops 262144 | bytes 458752 | tf_op jit(solution)/shard_map/convert.21
  91.6 0.8 fusion.51
  92.4 2.3 %fusion.104 = (f32[2,512]{1,0:T(2,128)S(1)}, bf16[2,512,1024]{2,1,0:T(8,128)(2,1)S(1)}) fusion(f32[2,512,1024]{2,1,0:T(8,128)S(1)} %fusion.51, pred[512,1024]{1,0:T(8,128)(4,1)S(1)} %copy-done.2), kind=kOutput, calls=%fused_computation.180 | output fusion | flops 8389631 | bytes 6819840 | tf_op jit(solution)/shard_map/while/body/eval_jaxpr/sub | solution.py:125
  94.9 0.8 fusion.25
  95.8 0.3 fusion.107
  96.2 0.2 fusion.44
  96.6 2.3 %fusion.106 = (f32[4,2]{1,0:T(4,128)S(1)}, f32[4,2,1024]{2,1,0:T(2,128)S(1)}) fusion(bf16[8,2,1024,256]{3,2,1,0:T(8,128)(2,1)} %param.21, pred[256,2]{0,1:T(4,128)(4,1)S(1)} %bitcast.157, bf16[4,256]{1,0:T(4,128)(2,1)S(1)} %slice.322, pred[4,1024]{1,0:T(4,128)(4,1)S(1)} %iota_compare_fusion.2), kind=kOutput, calls=%fused_computation.182 | convolution fusion | flops 4220920 | bytes 2136608 | tf_op jit(solution)/shard_map/rkf,rfh->rhk/dot_general | solution.py:160
  99.0 2.0 %fusion.6 = f32[4,2,256]{2,1,0:T(2,128)S(1)} fusion(bf16[8,2,1024,256]{3,2,1,0:T(8,128)(2,1)} %param.21, f32[4,2,1024]{2,1,0:T(2,128)S(1)} %get-tuple-element.80, pred[4,1024]{1,0:T(4,128)(4,1)S(1)} %iota_compare_fusion.2, f32[4,2]{1,0:T(4,128)S(1)} %get-tuple-element.79), kind=kOutput, calls=%fused_computation.10 | convolution fusion | flops 4218880 | bytes 2142240 | tf_op jit(solution)/shard_map/rhk,rkf->rhf/dot_general | solution.py:167
  101.0 0.2 fusion.66
  101.5 2.3 %fusion.105 = (f32[4,2]{1,0:T(4,128)S(1)}, f32[4,2,1024]{2,1,0:T(2,128)S(1)}) fusion(bf16[8,2,1024,256]{3,2,1,0:T(8,128)(2,1)} %param.21, pred[256,2]{0,1:T(4,128)(4,1)S(1)} %bitcast.158, bf16[4,256]{1,0:T(4,128)(2,1)S(1)} %slice.320, pred[4,1024]{1,0:T(4,128)(4,1)S(1)} %iota_compare_fusion.1), kind=kOutput, calls=%fused_computation.181 | convolution fusion | flops 4220920 | bytes 2136608 | tf_op jit(solution)/shard_map/rkf,rfh->rhk/dot_general | solution.py:160
  103.8 2.0 %fusion.2 = f32[4,2,256]{2,1,0:T(2,128)S(1)} fusion(bf16[8,2,1024,256]{3,2,1,0:T(8,128)(2,1)} %param.21, f32[4,2,1024]{2,1,0:T(2,128)S(1)} %get-tuple-element.78, pred[4,1024]{1,0:T(4,128)(4,1)S(1)} %iota_compare_fusion.1, f32[4,2]{1,0:T(4,128)S(1)} %get-tuple-element.77), kind=kOutput, calls=%fused_computation.6 | convolution fusion | flops 4218880 | bytes 2142240 | tf_op jit(solution)/shard_map/rhk,rkf->rhf/dot_general | solution.py:167
  106.6 0.3 collective-permute-start.10
  107.2 0.4 collective-permute-start.12
  108.0 0.8 copy.247
  108.8 0.5 collective-permute-done.10
  109.3 2.6 %collective-permute-done.12 = f32[4,2,130]{0,1,2:T(2,128)S(1)} collective-permute-done((f32[4,2,130]{0,1,2:T(2,128)S(1)}, f32[4,2,130]{0,1,2:T(2,128)S(1)}, u32[]{:S(2)}, u32[]{:S(2)}) %collective-permute-start.12) | collective-permute-done | bytes 4192 | tf_op jit(solution)/shard_map/ppermute | solution.py:268
  112.8 0.7 copy.246
  (108 shorter events, 4.8 us)
Async XLA Ops:
  0.6 21.7 %copy-start.1 = (bf16[4,2,256,256]{3,2,1,0:T(8,128)(2,1)S(1)}, bf16[4,2,256,256]{3,2,1,0:T(8,128)(2,1)}, u32[]{:S(2)}) copy-start(bf16[4,2,256,256]{3,2,1,0:T(8,128)(2,1)} %param.19) | copy-start | bytes 3145732
  0.6 33.7 %copy-start.6 = (f32[4096]{0:T(1024)S(1)}, f32[4096]{0:T(1024)}, u32[]{:S(2)}) copy-start(f32[4096]{0:T(1024)} %param.13) | copy-start | bytes 49156
  0.7 34.3 %copy-start.7 = (f32[4096]{0:T(1024)S(1)}, f32[4096]{0:T(1024)}, u32[]{:S(2)}) copy-start(f32[4096]{0:T(1024)} %param.14) | copy-start | bytes 49156
  4.0 26.1 %collective-permute-start = (bf16[516,512]{1,0:T(8,128)(2,1)S(1)}, bf16[516,512]{1,0:T(8,128)(2,1)S(1)}, u32[]{:S(2)}, u32[]{:S(2)}) collective-permute-start(bf16[516,512]{1,0:T(8,128)(2,1)S(1)} %get-tuple-element.65), channel_id=1, source_target_pairs={{0,2},{2,4},{4,6},{6,0},{1,3},{3,5},{5,7},{7,1},{8,10},{10,12},{12... | collective-permute-start | bytes 1585160 | tf_op jit(solution)/shard_map/ppermute | solution.py:222
  6.1 24.7 %collective-permute-start.1 = (bf16[516,512]{1,0:T(8,128)(2,1)S(1)}, bf16[516,512]{1,0:T(8,128)(2,1)S(1)}, u32[]{:S(2)}, u32[]{:S(2)}) collective-permute-start(bf16[516,512]{1,0:T(8,128)(2,1)S(1)} %get-tuple-element.65), channel_id=1, source_target_pairs={{0,6},{2,0},{4,2},{6,4},{1,7},{3,1},{5,3},{7,5},{8,14},{10,8},{12,... | collective-permute-start | bytes 1585160 | tf_op jit(solution)/shard_map/ppermute | solution.py:223
  7.5 19.9 %collective-permute-start.4 = (bf16[516,512]{1,0:T(8,128)(2,1)S(1)}, bf16[516,512]{1,0:T(8,128)(2,1)}, u32[]{:S(2)}, u32[]{:S(2)}) collective-permute-start(bf16[516,512]{1,0:T(8,128)(2,1)S(1)} %get-tuple-element.65), channel_id=1, source_target_pairs={{0,1},{1,0},{2,3},{3,2},{4,5},{5,4},{6,7},{7,6},{8,9},{9,8},{10,11... | collective-permute-start | bytes 1585160 | tf_op jit(solution)/shard_map/ppermute | solution.py:229
  17.0 2.1 %copy-start.11 = (pred[2,2]{1,0:T(4,128)(4,1)}, pred[2,2]{1,0:T(4,128)(4,1)S(1)}, u32[]{:S(2)}) copy-start(pred[2,2]{1,0:T(4,128)(4,1)S(1)} %iota_compare_fusion.5) | copy-start | bytes 16
  27.4 20.3 %collective-permute-start.5 = (bf16[516,512]{1,0:T(8,128)(2,1)}, bf16[516,512]{1,0:T(8,128)(2,1)S(1)}, u32[]{:S(2)}, u32[]{:S(2)}) collective-permute-start(bf16[516,512]{1,0:T(8,128)(2,1)} %collective-permute-done.4), channel_id=1, source_target_pairs={{0,2},{2,4},{4,6},{6,0},{1,3},{3,5},{5,7},{7,1},{8,10},{10,12},{12... | collective-permute-start | bytes 1585160 | tf_op jit(solution)/shard_map/ppermute | solution.py:222
  27.9 20.8 %collective-permute-start.6 = (bf16[516,512]{1,0:T(8,128)(2,1)}, bf16[516,512]{1,0:T(8,128)(2,1)S(1)}, u32[]{:S(2)}, u32[]{:S(2)}) collective-permute-start(bf16[516,512]{1,0:T(8,128)(2,1)} %collective-permute-done.4), channel_id=1, source_target_pairs={{0,6},{2,0},{4,2},{6,4},{1,7},{3,1},{5,3},{7,5},{8,14},{10,8},{12,... | collective-permute-start | bytes 1585160 | tf_op jit(solution)/shard_map/ppermute | solution.py:223
  30.8 14.9 %collective-permute-start.2 = (bf16[258,512]{1,0:T(8,128)(2,1)}, bf16[258,512]{1,0:T(8,128)(2,1)}, u32[]{:S(2)}, u32[]{:S(2)}) collective-permute-start(bf16[258,512]{1,0:T(8,128)(2,1)} %slice.198), channel_id=1, source_target_pairs={{0,2},{2,4},{4,6},{6,0},{1,3},{3,5},{5,7},{7,1},{8,10},{10,12},{12... | collective-permute-start | bytes 792584 | tf_op jit(solution)/shard_map/ppermute | solution.py:225
  31.6 14.2 %collective-permute-start.3 = (bf16[258,512]{1,0:T(8,128)(2,1)}, bf16[258,512]{1,0:T(8,128)(2,1)}, u32[]{:S(2)}, u32[]{:S(2)}) collective-permute-start(bf16[258,512]{1,0:T(8,128)(2,1)} %slice.199), channel_id=1, source_target_pairs={{0,6},{2,0},{4,2},{6,4},{1,7},{3,1},{5,3},{7,5},{8,14},{10,8},{12,... | collective-permute-start | bytes 792584 | tf_op jit(solution)/shard_map/ppermute | solution.py:225
  47.7 6.9 %collective-permute-start.7 = (bf16[258,512]{1,0:T(8,128)(2,1)S(1)}, bf16[258,512]{1,0:T(8,128)(2,1)S(1)}, u32[]{:S(2)}, u32[]{:S(2)}) collective-permute-start(bf16[258,512]{1,0:T(8,128)(2,1)S(1)} %slice.200), channel_id=1, source_target_pairs={{0,2},{2,4},{4,6},{6,0},{1,3},{3,5},{5,7},{7,1},{8,10},{10,12},{12... | collective-permute-start | bytes 792584 | tf_op jit(solution)/shard_map/ppermute | solution.py:225
  48.7 6.0 %collective-permute-start.8 = (bf16[258,512]{1,0:T(8,128)(2,1)S(1)}, bf16[258,512]{1,0:T(8,128)(2,1)S(1)}, u32[]{:S(2)}, u32[]{:S(2)}) collective-permute-start(bf16[258,512]{1,0:T(8,128)(2,1)S(1)} %slice.201), channel_id=1, source_target_pairs={{0,6},{2,0},{4,2},{6,4},{1,7},{3,1},{5,3},{7,5},{8,14},{10,8},{12,... | collective-permute-start | bytes 792584 | tf_op jit(solution)/shard_map/ppermute | solution.py:225
  70.9 2.3 %copy-start.8 = (f32[4,16]{1,0:T(4,128)S(1)}, f32[4,16]{1,0:T(4,128)}, u32[]{:S(2)}) copy-start(f32[4,16]{1,0:T(4,128)} %get-tuple-element.74) | copy-start | bytes 772
  71.0 2.5 %copy-start.9 = (f32[4,1]{1,0:T(4,128)S(1)}, f32[4,1]{1,0:T(4,128)}, u32[]{:S(2)}) copy-start(f32[4,1]{1,0:T(4,128)} %get-tuple-element.71) | copy-start | bytes 52
  71.0 2.5 %copy-start.10 = (f32[4,1]{1,0:T(4,128)S(1)}, f32[4,1]{1,0:T(4,128)}, u32[]{:S(2)}) copy-start(f32[4,1]{1,0:T(4,128)} %get-tuple-element.72) | copy-start | bytes 52
  73.2 18.4 %copy-start = (bf16[512,2,128]{2,0,1:T(8,128)(2,1)S(1)}, bf16[512,2,128]{2,0,1:T(8,128)(2,1)}, u32[]{:S(2)}) copy-start(bf16[512,2,128]{2,0,1:T(8,128)(2,1)} %copy.214) | copy-start | bytes 786436
  73.5 22.9 %collective-permute-start.9 = (f32[4,257]{1,0:T(4,128)S(1)}, f32[4,257]{1,0:T(4,128)S(1)}, u32[]{:S(2)}, u32[]{:S(2)}) collective-permute-start(f32[4,257]{1,0:T(4,128)S(1)} %get-tuple-element.63), channel_id=1, source_target_pairs={{8,0},{16,8},{24,16},{32,24},{40,32},{48,40},{56,48},{64,56},{72,6... | collective-permute-start | bytes 12344 | tf_op jit(solution)/shard_map/ppermute | solution.py:262
  77.9 23.4 %collective-permute-start.11 = (f32[4,257]{1,0:T(4,128)S(1)}, f32[4,257]{1,0:T(4,128)S(1)}, u32[]{:S(2)}, u32[]{:S(2)}) collective-permute-start(f32[4,257]{1,0:T(4,128)S(1)} %get-tuple-element.64), channel_id=1, source_target_pairs={{0,8},{8,16},{16,24},{24,32},{32,40},{40,48},{48,56},{56,64},{64,7... | collective-permute-start | bytes 12344 | tf_op jit(solution)/shard_map/ppermute | solution.py:262
  90.1 2.3 %copy-start.2 = (pred[512,1024]{1,0:T(8,128)(4,1)S(1)}, pred[512,1024]{1,0:T(8,128)(4,1)}, u32[]{:S(2)}) copy-start(pred[512,1024]{1,0:T(8,128)(4,1)} %pad_add_fusion) | copy-start | bytes 1572868
  92.4 2.4 %copy-start.5 = (bf16[1,1,512,256]{2,3,1,0:T(8,128)(2,1)S(1)}, bf16[1,1,512,256]{2,3,1,0:T(8,128)(2,1)}, u32[]{:S(2)}) copy-start(bf16[1,1,512,256]{2,3,1,0:T(8,128)(2,1)} %copy.207) | copy-start | bytes 786436
  94.8 1.0 copy-start.4
  94.8 1.4 %copy-start.3 = (bf16[4,256,256]{2,1,0:T(8,128)(2,1)S(1)}, bf16[4,256,256]{2,1,0:T(8,128)(2,1)}, u32[]{:S(2)}) copy-start(bf16[4,256,256]{2,1,0:T(8,128)(2,1)} %get-tuple-element.42) | copy-start | bytes 1572868
  96.6 9.6 %copy-start.12 = (pred[2,2]{1,0:T(4,128)(4,1)S(1)}, pred[2,2]{1,0:T(4,128)(4,1)}, u32[]{:S(2)}) copy-start(pred[2,2]{1,0:T(4,128)(4,1)} %copy-done.11) | copy-start | bytes 16
  106.6 2.7 %collective-permute-start.10 = (f32[4,2,130]{0,1,2:T(2,128)S(1)}, f32[4,2,130]{0,1,2:T(2,128)S(1)}, u32[]{:S(2)}, u32[]{:S(2)}) collective-permute-start(f32[4,2,130]{0,1,2:T(2,128)S(1)} %pad_maximum_fusion), channel_id=1, source_target_pairs={{0,8},{8,16},{16,24},{24,32},{32,40},{40,48},{48,56},{56,64},{64,7... | collective-permute-start | bytes 12488 | tf_op jit(solution)/shard_map/ppermute | solution.py:268
  107.2 4.7 %collective-permute-start.12 = (f32[4,2,130]{0,1,2:T(2,128)S(1)}, f32[4,2,130]{0,1,2:T(2,128)S(1)}, u32[]{:S(2)}, u32[]{:S(2)}) collective-permute-start(f32[4,2,130]{0,1,2:T(2,128)S(1)} %pad_maximum_fusion.1), channel_id=1, source_target_pairs={{8,0},{16,8},{24,16},{32,24},{40,32},{48,40},{56,48},{64,56},{72,6... | collective-permute-start | bytes 12488 | tf_op jit(solution)/shard_map/ppermute | solution.py:268

commit v11 on v10

--- a/solution.py
+++ b/solution.py
@@ -270,8 +270,8 @@
 
     prev_query, prev_len = ask(piece_len[:, 2], forward)
     next_query, next_len = ask(piece_len[:, 0], backward)
-    right_parts = answer(piece_batch(prev_query, side_store[:requests], prev_len), backward)
-    left_parts = answer(piece_batch(next_query, side_store[requests:], next_len), forward)
+    right_for_prev = piece_batch(prev_query, side_store[:requests], prev_len)
+    left_for_next = piece_batch(next_query, side_store[requests:], next_len)
     query, fresh_key, fresh_value = project(
         whole,
         0,
@@ -283,6 +283,11 @@
         prefill_offset[0] + jnp.arange(count, dtype=jnp.int32),
         order,
     )
+    right_for_prev, left_for_next, query, fresh_key, fresh_value = lax.optimization_barrier(
+        (right_for_prev, left_for_next, query, fresh_key, fresh_value)
+    )
+    right_parts = answer(right_for_prev, backward)
+    left_parts = answer(left_for_next, forward)
     prefill_out = prefill_attend(query, fresh_key, fresh_value, prior_cache[0], prefill_offset[0])
     decode_out = combine([left_parts, home_parts, right_parts]).reshape(requests, -1)
     return (prefill_out, decode_out)

time: 114 us -> 118 us (1.035)
  the two profiles are of different devices: /device:TPU:1 before, /device:TPU:128 now
where the time goes in v11:
time: 118 us; the launch traced here: 117 us
  waiting for transfers between devices  28.7 us (24%)
  local copies, waits for them, and re-layouts  25 us (21%)
  starting transfers between devices  22.2 us (19%)
  Pallas kernels  14.3 us (12%)
  other arithmetic  13.1 us (11%)
  matrix products  11.9 us (10%)
  between operations  1.79 us (2%)
    ppermute x1, waiting for transfers between devices, local(): partner = lax.ppermute(rows, 'tz', [(0, 1), (1, 0)])  19.3 us
    pallas_call x2, Pallas kernels, qkv_matmul(): pl.pallas_call(qkv_kernel, out_shape=jax.ShapeDtypeStruct((rows, parts *...  14.3 us
    unnamed x45, local copies, waits for them, and re-layouts  9.32 us
    ppermute x2, starting transfers between devices, ask(): got = lax.ppermute(packed, 'group', pairs)  5.72 us
    dot_general x3, matrix products, piece_rows(): jnp.einsum('rhk,rkf->rhf', weights.astype(jnp.bfloat16), values, preferre...  5.33 us
    dot_general x3, matrix products, piece_rows(): jnp.einsum('rkf,rfh->rhk', keys, spread, preferred_element_type=jnp.float32)  5.04 us
    ppermute x2, starting transfers between devices, around(): above = lax.ppermute(block, 'ty', down)  4.59 us
    ppermute x2, starting transfers between devices, around(): lax.ppermute(above[half:], 'ty', down)  4.3 us
  transfers between devices with their start and end apart: 13, of which 4 were waited for; matrix products, arithmetic and copies ran while one was open for 27% of the time, Pallas kernels for 0%

profile of v11, /device:TPU:128, one launch (start us, length us, event | category | flops | bytes accessed | tf_op | source)
XLA Modules:
  0.0 117.1 jit_solution(8401642653352801596)
XLA Ops:
  0.7 2.0 %constant_dynamic-update-slice_fusion.1 = (bf16[516,512]{1,0:T(8,128)(2,1)S(1)}, bf16[516,4096]{1,0:T(8,128)(2,1)}) fusion(bf16[512,512]{1,0:T(8,128)(2,1)} %param.11), kind=kLoop, calls=%fused_computation.71 | loop fusion | bytes 1572864
  2.7 1.3 %constant_dynamic-update-slice_fusion = (bf16[516,512]{1,0:T(8,128)(2,1)S(1)}, bf16[516,4096]{1,0:T(8,128)(2,1)}) fusion(bf16[516,512]{1,0:T(8,128)(2,1)S(1)} %get-tuple-element.71, bf16[4,512]{1,0:T(4,128)(2,1)} %param.12, bf16[516,4096]{1,0:T(8,128)(2,1)} %get-tuple-element.72), kind=kLoop, calls=%fused_computation.70 | loop fusion | bytes 12288 | tf_op jit(solution)/shard_map/concatenate | solution.py:213
  4.0 1.6 %collective-permute-start = (bf16[516,512]{1,0:T(8,128)(2,1)S(1)}, bf16[516,512]{1,0:T(8,128)(2,1)S(1)}, u32[]{:S(2)}, u32[]{:S(2)}) collective-permute-start(bf16[516,512]{1,0:T(8,128)(2,1)S(1)} %get-tuple-element.85), channel_id=1, source_target_pairs={{0,2},{2,4},{4,6},{6,0},{1,3},{3,5},{5,7},{7,1},{8,10},{10,12},{12... | collective-permute-start | bytes 1585160 | tf_op jit(solution)/shard_map/ppermute | solution.py:222
  5.6 1.7 %collective-permute-start.1 = (bf16[516,512]{1,0:T(8,128)(2,1)S(1)}, bf16[516,512]{1,0:T(8,128)(2,1)S(1)}, u32[]{:S(2)}, u32[]{:S(2)}) collective-permute-start(bf16[516,512]{1,0:T(8,128)(2,1)S(1)} %get-tuple-element.85), channel_id=1, source_target_pairs={{0,6},{2,0},{4,2},{6,4},{1,7},{3,1},{5,3},{7,5},{8,14},{10,8},{12,... | collective-permute-start | bytes 1585160 | tf_op jit(solution)/shard_map/ppermute | solution.py:223
  7.2 0.5 collective-permute-start.4
  7.7 1.0 convert_reduce_fusion
  8.7 1.5 %slice_convert_fusion.10 = (f32[4,1]{1,0:T(4,128)}, f32[4,1]{1,0:T(4,128)}, s32[4]{0:T(128)S(1)}) fusion(s32[4,3]{1,0:T(4,128)} %param.20), kind=kLoop, calls=%fused_computation.135 | loop fusion | flops 8 | bytes 96 | tf_op jit(solution)/shard_map/convert_element_type | solution.py:259
  10.5 0.6 iota_compare_fusion.3
  11.9 0.7 multiply_cosine_fusion.1
  12.5 0.2 multiply_cosine_fusion
  12.7 1.1 fusion.94
  13.9 1.0 pad_add_fusion
  15.0 1.1 slice_bitcast_fusion.1
  16.1 19.3 %collective-permute-done.4 = bf16[516,512]{1,0:T(8,128)(2,1)} collective-permute-done((bf16[516,512]{1,0:T(8,128)(2,1)S(1)}, bf16[516,512]{1,0:T(8,128)(2,1)}, u32[]{:S(2)}, u32[]{:S(2)}) %collective-permute-start.4) | collective-permute-done | bytes 528416 | tf_op jit(solution)/shard_map/ppermute | solution.py:229
  35.4 0.3 collective-permute-start.5
  35.7 2.9 %collective-permute-start.6 = (bf16[516,512]{1,0:T(8,128)(2,1)}, bf16[516,512]{1,0:T(8,128)(2,1)S(1)}, u32[]{:S(2)}, u32[]{:S(2)}) collective-permute-start(bf16[516,512]{1,0:T(8,128)(2,1)} %collective-permute-done.4), channel_id=1, source_target_pairs={{0,6},{2,0},{4,2},{6,4},{1,7},{3,1},{5,3},{7,5},{8,14},{10,8},{12,... | collective-permute-start | bytes 1585160 | tf_op jit(solution)/shard_map/ppermute | solution.py:223
  38.6 0.8 slice.199
  39.4 0.5 collective-permute-start.3
  40.0 0.7 slice.198
  40.7 1.5 %collective-permute-start.2 = (bf16[258,512]{1,0:T(8,128)(2,1)}, bf16[258,512]{1,0:T(8,128)(2,1)}, u32[]{:S(2)}, u32[]{:S(2)}) collective-permute-start(bf16[258,512]{1,0:T(8,128)(2,1)} %slice.198), channel_id=1, source_target_pairs={{0,2},{2,4},{4,6},{6,0},{1,3},{3,5},{5,7},{7,1},{8,10},{10,12},{12... | collective-permute-start | bytes 792584 | tf_op jit(solution)/shard_map/ppermute | solution.py:225
  42.3 0.6 gather_fusion
  42.9 0.6 gather_fusion.1
  43.5 0.7 add.146
  44.3 0.8 copy.221
  45.3 0.8 copy.226
  46.1 0.8 copy.213
  47.0 0.7 concatenate.140
  47.6 0.9 constant_dynamic-update-slice_fusion.6
  48.6 0.9 constant_dynamic-update-slice_fusion.5
  49.5 2.0 %collective-permute-done.3 = bf16[258,512]{1,0:T(8,128)(2,1)} collective-permute-done((bf16[258,512]{1,0:T(8,128)(2,1)}, bf16[258,512]{1,0:T(8,128)(2,1)}, u32[]{:S(2)}, u32[]{:S(2)}) %collective-permute-start.3) | collective-permute-done | bytes 264224 | tf_op jit(solution)/shard_map/ppermute | solution.py:225
  51.5 1.9 %maximum_dynamic-update-slice_fusion.1 = bf16[516,4096]{1,0:T(8,128)(2,1)} fusion(bf16[516,4096]{1,0:T(8,128)(2,1)} %constant_dynamic-update-slice_fusion.5, bf16[258,512]{1,0:T(8,128)(2,1)} %collective-permute-done.3, bf16[258,512]{1,0:T(8,128)(2,1)} %collective-permute-done.2), kind=kLoop, calls=%fused_computation.43 | loop fusion | flops 1056768 | bytes 1073152
  53.5 3.8 %collective-permute-start.8 = (bf16[258,512]{1,0:T(8,128)(2,1)S(1)}, bf16[258,512]{1,0:T(8,128)(2,1)S(1)}, u32[]{:S(2)}, u32[]{:S(2)}) collective-permute-start(bf16[258,512]{1,0:T(8,128)(2,1)S(1)} %slice.201), channel_id=1, source_target_pairs={{0,6},{2,0},{4,2},{6,4},{1,7},{3,1},{5,3},{7,5},{8,14},{10,8},{12,... | collective-permute-start | bytes 792584 | tf_op jit(solution)/shard_map/ppermute | solution.py:225
  57.3 0.3 collective-permute-start.7
  57.6 1.9 %constant_dynamic-update-slice_fusion.4 = bf16[516,4096]{1,0:T(8,128)(2,1)} fusion(bf16[516,4096]{1,0:T(8,128)(2,1)} %maximum_dynamic-update-slice_fusion.1, bf16[516,512]{1,0:T(8,128)(2,1)} %collective-permute-done.4), kind=kLoop, calls=%fused_computation.74 | loop fusion | bytes 1064960
  59.5 0.9 constant_dynamic-update-slice_fusion.3
  60.4 0.9 constant_dynamic-update-slice_fusion.2
  61.3 4.0 %collective-permute-done.7 = bf16[258,512]{1,0:T(8,128)(2,1)S(1)} collective-permute-done((bf16[258,512]{1,0:T(8,128)(2,1)S(1)}, bf16[258,512]{1,0:T(8,128)(2,1)S(1)}, u32[]{:S(2)}, u32[]{:S(2)}) %collective-permute-start.7) | collective-permute-done | bytes 264224 | tf_op jit(solution)/shard_map/ppermute | solution.py:225
  65.3 0.9 maximum_dynamic-update-slice_fusion.x_ref
  66.2 0.8 slice.202.x_ref
  67.0 4.4 %shard_map.122 = f32[4,768]{1,0:T(4,128)S(1)} custom-call(s32[8]{0:T(128)S(1)} %pad_add_fusion.1.order_ref, bf16[4,4096]{1,0:T(4,128)(2,1)S(1)} %slice.202.x_ref, f32[1,4096]{1,0:T(1,128)S(1)} %bitcast.136, f32[1,4096]{1,0:T(1,128)S(1)} %bitcast.138, bf16[3,4096,256]{2,1,0:T(8,128)(2,1)} %bitcast.140), custom_call_target="tpu_custom_call" | custom-call | flops 25165824 | bytes 6336512 | tf_op jit(solution)/shard_map/pallas_call | solution.py:84
  71.7 9.9 %shard_map.123 = f32[512,768]{1,0:T(8,128)S(1)} custom-call(s32[8]{0:T(128)S(1)} %pad_add_fusion.1.order_ref, bf16[516,4096]{1,0:T(8,128)(2,1)} %maximum_dynamic-update-slice_fusion.x_ref, f32[1,4096]{1,0:T(1,128)S(1)} %bitcast.137, f32[1,4096]{1,0:T(1,128)S(1)} %bitcast.139, bf16[3,4096,256]{2,1,0:T(8,128)(2,1)} %bitcast.141), custom_call_target="tpu_custom_call" | custom-call | flops 3221225472 | bytes 12058624 | tf_op jit(solution)/shard_map/pallas_call | solution.py:84
  81.7 0.8 reshape.542
  82.5 0.4 fusion.93
  82.9 0.9 slice.219
  84.1 5.6 %collective-permute-start.10 = (f32[4,257]{1,0:T(4,128)S(1)}, f32[4,257]{1,0:T(4,128)S(1)}, u32[]{:S(2)}, u32[]{:S(2)}) collective-permute-start(f32[4,257]{1,0:T(4,128)S(1)} %get-tuple-element.81), channel_id=1, source_target_pairs={{8,0},{16,8},{24,16},{32,24},{40,32},{48,40},{56,48},{64,56},{72,6... | collective-permute-start | bytes 12344 | tf_op jit(solution)/shard_map/ppermute | solution.py:262
  90.3 0.3 fusion.96
  90.8 0.2 fusion.70
  90.9 0.4 subtract_convert_fusion
  91.4 0.3 pad_maximum_fusion
  91.6 0.3 pad_maximum_fusion.1
  91.9 1.3 %fusion.44 = f32[4,2,256]{2,1,0:T(2,128)S(1)} fusion(bf16[4,1,256]{2,1,0:T(2,128)(2,1)S(1)} %copy.245, bf16[4,256,256]{2,1,0:T(8,128)(2,1)} %get-tuple-element.66, f32[4,2,257]{2,1,0:T(2,128)S(1)} %get-tuple-element.98, pred[4,257]{1,0:T(4,128)(4,1)S(1)} %concatenate.140, f32[4,2]{1,0:T(4,128)S(1)} %get-tuple-element.97), kind=kOutput, calls=%fused_computation.38 | convolution fusion | flops 2111512 | bytes 543812 | tf_op jit(solution)/shard_map/rhk,rkf->rhf/dot_general | solution.py:167
  93.9 2.3 %fusion.95 = (f32[4,2]{1,0:T(4,128)S(1)}, f32[4,2,1024]{2,1,0:T(2,128)S(1)}) fusion(bf16[8,2,1024,256]{3,2,1,0:T(8,128)(2,1)} %param.21, pred[256,2]{0,1:T(4,128)(4,1)S(1)} %bitcast.158, bf16[4,256]{1,0:T(4,128)(2,1)S(1)} %slice.322, pred[4,1024]{1,0:T(4,128)(4,1)S(1)} %iota_compare_fusion.2), kind=kOutput, calls=%fused_computation.173 | convolution fusion | flops 4220920 | bytes 2136608 | tf_op jit(solution)/shard_map/rkf,rfh->rhk/dot_general | solution.py:160
  96.2 2.4 %fusion.97 = (f32[4,2]{1,0:T(4,128)S(1)}, f32[4,2,1024]{2,1,0:T(2,128)S(1)}) fusion(bf16[8,2,1024,256]{3,2,1,0:T(8,128)(2,1)} %param.21, pred[256,2]{0,1:T(4,128)(4,1)S(1)} %bitcast.159, bf16[4,256]{1,0:T(4,128)(2,1)S(1)} %slice.321, pred[4,1024]{1,0:T(4,128)(4,1)S(1)} %iota_compare_fusion.1), kind=kOutput, calls=%fused_computation.175 | convolution fusion | flops 4220920 | bytes 2136608 | tf_op jit(solution)/shard_map/rkf,rfh->rhk/dot_general | solution.py:160
  98.6 2.0 %fusion.2 = f32[4,2,256]{2,1,0:T(2,128)S(1)} fusion(bf16[8,2,1024,256]{3,2,1,0:T(8,128)(2,1)} %param.21, f32[4,2,1024]{2,1,0:T(2,128)S(1)} %get-tuple-element.100, pred[4,1024]{1,0:T(4,128)(4,1)S(1)} %iota_compare_fusion.1, f32[4,2]{1,0:T(4,128)S(1)} %get-tuple-element.33), kind=kOutput, calls=%fused_computation.6 | convolution fusion | flops 4218880 | bytes 2142240 | tf_op jit(solution)/shard_map/rhk,rkf->rhf/dot_general | solution.py:167
  100.6 0.2 fusion.57
  100.8 2.0 %fusion.6 = f32[4,2,256]{2,1,0:T(2,128)S(1)} fusion(bf16[8,2,1024,256]{3,2,1,0:T(8,128)(2,1)} %param.21, f32[4,2,1024]{2,1,0:T(2,128)S(1)} %get-tuple-element.96, pred[4,1024]{1,0:T(4,128)(4,1)S(1)} %iota_compare_fusion.2, f32[4,2]{1,0:T(4,128)S(1)} %get-tuple-element.36), kind=kOutput, calls=%fused_computation.10 | convolution fusion | flops 4218880 | bytes 2142240 | tf_op jit(solution)/shard_map/rhk,rkf->rhf/dot_general | solution.py:167
  103.4 3.1 %collective-permute-start.12 = (f32[4,2,130]{0,1,2:T(2,128)S(1)}, f32[4,2,130]{0,1,2:T(2,128)S(1)}, u32[]{:S(2)}, u32[]{:S(2)}) collective-permute-start(f32[4,2,130]{0,1,2:T(2,128)S(1)} %pad_maximum_fusion.3), channel_id=1, source_target_pairs={{8,0},{16,8},{24,16},{32,24},{40,32},{48,40},{56,48},{64,56},{72,6... | collective-permute-start | bytes 12488 | tf_op jit(solution)/shard_map/ppermute | solution.py:268
  107.0 0.3 collective-permute-start.11
  107.3 0.7 fusion.51
  108.1 2.3 %fusion.98 = (f32[2,512]{1,0:T(2,128)S(1)}, bf16[2,512,1024]{2,1,0:T(8,128)(2,1)S(1)}) fusion(f32[2,512,1024]{2,1,0:T(8,128)S(1)} %fusion.51, pred[512,1024]{1,0:T(8,128)(4,1)S(1)} %copy-done.4), kind=kOutput, calls=%fused_computation.176 | output fusion | flops 8389631 | bytes 6819840 | tf_op jit(solution)/shard_map/while/body/eval_jaxpr/sub | solution.py:125
  110.4 0.8 fusion.25
  111.3 0.8 copy.253
  112.2 3.4 %collective-permute-done.11 = f32[4,2,130]{0,1,2:T(2,128)S(1)} collective-permute-done((f32[4,2,130]{0,1,2:T(2,128)S(1)}, f32[4,2,130]{0,1,2:T(2,128)S(1)}, u32[]{:S(2)}, u32[]{:S(2)}) %collective-permute-start.11) | collective-permute-done | bytes 4192 | tf_op jit(solution)/shard_map/ppermute | solution.py:268
  116.4 0.7 copy.252
  (111 shorter events, 4.7 us)
Async XLA Ops:
  0.6 14.4 %copy-start.2 = (bf16[4,2,256,256]{3,2,1,0:T(8,128)(2,1)S(1)}, bf16[4,2,256,256]{3,2,1,0:T(8,128)(2,1)}, u32[]{:S(2)}) copy-start(bf16[4,2,256,256]{3,2,1,0:T(8,128)(2,1)} %param.19) | copy-start | bytes 3145732
  0.6 41.6 %copy-start.7 = (f32[4096]{0:T(1024)S(1)}, f32[4096]{0:T(1024)}, u32[]{:S(2)}) copy-start(f32[4096]{0:T(1024)} %param.13) | copy-start | bytes 49156
  0.7 42.2 %copy-start.8 = (f32[4096]{0:T(1024)S(1)}, f32[4096]{0:T(1024)}, u32[]{:S(2)}) copy-start(f32[4096]{0:T(1024)} %param.14) | copy-start | bytes 49156
  4.0 36.0 %collective-permute-start = (bf16[516,512]{1,0:T(8,128)(2,1)S(1)}, bf16[516,512]{1,0:T(8,128)(2,1)S(1)}, u32[]{:S(2)}, u32[]{:S(2)}) collective-permute-start(bf16[516,512]{1,0:T(8,128)(2,1)S(1)} %get-tuple-element.85), channel_id=1, source_target_pairs={{0,2},{2,4},{4,6},{6,0},{1,3},{3,5},{5,7},{7,1},{8,10},{10,12},{12... | collective-permute-start | bytes 1585160 | tf_op jit(solution)/shard_map/ppermute | solution.py:222
  5.6 33.1 %collective-permute-start.1 = (bf16[516,512]{1,0:T(8,128)(2,1)S(1)}, bf16[516,512]{1,0:T(8,128)(2,1)S(1)}, u32[]{:S(2)}, u32[]{:S(2)}) collective-permute-start(bf16[516,512]{1,0:T(8,128)(2,1)S(1)} %get-tuple-element.85), channel_id=1, source_target_pairs={{0,6},{2,0},{4,2},{6,4},{1,7},{3,1},{5,3},{7,5},{8,14},{10,8},{12,... | collective-permute-start | bytes 1585160 | tf_op jit(solution)/shard_map/ppermute | solution.py:223
  7.2 28.2 %collective-permute-start.4 = (bf16[516,512]{1,0:T(8,128)(2,1)S(1)}, bf16[516,512]{1,0:T(8,128)(2,1)}, u32[]{:S(2)}, u32[]{:S(2)}) collective-permute-start(bf16[516,512]{1,0:T(8,128)(2,1)S(1)} %get-tuple-element.85), channel_id=1, source_target_pairs={{0,1},{1,0},{2,3},{3,2},{4,5},{5,4},{6,7},{7,6},{8,9},{9,8},{10,11... | collective-permute-start | bytes 1585160 | tf_op jit(solution)/shard_map/ppermute | solution.py:229
  7.7 4.1 %copy-start.12 = (pred[2,2]{1,0:T(4,128)(4,1)}, pred[2,2]{1,0:T(4,128)(4,1)S(1)}, u32[]{:S(2)}) copy-start(pred[2,2]{1,0:T(4,128)(4,1)S(1)} %iota_compare_fusion.5) | copy-start | bytes 16
  35.4 21.9 %collective-permute-start.5 = (bf16[516,512]{1,0:T(8,128)(2,1)}, bf16[516,512]{1,0:T(8,128)(2,1)S(1)}, u32[]{:S(2)}, u32[]{:S(2)}) collective-permute-start(bf16[516,512]{1,0:T(8,128)(2,1)} %collective-permute-done.4), channel_id=1, source_target_pairs={{0,2},{2,4},{4,6},{6,0},{1,3},{3,5},{5,7},{7,1},{8,10},{10,12},{12... | collective-permute-start | bytes 1585160 | tf_op jit(solution)/shard_map/ppermute | solution.py:222
  35.7 17.8 %collective-permute-start.6 = (bf16[516,512]{1,0:T(8,128)(2,1)}, bf16[516,512]{1,0:T(8,128)(2,1)S(1)}, u32[]{:S(2)}, u32[]{:S(2)}) collective-permute-start(bf16[516,512]{1,0:T(8,128)(2,1)} %collective-permute-done.4), channel_id=1, source_target_pairs={{0,6},{2,0},{4,2},{6,4},{1,7},{3,1},{5,3},{7,5},{8,14},{10,8},{12,... | collective-permute-start | bytes 1585160 | tf_op jit(solution)/shard_map/ppermute | solution.py:223
  39.4 12.1 %collective-permute-start.3 = (bf16[258,512]{1,0:T(8,128)(2,1)}, bf16[258,512]{1,0:T(8,128)(2,1)}, u32[]{:S(2)}, u32[]{:S(2)}) collective-permute-start(bf16[258,512]{1,0:T(8,128)(2,1)} %slice.199), channel_id=1, source_target_pairs={{0,6},{2,0},{4,2},{6,4},{1,7},{3,1},{5,3},{7,5},{8,14},{10,8},{12,... | collective-permute-start | bytes 792584 | tf_op jit(solution)/shard_map/ppermute | solution.py:225
  40.7 10.8 %collective-permute-start.2 = (bf16[258,512]{1,0:T(8,128)(2,1)}, bf16[258,512]{1,0:T(8,128)(2,1)}, u32[]{:S(2)}, u32[]{:S(2)}) collective-permute-start(bf16[258,512]{1,0:T(8,128)(2,1)} %slice.198), channel_id=1, source_target_pairs={{0,2},{2,4},{4,6},{6,0},{1,3},{3,5},{5,7},{7,1},{8,10},{10,12},{12... | collective-permute-start | bytes 792584 | tf_op jit(solution)/shard_map/ppermute | solution.py:225
  53.5 7.8 %collective-permute-start.8 = (bf16[258,512]{1,0:T(8,128)(2,1)S(1)}, bf16[258,512]{1,0:T(8,128)(2,1)S(1)}, u32[]{:S(2)}, u32[]{:S(2)}) collective-permute-start(bf16[258,512]{1,0:T(8,128)(2,1)S(1)} %slice.201), channel_id=1, source_target_pairs={{0,6},{2,0},{4,2},{6,4},{1,7},{3,1},{5,3},{7,5},{8,14},{10,8},{12,... | collective-permute-start | bytes 792584 | tf_op jit(solution)/shard_map/ppermute | solution.py:225
  57.3 7.9 %collective-permute-start.7 = (bf16[258,512]{1,0:T(8,128)(2,1)S(1)}, bf16[258,512]{1,0:T(8,128)(2,1)S(1)}, u32[]{:S(2)}, u32[]{:S(2)}) collective-permute-start(bf16[258,512]{1,0:T(8,128)(2,1)S(1)} %slice.200), channel_id=1, source_target_pairs={{0,2},{2,4},{4,6},{6,0},{1,3},{3,5},{5,7},{7,1},{8,10},{10,12},{12... | collective-permute-start | bytes 792584 | tf_op jit(solution)/shard_map/ppermute | solution.py:225
  81.6 2.3 %copy-start.9 = (f32[4,16]{1,0:T(4,128)S(1)}, f32[4,16]{1,0:T(4,128)}, u32[]{:S(2)}) copy-start(f32[4,16]{1,0:T(4,128)} %get-tuple-element.94) | copy-start | bytes 772
  81.6 2.5 %copy-start.10 = (f32[4,1]{1,0:T(4,128)S(1)}, f32[4,1]{1,0:T(4,128)}, u32[]{:S(2)}) copy-start(f32[4,1]{1,0:T(4,128)} %get-tuple-element.90) | copy-start | bytes 52
  81.6 2.4 %copy-start.11 = (f32[4,1]{1,0:T(4,128)S(1)}, f32[4,1]{1,0:T(4,128)}, u32[]{:S(2)}) copy-start(f32[4,1]{1,0:T(4,128)} %get-tuple-element.91) | copy-start | bytes 52
  82.5 7.8 %copy-start.5 = (bf16[4,256,256]{2,1,0:T(8,128)(2,1)S(1)}, bf16[4,256,256]{2,1,0:T(8,128)(2,1)}, u32[]{:S(2)}) copy-start(bf16[4,256,256]{2,1,0:T(8,128)(2,1)} %get-tuple-element.65) | copy-start | bytes 1572868
  83.8 7.1 %copy-start = (f32[512,16]{1,0:T(8,128)S(1)}, f32[512,16]{1,0:T(8,128)}, u32[]{:S(2)}) copy-start(f32[512,16]{1,0:T(8,128)} %copy.221) | copy-start | bytes 98308
  84.0 9.4 %collective-permute-start.9 = (f32[4,257]{1,0:T(4,128)S(1)}, f32[4,257]{1,0:T(4,128)S(1)}, u32[]{:S(2)}, u32[]{:S(2)}) collective-permute-start(f32[4,257]{1,0:T(4,128)S(1)} %get-tuple-element.82), channel_id=1, source_target_pairs={{0,8},{8,16},{16,24},{24,32},{32,40},{40,48},{48,56},{56,64},{64,7... | collective-permute-start | bytes 12344 | tf_op jit(solution)/shard_map/ppermute | solution.py:262
  84.1 9.5 %collective-permute-start.10 = (f32[4,257]{1,0:T(4,128)S(1)}, f32[4,257]{1,0:T(4,128)S(1)}, u32[]{:S(2)}, u32[]{:S(2)}) collective-permute-start(f32[4,257]{1,0:T(4,128)S(1)} %get-tuple-element.81), channel_id=1, source_target_pairs={{8,0},{16,8},{24,16},{32,24},{40,32},{48,40},{56,48},{64,56},{72,6... | collective-permute-start | bytes 12344 | tf_op jit(solution)/shard_map/ppermute | solution.py:262
  89.9 3.2 %copy-start.3 = (bf16[512,1,2,128]{3,2,1,0:T(2,128)(2,1)S(1)}, bf16[512,1,2,128]{3,2,1,0:T(2,128)(2,1)}, u32[]{:S(2)}) copy-start(bf16[512,1,2,128]{3,2,1,0:T(2,128)(2,1)} %slice.219) | copy-start | bytes 786436
  93.9 9.0 %copy-start.13 = (pred[2,2]{1,0:T(4,128)(4,1)S(1)}, pred[2,2]{1,0:T(4,128)(4,1)}, u32[]{:S(2)}) copy-start(pred[2,2]{1,0:T(4,128)(4,1)} %copy-done.12) | copy-start | bytes 16
  96.2 11.1 %copy-start.1 = (bf16[512,2,128]{2,0,1:T(8,128)(2,1)S(1)}, bf16[512,2,128]{2,0,1:T(8,128)(2,1)}, u32[]{:S(2)}) copy-start(bf16[512,2,128]{2,0,1:T(8,128)(2,1)} %copy.226) | copy-start | bytes 786436
  100.6 7.4 %copy-start.4 = (pred[512,1024]{1,0:T(8,128)(4,1)S(1)}, pred[512,1024]{1,0:T(8,128)(4,1)}, u32[]{:S(2)}) copy-start(pred[512,1024]{1,0:T(8,128)(4,1)} %pad_add_fusion) | copy-start | bytes 1572868
  103.4 8.7 %collective-permute-start.12 = (f32[4,2,130]{0,1,2:T(2,128)S(1)}, f32[4,2,130]{0,1,2:T(2,128)S(1)}, u32[]{:S(2)}, u32[]{:S(2)}) collective-permute-start(f32[4,2,130]{0,1,2:T(2,128)S(1)} %pad_maximum_fusion.3), channel_id=1, source_target_pairs={{8,0},{16,8},{24,16},{32,24},{40,32},{48,40},{56,48},{64,56},{72,6... | collective-permute-start | bytes 12488 | tf_op jit(solution)/shard_map/ppermute | solution.py:268
  107.0 8.6 %collective-permute-start.11 = (f32[4,2,130]{0,1,2:T(2,128)S(1)}, f32[4,2,130]{0,1,2:T(2,128)S(1)}, u32[]{:S(2)}, u32[]{:S(2)}) collective-permute-start(f32[4,2,130]{0,1,2:T(2,128)S(1)} %pad_maximum_fusion.2), channel_id=1, source_target_pairs={{0,8},{8,16},{16,24},{24,32},{32,40},{40,48},{48,56},{56,64},{64,7... | collective-permute-start | bytes 12488 | tf_op jit(solution)/shard_map/ppermute | solution.py:268
  108.1 2.4 %copy-start.6 = (bf16[1,1,512,256]{2,3,1,0:T(8,128)(2,1)S(1)}, bf16[1,1,512,256]{2,3,1,0:T(8,128)(2,1)}, u32[]{:S(2)}) copy-start(bf16[1,1,512,256]{2,3,1,0:T(8,128)(2,1)} %copy.213) | copy-start | bytes 786436

commit v12 on v10

--- a/solution.py
+++ b/solution.py
@@ -79,7 +79,7 @@
 def qkv_matmul(whole, first, rows, gain, shift, weight, order):
     depth = whole.shape[1]
     parts, _, width = weight.shape
-    chunk = 128 if rows % 128 == 0 else rows
+    chunk = 256 if rows % 256 == 0 else rows
     skip = first // chunk
     return pl.pallas_call(
         qkv_kernel,

time: 114 us -> 114 us (level)
  no operation moved by 1% of the time
where the time goes in v12:
time: 114 us; the launch traced here: 113 us
  starting transfers between devices  34.6 us (30%)
  local copies, waits for them, and re-layouts  27.3 us (24%)
  Pallas kernels  14.1 us (12%)
  other arithmetic  13.8 us (12%)
  matrix products  10.9 us (10%)
  waiting for transfers between devices  10.8 us (9%)
  between operations  1.76 us (2%)
    ppermute x2, starting transfers between devices, ask(): got = lax.ppermute(packed, 'group', pairs)  15.1 us
    pallas_call x2, Pallas kernels, qkv_matmul(): pl.pallas_call(qkv_kernel, out_shape=jax.ShapeDtypeStruct((rows, parts *...  14.1 us
    unnamed x43, local copies, waits for them, and re-layouts  11.6 us
    ppermute x1, starting transfers between devices, local(): partner = lax.ppermute(rows, 'tz', [(0, 1), (1, 0)])  6.91 us
    dot_general x3, matrix products, piece_rows(): jnp.einsum('rkf,rfh->rhk', keys, spread, preferred_element_type=jnp.float32)  4.99 us
    ppermute x2, starting transfers between devices, around(): lax.ppermute(above[half:], 'ty', down)  4.82 us
    dot_general x3, matrix products, piece_rows(): jnp.einsum('rhk,rkf->rhf', weights.astype(jnp.bfloat16), values, preferre...  4.3 us
    ppermute x1, waiting for transfers between devices, local(): partner = lax.ppermute(rows, 'tz', [(0, 1), (1, 0)])  4 us
  transfers between devices with their start and end apart: 13, of which 4 were waited for; matrix products, arithmetic and copies ran while one was open for 33% of the time, Pallas kernels for 0%

profile of v12, /device:TPU:1, one launch (start us, length us, event | category | flops | bytes accessed | tf_op | source)
XLA Modules:
  0.0 113.2 jit_solution(11947061239992893824)
XLA Ops:
  0.7 2.0 %constant_dynamic-update-slice_fusion.1 = (bf16[516,512]{1,0:T(8,128)(2,1)S(1)}, bf16[516,4096]{1,0:T(8,128)(2,1)}) fusion(bf16[512,512]{1,0:T(8,128)(2,1)} %param.11), kind=kLoop, calls=%fused_computation.78 | loop fusion | bytes 1572864
  2.7 1.3 %constant_dynamic-update-slice_fusion = (bf16[516,512]{1,0:T(8,128)(2,1)S(1)}, bf16[516,4096]{1,0:T(8,128)(2,1)}) fusion(bf16[516,512]{1,0:T(8,128)(2,1)S(1)} %get-tuple-element.51, bf16[4,512]{1,0:T(4,128)(2,1)} %param.12, bf16[516,4096]{1,0:T(8,128)(2,1)} %get-tuple-element.52), kind=kLoop, calls=%fused_computation.77 | loop fusion | bytes 12288 | tf_op jit(solution)/shard_map/concatenate | solution.py:213
  4.0 2.1 %collective-permute-start = (bf16[516,512]{1,0:T(8,128)(2,1)S(1)}, bf16[516,512]{1,0:T(8,128)(2,1)S(1)}, u32[]{:S(2)}, u32[]{:S(2)}) collective-permute-start(bf16[516,512]{1,0:T(8,128)(2,1)S(1)} %get-tuple-element.65), channel_id=1, source_target_pairs={{0,2},{2,4},{4,6},{6,0},{1,3},{3,5},{5,7},{7,1},{8,10},{10,12},{12... | collective-permute-start | bytes 1585160 | tf_op jit(solution)/shard_map/ppermute | solution.py:222
  6.1 1.4 %collective-permute-start.1 = (bf16[516,512]{1,0:T(8,128)(2,1)S(1)}, bf16[516,512]{1,0:T(8,128)(2,1)S(1)}, u32[]{:S(2)}, u32[]{:S(2)}) collective-permute-start(bf16[516,512]{1,0:T(8,128)(2,1)S(1)} %get-tuple-element.65), channel_id=1, source_target_pairs={{0,6},{2,0},{4,2},{6,4},{1,7},{3,1},{5,3},{7,5},{8,14},{10,8},{12,... | collective-permute-start | bytes 1585160 | tf_op jit(solution)/shard_map/ppermute | solution.py:223
  7.5 6.9 %collective-permute-start.4 = (bf16[516,512]{1,0:T(8,128)(2,1)S(1)}, bf16[516,512]{1,0:T(8,128)(2,1)}, u32[]{:S(2)}, u32[]{:S(2)}) collective-permute-start(bf16[516,512]{1,0:T(8,128)(2,1)S(1)} %get-tuple-element.65), channel_id=1, source_target_pairs={{0,1},{1,0},{2,3},{3,2},{4,5},{5,4},{6,7},{7,6},{8,9},{9,8},{10,11... | collective-permute-start | bytes 1585160 | tf_op jit(solution)/shard_map/ppermute | solution.py:229
  14.5 1.0 convert_reduce_fusion
  15.4 1.6 %slice_reduce_fusion = (s32[4]{0:T(128)S(1)}, f32[4,1]{1,0:T(4,128)}, f32[4,1]{1,0:T(4,128)}) fusion(s32[4,3]{1,0:T(4,128)} %param.20), kind=kLoop, calls=%fused_computation.141 | loop fusion | flops 8 | bytes 96 | tf_op jit(solution)/shard_map/slice | solution.py:248
  17.1 0.6 iota_compare_fusion.3
  17.8 0.6 broadcast_bitcast_fusion
  19.2 0.7 multiply_cosine_fusion.1
  19.8 0.2 multiply_cosine_fusion
  20.0 1.1 fusion.103
  21.2 1.0 pad_add_fusion
  22.3 1.1 slice_bitcast_fusion.1
  23.4 4.0 %collective-permute-done.4 = bf16[516,512]{1,0:T(8,128)(2,1)} collective-permute-done((bf16[516,512]{1,0:T(8,128)(2,1)S(1)}, bf16[516,512]{1,0:T(8,128)(2,1)}, u32[]{:S(2)}, u32[]{:S(2)}) %collective-permute-start.4) | collective-permute-done | bytes 528416 | tf_op jit(solution)/shard_map/ppermute | solution.py:229
  27.4 0.5 collective-permute-start.5
  27.9 2.2 %collective-permute-start.6 = (bf16[516,512]{1,0:T(8,128)(2,1)}, bf16[516,512]{1,0:T(8,128)(2,1)S(1)}, u32[]{:S(2)}, u32[]{:S(2)}) collective-permute-start(bf16[516,512]{1,0:T(8,128)(2,1)} %collective-permute-done.4), channel_id=1, source_target_pairs={{0,6},{2,0},{4,2},{6,4},{1,7},{3,1},{5,3},{7,5},{8,14},{10,8},{12,... | collective-permute-start | bytes 1585160 | tf_op jit(solution)/shard_map/ppermute | solution.py:223
  30.1 0.7 slice.198
  30.8 0.8 slice.199
  31.6 2.7 %collective-permute-start.3 = (bf16[258,512]{1,0:T(8,128)(2,1)}, bf16[258,512]{1,0:T(8,128)(2,1)}, u32[]{:S(2)}, u32[]{:S(2)}) collective-permute-start(bf16[258,512]{1,0:T(8,128)(2,1)} %slice.199), channel_id=1, source_target_pairs={{0,6},{2,0},{4,2},{6,4},{1,7},{3,1},{5,3},{7,5},{8,14},{10,8},{12,... | collective-permute-start | bytes 792584 | tf_op jit(solution)/shard_map/ppermute | solution.py:225
  34.4 0.6 gather_fusion
  35.0 0.6 gather_fusion.1
  35.6 0.7 add.144
  36.3 0.7 copy.270
  37.1 0.8 copy.211
  38.1 0.8 copy.214
  38.9 0.8 copy.207
  39.7 0.6 concatenate.139
  40.4 0.9 constant_dynamic-update-slice_fusion.6
  41.3 0.9 constant_dynamic-update-slice_fusion.5
  42.1 3.6 %collective-permute-done.2 = bf16[258,512]{1,0:T(8,128)(2,1)} collective-permute-done((bf16[258,512]{1,0:T(8,128)(2,1)}, bf16[258,512]{1,0:T(8,128)(2,1)}, u32[]{:S(2)}, u32[]{:S(2)}) %collective-permute-start.2) | collective-permute-done | bytes 264224 | tf_op jit(solution)/shard_map/ppermute | solution.py:225
  45.8 2.0 %maximum_dynamic-update-slice_fusion.1 = bf16[516,4096]{1,0:T(8,128)(2,1)} fusion(bf16[516,4096]{1,0:T(8,128)(2,1)} %constant_dynamic-update-slice_fusion.5, bf16[258,512]{1,0:T(8,128)(2,1)} %collective-permute-done.3, bf16[258,512]{1,0:T(8,128)(2,1)} %collective-permute-done.2), kind=kLoop, calls=%fused_computation.43 | loop fusion | flops 1056768 | bytes 1073152
  47.7 0.9 collective-permute-start.7
  48.7 2.1 %collective-permute-start.8 = (bf16[258,512]{1,0:T(8,128)(2,1)S(1)}, bf16[258,512]{1,0:T(8,128)(2,1)S(1)}, u32[]{:S(2)}, u32[]{:S(2)}) collective-permute-start(bf16[258,512]{1,0:T(8,128)(2,1)S(1)} %slice.201), channel_id=1, source_target_pairs={{0,6},{2,0},{4,2},{6,4},{1,7},{3,1},{5,3},{7,5},{8,14},{10,8},{12,... | collective-permute-start | bytes 792584 | tf_op jit(solution)/shard_map/ppermute | solution.py:225
  50.8 1.9 %constant_dynamic-update-slice_fusion.4 = bf16[516,4096]{1,0:T(8,128)(2,1)} fusion(bf16[516,4096]{1,0:T(8,128)(2,1)} %maximum_dynamic-update-slice_fusion.1, bf16[516,512]{1,0:T(8,128)(2,1)} %collective-permute-done.4), kind=kLoop, calls=%fused_computation.81 | loop fusion | bytes 1064960
  52.8 0.9 constant_dynamic-update-slice_fusion.3
  53.7 0.9 constant_dynamic-update-slice_fusion.2
  54.7 0.9 maximum_dynamic-update-slice_fusion.x_ref
  55.6 0.8 slice.211.x_ref
  56.4 4.4 %shard_map.123 = f32[4,768]{1,0:T(4,128)S(1)} custom-call(s32[8]{0:T(128)S(1)} %pad_add_fusion.1.order_ref, bf16[4,4096]{1,0:T(4,128)(2,1)S(1)} %slice.211.x_ref, f32[1,4096]{1,0:T(1,128)S(1)} %bitcast.135, f32[1,4096]{1,0:T(1,128)S(1)} %bitcast.137, bf16[3,4096,256]{2,1,0:T(8,128)(2,1)} %bitcast.139), custom_call_target="tpu_custom_call" | custom-call | flops 25165824 | bytes 6336512 | tf_op jit(solution)/shard_map/pallas_call | solution.py:84
  61.0 9.6 %shard_map.122 = f32[512,768]{1,0:T(8,128)S(1)} custom-call(s32[8]{0:T(128)S(1)} %pad_add_fusion.1.order_ref, bf16[516,4096]{1,0:T(8,128)(2,1)} %maximum_dynamic-update-slice_fusion.x_ref, f32[1,4096]{1,0:T(1,128)S(1)} %bitcast.136, f32[1,4096]{1,0:T(1,128)S(1)} %bitcast.138, bf16[3,4096,256]{2,1,0:T(8,128)(2,1)} %bitcast.140), custom_call_target="tpu_custom_call" | custom-call | flops 3221225472 | bytes 12058624 | tf_op jit(solution)/shard_map/pallas_call | solution.py:84
  70.8 0.8 reshape.539
  71.6 0.4 fusion.102
  72.0 0.9 slice.202
  73.2 4.4 %collective-permute-start.9 = (f32[4,257]{1,0:T(4,128)S(1)}, f32[4,257]{1,0:T(4,128)S(1)}, u32[]{:S(2)}, u32[]{:S(2)}) collective-permute-start(f32[4,257]{1,0:T(4,128)S(1)} %get-tuple-element.63), channel_id=1, source_target_pairs={{8,0},{16,8},{24,16},{32,24},{40,32},{48,40},{56,48},{64,56},{72,6... | collective-permute-start | bytes 12344 | tf_op jit(solution)/shard_map/ppermute | solution.py:262
  77.6 10.8 %collective-permute-start.11 = (f32[4,257]{1,0:T(4,128)S(1)}, f32[4,257]{1,0:T(4,128)S(1)}, u32[]{:S(2)}, u32[]{:S(2)}) collective-permute-start(f32[4,257]{1,0:T(4,128)S(1)} %get-tuple-element.64), channel_id=1, source_target_pairs={{0,8},{8,16},{16,24},{24,32},{32,40},{40,48},{48,56},{56,64},{64,7... | collective-permute-start | bytes 12344 | tf_op jit(solution)/shard_map/ppermute | solution.py:262
  88.7 1.1 copy.263
  89.9 1.4 %subtract_convert_fusion.1 = (bf16[512,2,16]{2,0,1:T(8,128)(2,1)S(1)}, bf16[512,2,16]{2,0,1:T(8,128)(2,1)S(1)}, bf16[512,2,16]{2,0,1:T(8,128)(2,1)S(1)}, bf16[512,2,16]{2,0,1:T(8,128)(2,1)S(1)}) fusion(f32[512,2,128]{2,0,1:T(8,128)S(1)} %get-tuple-element.84, f32[512,16]{1,0:T(8,128)} %copy.211, f32[512,16]{1,0:T(8,128)S(1)} %copy.210, ...), kind=kLoop, calls=%fused_computation.64 | loop fusion | flops 262144 | bytes 458752 | tf_op jit(solution)/shard_map/convert.21
  91.3 0.8 fusion.51
  92.2 2.3 %fusion.104 = (f32[2,512]{1,0:T(2,128)S(1)}, bf16[2,512,1024]{2,1,0:T(8,128)(2,1)S(1)}) fusion(f32[2,512,1024]{2,1,0:T(8,128)S(1)} %fusion.51, pred[512,1024]{1,0:T(8,128)(4,1)S(1)} %copy-done.2), kind=kOutput, calls=%fused_computation.180 | output fusion | flops 8389631 | bytes 6819840 | tf_op jit(solution)/shard_map/while/body/eval_jaxpr/sub | solution.py:125
  94.6 0.8 fusion.25
  95.5 0.3 fusion.107
  95.9 0.2 fusion.44
  96.4 2.3 %fusion.106 = (f32[4,2]{1,0:T(4,128)S(1)}, f32[4,2,1024]{2,1,0:T(2,128)S(1)}) fusion(bf16[8,2,1024,256]{3,2,1,0:T(8,128)(2,1)} %param.21, pred[256,2]{0,1:T(4,128)(4,1)S(1)} %bitcast.157, bf16[4,256]{1,0:T(4,128)(2,1)S(1)} %slice.322, pred[4,1024]{1,0:T(4,128)(4,1)S(1)} %iota_compare_fusion.2), kind=kOutput, calls=%fused_computation.182 | convolution fusion | flops 4220920 | bytes 2136608 | tf_op jit(solution)/shard_map/rkf,rfh->rhk/dot_general | solution.py:160
  98.7 2.0 %fusion.6 = f32[4,2,256]{2,1,0:T(2,128)S(1)} fusion(bf16[8,2,1024,256]{3,2,1,0:T(8,128)(2,1)} %param.21, f32[4,2,1024]{2,1,0:T(2,128)S(1)} %get-tuple-element.80, pred[4,1024]{1,0:T(4,128)(4,1)S(1)} %iota_compare_fusion.2, f32[4,2]{1,0:T(4,128)S(1)} %get-tuple-element.79), kind=kOutput, calls=%fused_computation.10 | convolution fusion | flops 4218880 | bytes 2142240 | tf_op jit(solution)/shard_map/rhk,rkf->rhf/dot_general | solution.py:167
  100.7 0.2 fusion.66
  101.2 2.3 %fusion.105 = (f32[4,2]{1,0:T(4,128)S(1)}, f32[4,2,1024]{2,1,0:T(2,128)S(1)}) fusion(bf16[8,2,1024,256]{3,2,1,0:T(8,128)(2,1)} %param.21, pred[256,2]{0,1:T(4,128)(4,1)S(1)} %bitcast.158, bf16[4,256]{1,0:T(4,128)(2,1)S(1)} %slice.320, pred[4,1024]{1,0:T(4,128)(4,1)S(1)} %iota_compare_fusion.1), kind=kOutput, calls=%fused_computation.181 | convolution fusion | flops 4220920 | bytes 2136608 | tf_op jit(solution)/shard_map/rkf,rfh->rhk/dot_general | solution.py:160
  103.5 2.0 %fusion.2 = f32[4,2,256]{2,1,0:T(2,128)S(1)} fusion(bf16[8,2,1024,256]{3,2,1,0:T(8,128)(2,1)} %param.21, f32[4,2,1024]{2,1,0:T(2,128)S(1)} %get-tuple-element.78, pred[4,1024]{1,0:T(4,128)(4,1)S(1)} %iota_compare_fusion.1, f32[4,2]{1,0:T(4,128)S(1)} %get-tuple-element.77), kind=kOutput, calls=%fused_computation.6 | convolution fusion | flops 4218880 | bytes 2142240 | tf_op jit(solution)/shard_map/rhk,rkf->rhf/dot_general | solution.py:167
  106.3 0.3 collective-permute-start.10
  107.0 0.4 collective-permute-start.12
  107.7 0.8 copy.247
  108.5 0.6 collective-permute-done.10
  109.1 2.6 %collective-permute-done.12 = f32[4,2,130]{0,1,2:T(2,128)S(1)} collective-permute-done((f32[4,2,130]{0,1,2:T(2,128)S(1)}, f32[4,2,130]{0,1,2:T(2,128)S(1)}, u32[]{:S(2)}, u32[]{:S(2)}) %collective-permute-start.12) | collective-permute-done | bytes 4192 | tf_op jit(solution)/shard_map/ppermute | solution.py:268
  112.5 0.7 copy.246
  (108 shorter events, 4.8 us)
Async XLA Ops:
  0.6 21.7 %copy-start.1 = (bf16[4,2,256,256]{3,2,1,0:T(8,128)(2,1)S(1)}, bf16[4,2,256,256]{3,2,1,0:T(8,128)(2,1)}, u32[]{:S(2)}) copy-start(bf16[4,2,256,256]{3,2,1,0:T(8,128)(2,1)} %param.19) | copy-start | bytes 3145732
  0.6 33.7 %copy-start.6 = (f32[4096]{0:T(1024)S(1)}, f32[4096]{0:T(1024)}, u32[]{:S(2)}) copy-start(f32[4096]{0:T(1024)} %param.13) | copy-start | bytes 49156
  0.7 34.3 %copy-start.7 = (f32[4096]{0:T(1024)S(1)}, f32[4096]{0:T(1024)}, u32[]{:S(2)}) copy-start(f32[4096]{0:T(1024)} %param.14) | copy-start | bytes 49156
  4.0 26.1 %collective-permute-start = (bf16[516,512]{1,0:T(8,128)(2,1)S(1)}, bf16[516,512]{1,0:T(8,128)(2,1)S(1)}, u32[]{:S(2)}, u32[]{:S(2)}) collective-permute-start(bf16[516,512]{1,0:T(8,128)(2,1)S(1)} %get-tuple-element.65), channel_id=1, source_target_pairs={{0,2},{2,4},{4,6},{6,0},{1,3},{3,5},{5,7},{7,1},{8,10},{10,12},{12... | collective-permute-start | bytes 1585160 | tf_op jit(solution)/shard_map/ppermute | solution.py:222
  6.1 24.7 %collective-permute-start.1 = (bf16[516,512]{1,0:T(8,128)(2,1)S(1)}, bf16[516,512]{1,0:T(8,128)(2,1)S(1)}, u32[]{:S(2)}, u32[]{:S(2)}) collective-permute-start(bf16[516,512]{1,0:T(8,128)(2,1)S(1)} %get-tuple-element.65), channel_id=1, source_target_pairs={{0,6},{2,0},{4,2},{6,4},{1,7},{3,1},{5,3},{7,5},{8,14},{10,8},{12,... | collective-permute-start | bytes 1585160 | tf_op jit(solution)/shard_map/ppermute | solution.py:223
  7.5 19.9 %collective-permute-start.4 = (bf16[516,512]{1,0:T(8,128)(2,1)S(1)}, bf16[516,512]{1,0:T(8,128)(2,1)}, u32[]{:S(2)}, u32[]{:S(2)}) collective-permute-start(bf16[516,512]{1,0:T(8,128)(2,1)S(1)} %get-tuple-element.65), channel_id=1, source_target_pairs={{0,1},{1,0},{2,3},{3,2},{4,5},{5,4},{6,7},{7,6},{8,9},{9,8},{10,11... | collective-permute-start | bytes 1585160 | tf_op jit(solution)/shard_map/ppermute | solution.py:229
  17.0 2.1 %copy-start.11 = (pred[2,2]{1,0:T(4,128)(4,1)}, pred[2,2]{1,0:T(4,128)(4,1)S(1)}, u32[]{:S(2)}) copy-start(pred[2,2]{1,0:T(4,128)(4,1)S(1)} %iota_compare_fusion.5) | copy-start | bytes 16
  27.4 20.3 %collective-permute-start.5 = (bf16[516,512]{1,0:T(8,128)(2,1)}, bf16[516,512]{1,0:T(8,128)(2,1)S(1)}, u32[]{:S(2)}, u32[]{:S(2)}) collective-permute-start(bf16[516,512]{1,0:T(8,128)(2,1)} %collective-permute-done.4), channel_id=1, source_target_pairs={{0,2},{2,4},{4,6},{6,0},{1,3},{3,5},{5,7},{7,1},{8,10},{10,12},{12... | collective-permute-start | bytes 1585160 | tf_op jit(solution)/shard_map/ppermute | solution.py:222
  27.9 20.8 %collective-permute-start.6 = (bf16[516,512]{1,0:T(8,128)(2,1)}, bf16[516,512]{1,0:T(8,128)(2,1)S(1)}, u32[]{:S(2)}, u32[]{:S(2)}) collective-permute-start(bf16[516,512]{1,0:T(8,128)(2,1)} %collective-permute-done.4), channel_id=1, source_target_pairs={{0,6},{2,0},{4,2},{6,4},{1,7},{3,1},{5,3},{7,5},{8,14},{10,8},{12,... | collective-permute-start | bytes 1585160 | tf_op jit(solution)/shard_map/ppermute | solution.py:223
  30.8 14.9 %collective-permute-start.2 = (bf16[258,512]{1,0:T(8,128)(2,1)}, bf16[258,512]{1,0:T(8,128)(2,1)}, u32[]{:S(2)}, u32[]{:S(2)}) collective-permute-start(bf16[258,512]{1,0:T(8,128)(2,1)} %slice.198), channel_id=1, source_target_pairs={{0,2},{2,4},{4,6},{6,0},{1,3},{3,5},{5,7},{7,1},{8,10},{10,12},{12... | collective-permute-start | bytes 792584 | tf_op jit(solution)/shard_map/ppermute | solution.py:225
  31.6 14.2 %collective-permute-start.3 = (bf16[258,512]{1,0:T(8,128)(2,1)}, bf16[258,512]{1,0:T(8,128)(2,1)}, u32[]{:S(2)}, u32[]{:S(2)}) collective-permute-start(bf16[258,512]{1,0:T(8,128)(2,1)} %slice.199), channel_id=1, source_target_pairs={{0,6},{2,0},{4,2},{6,4},{1,7},{3,1},{5,3},{7,5},{8,14},{10,8},{12,... | collective-permute-start | bytes 792584 | tf_op jit(solution)/shard_map/ppermute | solution.py:225
  47.7 6.9 %collective-permute-start.7 = (bf16[258,512]{1,0:T(8,128)(2,1)S(1)}, bf16[258,512]{1,0:T(8,128)(2,1)S(1)}, u32[]{:S(2)}, u32[]{:S(2)}) collective-permute-start(bf16[258,512]{1,0:T(8,128)(2,1)S(1)} %slice.200), channel_id=1, source_target_pairs={{0,2},{2,4},{4,6},{6,0},{1,3},{3,5},{5,7},{7,1},{8,10},{10,12},{12... | collective-permute-start | bytes 792584 | tf_op jit(solution)/shard_map/ppermute | solution.py:225
  48.7 6.0 %collective-permute-start.8 = (bf16[258,512]{1,0:T(8,128)(2,1)S(1)}, bf16[258,512]{1,0:T(8,128)(2,1)S(1)}, u32[]{:S(2)}, u32[]{:S(2)}) collective-permute-start(bf16[258,512]{1,0:T(8,128)(2,1)S(1)} %slice.201), channel_id=1, source_target_pairs={{0,6},{2,0},{4,2},{6,4},{1,7},{3,1},{5,3},{7,5},{8,14},{10,8},{12,... | collective-permute-start | bytes 792584 | tf_op jit(solution)/shard_map/ppermute | solution.py:225
  70.7 2.3 %copy-start.8 = (f32[4,16]{1,0:T(4,128)S(1)}, f32[4,16]{1,0:T(4,128)}, u32[]{:S(2)}) copy-start(f32[4,16]{1,0:T(4,128)} %get-tuple-element.74) | copy-start | bytes 772
  70.7 2.5 %copy-start.9 = (f32[4,1]{1,0:T(4,128)S(1)}, f32[4,1]{1,0:T(4,128)}, u32[]{:S(2)}) copy-start(f32[4,1]{1,0:T(4,128)} %get-tuple-element.71) | copy-start | bytes 52
  70.7 2.5 %copy-start.10 = (f32[4,1]{1,0:T(4,128)S(1)}, f32[4,1]{1,0:T(4,128)}, u32[]{:S(2)}) copy-start(f32[4,1]{1,0:T(4,128)} %get-tuple-element.72) | copy-start | bytes 52
  72.9 18.4 %copy-start = (bf16[512,2,128]{2,0,1:T(8,128)(2,1)S(1)}, bf16[512,2,128]{2,0,1:T(8,128)(2,1)}, u32[]{:S(2)}) copy-start(bf16[512,2,128]{2,0,1:T(8,128)(2,1)} %copy.214) | copy-start | bytes 786436
  73.2 22.9 %collective-permute-start.9 = (f32[4,257]{1,0:T(4,128)S(1)}, f32[4,257]{1,0:T(4,128)S(1)}, u32[]{:S(2)}, u32[]{:S(2)}) collective-permute-start(f32[4,257]{1,0:T(4,128)S(1)} %get-tuple-element.63), channel_id=1, source_target_pairs={{8,0},{16,8},{24,16},{32,24},{40,32},{48,40},{56,48},{64,56},{72,6... | collective-permute-start | bytes 12344 | tf_op jit(solution)/shard_map/ppermute | solution.py:262
  77.6 23.4 %collective-permute-start.11 = (f32[4,257]{1,0:T(4,128)S(1)}, f32[4,257]{1,0:T(4,128)S(1)}, u32[]{:S(2)}, u32[]{:S(2)}) collective-permute-start(f32[4,257]{1,0:T(4,128)S(1)} %get-tuple-element.64), channel_id=1, source_target_pairs={{0,8},{8,16},{16,24},{24,32},{32,40},{40,48},{48,56},{56,64},{64,7... | collective-permute-start | bytes 12344 | tf_op jit(solution)/shard_map/ppermute | solution.py:262
  89.8 2.3 %copy-start.2 = (pred[512,1024]{1,0:T(8,128)(4,1)S(1)}, pred[512,1024]{1,0:T(8,128)(4,1)}, u32[]{:S(2)}) copy-start(pred[512,1024]{1,0:T(8,128)(4,1)} %pad_add_fusion) | copy-start | bytes 1572868
  92.1 2.4 %copy-start.5 = (bf16[1,1,512,256]{2,3,1,0:T(8,128)(2,1)S(1)}, bf16[1,1,512,256]{2,3,1,0:T(8,128)(2,1)}, u32[]{:S(2)}) copy-start(bf16[1,1,512,256]{2,3,1,0:T(8,128)(2,1)} %copy.207) | copy-start | bytes 786436
  94.5 1.0 copy-start.4
  94.5 1.4 %copy-start.3 = (bf16[4,256,256]{2,1,0:T(8,128)(2,1)S(1)}, bf16[4,256,256]{2,1,0:T(8,128)(2,1)}, u32[]{:S(2)}) copy-start(bf16[4,256,256]{2,1,0:T(8,128)(2,1)} %get-tuple-element.42) | copy-start | bytes 1572868
  96.4 9.6 %copy-start.12 = (pred[2,2]{1,0:T(4,128)(4,1)S(1)}, pred[2,2]{1,0:T(4,128)(4,1)}, u32[]{:S(2)}) copy-start(pred[2,2]{1,0:T(4,128)(4,1)} %copy-done.11) | copy-start | bytes 16
  106.3 2.7 %collective-permute-start.10 = (f32[4,2,130]{0,1,2:T(2,128)S(1)}, f32[4,2,130]{0,1,2:T(2,128)S(1)}, u32[]{:S(2)}, u32[]{:S(2)}) collective-permute-start(f32[4,2,130]{0,1,2:T(2,128)S(1)} %pad_maximum_fusion), channel_id=1, source_target_pairs={{0,8},{8,16},{16,24},{24,32},{32,40},{40,48},{48,56},{56,64},{64,7... | collective-permute-start | bytes 12488 | tf_op jit(solution)/shard_map/ppermute | solution.py:268
  107.0 4.7 %collective-permute-start.12 = (f32[4,2,130]{0,1,2:T(2,128)S(1)}, f32[4,2,130]{0,1,2:T(2,128)S(1)}, u32[]{:S(2)}, u32[]{:S(2)}) collective-permute-start(f32[4,2,130]{0,1,2:T(2,128)S(1)} %pad_maximum_fusion.1), channel_id=1, source_target_pairs={{8,0},{16,8},{24,16},{32,24},{40,32},{48,40},{56,48},{64,56},{72,6... | collective-permute-start | bytes 12488 | tf_op jit(solution)/shard_map/ppermute | solution.py:268

commit v13 on v10

--- a/solution.py
+++ b/solution.py
@@ -117,17 +117,23 @@
 
 
 def attend_rows(query, keys, values, live):
-    scores = jnp.einsum("qhd,khd->hqk", query, keys, preferred_element_type=jnp.float32) * (
-        1.0 / math.sqrt(HD)
-    )
-    masked = jnp.where(live[None], scores, NEG)
-    highest = jnp.max(masked, axis=2, keepdims=True)
-    weights = jnp.where(live[None], jnp.exp(masked - highest), 0.0)
-    total = jnp.sum(weights, axis=2)
-    mixed = jnp.einsum(
-        "hqk,khd->qhd", weights.astype(jnp.bfloat16), values, preferred_element_type=jnp.float32
-    )
-    return (mixed / jnp.transpose(total)[:, :, None]).astype(jnp.bfloat16)
+    outs = []
+    for h in range(query.shape[1]):
+        scores = lax.dot_general(
+            query[:, h],
+            keys[:, h],
+            (((1,), (1,)), ((), ())),
+            preferred_element_type=jnp.float32,
+        ) * (1.0 / math.sqrt(HD))
+        masked = jnp.where(live, scores, NEG)
+        highest = jnp.max(masked, axis=1, keepdims=True)
+        weights = jnp.where(live, jnp.exp(masked - highest), 0.0)
+        total = jnp.sum(weights, axis=1, keepdims=True)
+        mixed = jnp.dot(
+            weights.astype(jnp.bfloat16), values[:, h], preferred_element_type=jnp.float32
+        )
+        outs.append((mixed / total).astype(jnp.bfloat16))
+    return jnp.stack(outs, axis=1)
 
 
 def prefill_attend(query, fresh_key, fresh_value, prior, offset):

time: 114 us -> 114 us (level)
  waiting for transfers between devices: 10.8 us -> 16.6 us
  other arithmetic: 13.8 us -> 9.7 us
  local copies, waits for them, and re-layouts: 27.3 us -> 24.3 us
  matrix products: 10.9 us -> 12.6 us
    ppermute x1, waiting for transfers between devices: 4 us -> 7.92 us  [local(): partner = lax.ppermute(rows, 'tz', [(0, 1), (1, 0)])]
    sub x1 -> x0, other arithmetic: 2.34 us -> none  [attend_rows(): weights = jnp.where(live[None], jnp.exp(masked - highest), 0.0)]
    ppermute x2, waiting for transfers between devices: 3.62 us -> 5.59 us  [around(): lax.ppermute(below[:half], 'ty', up)]
    slice x2 -> x1, local copies, waits for them, and re-layouts: 1.9 us -> 0.04 us  [prefill_attend(): prior[1].reshape(capacity, heads, HD)]
    dot_general x2 -> x4, matrix products: 1.65 us -> 3.29 us  [the longest x2 1.79 us: attend_rows(): lax.dot_general(query[:, h], keys[:, h], (((1,), (1,)), ((), ())), prefer...]
    unnamed x43 -> x44, local copies, waits for them, and re-layouts: 11.6 us -> 11.9 us
  transfers between devices with their start and end apart: 13 -> 13, of which waited for: 4 -> 4; matrix products, arithmetic and copies ran while one was open for 33% -> 27% of each run, Pallas kernels for 0% -> 0%
where the time goes in v13:
time: 114 us
  starting transfers between devices  34.7 us (30%)
  local copies, waits for them, and re-layouts  24.3 us (21%)
  waiting for transfers between devices  16.6 us (15%)
  Pallas kernels  14.3 us (13%)
  matrix products  12.6 us (11%)
  other arithmetic  9.7 us (9%)
  between operations  1.72 us (2%)
    ppermute x2, starting transfers between devices, ask(): got = lax.ppermute(packed, 'group', pairs)  15.2 us
    pallas_call x2, Pallas kernels, qkv_matmul(): pl.pallas_call(qkv_kernel, out_shape=jax.ShapeDtypeStruct((rows, parts *...  14.3 us
    unnamed x44, local copies, waits for them, and re-layouts  11.9 us
    ppermute x1, waiting for transfers between devices, local(): partner = lax.ppermute(rows, 'tz', [(0, 1), (1, 0)])  7.92 us
    ppermute x1, starting transfers between devices, local(): partner = lax.ppermute(rows, 'tz', [(0, 1), (1, 0)])  6.91 us
    ppermute x2, waiting for transfers between devices, around(): lax.ppermute(below[:half], 'ty', up)  5.59 us
    dot_general x3, matrix products, piece_rows(): jnp.einsum('rkf,rfh->rhk', keys, spread, preferred_element_type=jnp.float32)  4.99 us
    ppermute x2, starting transfers between devices, around(): lax.ppermute(above[half:], 'ty', down)  4.87 us
  transfers between devices with their start and end apart: 13, of which 4 were waited for; matrix products, arithmetic and copies ran while one was open for 27% of the time, Pallas kernels for 0%

profile of v13, /device:TPU:1, one launch (start us, length us, event | category | flops | bytes accessed | tf_op | source)
XLA Modules:
  0.0 113.9 jit_solution(9547609419609944146)
XLA Ops:
  0.7 2.2 %constant_dynamic-update-slice_fusion.1 = (bf16[516,512]{1,0:T(8,128)(2,1)}, bf16[516,4096]{1,0:T(8,128)(2,1)}) fusion(bf16[512,512]{1,0:T(8,128)(2,1)} %param.11), kind=kLoop, calls=%fused_computation.85 | loop fusion | bytes 1572864
  2.9 1.3 %constant_dynamic-update-slice_fusion = (bf16[516,512]{1,0:T(8,128)(2,1)}, bf16[516,4096]{1,0:T(8,128)(2,1)}) fusion(bf16[516,512]{1,0:T(8,128)(2,1)} %get-tuple-element.55, bf16[4,512]{1,0:T(4,128)(2,1)} %param.12, bf16[516,4096]{1,0:T(8,128)(2,1)} %get-tuple-element.56), kind=kLoop, calls=%fused_computation.84 | loop fusion | bytes 12288 | tf_op jit(solution)/shard_map/concatenate | solution.py:219
  4.2 2.1 %collective-permute-start = (bf16[516,512]{1,0:T(8,128)(2,1)}, bf16[516,512]{1,0:T(8,128)(2,1)S(1)}, u32[]{:S(2)}, u32[]{:S(2)}) collective-permute-start(bf16[516,512]{1,0:T(8,128)(2,1)} %get-tuple-element.69), channel_id=1, source_target_pairs={{0,2},{2,4},{4,6},{6,0},{1,3},{3,5},{5,7},{7,1},{8,10},{10,12},{12... | collective-permute-start | bytes 1585160 | tf_op jit(solution)/shard_map/ppermute | solution.py:228
  6.3 1.4 %collective-permute-start.1 = (bf16[516,512]{1,0:T(8,128)(2,1)}, bf16[516,512]{1,0:T(8,128)(2,1)S(1)}, u32[]{:S(2)}, u32[]{:S(2)}) collective-permute-start(bf16[516,512]{1,0:T(8,128)(2,1)} %get-tuple-element.69), channel_id=1, source_target_pairs={{0,6},{2,0},{4,2},{6,4},{1,7},{3,1},{5,3},{7,5},{8,14},{10,8},{12,... | collective-permute-start | bytes 1585160 | tf_op jit(solution)/shard_map/ppermute | solution.py:229
  7.7 6.9 %collective-permute-start.4 = (bf16[516,512]{1,0:T(8,128)(2,1)}, bf16[516,512]{1,0:T(8,128)(2,1)}, u32[]{:S(2)}, u32[]{:S(2)}) collective-permute-start(bf16[516,512]{1,0:T(8,128)(2,1)} %get-tuple-element.69), channel_id=1, source_target_pairs={{0,1},{1,0},{2,3},{3,2},{4,5},{5,4},{6,7},{7,6},{8,9},{9,8},{10,11... | collective-permute-start | bytes 1585160 | tf_op jit(solution)/shard_map/ppermute | solution.py:235
  14.7 1.0 convert_reduce_fusion
  15.7 1.0 slice_reduce_fusion
  17.8 0.2 multiply_cosine_fusion
  18.1 0.8 iota_compare_fusion
  18.9 1.0 slice_bitcast_fusion.1
  20.0 7.9 %collective-permute-done.4 = bf16[516,512]{1,0:T(8,128)(2,1)} collective-permute-done((bf16[516,512]{1,0:T(8,128)(2,1)}, bf16[516,512]{1,0:T(8,128)(2,1)}, u32[]{:S(2)}, u32[]{:S(2)}) %collective-permute-start.4) | collective-permute-done | bytes 528416 | tf_op jit(solution)/shard_map/ppermute | solution.py:235
  27.9 0.4 collective-permute-start.5
  28.3 2.3 %collective-permute-start.6 = (bf16[516,512]{1,0:T(8,128)(2,1)}, bf16[516,512]{1,0:T(8,128)(2,1)S(1)}, u32[]{:S(2)}, u32[]{:S(2)}) collective-permute-start(bf16[516,512]{1,0:T(8,128)(2,1)} %collective-permute-done.4), channel_id=1, source_target_pairs={{0,6},{2,0},{4,2},{6,4},{1,7},{3,1},{5,3},{7,5},{8,14},{10,8},{12,... | collective-permute-start | bytes 1585160 | tf_op jit(solution)/shard_map/ppermute | solution.py:229
  30.6 0.7 slice.228
  31.4 0.8 slice.229
  32.1 2.7 %collective-permute-start.3 = (bf16[258,512]{1,0:T(8,128)(2,1)}, bf16[258,512]{1,0:T(8,128)(2,1)}, u32[]{:S(2)}, u32[]{:S(2)}) collective-permute-start(bf16[258,512]{1,0:T(8,128)(2,1)} %slice.229), channel_id=1, source_target_pairs={{0,6},{2,0},{4,2},{6,4},{1,7},{3,1},{5,3},{7,5},{8,14},{10,8},{12,... | collective-permute-start | bytes 792584 | tf_op jit(solution)/shard_map/ppermute | solution.py:231
  34.8 0.6 gather_fusion
  35.4 0.6 gather_fusion.1
  36.2 0.8 copy.243
  37.2 0.8 copy.246
  38.0 0.8 copy.289
  38.9 0.9 constant_dynamic-update-slice_fusion.6
  39.8 0.9 constant_dynamic-update-slice_fusion.5
  40.7 5.6 %collective-permute-done.2 = bf16[258,512]{1,0:T(8,128)(2,1)} collective-permute-done((bf16[258,512]{1,0:T(8,128)(2,1)}, bf16[258,512]{1,0:T(8,128)(2,1)}, u32[]{:S(2)}, u32[]{:S(2)}) %collective-permute-start.2) | collective-permute-done | bytes 264224 | tf_op jit(solution)/shard_map/ppermute | solution.py:231
  46.3 2.0 %maximum_dynamic-update-slice_fusion.1 = bf16[516,4096]{1,0:T(8,128)(2,1)} fusion(bf16[516,4096]{1,0:T(8,128)(2,1)} %constant_dynamic-update-slice_fusion.5, bf16[258,512]{1,0:T(8,128)(2,1)} %collective-permute-done.3, bf16[258,512]{1,0:T(8,128)(2,1)} %collective-permute-done.2), kind=kLoop, calls=%fused_computation.50 | loop fusion | flops 1056768 | bytes 1073152
  48.3 0.8 collective-permute-start.7
  49.2 2.2 %collective-permute-start.8 = (bf16[258,512]{1,0:T(8,128)(2,1)S(1)}, bf16[258,512]{1,0:T(8,128)(2,1)S(1)}, u32[]{:S(2)}, u32[]{:S(2)}) collective-permute-start(bf16[258,512]{1,0:T(8,128)(2,1)S(1)} %slice.231), channel_id=1, source_target_pairs={{0,6},{2,0},{4,2},{6,4},{1,7},{3,1},{5,3},{7,5},{8,14},{10,8},{12,... | collective-permute-start | bytes 792584 | tf_op jit(solution)/shard_map/ppermute | solution.py:231
  51.4 2.0 %constant_dynamic-update-slice_fusion.4 = bf16[516,4096]{1,0:T(8,128)(2,1)} fusion(bf16[516,4096]{1,0:T(8,128)(2,1)} %maximum_dynamic-update-slice_fusion.1, bf16[516,512]{1,0:T(8,128)(2,1)} %collective-permute-done.4), kind=kLoop, calls=%fused_computation.88 | loop fusion | bytes 1064960
  53.4 0.9 constant_dynamic-update-slice_fusion.3
  54.2 0.9 constant_dynamic-update-slice_fusion.2
  55.1 0.9 maximum_dynamic-update-slice_fusion.x_ref
  56.0 0.8 slice.247.x_ref
  56.9 4.4 %shard_map.123 = f32[4,768]{1,0:T(4,128)S(1)} custom-call(s32[8]{0:T(128)S(1)} %pad_add_fusion.1.order_ref, bf16[4,4096]{1,0:T(4,128)(2,1)S(1)} %slice.247.x_ref, f32[1,4096]{1,0:T(1,128)S(1)} %bitcast.159, f32[1,4096]{1,0:T(1,128)S(1)} %bitcast.161, bf16[3,4096,256]{2,1,0:T(8,128)(2,1)} %bitcast.163), custom_call_target="tpu_custom_call" | custom-call | flops 25165824 | bytes 6336512 | tf_op jit(solution)/shard_map/pallas_call | solution.py:84
  61.5 9.9 %shard_map.122 = f32[512,768]{1,0:T(8,128)S(1)} custom-call(s32[8]{0:T(128)S(1)} %pad_add_fusion.1.order_ref, bf16[516,4096]{1,0:T(8,128)(2,1)} %maximum_dynamic-update-slice_fusion.x_ref, f32[1,4096]{1,0:T(1,128)S(1)} %bitcast.160, f32[1,4096]{1,0:T(1,128)S(1)} %bitcast.162, bf16[3,4096,256]{2,1,0:T(8,128)(2,1)} %bitcast.164), custom_call_target="tpu_custom_call" | custom-call | flops 3221225472 | bytes 12058624 | tf_op jit(solution)/shard_map/pallas_call | solution.py:84
  71.5 0.8 reshape.540
  72.3 0.4 fusion.97
  72.7 0.9 slice.242
  73.9 4.5 %collective-permute-start.9 = (f32[4,257]{1,0:T(4,128)S(1)}, f32[4,257]{1,0:T(4,128)S(1)}, u32[]{:S(2)}, u32[]{:S(2)}) collective-permute-start(f32[4,257]{1,0:T(4,128)S(1)} %get-tuple-element.67), channel_id=1, source_target_pairs={{8,0},{16,8},{24,16},{32,24},{40,32},{48,40},{56,48},{64,56},{72,6... | collective-permute-start | bytes 12344 | tf_op jit(solution)/shard_map/ppermute | solution.py:268
  78.4 10.7 %collective-permute-start.11 = (f32[4,257]{1,0:T(4,128)S(1)}, f32[4,257]{1,0:T(4,128)S(1)}, u32[]{:S(2)}, u32[]{:S(2)}) collective-permute-start(f32[4,257]{1,0:T(4,128)S(1)} %get-tuple-element.68), channel_id=1, source_target_pairs={{0,8},{8,16},{16,24},{24,32},{32,40},{40,48},{48,56},{56,64},{64,7... | collective-permute-start | bytes 12344 | tf_op jit(solution)/shard_map/ppermute | solution.py:268
  89.5 0.9 copy.300
  90.3 0.4 subtract_convert_fusion.1
  90.8 0.3 pad_maximum_fusion.1
  91.0 0.3 copy-done.4
  91.3 0.3 maximum_maximum_fusion
  91.5 0.2 copy-done.1
  91.7 0.6 fusion.12
  92.3 1.2 %fusion.14 = (f32[512]{0:T(512)S(1)}, f32[512]{0:T(512)S(1)}, f32[512,1024]{1,0:T(8,128)S(1)}) fusion(f32[512,1024]{1,0:T(8,128)S(1)} %get-tuple-element.80, f32[512]{0:T(512)S(1)} %get-tuple-element.79, pred[512,512]{1,0:T(32,128)(4,1)S(1)} %copy-done.1, pred[1024]{0:T(1024)(128)(4,1)S(1)} %pad.47.clone, ...), kind=kOutput, calls=%fused_computation.21 | convolution fusion | flops 138935296 | bytes 4856832 | tf_op jit(solution)/shard_map/while/body/eval_jaxpr/dot_general | solution.py:122
  93.5 0.7 fusion.16
  94.2 0.2 copy-done.8
  94.5 0.7 fusion.21
  95.3 0.8 fusion.20
  96.2 0.2 copy-done.7
  96.3 0.3 fusion.101
  96.7 0.2 fusion.43
  97.2 2.3 %fusion.100 = (f32[4,2]{1,0:T(4,128)S(1)}, f32[4,2,1024]{2,1,0:T(2,128)S(1)}) fusion(bf16[8,2,1024,256]{3,2,1,0:T(8,128)(2,1)} %param.21, pred[256,2]{0,1:T(4,128)(4,1)S(1)} %bitcast.183, bf16[4,256]{1,0:T(4,128)(2,1)S(1)} %slice.376, pred[4,1024]{1,0:T(4,128)(4,1)S(1)} %iota_compare_fusion.2), kind=kOutput, calls=%fused_computation.192 | convolution fusion | flops 4220920 | bytes 2136608 | tf_op jit(solution)/shard_map/rkf,rfh->rhk/dot_general | solution.py:166
  99.5 2.0 %fusion.4 = f32[4,2,256]{2,1,0:T(2,128)S(1)} fusion(bf16[8,2,1024,256]{3,2,1,0:T(8,128)(2,1)} %param.21, f32[4,2,1024]{2,1,0:T(2,128)S(1)} %get-tuple-element.85, pred[4,1024]{1,0:T(4,128)(4,1)S(1)} %iota_compare_fusion.2, f32[4,2]{1,0:T(4,128)S(1)} %get-tuple-element.84), kind=kOutput, calls=%fused_computation.6 | convolution fusion | flops 4218880 | bytes 2142240 | tf_op jit(solution)/shard_map/rhk,rkf->rhf/dot_general | solution.py:173
  102.0 2.3 %fusion.99 = (f32[4,2]{1,0:T(4,128)S(1)}, f32[4,2,1024]{2,1,0:T(2,128)S(1)}) fusion(bf16[8,2,1024,256]{3,2,1,0:T(8,128)(2,1)} %param.21, pred[256,2]{0,1:T(4,128)(4,1)S(1)} %bitcast.184, bf16[4,256]{1,0:T(4,128)(2,1)S(1)} %slice.374, pred[4,1024]{1,0:T(4,128)(4,1)S(1)} %iota_compare_fusion.1), kind=kOutput, calls=%fused_computation.191 | convolution fusion | flops 4220920 | bytes 2136608 | tf_op jit(solution)/shard_map/rkf,rfh->rhk/dot_general | solution.py:166
  104.4 2.0 %fusion = f32[4,2,256]{2,1,0:T(2,128)S(1)} fusion(bf16[8,2,1024,256]{3,2,1,0:T(8,128)(2,1)} %param.21, f32[4,2,1024]{2,1,0:T(2,128)S(1)} %get-tuple-element.83, pred[4,1024]{1,0:T(4,128)(4,1)S(1)} %iota_compare_fusion.1, f32[4,2]{1,0:T(4,128)S(1)} %get-tuple-element.82), kind=kOutput, calls=%fused_computation.2 | convolution fusion | flops 4218880 | bytes 2142240 | tf_op jit(solution)/shard_map/rhk,rkf->rhf/dot_general | solution.py:173
  107.2 0.3 collective-permute-start.10
  107.8 0.4 collective-permute-start.12
  108.5 0.8 copy.283
  109.4 0.5 collective-permute-done.10
  109.8 2.6 %collective-permute-done.12 = f32[4,2,130]{0,1,2:T(2,128)S(1)} collective-permute-done((f32[4,2,130]{0,1,2:T(2,128)S(1)}, f32[4,2,130]{0,1,2:T(2,128)S(1)}, u32[]{:S(2)}, u32[]{:S(2)}) %collective-permute-start.12) | collective-permute-done | bytes 4192 | tf_op jit(solution)/shard_map/ppermute | solution.py:274
  113.2 0.7 copy.282
  (112 shorter events, 5.2 us)
Async XLA Ops:
  0.6 17.3 %copy-start.5 = (bf16[1,2,512,256]{3,2,1,0:T(8,128)(2,1)S(1)}, bf16[1,2,512,256]{3,2,1,0:T(8,128)(2,1)}, u32[]{:S(2)}) copy-start(bf16[1,2,512,256]{3,2,1,0:T(8,128)(2,1)} %param.17) | copy-start | bytes 1572868
  0.6 18.3 %copy-start.2 = (bf16[4,2,256,256]{3,2,1,0:T(8,128)(2,1)S(1)}, bf16[4,2,256,256]{3,2,1,0:T(8,128)(2,1)}, u32[]{:S(2)}) copy-start(bf16[4,2,256,256]{3,2,1,0:T(8,128)(2,1)} %param.19) | copy-start | bytes 3145732
  4.2 26.5 %collective-permute-start = (bf16[516,512]{1,0:T(8,128)(2,1)}, bf16[516,512]{1,0:T(8,128)(2,1)S(1)}, u32[]{:S(2)}, u32[]{:S(2)}) collective-permute-start(bf16[516,512]{1,0:T(8,128)(2,1)} %get-tuple-element.69), channel_id=1, source_target_pairs={{0,2},{2,4},{4,6},{6,0},{1,3},{3,5},{5,7},{7,1},{8,10},{10,12},{12... | collective-permute-start | bytes 1585160 | tf_op jit(solution)/shard_map/ppermute | solution.py:228
  6.3 25.1 %collective-permute-start.1 = (bf16[516,512]{1,0:T(8,128)(2,1)}, bf16[516,512]{1,0:T(8,128)(2,1)S(1)}, u32[]{:S(2)}, u32[]{:S(2)}) collective-permute-start(bf16[516,512]{1,0:T(8,128)(2,1)} %get-tuple-element.69), channel_id=1, source_target_pairs={{0,6},{2,0},{4,2},{6,4},{1,7},{3,1},{5,3},{7,5},{8,14},{10,8},{12,... | collective-permute-start | bytes 1585160 | tf_op jit(solution)/shard_map/ppermute | solution.py:229
  7.7 20.1 %collective-permute-start.4 = (bf16[516,512]{1,0:T(8,128)(2,1)}, bf16[516,512]{1,0:T(8,128)(2,1)}, u32[]{:S(2)}, u32[]{:S(2)}) collective-permute-start(bf16[516,512]{1,0:T(8,128)(2,1)} %get-tuple-element.69), channel_id=1, source_target_pairs={{0,1},{1,0},{2,3},{3,2},{4,5},{5,4},{6,7},{7,6},{8,9},{9,8},{10,11... | collective-permute-start | bytes 1585160 | tf_op jit(solution)/shard_map/ppermute | solution.py:235
  18.0 16.9 %copy-start.10 = (f32[4096]{0:T(1024)S(1)}, f32[4096]{0:T(1024)}, u32[]{:S(2)}) copy-start(f32[4096]{0:T(1024)} %param.13) | copy-start | bytes 49156
  18.0 17.4 %copy-start.11 = (f32[4096]{0:T(1024)S(1)}, f32[4096]{0:T(1024)}, u32[]{:S(2)}) copy-start(f32[4096]{0:T(1024)} %param.14) | copy-start | bytes 49156
  18.0 18.0 %copy-start.12 = (f32[3,256]{1,0:T(4,128)S(1)}, f32[3,256]{1,0:T(4,128)}, u32[]{:S(2)}) copy-start(f32[3,256]{1,0:T(4,128)} %param.16) | copy-start | bytes 9220
  27.9 20.4 %collective-permute-start.5 = (bf16[516,512]{1,0:T(8,128)(2,1)}, bf16[516,512]{1,0:T(8,128)(2,1)S(1)}, u32[]{:S(2)}, u32[]{:S(2)}) collective-permute-start(bf16[516,512]{1,0:T(8,128)(2,1)} %collective-permute-done.4), channel_id=1, source_target_pairs={{0,2},{2,4},{4,6},{6,0},{1,3},{3,5},{5,7},{7,1},{8,10},{10,12},{12... | collective-permute-start | bytes 1585160 | tf_op jit(solution)/shard_map/ppermute | solution.py:228
  28.3 20.8 %collective-permute-start.6 = (bf16[516,512]{1,0:T(8,128)(2,1)}, bf16[516,512]{1,0:T(8,128)(2,1)S(1)}, u32[]{:S(2)}, u32[]{:S(2)}) collective-permute-start(bf16[516,512]{1,0:T(8,128)(2,1)} %collective-permute-done.4), channel_id=1, source_target_pairs={{0,6},{2,0},{4,2},{6,4},{1,7},{3,1},{5,3},{7,5},{8,14},{10,8},{12,... | collective-permute-start | bytes 1585160 | tf_op jit(solution)/shard_map/ppermute | solution.py:229
  31.4 14.9 %collective-permute-start.2 = (bf16[258,512]{1,0:T(8,128)(2,1)}, bf16[258,512]{1,0:T(8,128)(2,1)}, u32[]{:S(2)}, u32[]{:S(2)}) collective-permute-start(bf16[258,512]{1,0:T(8,128)(2,1)} %slice.228), channel_id=1, source_target_pairs={{0,2},{2,4},{4,6},{6,0},{1,3},{3,5},{5,7},{7,1},{8,10},{10,12},{12... | collective-permute-start | bytes 792584 | tf_op jit(solution)/shard_map/ppermute | solution.py:231
  32.1 14.1 %collective-permute-start.3 = (bf16[258,512]{1,0:T(8,128)(2,1)}, bf16[258,512]{1,0:T(8,128)(2,1)}, u32[]{:S(2)}, u32[]{:S(2)}) collective-permute-start(bf16[258,512]{1,0:T(8,128)(2,1)} %slice.229), channel_id=1, source_target_pairs={{0,6},{2,0},{4,2},{6,4},{1,7},{3,1},{5,3},{7,5},{8,14},{10,8},{12,... | collective-permute-start | bytes 792584 | tf_op jit(solution)/shard_map/ppermute | solution.py:231
  48.3 6.8 %collective-permute-start.7 = (bf16[258,512]{1,0:T(8,128)(2,1)S(1)}, bf16[258,512]{1,0:T(8,128)(2,1)S(1)}, u32[]{:S(2)}, u32[]{:S(2)}) collective-permute-start(bf16[258,512]{1,0:T(8,128)(2,1)S(1)} %slice.230), channel_id=1, source_target_pairs={{0,2},{2,4},{4,6},{6,0},{1,3},{3,5},{5,7},{7,1},{8,10},{10,12},{12... | collective-permute-start | bytes 792584 | tf_op jit(solution)/shard_map/ppermute | solution.py:231
  49.2 5.9 %collective-permute-start.8 = (bf16[258,512]{1,0:T(8,128)(2,1)S(1)}, bf16[258,512]{1,0:T(8,128)(2,1)S(1)}, u32[]{:S(2)}, u32[]{:S(2)}) collective-permute-start(bf16[258,512]{1,0:T(8,128)(2,1)S(1)} %slice.231), channel_id=1, source_target_pairs={{0,6},{2,0},{4,2},{6,4},{1,7},{3,1},{5,3},{7,5},{8,14},{10,8},{12,... | collective-permute-start | bytes 792584 | tf_op jit(solution)/shard_map/ppermute | solution.py:231
  73.6 15.9 %copy-start.3 = (bf16[512,1,2,128]{3,2,1,0:T(2,128)(2,1)S(1)}, bf16[512,1,2,128]{3,2,1,0:T(2,128)(2,1)}, u32[]{:S(2)}) copy-start(bf16[512,1,2,128]{3,2,1,0:T(2,128)(2,1)} %slice.242) | copy-start | bytes 786436
  73.6 16.8 %copy-start = (f32[512,16]{1,0:T(8,128)S(1)}, f32[512,16]{1,0:T(8,128)}, u32[]{:S(2)}) copy-start(f32[512,16]{1,0:T(8,128)} %copy.243) | copy-start | bytes 98308
  73.9 23.1 %collective-permute-start.9 = (f32[4,257]{1,0:T(4,128)S(1)}, f32[4,257]{1,0:T(4,128)S(1)}, u32[]{:S(2)}, u32[]{:S(2)}) collective-permute-start(f32[4,257]{1,0:T(4,128)S(1)} %get-tuple-element.67), channel_id=1, source_target_pairs={{8,0},{16,8},{24,16},{32,24},{40,32},{48,40},{56,48},{64,56},{72,6... | collective-permute-start | bytes 12344 | tf_op jit(solution)/shard_map/ppermute | solution.py:268
  78.4 23.5 %collective-permute-start.11 = (f32[4,257]{1,0:T(4,128)S(1)}, f32[4,257]{1,0:T(4,128)S(1)}, u32[]{:S(2)}, u32[]{:S(2)}) collective-permute-start(f32[4,257]{1,0:T(4,128)S(1)} %get-tuple-element.68), channel_id=1, source_target_pairs={{0,8},{8,16},{16,24},{24,32},{32,40},{40,48},{48,56},{56,64},{64,7... | collective-permute-start | bytes 12344 | tf_op jit(solution)/shard_map/ppermute | solution.py:268
  90.3 1.0 copy-start.4
  90.7 1.0 copy-start.1
  93.5 1.0 copy-start.8
  93.5 1.0 copy-start.9
  95.3 1.0 copy-start.7
  95.3 1.4 %copy-start.6 = (bf16[4,256,256]{2,1,0:T(8,128)(2,1)S(1)}, bf16[4,256,256]{2,1,0:T(8,128)(2,1)}, u32[]{:S(2)}) copy-start(bf16[4,256,256]{2,1,0:T(8,128)(2,1)} %get-tuple-element.46) | copy-start | bytes 1572868
  107.2 2.7 %collective-permute-start.10 = (f32[4,2,130]{0,1,2:T(2,128)S(1)}, f32[4,2,130]{0,1,2:T(2,128)S(1)}, u32[]{:S(2)}, u32[]{:S(2)}) collective-permute-start(f32[4,2,130]{0,1,2:T(2,128)S(1)} %pad_maximum_fusion.3), channel_id=1, source_target_pairs={{0,8},{8,16},{16,24},{24,32},{32,40},{40,48},{48,56},{56,64},{64,7... | collective-permute-start | bytes 12488 | tf_op jit(solution)/shard_map/ppermute | solution.py:274
  107.8 4.6 %collective-permute-start.12 = (f32[4,2,130]{0,1,2:T(2,128)S(1)}, f32[4,2,130]{0,1,2:T(2,128)S(1)}, u32[]{:S(2)}, u32[]{:S(2)}) collective-permute-start(f32[4,2,130]{0,1,2:T(2,128)S(1)} %pad_maximum_fusion.4), channel_id=1, source_target_pairs={{8,0},{16,8},{24,16},{32,24},{40,32},{48,40},{56,48},{64,56},{72,6... | collective-permute-start | bytes 12488 | tf_op jit(solution)/shard_map/ppermute | solution.py:274

commit v14 on v10

--- a/solution.py
+++ b/solution.py
@@ -270,10 +270,13 @@
 
     prev_query, prev_len = ask(piece_len[:, 2], forward)
     next_query, next_len = ask(piece_len[:, 0], backward)
+    prefill_rows, prev_query, prev_len, next_query, next_len = lax.optimization_barrier(
+        (whole, prev_query, prev_len, next_query, next_len)
+    )
     right_parts = answer(piece_batch(prev_query, side_store[:requests], prev_len), backward)
     left_parts = answer(piece_batch(next_query, side_store[requests:], next_len), forward)
     query, fresh_key, fresh_value = project(
-        whole,
+        prefill_rows,
         0,
         count,
         gain,

time: 114 us -> 121 us (1.061)
  the two profiles are of different devices: /device:TPU:1 before, /device:TPU:128 now
where the time goes in v14:
time: 121 us
  local copies, waits for them, and re-layouts  28 us (23%)
  waiting for transfers between devices  27.5 us (23%)
  starting transfers between devices  24.1 us (20%)
  Pallas kernels  14.3 us (12%)
  other arithmetic  14.1 us (12%)
  matrix products  11 us (9%)
  between operations  1.68 us (1%)
    ppermute x1, waiting for transfers between devices, local(): partner = lax.ppermute(rows, 'tz', [(0, 1), (1, 0)])  18.7 us
    pallas_call x2, Pallas kernels, qkv_matmul(): pl.pallas_call(qkv_kernel, out_shape=jax.ShapeDtypeStruct((rows, parts *...  14.3 us
    unnamed x49, local copies, waits for them, and re-layouts  11.5 us
    ppermute x2, starting transfers between devices, ask(): got = lax.ppermute(packed, 'group', pairs)  5.72 us
    ppermute x2, starting transfers between devices, answer(): got = lax.ppermute(packed, 'group', pairs)  5.63 us
    dot_general x3, matrix products, piece_rows(): jnp.einsum('rkf,rfh->rhk', keys, spread, preferred_element_type=jnp.float32)  5.09 us
    ppermute x2, starting transfers between devices, around(): above = lax.ppermute(block, 'ty', down)  4.59 us
    dot_general x3, matrix products, piece_rows(): jnp.einsum('rhk,rkf->rhf', weights.astype(jnp.bfloat16), values, preferre...  4.28 us
  transfers between devices with their start and end apart: 13, of which 7 were waited for; matrix products, arithmetic and copies ran while one was open for 25% of the time, Pallas kernels for 0%

profile of v14, /device:TPU:128, one launch (start us, length us, event | category | flops | bytes accessed | tf_op | source)
XLA Modules:
  0.0 120.8 jit_solution(2738321168306568519)
XLA Ops:
  0.7 2.1 %constant_dynamic-update-slice_fusion.1 = (bf16[516,512]{1,0:T(8,128)(2,1)S(1)}, bf16[516,4096]{1,0:T(8,128)(2,1)}) fusion(bf16[512,512]{1,0:T(8,128)(2,1)} %param.11), kind=kLoop, calls=%fused_computation.78 | loop fusion | bytes 1572864
  2.8 1.3 %constant_dynamic-update-slice_fusion = (bf16[516,512]{1,0:T(8,128)(2,1)S(1)}, bf16[516,4096]{1,0:T(8,128)(2,1)}) fusion(bf16[516,512]{1,0:T(8,128)(2,1)S(1)} %get-tuple-element.63, bf16[4,512]{1,0:T(4,128)(2,1)} %param.12, bf16[516,4096]{1,0:T(8,128)(2,1)} %get-tuple-element.64), kind=kLoop, calls=%fused_computation.77 | loop fusion | bytes 12288 | tf_op jit(solution)/shard_map/concatenate | solution.py:213
  4.0 1.6 %collective-permute-start = (bf16[516,512]{1,0:T(8,128)(2,1)S(1)}, bf16[516,512]{1,0:T(8,128)(2,1)S(1)}, u32[]{:S(2)}, u32[]{:S(2)}) collective-permute-start(bf16[516,512]{1,0:T(8,128)(2,1)S(1)} %get-tuple-element.77), channel_id=1, source_target_pairs={{0,2},{2,4},{4,6},{6,0},{1,3},{3,5},{5,7},{7,1},{8,10},{10,12},{12... | collective-permute-start | bytes 1585160 | tf_op jit(solution)/shard_map/ppermute | solution.py:222
  5.6 1.7 %collective-permute-start.1 = (bf16[516,512]{1,0:T(8,128)(2,1)S(1)}, bf16[516,512]{1,0:T(8,128)(2,1)S(1)}, u32[]{:S(2)}, u32[]{:S(2)}) collective-permute-start(bf16[516,512]{1,0:T(8,128)(2,1)S(1)} %get-tuple-element.77), channel_id=1, source_target_pairs={{0,6},{2,0},{4,2},{6,4},{1,7},{3,1},{5,3},{7,5},{8,14},{10,8},{12,... | collective-permute-start | bytes 1585160 | tf_op jit(solution)/shard_map/ppermute | solution.py:223
  7.3 0.5 collective-permute-start.4
  7.8 1.0 convert_reduce_fusion
  8.8 1.5 %slice_reduce_fusion = (s32[4]{0:T(128)S(1)}, f32[4,1]{1,0:T(4,128)}, f32[4,1]{1,0:T(4,128)}) fusion(s32[4,3]{1,0:T(4,128)} %param.20), kind=kLoop, calls=%fused_computation.143 | loop fusion | flops 8 | bytes 96 | tf_op jit(solution)/shard_map/slice | solution.py:248
  11.1 0.7 multiply_cosine_fusion.1
  11.8 0.2 multiply_cosine_fusion
  12.0 1.1 fusion.103
  13.2 0.7 broadcast_bitcast_fusion
  13.8 0.6 iota_compare_fusion.3
  14.6 1.0 pad_add_fusion
  15.7 1.1 slice_bitcast_fusion.1
  16.7 18.7 %collective-permute-done.4 = bf16[516,512]{1,0:T(8,128)(2,1)} collective-permute-done((bf16[516,512]{1,0:T(8,128)(2,1)S(1)}, bf16[516,512]{1,0:T(8,128)(2,1)}, u32[]{:S(2)}, u32[]{:S(2)}) %collective-permute-start.4) | collective-permute-done | bytes 528416 | tf_op jit(solution)/shard_map/ppermute | solution.py:229
  35.5 0.3 collective-permute-start.5
  35.8 2.9 %collective-permute-start.6 = (bf16[516,512]{1,0:T(8,128)(2,1)}, bf16[516,512]{1,0:T(8,128)(2,1)S(1)}, u32[]{:S(2)}, u32[]{:S(2)}) collective-permute-start(bf16[516,512]{1,0:T(8,128)(2,1)} %collective-permute-done.4), channel_id=1, source_target_pairs={{0,6},{2,0},{4,2},{6,4},{1,7},{3,1},{5,3},{7,5},{8,14},{10,8},{12,... | collective-permute-start | bytes 1585160 | tf_op jit(solution)/shard_map/ppermute | solution.py:223
  38.7 0.8 slice.199
  39.5 0.5 collective-permute-start.3
  40.0 0.7 slice.198
  40.7 1.5 %collective-permute-start.2 = (bf16[258,512]{1,0:T(8,128)(2,1)}, bf16[258,512]{1,0:T(8,128)(2,1)}, u32[]{:S(2)}, u32[]{:S(2)}) collective-permute-start(bf16[258,512]{1,0:T(8,128)(2,1)} %slice.198), channel_id=1, source_target_pairs={{0,2},{2,4},{4,6},{6,0},{1,3},{3,5},{5,7},{7,1},{8,10},{10,12},{12... | collective-permute-start | bytes 792584 | tf_op jit(solution)/shard_map/ppermute | solution.py:225
  42.3 0.6 gather_fusion
  42.9 0.6 gather_fusion.1
  43.5 0.7 add.144
  44.3 0.8 copy.217
  45.3 0.8 copy.221
  46.2 0.8 copy.213
  47.0 0.7 copy.280
  47.7 0.7 concatenate.140
  48.4 0.9 constant_dynamic-update-slice_fusion.6
  49.2 0.9 constant_dynamic-update-slice_fusion.5
  50.1 1.5 %collective-permute-done.3 = bf16[258,512]{1,0:T(8,128)(2,1)} collective-permute-done((bf16[258,512]{1,0:T(8,128)(2,1)}, bf16[258,512]{1,0:T(8,128)(2,1)}, u32[]{:S(2)}, u32[]{:S(2)}) %collective-permute-start.3) | collective-permute-done | bytes 264224 | tf_op jit(solution)/shard_map/ppermute | solution.py:225
  51.6 2.0 %maximum_dynamic-update-slice_fusion.1 = bf16[516,4096]{1,0:T(8,128)(2,1)} fusion(bf16[516,4096]{1,0:T(8,128)(2,1)} %constant_dynamic-update-slice_fusion.5, bf16[258,512]{1,0:T(8,128)(2,1)} %collective-permute-done.3, bf16[258,512]{1,0:T(8,128)(2,1)} %collective-permute-done.2), kind=kLoop, calls=%fused_computation.43 | loop fusion | flops 1056768 | bytes 1073152
  53.7 3.7 %collective-permute-start.8 = (bf16[258,512]{1,0:T(8,128)(2,1)S(1)}, bf16[258,512]{1,0:T(8,128)(2,1)S(1)}, u32[]{:S(2)}, u32[]{:S(2)}) collective-permute-start(bf16[258,512]{1,0:T(8,128)(2,1)S(1)} %slice.201), channel_id=1, source_target_pairs={{0,6},{2,0},{4,2},{6,4},{1,7},{3,1},{5,3},{7,5},{8,14},{10,8},{12,... | collective-permute-start | bytes 792584 | tf_op jit(solution)/shard_map/ppermute | solution.py:225
  57.5 1.9 %constant_dynamic-update-slice_fusion.4 = bf16[516,4096]{1,0:T(8,128)(2,1)} fusion(bf16[516,4096]{1,0:T(8,128)(2,1)} %maximum_dynamic-update-slice_fusion.1, bf16[516,512]{1,0:T(8,128)(2,1)} %collective-permute-done.4), kind=kLoop, calls=%fused_computation.81 | loop fusion | bytes 1064960
  59.4 0.9 constant_dynamic-update-slice_fusion.3
  60.3 0.9 constant_dynamic-update-slice_fusion.2
  61.4 3.8 %collective-permute-done.7 = bf16[258,512]{1,0:T(8,128)(2,1)S(1)} collective-permute-done((bf16[258,512]{1,0:T(8,128)(2,1)S(1)}, bf16[258,512]{1,0:T(8,128)(2,1)S(1)}, u32[]{:S(2)}, u32[]{:S(2)}) %collective-permute-start.7) | collective-permute-done | bytes 264224 | tf_op jit(solution)/shard_map/ppermute | solution.py:225
  65.2 1.0 maximum_dynamic-update-slice_fusion.x_ref
  66.1 0.8 slice.202.x_ref
  67.0 4.4 %shard_map.122 = f32[4,768]{1,0:T(4,128)S(1)} custom-call(s32[8]{0:T(128)S(1)} %pad_add_fusion.1.order_ref, bf16[4,4096]{1,0:T(4,128)(2,1)S(1)} %slice.202.x_ref, f32[1,4096]{1,0:T(1,128)S(1)} %bitcast.143, f32[1,4096]{1,0:T(1,128)S(1)} %bitcast.145, bf16[3,4096,256]{2,1,0:T(8,128)(2,1)} %bitcast.147), custom_call_target="tpu_custom_call" | custom-call | flops 25165824 | bytes 6336512 | tf_op jit(solution)/shard_map/pallas_call | solution.py:84
  72.0 5.6 %collective-permute-start.10 = (f32[4,257]{1,0:T(4,128)S(1)}, f32[4,257]{1,0:T(4,128)S(1)}, u32[]{:S(2)}, u32[]{:S(2)}) collective-permute-start(f32[4,257]{1,0:T(4,128)S(1)} %get-tuple-element.75), channel_id=1, source_target_pairs={{8,0},{16,8},{24,16},{32,24},{40,32},{48,40},{56,48},{64,56},{72,6... | collective-permute-start | bytes 12344 | tf_op jit(solution)/shard_map/ppermute | solution.py:262
  77.8 0.3 fusion.107
  78.1 0.2 fusion.44
  79.2 9.9 %shard_map.123 = f32[512,768]{1,0:T(8,128)S(1)} custom-call(s32[8]{0:T(128)S(1)} %pad_add_fusion.1.order_ref, bf16[516,4096]{1,0:T(8,128)(2,1)} %maximum_dynamic-update-slice_fusion.x_ref, f32[1,4096]{1,0:T(1,128)S(1)} %bitcast.144, f32[1,4096]{1,0:T(1,128)S(1)} %bitcast.146, bf16[3,4096,256]{2,1,0:T(8,128)(2,1)} %bitcast.148), custom_call_target="tpu_custom_call" | custom-call | flops 3221225472 | bytes 12058624 | tf_op jit(solution)/shard_map/pallas_call | solution.py:84
  89.2 0.8 reshape.536
  90.0 1.1 fusion.102
  91.2 0.9 slice.211
  92.2 2.4 %fusion.105 = (f32[4,2]{1,0:T(4,128)S(1)}, f32[4,2,1024]{2,1,0:T(2,128)S(1)}) fusion(bf16[8,2,1024,256]{3,2,1,0:T(8,128)(2,1)} %param.21, pred[256,2]{0,1:T(4,128)(4,1)S(1)} %bitcast.169, bf16[4,256]{1,0:T(4,128)(2,1)S(1)} %bitcast.166, pred[4,1024]{1,0:T(4,128)(4,1)S(1)} %get-tuple-element.95), kind=kOutput, calls=%fused_computation.183 | convolution fusion | flops 4220920 | bytes 2136608 | tf_op jit(solution)/shard_map/rkf,rfh->rhk/dot_general | solution.py:160
  94.7 0.2 fusion.67
  94.8 2.0 %fusion.2 = f32[4,2,256]{2,1,0:T(2,128)S(1)} fusion(bf16[8,2,1024,256]{3,2,1,0:T(8,128)(2,1)} %param.21, f32[4,2,1024]{2,1,0:T(2,128)S(1)} %get-tuple-element.90, pred[4,1024]{1,0:T(4,128)(4,1)S(1)} %get-tuple-element.95, f32[4,2]{1,0:T(4,128)S(1)} %get-tuple-element.89), kind=kOutput, calls=%fused_computation.6 | convolution fusion | flops 4218880 | bytes 2142240 | tf_op jit(solution)/shard_map/rhk,rkf->rhf/dot_general | solution.py:167
  96.9 2.4 %fusion.106 = (f32[4,2]{1,0:T(4,128)S(1)}, f32[4,2,1024]{2,1,0:T(2,128)S(1)}) fusion(bf16[8,2,1024,256]{3,2,1,0:T(8,128)(2,1)} %param.21, pred[256,2]{0,1:T(4,128)(4,1)S(1)} %bitcast.170, bf16[4,256]{1,0:T(4,128)(2,1)S(1)} %bitcast.167, pred[4,1024]{1,0:T(4,128)(4,1)S(1)} %get-tuple-element.96), kind=kOutput, calls=%fused_computation.184 | convolution fusion | flops 4220920 | bytes 2136608 | tf_op jit(solution)/shard_map/rkf,rfh->rhk/dot_general | solution.py:160
  99.3 2.0 %fusion.6 = f32[4,2,256]{2,1,0:T(2,128)S(1)} fusion(bf16[8,2,1024,256]{3,2,1,0:T(8,128)(2,1)} %param.21, f32[4,2,1024]{2,1,0:T(2,128)S(1)} %get-tuple-element.92, pred[4,1024]{1,0:T(4,128)(4,1)S(1)} %get-tuple-element.96, f32[4,2]{1,0:T(4,128)S(1)} %get-tuple-element.91), kind=kOutput, calls=%fused_computation.10 | convolution fusion | flops 4218880 | bytes 2142240 | tf_op jit(solution)/shard_map/rhk,rkf->rhf/dot_general | solution.py:167
  101.9 1.1 copy.269
  103.5 0.7 pad_maximum_fusion.1
  104.2 5.6 %collective-permute-start.12 = (f32[4,2,130]{0,1,2:T(2,128)}, f32[4,2,130]{0,1,2:T(2,128)S(1)}, u32[]{:S(2)}, u32[]{:S(2)}) collective-permute-start(f32[4,2,130]{0,1,2:T(2,128)} %pad_maximum_fusion.1), channel_id=1, source_target_pairs={{8,0},{16,8},{24,16},{32,24},{40,32},{48,40},{56,48},{64,56},{72,6... | collective-permute-start | bytes 12488 | tf_op jit(solution)/shard_map/ppermute | solution.py:268
  110.1 0.7 pad_maximum_fusion
  110.8 0.4 subtract_convert_fusion.1
  111.2 0.8 fusion.51
  112.1 2.3 %fusion.104 = (f32[2,512]{1,0:T(2,128)S(1)}, bf16[2,512,1024]{2,1,0:T(8,128)(2,1)S(1)}) fusion(f32[2,512,1024]{2,1,0:T(8,128)S(1)} %fusion.51, pred[512,1024]{1,0:T(8,128)(4,1)S(1)} %copy-done.4), kind=kOutput, calls=%fused_computation.182 | output fusion | flops 8389631 | bytes 6819840 | tf_op jit(solution)/shard_map/while/body/eval_jaxpr/sub | solution.py:125
  114.4 0.8 fusion.25
  115.3 0.8 copy.253
  116.2 3.1 %collective-permute-done.11 = f32[4,2,130]{0,1,2:T(2,128)S(1)} collective-permute-done((f32[4,2,130]{0,1,2:T(2,128)}, f32[4,2,130]{0,1,2:T(2,128)S(1)}, u32[]{:S(2)}, u32[]{:S(2)}) %collective-permute-start.11) | collective-permute-done | bytes 4192 | tf_op jit(solution)/shard_map/ppermute | solution.py:268
  120.1 0.7 copy.252
  (115 shorter events, 5.0 us)
Async XLA Ops:
  0.6 15.0 %copy-start.3 = (bf16[4,2,256,256]{3,2,1,0:T(8,128)(2,1)S(1)}, bf16[4,2,256,256]{3,2,1,0:T(8,128)(2,1)}, u32[]{:S(2)}) copy-start(bf16[4,2,256,256]{3,2,1,0:T(8,128)(2,1)} %param.19) | copy-start | bytes 3145732
  0.6 41.7 %copy-start.8 = (f32[4096]{0:T(1024)S(1)}, f32[4096]{0:T(1024)}, u32[]{:S(2)}) copy-start(f32[4096]{0:T(1024)} %param.13) | copy-start | bytes 49156
  0.7 42.3 %copy-start.9 = (f32[4096]{0:T(1024)S(1)}, f32[4096]{0:T(1024)}, u32[]{:S(2)}) copy-start(f32[4096]{0:T(1024)} %param.14) | copy-start | bytes 49156
  4.0 36.0 %collective-permute-start = (bf16[516,512]{1,0:T(8,128)(2,1)S(1)}, bf16[516,512]{1,0:T(8,128)(2,1)S(1)}, u32[]{:S(2)}, u32[]{:S(2)}) collective-permute-start(bf16[516,512]{1,0:T(8,128)(2,1)S(1)} %get-tuple-element.77), channel_id=1, source_target_pairs={{0,2},{2,4},{4,6},{6,0},{1,3},{3,5},{5,7},{7,1},{8,10},{10,12},{12... | collective-permute-start | bytes 1585160 | tf_op jit(solution)/shard_map/ppermute | solution.py:222
  5.6 33.1 %collective-permute-start.1 = (bf16[516,512]{1,0:T(8,128)(2,1)S(1)}, bf16[516,512]{1,0:T(8,128)(2,1)S(1)}, u32[]{:S(2)}, u32[]{:S(2)}) collective-permute-start(bf16[516,512]{1,0:T(8,128)(2,1)S(1)} %get-tuple-element.77), channel_id=1, source_target_pairs={{0,6},{2,0},{4,2},{6,4},{1,7},{3,1},{5,3},{7,5},{8,14},{10,8},{12,... | collective-permute-start | bytes 1585160 | tf_op jit(solution)/shard_map/ppermute | solution.py:223
  7.3 28.2 %collective-permute-start.4 = (bf16[516,512]{1,0:T(8,128)(2,1)S(1)}, bf16[516,512]{1,0:T(8,128)(2,1)}, u32[]{:S(2)}, u32[]{:S(2)}) collective-permute-start(bf16[516,512]{1,0:T(8,128)(2,1)S(1)} %get-tuple-element.77), channel_id=1, source_target_pairs={{0,1},{1,0},{2,3},{3,2},{4,5},{5,4},{6,7},{7,6},{8,9},{9,8},{10,11... | collective-permute-start | bytes 1585160 | tf_op jit(solution)/shard_map/ppermute | solution.py:229
  10.4 31.8 %copy-start.13 = (pred[2,2]{1,0:T(4,128)(4,1)}, pred[2,2]{1,0:T(4,128)(4,1)S(1)}, u32[]{:S(2)}) copy-start(pred[2,2]{1,0:T(4,128)(4,1)S(1)} %iota_compare_fusion.5) | copy-start | bytes 16
  35.5 21.9 %collective-permute-start.5 = (bf16[516,512]{1,0:T(8,128)(2,1)}, bf16[516,512]{1,0:T(8,128)(2,1)S(1)}, u32[]{:S(2)}, u32[]{:S(2)}) collective-permute-start(bf16[516,512]{1,0:T(8,128)(2,1)} %collective-permute-done.4), channel_id=1, source_target_pairs={{0,2},{2,4},{4,6},{6,0},{1,3},{3,5},{5,7},{7,1},{8,10},{10,12},{12... | collective-permute-start | bytes 1585160 | tf_op jit(solution)/shard_map/ppermute | solution.py:222
  35.8 17.8 %collective-permute-start.6 = (bf16[516,512]{1,0:T(8,128)(2,1)}, bf16[516,512]{1,0:T(8,128)(2,1)S(1)}, u32[]{:S(2)}, u32[]{:S(2)}) collective-permute-start(bf16[516,512]{1,0:T(8,128)(2,1)} %collective-permute-done.4), channel_id=1, source_target_pairs={{0,6},{2,0},{4,2},{6,4},{1,7},{3,1},{5,3},{7,5},{8,14},{10,8},{12,... | collective-permute-start | bytes 1585160 | tf_op jit(solution)/shard_map/ppermute | solution.py:223
  39.5 12.1 %collective-permute-start.3 = (bf16[258,512]{1,0:T(8,128)(2,1)}, bf16[258,512]{1,0:T(8,128)(2,1)}, u32[]{:S(2)}, u32[]{:S(2)}) collective-permute-start(bf16[258,512]{1,0:T(8,128)(2,1)} %slice.199), channel_id=1, source_target_pairs={{0,6},{2,0},{4,2},{6,4},{1,7},{3,1},{5,3},{7,5},{8,14},{10,8},{12,... | collective-permute-start | bytes 792584 | tf_op jit(solution)/shard_map/ppermute | solution.py:225
  40.7 10.9 %collective-permute-start.2 = (bf16[258,512]{1,0:T(8,128)(2,1)}, bf16[258,512]{1,0:T(8,128)(2,1)}, u32[]{:S(2)}, u32[]{:S(2)}) collective-permute-start(bf16[258,512]{1,0:T(8,128)(2,1)} %slice.198), channel_id=1, source_target_pairs={{0,2},{2,4},{4,6},{6,0},{1,3},{3,5},{5,7},{7,1},{8,10},{10,12},{12... | collective-permute-start | bytes 792584 | tf_op jit(solution)/shard_map/ppermute | solution.py:225
  53.7 7.7 %collective-permute-start.8 = (bf16[258,512]{1,0:T(8,128)(2,1)S(1)}, bf16[258,512]{1,0:T(8,128)(2,1)S(1)}, u32[]{:S(2)}, u32[]{:S(2)}) collective-permute-start(bf16[258,512]{1,0:T(8,128)(2,1)S(1)} %slice.201), channel_id=1, source_target_pairs={{0,6},{2,0},{4,2},{6,4},{1,7},{3,1},{5,3},{7,5},{8,14},{10,8},{12,... | collective-permute-start | bytes 792584 | tf_op jit(solution)/shard_map/ppermute | solution.py:225
  57.4 7.7 %collective-permute-start.7 = (bf16[258,512]{1,0:T(8,128)(2,1)S(1)}, bf16[258,512]{1,0:T(8,128)(2,1)S(1)}, u32[]{:S(2)}, u32[]{:S(2)}) collective-permute-start(bf16[258,512]{1,0:T(8,128)(2,1)S(1)} %slice.200), channel_id=1, source_target_pairs={{0,2},{2,4},{4,6},{6,0},{1,3},{3,5},{5,7},{7,1},{8,10},{10,12},{12... | collective-permute-start | bytes 792584 | tf_op jit(solution)/shard_map/ppermute | solution.py:225
  60.3 11.4 %copy-start.10 = (f32[4,16]{1,0:T(4,128)S(1)}, f32[4,16]{1,0:T(4,128)}, u32[]{:S(2)}) copy-start(f32[4,16]{1,0:T(4,128)} %get-tuple-element.86) | copy-start | bytes 772
  60.3 11.5 %copy-start.11 = (f32[4,1]{1,0:T(4,128)S(1)}, f32[4,1]{1,0:T(4,128)}, u32[]{:S(2)}) copy-start(f32[4,1]{1,0:T(4,128)} %get-tuple-element.83) | copy-start | bytes 52
  60.3 11.5 %copy-start.12 = (f32[4,1]{1,0:T(4,128)S(1)}, f32[4,1]{1,0:T(4,128)}, u32[]{:S(2)}) copy-start(f32[4,1]{1,0:T(4,128)} %get-tuple-element.84) | copy-start | bytes 52
  60.3 17.4 %copy-start.6 = (bf16[4,256,256]{2,1,0:T(8,128)(2,1)S(1)}, bf16[4,256,256]{2,1,0:T(8,128)(2,1)}, u32[]{:S(2)}) copy-start(bf16[4,256,256]{2,1,0:T(8,128)(2,1)} %get-tuple-element.53) | copy-start | bytes 1572868
  61.2 16.9 %copy-start.5 = (bf16[4,256,256]{2,1,0:T(8,128)(2,1)S(1)}, bf16[4,256,256]{2,1,0:T(8,128)(2,1)}, u32[]{:S(2)}) copy-start(bf16[4,256,256]{2,1,0:T(8,128)(2,1)} %get-tuple-element.54) | copy-start | bytes 1572868
  71.9 7.0 %collective-permute-start.9 = (f32[4,257]{1,0:T(4,128)S(1)}, f32[4,257]{1,0:T(4,128)S(1)}, u32[]{:S(2)}, u32[]{:S(2)}) collective-permute-start(f32[4,257]{1,0:T(4,128)S(1)} %get-tuple-element.76), channel_id=1, source_target_pairs={{0,8},{8,16},{16,24},{24,32},{32,40},{40,48},{48,56},{56,64},{64,7... | collective-permute-start | bytes 12344 | tf_op jit(solution)/shard_map/ppermute | solution.py:262
  72.0 7.0 %collective-permute-start.10 = (f32[4,257]{1,0:T(4,128)S(1)}, f32[4,257]{1,0:T(4,128)S(1)}, u32[]{:S(2)}, u32[]{:S(2)}) collective-permute-start(f32[4,257]{1,0:T(4,128)S(1)} %get-tuple-element.75), channel_id=1, source_target_pairs={{8,0},{16,8},{24,16},{32,24},{40,32},{48,40},{56,48},{64,56},{72,6... | collective-permute-start | bytes 12344 | tf_op jit(solution)/shard_map/ppermute | solution.py:262
  92.2 9.4 %copy-start = (f32[512,1,2,128]{3,2,1,0:T(2,128)S(1)}, f32[512,1,2,128]{3,2,1,0:T(2,128)}, u32[]{:S(2)}) copy-start(f32[512,1,2,128]{3,2,1,0:T(2,128)} %get-tuple-element.52) | copy-start | bytes 1572868
  96.9 6.3 %copy-start.14 = (pred[2,2]{1,0:T(4,128)(4,1)S(1)}, pred[2,2]{1,0:T(4,128)(4,1)}, u32[]{:S(2)}) copy-start(pred[2,2]{1,0:T(4,128)(4,1)} %copy-done.13) | copy-start | bytes 16
  96.9 13.9 %copy-start.1 = (f32[512,16]{1,0:T(8,128)S(1)}, f32[512,16]{1,0:T(8,128)}, u32[]{:S(2)}) copy-start(f32[512,16]{1,0:T(8,128)} %copy.217) | copy-start | bytes 98308
  101.3 9.9 %copy-start.2 = (bf16[512,2,128]{2,0,1:T(8,128)(2,1)S(1)}, bf16[512,2,128]{2,0,1:T(8,128)(2,1)}, u32[]{:S(2)}) copy-start(bf16[512,2,128]{2,0,1:T(8,128)(2,1)} %copy.221) | copy-start | bytes 786436
  104.2 11.9 %collective-permute-start.12 = (f32[4,2,130]{0,1,2:T(2,128)}, f32[4,2,130]{0,1,2:T(2,128)S(1)}, u32[]{:S(2)}, u32[]{:S(2)}) collective-permute-start(f32[4,2,130]{0,1,2:T(2,128)} %pad_maximum_fusion.1), channel_id=1, source_target_pairs={{8,0},{16,8},{24,16},{32,24},{40,32},{48,40},{56,48},{64,56},{72,6... | collective-permute-start | bytes 12488 | tf_op jit(solution)/shard_map/ppermute | solution.py:268
  110.8 1.3 %copy-start.4 = (pred[512,1024]{1,0:T(8,128)(4,1)S(1)}, pred[512,1024]{1,0:T(8,128)(4,1)}, u32[]{:S(2)}) copy-start(pred[512,1024]{1,0:T(8,128)(4,1)} %pad_add_fusion) | copy-start | bytes 1572868
  110.8 8.5 %collective-permute-start.11 = (f32[4,2,130]{0,1,2:T(2,128)}, f32[4,2,130]{0,1,2:T(2,128)S(1)}, u32[]{:S(2)}, u32[]{:S(2)}) collective-permute-start(f32[4,2,130]{0,1,2:T(2,128)} %pad_maximum_fusion), channel_id=1, source_target_pairs={{0,8},{8,16},{16,24},{24,32},{32,40},{40,48},{48,56},{56,64},{64,7... | collective-permute-start | bytes 12488 | tf_op jit(solution)/shard_map/ppermute | solution.py:268
  112.1 2.4 %copy-start.7 = (bf16[1,1,512,256]{2,3,1,0:T(8,128)(2,1)S(1)}, bf16[1,1,512,256]{2,3,1,0:T(8,128)(2,1)}, u32[]{:S(2)}) copy-start(bf16[1,1,512,256]{2,3,1,0:T(8,128)(2,1)} %copy.213) | copy-start | bytes 786436
